TPU v7x, 32 devices: a whole 2x2x4 slice. The times are simulated.
32 devices in a mesh: blk: 2 (over y), req: 16 (over z, x, core).
Axes of the slice: x: 2, y: 2, z: 4, core: 2. Of those that a mesh axis runs over, the one named last changes fastest.
Arguments:
- hidden: bfloat16 [6144, 8192], P('req', 'blk'), may hold values from -120 to 120
- input_norm_gain: float32 [8192], replicated, may hold values from 0.1 to 1.9
- query_weight: bfloat16 [8192, 2048], P('req', 'blk')
- keyvalue_weight: bfloat16 [8192, 512], P('req', 'blk')
- adapter_down: bfloat16 [16, 3, 16, 8192], P('req', None, None, 'blk'), may hold values from -0.0625 to 0.0625
- adapter_up_query: bfloat16 [16, 16, 2048], P('req', None, 'blk'), may hold values from -1.5 to 1.5
- adapter_up_keyvalue: bfloat16 [16, 16, 512], P('req', None, 'blk'), may hold values from -1.5 to 1.5
- packed_lengths: int32 [16, 4], P('req'), may hold values from 1 to 192, 384 in all within a row
- prompt_adapter: int32 [16, 4], P('req'), may hold values from 0 to 15
Outputs:
- context: bfloat16 [6144, 2048], P('req', 'blk')
- key_cache: bfloat16 [6144, 256], P('req', 'blk')
- value_cache: bfloat16 [6144, 256], P('req', 'blk')
Inputs may be any that keep to these rules, and one draw needn't show every extreme that they name: `packed_lengths`: each row sums to 384; the longest prompt of the whole draw has 192 tokens.
All inputs are finite; a program needn't handle non-finite values.
Results may differ from a plain program's by a relative error of at most 0.012.
The roundings to bfloat16 on the way count: a program that leaves them out, or rounds other values in their place, can miss the bound.
Values may be sent and summed in bfloat16 or wider, within the bound.
No kernel may reach another device: no remote copies, remote signals or barrier semaphores. Data moves between devices by JAX's collectives and lax.ppermute only.
A program may use at most 128 MiB of HBM per device.

v0:
```python
import math

import jax
import jax.numpy as jnp
from jax import lax
from jax.sharding import PartitionSpec as P

HEAD_WIDTH = 128
QUERY_LOCAL = 8
KEYVALUE_LOCAL = 1


epsilon = 1e-05
adapter_scale = 2.0
rope_base = 10000.0


def apply_rotation(vectors, cosine_table, sine_table):
    half_size = vectors.shape[-1] // 2
    first_half = vectors[..., :half_size]
    second_half = vectors[..., half_size:]
    turned = jnp.concatenate([-second_half, first_half], axis=-1)
    return vectors * cosine_table + turned * sine_table


def layout(lengths, count):
    slot_index = jnp.arange(count, dtype=jnp.int32)
    prompt_ends = jnp.cumsum(lengths)
    prompt_starts = prompt_ends - lengths
    member = (slot_index[:, None] >= prompt_starts[None, :]) & (
        slot_index[:, None] < prompt_ends[None, :]
    )
    position = jnp.sum(jnp.where(member, slot_index[:, None] - prompt_starts[None, :], 0), axis=1)
    owner = jnp.sum((slot_index[:, None] >= prompt_ends[None, :]).astype(jnp.int32), axis=1)
    return (member.astype(jnp.float32), position, owner, slot_index)


def rope_tables(position, head_size):
    frequency = rope_base ** (-(jnp.arange(head_size // 2, dtype=jnp.float32) * 2.0 / head_size))
    angles = position.astype(jnp.float32)[:, None] * frequency[None, :]
    cosine_table = jnp.cos(angles)
    sine_table = jnp.sin(angles)
    return (
        jnp.concatenate([cosine_table, cosine_table], 1)[:, None, :],
        jnp.concatenate([sine_table, sine_table], 1)[:, None, :],
    )


def shards(
    hidden,
    input_norm_gain,
    query_weight,
    keyvalue_weight,
    adapter_down,
    adapter_up_query,
    adapter_up_keyvalue,
    packed_lengths,
    prompt_adapter,
):
    row_number, feature_cols = hidden.shape
    full_width = feature_cols * lax.axis_size("blk")
    offset = lax.axis_index("blk") * feature_cols
    values = hidden.astype(jnp.float32)
    gain_part = lax.dynamic_slice_in_dim(input_norm_gain, offset, feature_cols, 0)
    squares = lax.psum(jnp.sum(values * values, axis=1), "blk")
    factor = lax.rsqrt(squares / full_width + epsilon)
    normed_part = (values * factor[:, None] * gain_part[None, :]).astype(jnp.bfloat16)
    normed = lax.all_gather(normed_part, "blk", axis=1, tiled=True)
    query_cols = query_weight.shape[1]

    def add_rows(weight_piece):
        return jnp.dot(normed, weight_piece, preferred_element_type=jnp.float32)

    query_plain = add_rows(lax.all_gather(query_weight, "req", axis=0, tiled=True))
    base_pair = add_rows(lax.all_gather(keyvalue_weight, "req", axis=0, tiled=True))
    down_all, up_query_all, up_pair_all = (
        lax.all_gather(adapter_down, "req", axis=0, tiled=True),
        lax.all_gather(adapter_up_query, "req", axis=0, tiled=True),
        lax.all_gather(adapter_up_keyvalue, "req", axis=0, tiled=True),
    )
    adapter_count = down_all.shape[0]
    lengths = packed_lengths[0]
    member, position, owner, slot_index = layout(lengths, row_number)
    prompt_count = lengths.shape[0]
    picked_adapter = (
        prompt_adapter[0][:, None] == jnp.arange(adapter_count, dtype=jnp.int32)[None, :]
    ).astype(jnp.bfloat16)
    down_selected = jnp.einsum(
        "pa,ajrd->pjrd", picked_adapter, down_all, preferred_element_type=jnp.float32
    ).astype(jnp.bfloat16)
    rank_size = down_selected.shape[2]
    partial_value = lax.dot_general(
        normed_part,
        down_selected.reshape(prompt_count * 3 * rank_size, feature_cols),
        (((1,), (1,)), ((), ())),
        preferred_element_type=jnp.float32,
    )
    partial_value = partial_value.reshape(row_number, prompt_count, 3, rank_size)
    masked = jnp.sum(partial_value * member[:, :, None, None], axis=1).reshape(
        row_number, 3 * rank_size
    )
    low_rank = lax.psum(masked, "blk").reshape(row_number, 3, rank_size).astype(jnp.bfloat16)
    low_float = low_rank.astype(jnp.float32)

    def spread(column):
        return (
            (member[:, :, None] * low_float[:, None, column, :])
            .astype(jnp.bfloat16)
            .reshape(row_number, prompt_count * rank_size)
        )

    up_query_selected = jnp.einsum(
        "pa,arc->prc", picked_adapter, up_query_all, preferred_element_type=jnp.float32
    ).astype(jnp.bfloat16)
    up_keyvalue_selected = jnp.einsum(
        "pa,arc->prc", picked_adapter, up_pair_all, preferred_element_type=jnp.float32
    ).astype(jnp.bfloat16)
    up_keyvalue_selected = up_keyvalue_selected.reshape(
        prompt_count, rank_size, KEYVALUE_LOCAL, 2, HEAD_WIDTH
    )
    query_update = jnp.dot(
        spread(0),
        up_query_selected.reshape(prompt_count * rank_size, query_cols),
        preferred_element_type=jnp.float32,
    )
    key_update = jnp.dot(
        spread(1),
        up_keyvalue_selected[:, :, :, 0].reshape(
            prompt_count * rank_size, KEYVALUE_LOCAL * HEAD_WIDTH
        ),
        preferred_element_type=jnp.float32,
    )
    value_update = jnp.dot(
        spread(2),
        up_keyvalue_selected[:, :, :, 1].reshape(
            prompt_count * rank_size, KEYVALUE_LOCAL * HEAD_WIDTH
        ),
        preferred_element_type=jnp.float32,
    )
    cosine_table, sine_table = rope_tables(position, HEAD_WIDTH)
    query_complete = (query_plain + adapter_scale * query_update).reshape(
        row_number, QUERY_LOCAL * KEYVALUE_LOCAL, HEAD_WIDTH
    )
    query_states = apply_rotation(query_complete, cosine_table, sine_table).astype(jnp.bfloat16)
    keyvalue_plain = base_pair.reshape(row_number, KEYVALUE_LOCAL, 2, HEAD_WIDTH)
    key_vectors = apply_rotation(
        keyvalue_plain[:, :, 0]
        + adapter_scale * key_update.reshape(row_number, KEYVALUE_LOCAL, HEAD_WIDTH),
        cosine_table,
        sine_table,
    ).astype(jnp.bfloat16)
    value_vectors = (
        keyvalue_plain[:, :, 1]
        + adapter_scale * value_update.reshape(row_number, KEYVALUE_LOCAL, HEAD_WIDTH)
    ).astype(jnp.bfloat16)
    grouped = query_states.reshape(row_number, KEYVALUE_LOCAL, QUERY_LOCAL, HEAD_WIDTH)
    scores = jnp.einsum(
        "tkgc,skc->kgts", grouped, key_vectors, preferred_element_type=jnp.float32
    ) / math.sqrt(HEAD_WIDTH)
    allowed = (owner[:, None] == owner[None, :]) & (slot_index[None, :] <= slot_index[:, None])
    scores = jnp.where(allowed[None, None], scores, -1e30)
    row_max = jnp.max(scores, axis=-1, keepdims=True)
    exponent = jnp.exp(scores - row_max)
    attend = (exponent / jnp.sum(exponent, axis=-1, keepdims=True)).astype(jnp.bfloat16)
    context = jnp.einsum(
        "kgts,skc->tkgc", attend, value_vectors, preferred_element_type=jnp.float32
    ).astype(jnp.bfloat16)
    return (
        context.reshape(row_number, KEYVALUE_LOCAL * QUERY_LOCAL * HEAD_WIDTH),
        key_vectors.reshape(row_number, KEYVALUE_LOCAL * HEAD_WIDTH),
        value_vectors.reshape(row_number, KEYVALUE_LOCAL * HEAD_WIDTH),
    )


def solution(mesh):
    in_specs = (
        P("req", "blk"),
        P(),
        P("req", "blk"),
        P("req", "blk"),
        P("req", None, None, "blk"),
        P("req", None, "blk"),
        P("req", None, "blk"),
        P("req", None),
        P("req", None),
    )
    out_specs = (P("req", "blk"), P("req", "blk"), P("req", "blk"))
    return jax.shard_map(shards, mesh=mesh, in_specs=in_specs, out_specs=out_specs, check_vma=False)
```

profile of v0, /device:TPU:0, one launch (start us, length us, event | category | flops | bytes accessed | tf_op | source)
XLA Modules:
  0.0 369.3 jit_solution(2465594138343050655)
XLA Ops:
  7.2 2.7 fusion
  10.0 5.9 %psum.14 = f32[384]{0:T(512)S(1)} all-reduce(f32[384]{0:T(512)S(1)} %fusion), channel_id=1, replica_groups=mesh['blk'=2,'req'=16] {'blk'}, use_global_device_ids=true, to_apply=%region_1.0 | all-reduce | flops 384 | bytes 3072 | tf_op jit(solution)/shard_map/psum | solution.py:65
  15.9 2.6 fusion.2
  18.6 0.7 all-gather.7.cloned.1.call-update
  20.8 22.5 %all_gather.21 = bf16[16,16,256]{2,1,0:T(8,128)(2,1)S(1)} all-gather(bf16[1,16,256]{2,1,0:T(8,128)(2,1)S(1)} %copy-done.6), channel_id=1, replica_groups=mesh['blk'=2,'req'=16] {'req'}, dimensions={0}, use_global_device_ids=true | all-gather | bytes 139264 | tf_op jit(solution)/shard_map/all_gather | solution.py:79
  43.9 1.5 multiply_cosine_fusion
  45.4 19.0 %all_gather.23 = bf16[16,16,1024]{2,1,0:T(8,128)(2,1)S(1)} all-gather(bf16[1,16,1024]{2,1,0:T(8,128)(2,1)S(1)} %copy-done.5), channel_id=1, replica_groups=mesh['blk'=2,'req'=16] {'req'}, dimensions={0}, use_global_device_ids=true | all-gather | bytes 557056 | tf_op jit(solution)/shard_map/all_gather | solution.py:78
  64.5 1.1 convolution_convert_fusion
  65.5 35.3 %all-gather.5.cloned.1.call-done = bf16[384,8192]{1,0:T(8,128)(2,1)} async-done(((bf16[384,4096]{1,0:T(8,128)(2,1)}), bf16[384,8192]{1,0:T(8,128)(2,1)}) %all-gather.5.cloned.1.call-update) | async-done | bytes 6291472 | tf_op jit(solution)/shard_map/all_gather | solution.py:68
  100.9 52.9 %all-gather.7.cloned.1.call-done = bf16[8192,256]{1,0:T(8,128)(2,1)} async-done(((bf16[512,256]{1,0:T(8,128)(2,1)}), bf16[8192,256]{1,0:T(8,128)(2,1)}) %all-gather.7.cloned.1.call-update) | async-done | bytes 4194320 | tf_op jit(solution)/shard_map/all_gather | solution.py:75
  153.8 6.4 %fusion.65 = f32[384,256]{0,1:T(8,128)S(1)} fusion(bf16[384,8192]{1,0:T(8,128)(2,1)} %all-gather.5.cloned.1.call-done, bf16[8192,256]{1,0:T(8,128)(2,1)} %all-gather.7.cloned.1.call-done), kind=kOutput, calls=%fused_computation.87 | convolution fusion | flops 1610612736 | bytes 10878976 | tf_op jit(solution)/shard_map/dot_general | solution.py:72
  160.3 0.8 copy.50
  161.1 55.3 %all-gather.9.cloned.1.call-done = bf16[16,3,16,4096]{3,2,1,0:T(8,128)(2,1)} async-done(((bf16[1,3,16,4096]{3,2,1,0:T(8,128)(2,1)}), bf16[16,3,16,4096]{3,2,1,0:T(8,128)(2,1)}) %all-gather.9.cloned.1.call-update) | async-done | bytes 6291472 | tf_op jit(solution)/shard_map/all_gather | solution.py:77
  216.4 9.7 %fusion.5 = bf16[4,3,16,4096]{3,0,2,1:T(4,128)(2,1)S(1)} fusion(bf16[16,3,16,4096]{3,2,1,0:T(8,128)(2,1)} %all-gather.9.cloned.1.call-done, s32[4]{0:T(128)S(1)} %bitcast.141), kind=kOutput, calls=%fused_computation.7 | convolution fusion | flops 25952320 | bytes 7864336 | tf_op jit(solution)/shard_map/pa,ajrd->pjrd/dot_general | solution.py:88
  226.2 2.2 fusion.28
  228.4 9.9 %psum.15 = bf16[384,48]{0,1:T(8,128)(2,1)S(1)} all-reduce(f32[384,48]{0,1:T(8,128)} %bitcast.136), channel_id=1, replica_groups=mesh['blk'=2,'req'=16] {'blk'}, use_global_device_ids=true, to_apply=%region_4.5 | all-reduce | flops 18432 | bytes 110592 | tf_op jit(solution)/shard_map/psum | solution.py:102
  238.4 1.1 fusion.33
  239.9 1.5 fusion.42
  241.7 102.2 %all-gather.11.cloned.1.call-done = bf16[8192,1024]{1,0:T(8,128)(2,1)} async-done(((bf16[512,1024]{1,0:T(8,128)(2,1)}), bf16[8192,1024]{1,0:T(8,128)(2,1)}) %all-gather.11.cloned.1.call-update) | async-done | bytes 16777232 | tf_op jit(solution)/shard_map/all_gather | solution.py:74
  344.0 12.0 %fusion.16 = f32[384,1024]{1,0:T(8,128)S(1)} fusion(f32[384,1024,1]{1,0,2:T(8,128)S(1)} %fusion.43, bf16[384,8192]{1,0:T(8,128)(2,1)} %all-gather.5.cloned.1.call-done, bf16[8192,1024]{1,0:T(8,128)(2,1)} %all-gather.11.cloned.1.call-done), kind=kOutput, calls=%fused_computation.24 | convolution fusion | flops 6443237376 | bytes 26214400 | tf_op jit(solution)/shard_map/dot_general | solution.py:72
  357.6 1.4 fusion.9
  359.0 1.0 fusion.8
  360.0 1.6 fusion.18
  361.6 1.2 copy.43
  (53 shorter events, 4.6 us)
Async XLA Ops:
  7.2 8.7 %copy-start = (bf16[384,4096]{1,0:T(8,128)(2,1)S(1)}, bf16[384,4096]{1,0:T(8,128)(2,1)}, u32[]{:S(2)}) copy-start(bf16[384,4096]{1,0:T(8,128)(2,1)} %param.9) | copy-start | bytes 9437188
  7.2 8.7 %copy-start.7 = (f32[8192]{0:T(1024)S(1)}, f32[8192]{0:T(1024)}, u32[]{:S(2)}) copy-start(f32[8192]{0:T(1024)} %param.10) | copy-start | bytes 98308
  7.2 93.7 %all-gather.5.cloned.1.call-start = ((), (), s32[]{:S(2)}) async-start(), calls=%async_computation | async-start | bytes 9437184 | tf_op jit(solution)/shard_map/all_gather | solution.py:68
  18.5 2.1 copy-start.9
  18.5 2.3 copy-start.6
  18.5 24.8 %copy-start.8 = (s32[1,4]{1,0:T(1,128)S(1)}, s32[1,4]{1,0:T(1,128)}, u32[]{:S(2)}) copy-start(s32[1,4]{1,0:T(1,128)} %param.17) | copy-start | bytes 52
  18.5 26.9 %copy-start.5 = (bf16[1,16,1024]{2,1,0:T(8,128)(2,1)S(1)}, bf16[1,16,1024]{2,1,0:T(8,128)(2,1)}, u32[]{:S(2)}) copy-start(bf16[1,16,1024]{2,1,0:T(8,128)(2,1)} %param.14) | copy-start | bytes 98308
  18.5 135.2 %all-gather.7.cloned.1.call-start = ((), (), s32[]{:S(2)}) async-start(), calls=%async_computation.1 | async-start | bytes 4456448 | tf_op jit(solution)/shard_map/all_gather | solution.py:75
  19.3 197.1 %all-gather.9.cloned.1.call-start = ((), (), s32[]{:S(2)}) async-start(), calls=%async_computation.2 | async-start | bytes 6684672 | tf_op jit(solution)/shard_map/all_gather | solution.py:77
  20.0 323.9 %all-gather.11.cloned.1.call-start = ((), (), s32[]{:S(2)}) async-start(), calls=%async_computation.3 | async-start | bytes 17825792 | tf_op jit(solution)/shard_map/all_gather | solution.py:74
  161.1 65.0 %copy-start.1 = (bf16[384,4096]{1,0:T(8,128)(2,1)S(1)}, bf16[384,4096]{1,0:T(8,128)(2,1)}, u32[]{:S(2)}) copy-start(bf16[384,4096]{1,0:T(8,128)(2,1)} %fusion.2) | copy-start | bytes 9437188
  228.4 13.0 %copy-start.3 = (bf16[4,16,1024]{2,0,1:T(4,128)(2,1)S(1)}, bf16[4,16,1024]{2,0,1:T(4,128)(2,1)}, u32[]{:S(2)}) copy-start(bf16[4,16,1024]{2,0,1:T(4,128)(2,1)} %convolution_convert_fusion) | copy-start | bytes 393220
  239.5 120.5 %copy-start.4 = (bf16[384,128]{1,0:T(8,128)(2,1)}, bf16[384,128]{1,0:T(8,128)(2,1)S(1)}, u32[]{:S(2)}) copy-start(bf16[384,128]{1,0:T(8,128)(2,1)S(1)} %fusion.33) | copy-start | bytes 294916
  241.3 116.2 %copy-start.2 = (bf16[384,128]{1,0:T(8,128)(2,1)}, bf16[384,128]{1,0:T(8,128)(2,1)S(1)}, u32[]{:S(2)}) copy-start(bf16[384,128]{1,0:T(8,128)(2,1)S(1)} %get-tuple-element.18) | copy-start | bytes 294916
Sparse Core Ops, SparseCore 0:
  18.7 82.1 all-gather.4
  103.0 50.7 all-gather.6
  156.1 60.3 all-gather.8
  218.5 125.4 all-gather.10
where the time goes:
time: 370 us; the launch traced here: 369 us
  waiting for transfers between devices  248 us (67%)
  blocking collectives  57.3 us (15%)
  matrix products  36.4 us (10%)
  between operations  14 us (4%)
  other arithmetic  11 us (3%)
    all_gather x1, waiting for transfers between devices, shards(): lax.all_gather(query_weight, 'req', axis=0, tiled=True)  102 us
    all_gather x1, waiting for transfers between devices, shards(): lax.all_gather(adapter_down, 'req', axis=0, tiled=True)  55.3 us
    all_gather x1, waiting for transfers between devices, shards(): lax.all_gather(keyvalue_weight, 'req', axis=0, tiled=True)  52.9 us
    all_gather x1, waiting for transfers between devices, shards(): normed = lax.all_gather(normed_part, 'blk', axis=1, tiled=True)  35.3 us
    all_gather x1, blocking collectives, shards(): lax.all_gather(adapter_up_keyvalue, 'req', axis=0, tiled=True)  22.5 us
    all_gather x1, blocking collectives, shards(): lax.all_gather(adapter_up_query, 'req', axis=0, tiled=True)  19 us
    dot_general x2, matrix products, add_rows(): return jnp.dot(normed, weight_piece, preferred_element_type=jnp.float32)  18.4 us
    psum x1, blocking collectives, shards(): lax.psum(masked, 'blk').reshape(row_number, 3, rank_size)  9.92 us
  transfers between devices with their start and end apart: 4, of which 4 were waited for; matrix products, arithmetic and copies ran while one was open for 7% of the time, Pallas kernels for 0%

commit v1 on v0

--- a/solution.py
+++ b/solution.py
@@ -3,6 +3,7 @@
 import jax
 import jax.numpy as jnp
 from jax import lax
+from jax.sharding import Mesh
 from jax.sharding import PartitionSpec as P
 
 HEAD_WIDTH = 128
@@ -44,6 +45,30 @@
         jnp.concatenate([cosine_table, cosine_table], 1)[:, None, :],
         jnp.concatenate([sine_table, sine_table], 1)[:, None, :],
     )
+
+
+def gather_blk(piece, n_blk):
+    me = lax.axis_index("blk")
+    received = [piece]
+    for shift in range(1, n_blk):
+        pairs = [(i, (i + shift) % n_blk) for i in range(n_blk)]
+        received.append(lax.ppermute(piece, "blk", pairs))
+    ordered = []
+    for source in range(n_blk):
+        pick = (me - source) % n_blk
+        ordered.append(lax.switch(pick, [lambda s=s: received[s] for s in range(n_blk)]))
+    return ordered
+
+
+def sum_blk(piece, n_blk):
+    if n_blk == 2:
+        return piece + lax.ppermute(piece, "blk", [(0, 1), (1, 0)])
+    return lax.psum(piece, "blk")
+
+
+def gather_req(piece):
+    stacked = lax.all_gather(piece, "chip", axis=0, tiled=False)
+    return lax.all_gather(stacked, "core", axis=0, tiled=False)
 
 
 def shards(
@@ -57,37 +82,67 @@
     packed_lengths,
     prompt_adapter,
 ):
+    n_blk = lax.axis_size("blk")
+    n_lo = lax.axis_size("core")
+    n_chip = lax.axis_size("chip")
     row_number, feature_cols = hidden.shape
-    full_width = feature_cols * lax.axis_size("blk")
-    offset = lax.axis_index("blk") * feature_cols
-    values = hidden.astype(jnp.float32)
-    gain_part = lax.dynamic_slice_in_dim(input_norm_gain, offset, feature_cols, 0)
-    squares = lax.psum(jnp.sum(values * values, axis=1), "blk")
+    full_width = feature_cols * n_blk
+    me_blk = lax.axis_index("blk")
+
+    if n_blk == 2:
+        other = lax.ppermute(hidden, "blk", [(0, 1), (1, 0)])
+        halves = [lax.select(me_blk == 0, hidden, other), lax.select(me_blk == 0, other, hidden)]
+    else:
+        halves = gather_blk(hidden, n_blk)
+    full_hidden = jnp.concatenate(halves, axis=1)
+    values = full_hidden.astype(jnp.float32)
+    squares = jnp.sum(values * values, axis=1)
     factor = lax.rsqrt(squares / full_width + epsilon)
-    normed_part = (values * factor[:, None] * gain_part[None, :]).astype(jnp.bfloat16)
-    normed = lax.all_gather(normed_part, "blk", axis=1, tiled=True)
+    normed = (values * factor[:, None] * input_norm_gain[None, :]).astype(jnp.bfloat16)
+    normed_part = lax.dynamic_slice_in_dim(normed, me_blk * feature_cols, feature_cols, 1)
+
+    weight_rows = query_weight.shape[0]
     query_cols = query_weight.shape[1]
-
-    def add_rows(weight_piece):
-        return jnp.dot(normed, weight_piece, preferred_element_type=jnp.float32)
-
-    query_plain = add_rows(lax.all_gather(query_weight, "req", axis=0, tiled=True))
-    base_pair = add_rows(lax.all_gather(keyvalue_weight, "req", axis=0, tiled=True))
-    down_all, up_query_all, up_pair_all = (
-        lax.all_gather(adapter_down, "req", axis=0, tiled=True),
-        lax.all_gather(adapter_up_query, "req", axis=0, tiled=True),
-        lax.all_gather(adapter_up_keyvalue, "req", axis=0, tiled=True),
-    )
-    adapter_count = down_all.shape[0]
+    pair_cols = keyvalue_weight.shape[1]
+    query_all = gather_req(query_weight)
+    pair_all = gather_req(keyvalue_weight)
+    normed_blocks = normed.reshape(row_number, n_chip, n_lo, weight_rows)
+
+    def project(weight_all, cols):
+        total = None
+        for c in range(n_lo):
+            lhs = normed_blocks[:, :, c, :].reshape(row_number, n_chip * weight_rows)
+            rhs = weight_all[c].reshape(n_chip * weight_rows, cols)
+            part = jnp.dot(lhs, rhs, preferred_element_type=jnp.float32)
+            total = part if total is None else total + part
+        return total
+
+    down_size = adapter_down[0].size
+    upq_size = adapter_up_query[0].size
+    flat = jnp.concatenate(
+        [
+            adapter_down.reshape(-1),
+            adapter_up_query.reshape(-1),
+            adapter_up_keyvalue.reshape(-1),
+        ]
+    )
+    adapters_all = gather_req(flat)
+    picked = prompt_adapter[0]
+    chosen = adapters_all[picked % n_lo, picked // n_lo]
+    prompt_count = picked.shape[0]
+    down_selected = chosen[:, :down_size].reshape((prompt_count,) + adapter_down.shape[1:])
+    up_query_selected = chosen[:, down_size : down_size + upq_size].reshape(
+        (prompt_count,) + adapter_up_query.shape[1:]
+    )
+    up_pair_selected = chosen[:, down_size + upq_size :].reshape(
+        (prompt_count,) + adapter_up_keyvalue.shape[1:]
+    )
+
+    base_pair = project(pair_all, pair_cols)
+    query_plain = project(query_all, query_cols)
+
     lengths = packed_lengths[0]
     member, position, owner, slot_index = layout(lengths, row_number)
-    prompt_count = lengths.shape[0]
-    picked_adapter = (
-        prompt_adapter[0][:, None] == jnp.arange(adapter_count, dtype=jnp.int32)[None, :]
-    ).astype(jnp.bfloat16)
-    down_selected = jnp.einsum(
-        "pa,ajrd->pjrd", picked_adapter, down_all, preferred_element_type=jnp.float32
-    ).astype(jnp.bfloat16)
     rank_size = down_selected.shape[2]
     partial_value = lax.dot_general(
         normed_part,
@@ -99,7 +154,7 @@
     masked = jnp.sum(partial_value * member[:, :, None, None], axis=1).reshape(
         row_number, 3 * rank_size
     )
-    low_rank = lax.psum(masked, "blk").reshape(row_number, 3, rank_size).astype(jnp.bfloat16)
+    low_rank = sum_blk(masked, n_blk).reshape(row_number, 3, rank_size).astype(jnp.bfloat16)
     low_float = low_rank.astype(jnp.float32)
 
     def spread(column):
@@ -109,13 +164,7 @@
             .reshape(row_number, prompt_count * rank_size)
         )
 
-    up_query_selected = jnp.einsum(
-        "pa,arc->prc", picked_adapter, up_query_all, preferred_element_type=jnp.float32
-    ).astype(jnp.bfloat16)
-    up_keyvalue_selected = jnp.einsum(
-        "pa,arc->prc", picked_adapter, up_pair_all, preferred_element_type=jnp.float32
-    ).astype(jnp.bfloat16)
-    up_keyvalue_selected = up_keyvalue_selected.reshape(
+    up_keyvalue_selected = up_pair_selected.reshape(
         prompt_count, rank_size, KEYVALUE_LOCAL, 2, HEAD_WIDTH
     )
     query_update = jnp.dot(
@@ -173,16 +222,24 @@
 
 
 def solution(mesh):
+    n_blk = mesh.shape["blk"]
+    n_req = mesh.shape["req"]
+    n_lo = 2 if n_req % 2 == 0 else 1
+    devices = mesh.devices.reshape(n_blk, n_req // n_lo, n_lo)
+    split_mesh = Mesh(devices, ("blk", "chip", "core"))
+    req = ("chip", "core")
     in_specs = (
-        P("req", "blk"),
+        P(req, "blk"),
         P(),
-        P("req", "blk"),
-        P("req", "blk"),
-        P("req", None, None, "blk"),
-        P("req", None, "blk"),
-        P("req", None, "blk"),
-        P("req", None),
-        P("req", None),
-    )
-    out_specs = (P("req", "blk"), P("req", "blk"), P("req", "blk"))
-    return jax.shard_map(shards, mesh=mesh, in_specs=in_specs, out_specs=out_specs, check_vma=False)
+        P(req, "blk"),
+        P(req, "blk"),
+        P(req, None, None, "blk"),
+        P(req, None, "blk"),
+        P(req, None, "blk"),
+        P(req, None),
+        P(req, None),
+    )
+    out_specs = (P(req, "blk"), P(req, "blk"), P(req, "blk"))
+    return jax.shard_map(
+        shards, mesh=split_mesh, in_specs=in_specs, out_specs=out_specs, check_vma=False
+    )

time: 370 us -> 349 us (0.943)
  local copies, waits for them, and re-layouts: 2.72 us -> 72 us
  blocking collectives: 57.3 us -> 0 us
  waiting for transfers between devices: 248 us -> 207 us
  other arithmetic: 11 us -> 32.2 us
  matrix products: 36.4 us -> 19.6 us
    all_gather x4 -> x6, waiting for transfers between devices: 246 us -> 140 us  [the longest x3 135 us: gather_req(): stacked = lax.all_gather(piece, 'chip', axis=0, tiled=False)]
    ppermute x0 -> x2, waiting for transfers between devices: none -> 66.3 us  [the longest x1 64.3 us: shards(): other = lax.ppermute(hidden, 'blk', [(0, 1), (1, 0)])]
    all_gather x2 -> x0, blocking collectives: 41.5 us -> none  [the longest x1 22.5 us: shards(): lax.all_gather(adapter_up_keyvalue, 'req', axis=0, tiled=True)]
    concatenate x0 -> x4, local copies, waits for them, and re-layouts: none -> 25.1 us  [shards(): full_hidden = jnp.concatenate(halves, axis=1)]
    dot_general x5 -> x4, matrix products: 29.4 us -> 9.6 us  [project(): part = jnp.dot(lhs, rhs, preferred_element_type=jnp.float32)]
    gather x0 -> x3, local copies, waits for them, and re-layouts: none -> 16.1 us  [shards(): chosen = adapters_all[picked % n_lo, picked // n_lo]]
    psum x2 -> x0, blocking collectives: 15.8 us -> none  [the longest x1 9.92 us: shards(): lax.psum(masked, 'blk').reshape(row_number, 3, rank_size)]
    slice x0 -> x7, local copies, waits for them, and re-layouts: none -> 13.3 us  [the longest x2 10.9 us: project(): rhs = weight_all[c].reshape(n_chip * weight_rows, cols)]
  transfers between devices with their start and end apart: 4 -> 8, of which waited for: 4 -> 6; matrix products, arithmetic and copies ran while one was open for 7% -> 28% of each run, Pallas kernels for 0% -> 0%
where the time goes in v1:
time: 349 us; the launch traced here: 348 us
  waiting for transfers between devices  207 us (59%)
  local copies, waits for them, and re-layouts  72 us (21%)
  other arithmetic  32.2 us (9%)
  matrix products  19.6 us (6%)
  between operations  14.6 us (4%)
    all_gather x3, waiting for transfers between devices, gather_req(): stacked = lax.all_gather(piece, 'chip', axis=0, tiled=False)  135 us
    ppermute x1, waiting for transfers between devices, shards(): other = lax.ppermute(hidden, 'blk', [(0, 1), (1, 0)])  64.3 us
    concatenate x4, local copies, waits for them, and re-layouts, shards(): full_hidden = jnp.concatenate(halves, axis=1)  25.1 us
    gather x3, local copies, waits for them, and re-layouts, shards(): chosen = adapters_all[picked % n_lo, picked // n_lo]  16.1 us
    unnamed x52, local copies, waits for them, and re-layouts  11.2 us
    slice x2, local copies, waits for them, and re-layouts, project(): rhs = weight_all[c].reshape(n_chip * weight_rows, cols)  10.9 us
    unnamed x1, other arithmetic  9.68 us
    dot_general x4, matrix products, project(): part = jnp.dot(lhs, rhs, preferred_element_type=jnp.float32)  9.6 us
  transfers between devices with their start and end apart: 8, of which 6 were waited for; matrix products, arithmetic and copies ran while one was open for 28% of the time, Pallas kernels for 0%

profile of v1, /device:TPU:0, one launch (start us, length us, event | category | flops | bytes accessed | tf_op | source)
XLA Modules:
  0.0 348.2 jit_solution(15644823795323308427)
XLA Ops:
  11.3 50.8 %all-gather.13.cloned.1.call-done = bf16[4096,256]{1,0:T(8,128)(2,1)} async-done(((bf16[512,256]{1,0:T(8,128)(2,1)}), bf16[4096,256]{1,0:T(8,128)(2,1)}) %all-gather.13.cloned.1.call-update) | async-done | bytes 2097168 | tf_op jit(solution)/shard_map/all_gather | solution.py:70
  62.2 65.6 %all-gather.17.cloned.1.call-done = bf16[1736704]{0:T(1024)(128)(2,1)} async-done(((bf16[217088]{0:T(1024)(128)(2,1)}), bf16[1736704]{0:T(1024)(128)(2,1)}) %all-gather.17.cloned.1.call-update) | async-done | bytes 3473424 | tf_op jit(solution)/shard_map/all_gather | solution.py:70
  127.8 5.3 %reshape.438 = bf16[8,217088]{1,0:T(8,128)(2,1)} reshape(bf16[1736704]{0:T(1024)(128)(2,1)} %all-gather.17.cloned.1.call-done) | data formatting | bytes 6946816 | tf_op jit(solution)/shard_map/all_gather | solution.py:70
  133.1 2.2 copy-done.8
  139.7 64.3 %collective-permute-done = bf16[384,4096]{1,0:T(8,128)(2,1)} collective-permute-done((bf16[384,4096]{1,0:T(8,128)(2,1)S(1)}, bf16[384,4096]{1,0:T(8,128)(2,1)}, u32[]{:S(2)}, u32[]{:S(2)}) %collective-permute-start) | collective-permute-done | bytes 3145760 | tf_op jit(solution)/shard_map/ppermute | solution.py:93
  203.9 3.3 broadcast_select_fusion.1
  208.9 6.1 %maximum_convert_fusion = f32[384,8192]{1,0:T(8,128)} fusion(bf16[384,4096]{1,0:T(8,128)(2,1)S(1)} %get-tuple-element.24, bf16[384,4096]{1,0:T(8,128)(2,1)S(1)} %get-tuple-element.23), kind=kLoop, calls=%fused_computation.7 | loop fusion | flops 12582912 | bytes 18874368 | tf_op jit(solution)/shard_map/convert_element_type | solution.py:98
  214.9 6.2 %concatenate.35 = bf16[384,4,2,512]{3,2,1,0:T(2,128)(2,1)} reshape(bf16[384,4096]{1,0:T(8,128)(2,1)} %copy-done) | data formatting | bytes 6291456 | tf_op jit(solution)/shard_map/concatenate | solution.py:97
  221.2 4.0 %concatenate.36 = bf16[384,4,2,512]{3,2,1,0:T(2,128)(2,1)} reshape(bf16[384,4096]{1,0:T(8,128)(2,1)S(1)} %get-tuple-element.24) | data formatting | bytes 6291456 | tf_op jit(solution)/shard_map/concatenate | solution.py:97
  225.1 8.9 %copy.43 = bf16[384,4,2,512]{0,3,1,2:T(8,128)(2,1)} copy(bf16[384,4,2,512]{3,2,1,0:T(2,128)(2,1)} %concatenate.35) | data formatting | bytes 6291456 | tf_op jit(solution)/shard_map/concatenate | solution.py:97
  234.1 6.0 %copy.44 = bf16[384,4,2,512]{0,3,1,2:T(8,128)(2,1)} copy(bf16[384,4,2,512]{3,2,1,0:T(2,128)(2,1)S(1)} %copy-done.5) | data formatting | bytes 6291456 | tf_op jit(solution)/shard_map/concatenate | solution.py:97
  240.1 4.5 %multiply_convert_fusion = bf16[384,8,2,512]{0,3,1,2:T(8,128)(2,1)S(1)} fusion(bf16[384,4,2,512]{0,3,1,2:T(8,128)(2,1)} %copy.44, bf16[384,4,2,512]{0,3,1,2:T(8,128)(2,1)} %copy.43, f32[8,2,512]{2,0,1:T(8,128)S(1)} %copy.45, f32[384]{0:T(512)S(1)} %add_rsqrt_fusion), kind=kLoop, calls=%fused_computation.2 | loop fusion | flops 15728640 | bytes 12617216 | tf_op jit(solution)/shard_map/convert_element_type | solution.py:101
  244.6 2.4 fusion.47
  247.1 3.8 %fusion.48 = (bf16[8,512,256]{2,1,0:T(8,128)(2,1)S(1)}, bf16[8,512,256]{2,1,0:T(8,128)(2,1)S(1)}) fusion(bf16[16,512,256]{2,1,0:T(8,128)(2,1)} %all-gather.15.cloned.1.call-done), kind=kLoop, calls=%fused_computation.93 | loop fusion | bytes 8388608 | tf_op jit(solution)/shard_map/slice | solution.py:115
  255.7 5.3 %fusion.46 = (bf16[2,8,108544]{2,1,0:T(8,128)(2,1)S(1)}, bf16[2,8,108544]{2,1,0:T(8,128)(2,1)}) fusion(bf16[2,8,217088]{2,1,0:T(8,128)(2,1)} %bitcast.163), kind=kLoop, calls=%fused_computation.91 | loop fusion | bytes 13893632 | tf_op jit(solution)/shard_map/gather | solution.py:131
  261.0 5.5 %gather_fusion.1 = bf16[4,108544]{1,0:T(4,128)(2,1)} fusion(bf16[2,8,108544]{2,1,0:T(8,128)(2,1)} %get-tuple-element.20, s32[4]{0:T(128)S(1)} %fusion.40), kind=kCustom, calls=%fused_computation.1 | custom fusion | bytes 1736736 | tf_op jit(solution)/shard_map/gather | solution.py:131
  266.5 5.3 %gather_fusion = bf16[4,108544]{1,0:T(4,128)(2,1)} fusion(bf16[2,8,108544]{2,1,0:T(8,128)(2,1)S(1)} %get-tuple-element.19, s32[4]{0:T(128)S(1)} %fusion.40), kind=kCustom, calls=%fused_computation | custom fusion | bytes 1736736 | tf_op jit(solution)/shard_map/gather | solution.py:131
  271.8 18.2 %all-gather.21.cloned.1.call-done = bf16[4096,1024]{1,0:T(8,128)(2,1)} async-done(((bf16[512,1024]{1,0:T(8,128)(2,1)}), bf16[4096,1024]{1,0:T(8,128)(2,1)}) %all-gather.21.cloned.1.call-update) | async-done | bytes 8388624 | tf_op jit(solution)/shard_map/all_gather | solution.py:70
  291.4 9.7 %pad_maximum_fusion = bf16[4,196608]{1,0:T(4,128)(2,1)S(1)} fusion(bf16[4,108544]{1,0:T(4,128)(2,1)S(1)} %copy-done.6, bf16[4,108544]{1,0:T(4,128)(2,1)S(1)} %copy-done.7), kind=kLoop, calls=%fused_computation.24 | loop fusion | flops 3145728 | bytes 3309568
  302.0 5.5 %fusion.19 = f32[384,3,16]{0,2,1:T(8,128)S(1)} fusion(bf16[4,3,16,4096]{3,2,1,0:T(8,128)(2,1)S(1)} %bitcast.171, f32[384,8192]{1,0:T(8,128)} %maximum_convert_fusion, s32[]{:T(128)} %select_n.70, f32[4096]{0:T(1024)S(1)} %dynamic-slice-done, f32[384]{0:T(512)S(1)} %add_rsqrt_fusion, f32[384,4]{0,1:T(4,128)S(1)} %fusion.44), kind=kOutput, calls=%fused_computation.34 | convolution fusion | flops 608827392 | bytes 7962624 | tf_op jit(solution)/shard_map/dot_general | solution.py:147
  314.7 5.0 %all-gather.23.cloned.1.call-done = bf16[16,512,1024]{2,1,0:T(8,128)(2,1)} async-done(((bf16[8,512,1024]{2,1,0:T(8,128)(2,1)}), bf16[16,512,1024]{2,1,0:T(8,128)(2,1)}) %all-gather.23.cloned.1.call-update) | async-done | bytes 16777232 | tf_op jit(solution)/shard_map/all_gather | solution.py:71
  319.7 7.1 %fusion.45 = (bf16[8,512,1024]{2,1,0:T(8,128)(2,1)S(1)}, bf16[8,512,1024]{2,1,0:T(8,128)(2,1)S(1)}) fusion(bf16[16,512,1024]{2,1,0:T(8,128)(2,1)} %all-gather.23.cloned.1.call-done), kind=kLoop, calls=%fused_computation.90 | loop fusion | bytes 33554432 | tf_op jit(solution)/shard_map/slice | solution.py:115
  326.8 3.5 fusion.52
  330.3 3.5 fusion.53
  (109 shorter events, 31.9 us)
Async XLA Ops:
  7.2 55.0 %all-gather.13.cloned.1.call-start = ((), (), s32[]{:S(2)}) async-start(), calls=%async_computation | async-start | bytes 2359296 | tf_op jit(solution)/shard_map/all_gather | solution.py:70
  7.9 119.9 %all-gather.17.cloned.1.call-start = ((), (), s32[]{:S(2)}) async-start(), calls=%async_computation.2 | async-start | bytes 3907584 | tf_op jit(solution)/shard_map/all_gather | solution.py:70
  11.3 235.8 %all-gather.15.cloned.1.call-start = ((), (), s32[]{:S(2)}) async-start(), calls=%async_computation.1 | async-start | bytes 6291456 | tf_op jit(solution)/shard_map/all_gather | solution.py:71
  62.2 193.5 %all-gather.19.cloned.1.call-start = ((), (), s32[]{:S(2)}) async-start(), calls=%async_computation.3 | async-start | bytes 10420224 | tf_op jit(solution)/shard_map/all_gather | solution.py:71
  133.0 3.8 %copy-start.18 = (f32[8192]{0:T(1024)S(1)}, f32[8192]{0:T(1024)}, u32[]{:S(2)}) copy-start(f32[8192]{0:T(1024)} %param.10) | copy-start | bytes 98308
  133.0 3.9 %copy-start.19 = (s32[1,4]{1,0:T(1,128)S(1)}, s32[1,4]{1,0:T(1,128)}, u32[]{:S(2)}) copy-start(s32[1,4]{1,0:T(1,128)} %param.16) | copy-start | bytes 52
  133.0 4.2 %copy-start.20 = (s32[1,4]{1,0:T(1,128)S(1)}, s32[1,4]{1,0:T(1,128)}, u32[]{:S(2)}) copy-start(s32[1,4]{1,0:T(1,128)} %param.17) | copy-start | bytes 52
  133.1 156.9 %all-gather.21.cloned.1.call-start = ((), (), s32[]{:S(2)}) async-start(), calls=%async_computation.4 | async-start | bytes 9437184 | tf_op jit(solution)/shard_map/all_gather | solution.py:70
  135.3 68.6 %collective-permute-start = (bf16[384,4096]{1,0:T(8,128)(2,1)S(1)}, bf16[384,4096]{1,0:T(8,128)(2,1)}, u32[]{:S(2)}, u32[]{:S(2)}) collective-permute-start(bf16[384,4096]{1,0:T(8,128)(2,1)S(1)} %copy-done.8), channel_id=1, source_target_pairs={{0,16},{16,0},{1,17},{17,1},{2,18},{18,2},{3,19},{19,3},{4,20},{20... | collective-permute-start | bytes 9437192 | tf_op jit(solution)/shard_map/ppermute | solution.py:93
  136.8 182.9 %all-gather.23.cloned.1.call-start = ((), (), s32[]{:S(2)}) async-start(), calls=%async_computation.5 | async-start | bytes 25165824 | tf_op jit(solution)/shard_map/all_gather | solution.py:71
  225.1 8.9 %copy-start.5 = (bf16[384,4,2,512]{3,2,1,0:T(2,128)(2,1)S(1)}, bf16[384,4,2,512]{3,2,1,0:T(2,128)(2,1)}, u32[]{:S(2)}) copy-start(bf16[384,4,2,512]{3,2,1,0:T(2,128)(2,1)} %concatenate.36) | copy-start | bytes 9437188
  247.0 5.6 %copy-start.1 = (bf16[384,8,1,512]{0,3,1,2:T(8,128)(2,1)}, bf16[384,8,1,512]{0,3,1,2:T(8,128)(2,1)S(1)}, u32[]{:S(2)}) copy-start(bf16[384,8,1,512]{0,3,1,2:T(8,128)(2,1)S(1)} %get-tuple-element.21) | copy-start | bytes 9437188
  247.1 4.3 %copy-start.3 = (bf16[384,8,1,512]{0,3,1,2:T(8,128)(2,1)S(1)}, bf16[384,8,1,512]{0,3,1,2:T(8,128)(2,1)}, u32[]{:S(2)}) copy-start(bf16[384,8,1,512]{0,3,1,2:T(8,128)(2,1)} %get-tuple-element.22) | copy-start | bytes 9437188
  291.4 10.6 %dynamic-slice-start = ((f32[8192]{0:T(1024)}, s32[]{:T(128)}), f32[4096]{0:T(1024)S(1)}, s32[]{:S(2)}) async-start(f32[8192]{0:T(1024)} %param.10, s32[]{:T(128)} %select_n.70), calls=%async_computation.8 | async-start | bytes 33280 | tf_op jit(solution)/shard_map/dynamic_slice | solution.py:102
  302.0 7.1 %slice-start = ((bf16[4,108544]{1,0:T(4,128)(2,1)}), bf16[4,4096]{1,0:T(4,128)(2,1)S(1)}, s32[]{:S(2)}) async-start(bf16[4,108544]{1,0:T(4,128)(2,1)} %gather_fusion.1), calls=%async_computation.6 | async-start | bytes 65536 | tf_op jit(solution)/shard_map/slice | solution.py:137
  302.0 7.2 %slice-start.1 = ((bf16[4,108544]{1,0:T(4,128)(2,1)}), bf16[4,16384]{1,0:T(4,128)(2,1)S(1)}, s32[]{:S(2)}) async-start(bf16[4,108544]{1,0:T(4,128)(2,1)} %gather_fusion.1), calls=%async_computation.7 | async-start | bytes 262144 | tf_op jit(solution)/shard_map/slice | solution.py:134
  302.0 10.6 %copy-start.11 = (f32[384,1,1,128]{3,0,2,1:T(8,128)S(1)}, f32[384,1,1,128]{3,0,2,1:T(8,128)}, u32[]{:S(2)}) copy-start(f32[384,1,1,128]{3,0,2,1:T(8,128)} %copy.60) | copy-start | bytes 589828
  302.0 11.5 %copy-start.10 = (f32[384,1,1,128]{3,0,2,1:T(8,128)S(1)}, f32[384,1,1,128]{3,0,2,1:T(8,128)}, u32[]{:S(2)}) copy-start(f32[384,1,1,128]{3,0,2,1:T(8,128)} %copy.62) | copy-start | bytes 589828
  307.5 6.3 %copy-start.12 = (f32[384,64]{1,0:T(8,128)S(1)}, f32[384,64]{1,0:T(8,128)}, u32[]{:S(2)}) copy-start(f32[384,64]{1,0:T(8,128)} %get-tuple-element.44) | copy-start | bytes 294916
  307.5 6.3 %copy-start.13 = (f32[384,64]{1,0:T(8,128)S(1)}, f32[384,64]{1,0:T(8,128)}, u32[]{:S(2)}) copy-start(f32[384,64]{1,0:T(8,128)} %get-tuple-element.45) | copy-start | bytes 294916
  307.5 4.4 %collective-permute-start.1 = (f32[384,48]{0,1:T(8,128)S(1)}, f32[384,48]{0,1:T(8,128)S(1)}, u32[]{:S(2)}, u32[]{:S(2)}) collective-permute-start(f32[384,48]{0,1:T(8,128)S(1)} %bitcast.181), channel_id=1, source_target_pairs={{0,16},{16,0},{1,17},{17,1},{2,18},{18,2},{3,19},{19,3},{4,20},{20... | collective-permute-start | bytes 221192 | tf_op jit(solution)/shard_map/ppermute | solution.py:65
  314.7 12.1 %copy-start.4 = (bf16[384,8,1,512]{0,3,1,2:T(8,128)(2,1)S(1)}, bf16[384,8,1,512]{0,3,1,2:T(8,128)(2,1)}, u32[]{:S(2)}) copy-start(bf16[384,8,1,512]{0,3,1,2:T(8,128)(2,1)} %get-tuple-element.22) | copy-start | bytes 9437188
  330.3 3.5 %copy-start.14 = (bf16[64,1024]{1,0:T(8,128)(2,1)S(1)}, bf16[64,1024]{1,0:T(8,128)(2,1)}, u32[]{:S(2)}) copy-start(bf16[64,1024]{1,0:T(8,128)(2,1)} %reshape_reshape.8) | copy-start | bytes 393220
  330.3 3.5 %copy-start.16 = (bf16[384,4,16]{0,2,1:T(8,128)(2,1)S(1)}, bf16[384,4,16]{0,2,1:T(8,128)(2,1)}, u32[]{:S(2)}) copy-start(bf16[384,4,16]{0,2,1:T(8,128)(2,1)} %get-tuple-element.43) | copy-start | bytes 147460
  (8 other events, 12.9 us)
Sparse Core Ops, SparseCore 0:
  10.1 51.9 all-gather.12
  64.9 62.8 all-gather.16
  129.3 12.1 all-gather.14
  142.9 18.9 all-gather.18
  163.9 126.0 all-gather.20
  291.4 28.2 all-gather.22

commit v2 on v1

--- a/solution.py
+++ b/solution.py
@@ -66,9 +66,20 @@
     return lax.psum(piece, "blk")
 
 
-def gather_req(piece):
-    stacked = lax.all_gather(piece, "chip", axis=0, tiled=False)
-    return lax.all_gather(stacked, "core", axis=0, tiled=False)
+def ring_order(count):
+    if count % 2 == 0 and count > 2:
+        return list(range(0, count, 2)) + list(range(count - 1, 0, -2))
+    return list(range(count))
+
+
+def ring_gather(piece, count, order, direction):
+    pairs = [(order[i], order[(i + direction) % count]) for i in range(count)]
+    received = [piece]
+    current = piece
+    for _ in range(count - 1):
+        current = lax.ppermute(current, "chip", pairs)
+        received.append(current)
+    return received
 
 
 def shards(
@@ -88,6 +99,8 @@
     row_number, feature_cols = hidden.shape
     full_width = feature_cols * n_blk
     me_blk = lax.axis_index("blk")
+    me_core = lax.axis_index("core")
+    me_chip = lax.axis_index("chip")
 
     if n_blk == 2:
         other = lax.ppermute(hidden, "blk", [(0, 1), (1, 0)])
@@ -104,42 +117,82 @@
     weight_rows = query_weight.shape[0]
     query_cols = query_weight.shape[1]
     pair_cols = keyvalue_weight.shape[1]
-    query_all = gather_req(query_weight)
-    pair_all = gather_req(keyvalue_weight)
-    normed_blocks = normed.reshape(row_number, n_chip, n_lo, weight_rows)
-
-    def project(weight_all, cols):
-        total = None
-        for c in range(n_lo):
-            lhs = normed_blocks[:, :, c, :].reshape(row_number, n_chip * weight_rows)
-            rhs = weight_all[c].reshape(n_chip * weight_rows, cols)
-            part = jnp.dot(lhs, rhs, preferred_element_type=jnp.float32)
-            total = part if total is None else total + part
-        return total
-
-    down_size = adapter_down[0].size
-    upq_size = adapter_up_query[0].size
-    flat = jnp.concatenate(
-        [
-            adapter_down.reshape(-1),
-            adapter_up_query.reshape(-1),
-            adapter_up_keyvalue.reshape(-1),
-        ]
-    )
-    adapters_all = gather_req(flat)
+    half_rows = weight_rows // 2
+
+    weights = jnp.concatenate([query_weight, keyvalue_weight], axis=1)
+    down_rows = adapter_down.size // query_cols
+    upq_rows = adapter_up_query.size // query_cols
+    upkv_rows = adapter_up_keyvalue.size // query_cols
+    down_flat = adapter_down.reshape(down_rows, query_cols)
+    upq_flat = adapter_up_query.reshape(upq_rows, query_cols)
+    upkv_flat = adapter_up_keyvalue.reshape(upkv_rows, query_cols)
+    dh, uh, vh = down_rows // 2, upq_rows // 2, upkv_rows // 2
+    piece_rows = dh + uh + vh
+    pad_rows = (-piece_rows) % 8
+
+    def adapter_half(h):
+        return jnp.concatenate(
+            [
+                down_flat[h * dh : (h + 1) * dh],
+                upq_flat[h * uh : (h + 1) * uh],
+                upkv_flat[h * vh : (h + 1) * vh],
+                jnp.zeros((pad_rows, query_cols), jnp.bfloat16),
+            ]
+        )
+
+    order = ring_order(n_chip)
+    inverse = [0] * n_chip
+    for i, c in enumerate(order):
+        inverse[c] = i
+    order_table = jnp.asarray(order, jnp.int32)
+    inverse_table = jnp.asarray(inverse, jnp.int32)
+    pos = inverse_table[me_chip]
+    directions = (1, -1)
+
+    def swap_core(x):
+        if n_lo == 1:
+            return [x]
+        return [x, lax.ppermute(x, "core", [(0, 1), (1, 0)])]
+
+    total = None
+    adapter_pieces = []
+    for h, direction in enumerate(directions):
+        w_recv = ring_gather(weights[h * half_rows : (h + 1) * half_rows], n_chip, order, direction)
+        a_recv = ring_gather(adapter_half(h), n_chip, order, direction)
+        a_steps = []
+        for s in range(n_chip):
+            src_chip = order_table[(pos - s * direction) % n_chip]
+            w_both = swap_core(w_recv[s])
+            a_steps.append(jnp.stack(swap_core(a_recv[s])))
+            for slot, w_piece in enumerate(w_both):
+                src_core = me_core if slot == 0 else n_lo - 1 - me_core
+                start = (src_chip * n_lo + src_core) * weight_rows + h * half_rows
+                lhs = lax.dynamic_slice_in_dim(normed, start, half_rows, 1)
+                part = jnp.dot(lhs, w_piece, preferred_element_type=jnp.float32)
+                total = part if total is None else total + part
+        adapter_pieces.append(jnp.stack(a_steps))
+
     picked = prompt_adapter[0]
-    chosen = adapters_all[picked % n_lo, picked // n_lo]
     prompt_count = picked.shape[0]
-    down_selected = chosen[:, :down_size].reshape((prompt_count,) + adapter_down.shape[1:])
-    up_query_selected = chosen[:, down_size : down_size + upq_size].reshape(
-        (prompt_count,) + adapter_up_query.shape[1:]
-    )
-    up_pair_selected = chosen[:, down_size + upq_size :].reshape(
-        (prompt_count,) + adapter_up_keyvalue.shape[1:]
-    )
-
-    base_pair = project(pair_all, pair_cols)
-    query_plain = project(query_all, query_cols)
+    a_chip = picked // n_lo
+    a_core = picked % n_lo
+    a_slot = (a_core != me_core).astype(jnp.int32)
+    per_half = []
+    for h, direction in enumerate(directions):
+        a_step = ((pos - inverse_table[a_chip]) * direction) % n_chip
+        per_half.append(adapter_pieces[h][a_step, a_slot])
+    down_selected = jnp.concatenate(
+        [per_half[0][:, :dh], per_half[1][:, :dh]], axis=1
+    ).reshape((prompt_count,) + adapter_down.shape[1:])
+    up_query_selected = jnp.concatenate(
+        [per_half[0][:, dh : dh + uh], per_half[1][:, dh : dh + uh]], axis=1
+    ).reshape((prompt_count,) + adapter_up_query.shape[1:])
+    up_pair_selected = jnp.concatenate(
+        [per_half[0][:, dh + uh : piece_rows], per_half[1][:, dh + uh : piece_rows]], axis=1
+    ).reshape((prompt_count,) + adapter_up_keyvalue.shape[1:])
+
+    query_plain = total[:, :query_cols]
+    base_pair = total[:, query_cols:]
 
     lengths = packed_lengths[0]
     member, position, owner, slot_index = layout(lengths, row_number)

time: 349 us -> 252 us (0.72)
  waiting for transfers between devices: 207 us -> 122 us
  local copies, waits for them, and re-layouts: 72 us -> 19.2 us
  starting transfers between devices: 3.27 us -> 38.1 us
  other arithmetic: 32.2 us -> 23.9 us
  between operations: 14.6 us -> 22.6 us
  matrix products: 19.6 us -> 25.1 us
    all_gather x6 -> x0, waiting for transfers between devices: 140 us -> none  [the longest x3 135 us: gather_req(): stacked = lax.all_gather(piece, 'chip', axis=0, tiled=False)]
    ppermute x0 -> x60, waiting for transfers between devices: none -> 118 us  [the longest x28 118 us: ring_gather(): current = lax.ppermute(current, 'chip', pairs)]
    ppermute x1, waiting for transfers between devices: 64.3 us -> 0.01 us  [shards(): other = lax.ppermute(hidden, 'blk', [(0, 1), (1, 0)])]
    ppermute x0 -> x60, starting transfers between devices: none -> 35.9 us  [the longest x28 30.9 us: ring_gather(): current = lax.ppermute(current, 'chip', pairs)]
    concatenate x4 -> x2, local copies, waits for them, and re-layouts: 25.1 us -> 0.1 us  [the longest x1 0.08 us: adapter_half(): jnp.concatenate([down_flat[h * dh:(h + 1) * dh], upq_flat[h * uh:(h + 1)...]
    dot_general x4 -> x32, matrix products: 9.6 us -> 20.1 us  [shards(): part = jnp.dot(lhs, w_piece, preferred_element_type=jnp.float32)]
    gather x3, local copies, waits for them, and re-layouts: 16.1 us -> 5.93 us  [the longest x2 5.29 us: shards(): per_half.append(adapter_pieces[h][a_step, a_slot])]
    slice x7 -> x15, local copies, waits for them, and re-layouts: 13.3 us -> 4.14 us  [the longest x1 1.19 us: shards(): weights[h * half_rows:(h + 1) * half_rows]]
  transfers between devices with their start and end apart: 8 -> 62, of which waited for: 6 -> 20; matrix products, arithmetic and copies ran while one was open for 28% -> 22% of each run, Pallas kernels for 0% -> 0%
where the time goes in v2:
time: 252 us; the launch traced here: 251 us
  waiting for transfers between devices  122 us (48%)
  starting transfers between devices  38.1 us (15%)
  matrix products  25.1 us (10%)
  other arithmetic  23.9 us (9%)
  between operations  22.6 us (9%)
  local copies, waits for them, and re-layouts  19.2 us (8%)
    ppermute x28, waiting for transfers between devices, ring_gather(): current = lax.ppermute(current, 'chip', pairs)  118 us
    ppermute x28, starting transfers between devices, ring_gather(): current = lax.ppermute(current, 'chip', pairs)  30.9 us
    dot_general x32, matrix products, shards(): part = jnp.dot(lhs, w_piece, preferred_element_type=jnp.float32)  20.1 us
    unnamed x14, other arithmetic  9.67 us
    gather x2, local copies, waits for them, and re-layouts, shards(): per_half.append(adapter_pieces[h][a_step, a_slot])  5.29 us
  transfers between devices with their start and end apart: 62, of which 20 were waited for; matrix products, arithmetic and copies ran while one was open for 22% of the time, Pallas kernels for 0%

profile of v2, /device:TPU:0, one launch (start us, length us, event | category | flops | bytes accessed | tf_op | source)
XLA Modules:
  0.0 250.7 jit_solution(10261060483271918724)
XLA Ops:
  4.3 2.6 %collective-permute-start.47 = (bf16[112,1024]{1,0:T(8,128)(2,1)S(1)}, bf16[112,1024]{1,0:T(8,128)(2,1)}, u32[]{:S(2)}, u32[]{:S(2)}) collective-permute-start(bf16[112,1024]{1,0:T(8,128)(2,1)S(1)} %get-tuple-element.42), channel_id=1, source_target_pairs={{0,2},{4,0},{8,4},{12,8},{14,12},{10,14},{6,10},{2,6},{1,3},{5,1},... | collective-permute-start | bytes 688136 | tf_op jit(solution)/shard_map/ppermute | solution.py:80
  43.7 2.6 %collective-permute-done.34 = bf16[112,1024]{1,0:T(8,128)(2,1)S(1)} collective-permute-done((bf16[112,1024]{1,0:T(8,128)(2,1)}, bf16[112,1024]{1,0:T(8,128)(2,1)S(1)}, u32[]{:S(2)}, u32[]{:S(2)}) %collective-permute-start.34) | collective-permute-done | bytes 229408 | tf_op jit(solution)/shard_map/ppermute | solution.py:80
  46.8 1.8 fusion.50
  54.6 2.2 collective-permute-done.53
  60.7 4.1 %collective-permute-done.55 = bf16[112,1024]{1,0:T(8,128)(2,1)S(1)} collective-permute-done((bf16[112,1024]{1,0:T(8,128)(2,1)S(1)}, bf16[112,1024]{1,0:T(8,128)(2,1)S(1)}, u32[]{:S(2)}, u32[]{:S(2)}) %collective-permute-start.55) | collective-permute-done | bytes 229408 | tf_op jit(solution)/shard_map/ppermute | solution.py:80
  69.6 3.3 %collective-permute-done.57 = bf16[112,1024]{1,0:T(8,128)(2,1)S(1)} collective-permute-done((bf16[112,1024]{1,0:T(8,128)(2,1)S(1)}, bf16[112,1024]{1,0:T(8,128)(2,1)S(1)}, u32[]{:S(2)}, u32[]{:S(2)}) %collective-permute-start.57) | collective-permute-done | bytes 229408 | tf_op jit(solution)/shard_map/ppermute | solution.py:80
  75.3 14.3 %collective-permute-done.42 = bf16[112,1024]{1,0:T(8,128)(2,1)S(1)} collective-permute-done((bf16[112,1024]{1,0:T(8,128)(2,1)S(1)}, bf16[112,1024]{1,0:T(8,128)(2,1)S(1)}, u32[]{:S(2)}, u32[]{:S(2)}) %collective-permute-start.42) | collective-permute-done | bytes 229408 | tf_op jit(solution)/shard_map/ppermute | solution.py:80
  91.5 6.0 %collective-permute-done.44 = bf16[112,1024]{1,0:T(8,128)(2,1)S(1)} collective-permute-done((bf16[112,1024]{1,0:T(8,128)(2,1)S(1)}, bf16[112,1024]{1,0:T(8,128)(2,1)S(1)}, u32[]{:S(2)}, u32[]{:S(2)}) %collective-permute-start.44) | collective-permute-done | bytes 229408 | tf_op jit(solution)/shard_map/ppermute | solution.py:80
  100.2 2.6 %gather_fusion.2 = bf16[4,112,1024]{2,1,0:T(8,128)(2,1)S(1)} fusion(bf16[8,2,112,1024]{3,2,1,0:T(8,128)(2,1)} %fusion.56, s32[4]{0:T(128)S(1)} %fusion.163), kind=kCustom, calls=%fused_computation.2 | custom fusion | bytes 1835040 | tf_op jit(solution)/shard_map/gather | solution.py:183
  105.9 2.6 %gather_fusion.1 = bf16[4,112,1024]{2,1,0:T(8,128)(2,1)S(1)} fusion(bf16[8,2,112,1024]{3,2,1,0:T(8,128)(2,1)} %fusion.48, s32[4]{0:T(128)S(1)} %get-tuple-element.11), kind=kCustom, calls=%fused_computation.1 | custom fusion | bytes 1835040 | tf_op jit(solution)/shard_map/gather | solution.py:183
  110.1 2.3 dot_general.148
  112.6 2.6 %collective-permute-done.17 = bf16[256,1280]{1,0:T(8,128)(2,1)} collective-permute-done((bf16[256,1280]{1,0:T(8,128)(2,1)}, bf16[256,1280]{1,0:T(8,128)(2,1)}, u32[]{:S(2)}, u32[]{:S(2)}) %collective-permute-start.17) | collective-permute-done | bytes 655392 | tf_op jit(solution)/shard_map/ppermute | solution.py:80
  116.7 3.3 %broadcast_select_fusion.1 = (bf16[384,4096]{1,0:T(8,128)(2,1)S(1)}, bf16[384,4096]{1,0:T(8,128)(2,1)S(1)}) fusion(bf16[384,4096]{1,0:T(8,128)(2,1)} %param.11, bf16[384,4096]{1,0:T(8,128)(2,1)} %collective-permute-done, pred[]{:T(512)S(6)} %eq.42), kind=kLoop, calls=%fused_computation.18 | loop fusion | flops 3145728 | bytes 12582913 | tf_op jit(solution)/shard_map/select_n | solution.py:107
  121.5 1.8 fusion.2
  129.2 3.3 %collective-permute-done.19 = bf16[256,1280]{1,0:T(8,128)(2,1)S(1)} collective-permute-done((bf16[256,1280]{1,0:T(8,128)(2,1)}, bf16[256,1280]{1,0:T(8,128)(2,1)S(1)}, u32[]{:S(2)}, u32[]{:S(2)}) %collective-permute-start.19) | collective-permute-done | bytes 655392 | tf_op jit(solution)/shard_map/ppermute | solution.py:80
  137.2 7.1 %collective-permute-done.6 = bf16[256,1280]{1,0:T(8,128)(2,1)S(1)} collective-permute-done((bf16[256,1280]{1,0:T(8,128)(2,1)}, bf16[256,1280]{1,0:T(8,128)(2,1)S(1)}, u32[]{:S(2)}, u32[]{:S(2)}) %collective-permute-start.6) | collective-permute-done | bytes 655392 | tf_op jit(solution)/shard_map/ppermute | solution.py:80
  145.7 3.2 %collective-permute-done.21 = bf16[256,1280]{1,0:T(8,128)(2,1)S(1)} collective-permute-done((bf16[256,1280]{1,0:T(8,128)(2,1)S(1)}, bf16[256,1280]{1,0:T(8,128)(2,1)S(1)}, u32[]{:S(2)}, u32[]{:S(2)}) %collective-permute-start.21) | collective-permute-done | bytes 655392 | tf_op jit(solution)/shard_map/ppermute | solution.py:80
  149.3 12.6 %collective-permute-done.8 = bf16[256,1280]{1,0:T(8,128)(2,1)S(1)} collective-permute-done((bf16[256,1280]{1,0:T(8,128)(2,1)S(1)}, bf16[256,1280]{1,0:T(8,128)(2,1)S(1)}, u32[]{:S(2)}, u32[]{:S(2)}) %collective-permute-start.8) | collective-permute-done | bytes 655392 | tf_op jit(solution)/shard_map/ppermute | solution.py:80
  167.7 10.6 %collective-permute-done.23 = bf16[256,1280]{1,0:T(8,128)(2,1)S(1)} collective-permute-done((bf16[256,1280]{1,0:T(8,128)(2,1)S(1)}, bf16[256,1280]{1,0:T(8,128)(2,1)S(1)}, u32[]{:S(2)}, u32[]{:S(2)}) %collective-permute-start.23) | collective-permute-done | bytes 655392 | tf_op jit(solution)/shard_map/ppermute | solution.py:80
  179.3 3.4 %collective-permute-done.61 = f32[384,48]{0,1:T(8,128)S(1)} collective-permute-done((f32[384,48]{0,1:T(8,128)S(1)}, f32[384,48]{0,1:T(8,128)S(1)}, u32[]{:S(2)}, u32[]{:S(2)}) %collective-permute-start.61) | collective-permute-done | bytes 73760 | tf_op jit(solution)/shard_map/ppermute | solution.py:65
  185.6 12.0 %collective-permute-done.25 = bf16[256,1280]{1,0:T(8,128)(2,1)S(1)} collective-permute-done((bf16[256,1280]{1,0:T(8,128)(2,1)S(1)}, bf16[256,1280]{1,0:T(8,128)(2,1)S(1)}, u32[]{:S(2)}, u32[]{:S(2)}) %collective-permute-start.25) | collective-permute-done | bytes 655392 | tf_op jit(solution)/shard_map/ppermute | solution.py:80
  200.6 10.7 %collective-permute-done.27 = bf16[256,1280]{1,0:T(8,128)(2,1)S(1)} collective-permute-done((bf16[256,1280]{1,0:T(8,128)(2,1)S(1)}, bf16[256,1280]{1,0:T(8,128)(2,1)S(1)}, u32[]{:S(2)}, u32[]{:S(2)}) %collective-permute-start.27) | collective-permute-done | bytes 655392 | tf_op jit(solution)/shard_map/ppermute | solution.py:80
  212.8 11.4 %collective-permute-done.14 = bf16[256,1280]{1,0:T(8,128)(2,1)S(1)} collective-permute-done((bf16[256,1280]{1,0:T(8,128)(2,1)S(1)}, bf16[256,1280]{1,0:T(8,128)(2,1)S(1)}, u32[]{:S(2)}, u32[]{:S(2)}) %collective-permute-start.14) | collective-permute-done | bytes 655392 | tf_op jit(solution)/shard_map/ppermute | solution.py:80
  226.8 9.4 %collective-permute-done.29 = bf16[256,1280]{1,0:T(8,128)(2,1)S(1)} collective-permute-done((bf16[256,1280]{1,0:T(8,128)(2,1)S(1)}, bf16[256,1280]{1,0:T(8,128)(2,1)S(1)}, u32[]{:S(2)}, u32[]{:S(2)}) %collective-permute-start.29) | collective-permute-done | bytes 655392 | tf_op jit(solution)/shard_map/ppermute | solution.py:80
  (248 shorter events, 92.4 us)
Async XLA Ops:
  6.9 33.8 %collective-permute-start.31 = (bf16[112,1024]{1,0:T(8,128)(2,1)S(1)}, bf16[112,1024]{1,0:T(8,128)(2,1)}, u32[]{:S(2)}, u32[]{:S(2)}) collective-permute-start(bf16[112,1024]{1,0:T(8,128)(2,1)S(1)} %get-tuple-element.41), channel_id=1, source_target_pairs={{0,1},{1,0},{2,3},{3,2},{4,5},{5,4},{6,7},{7,6},{8,9},{9,8},{10,11... | collective-permute-start | bytes 688136 | tf_op jit(solution)/shard_map/ppermute | solution.py:155
  7.0 31.3 %collective-permute-start.32 = (bf16[112,1024]{1,0:T(8,128)(2,1)S(1)}, bf16[112,1024]{1,0:T(8,128)(2,1)}, u32[]{:S(2)}, u32[]{:S(2)}) collective-permute-start(bf16[112,1024]{1,0:T(8,128)(2,1)S(1)} %get-tuple-element.41), channel_id=1, source_target_pairs={{0,4},{4,8},{8,12},{12,14},{14,10},{10,6},{6,2},{2,0},{1,5},{5,9},... | collective-permute-start | bytes 688136 | tf_op jit(solution)/shard_map/ppermute | solution.py:80
  7.4 107.8 %collective-permute-start = (bf16[384,4096]{1,0:T(8,128)(2,1)}, bf16[384,4096]{1,0:T(8,128)(2,1)}, u32[]{:S(2)}, u32[]{:S(2)}) collective-permute-start(bf16[384,4096]{1,0:T(8,128)(2,1)} %param.11), channel_id=1, source_target_pairs={{0,16},{16,0},{1,17},{17,1},{2,18},{18,2},{3,19},{19,3},{4,20},{20... | collective-permute-start | bytes 9437192 | tf_op jit(solution)/shard_map/ppermute | solution.py:106
  14.3 26.9 %collective-permute-start.48 = (bf16[112,1024]{1,0:T(8,128)(2,1)}, bf16[112,1024]{1,0:T(8,128)(2,1)S(1)}, u32[]{:S(2)}, u32[]{:S(2)}) collective-permute-start(bf16[112,1024]{1,0:T(8,128)(2,1)} %collective-permute-done.47), channel_id=1, source_target_pairs={{0,1},{1,0},{2,3},{3,2},{4,5},{5,4},{6,7},{7,6},{8,9},{9,8},{10,11... | collective-permute-start | bytes 688136 | tf_op jit(solution)/shard_map/ppermute | solution.py:155
  14.4 26.3 %collective-permute-start.49 = (bf16[112,1024]{1,0:T(8,128)(2,1)}, bf16[112,1024]{1,0:T(8,128)(2,1)S(1)}, u32[]{:S(2)}, u32[]{:S(2)}) collective-permute-start(bf16[112,1024]{1,0:T(8,128)(2,1)} %collective-permute-done.47), channel_id=1, source_target_pairs={{0,2},{4,0},{8,4},{12,8},{14,12},{10,14},{6,10},{2,6},{1,3},{5,1},... | collective-permute-start | bytes 688136 | tf_op jit(solution)/shard_map/ppermute | solution.py:80
  67.5 36.4 %collective-permute-start.2 = (bf16[256,1280]{1,0:T(8,128)(2,1)}, bf16[256,1280]{1,0:T(8,128)(2,1)}, u32[]{:S(2)}, u32[]{:S(2)}) collective-permute-start(bf16[256,1280]{1,0:T(8,128)(2,1)} %get-tuple-element.17), channel_id=1, source_target_pairs={{0,4},{4,8},{8,12},{12,14},{14,10},{10,6},{6,2},{2,0},{1,5},{5,9},... | collective-permute-start | bytes 1966088 | tf_op jit(solution)/shard_map/ppermute | solution.py:80
  68.0 21.5 %collective-permute-start.42 = (bf16[112,1024]{1,0:T(8,128)(2,1)S(1)}, bf16[112,1024]{1,0:T(8,128)(2,1)S(1)}, u32[]{:S(2)}, u32[]{:S(2)}) collective-permute-start(bf16[112,1024]{1,0:T(8,128)(2,1)S(1)} %collective-permute-done.40), channel_id=1, source_target_pairs={{0,4},{4,8},{8,12},{12,14},{14,10},{10,6},{6,2},{2,0},{1,5},{5,9},... | collective-permute-start | bytes 688136 | tf_op jit(solution)/shard_map/ppermute | solution.py:80
  72.9 16.7 %collective-permute-start.58 = (bf16[112,1024]{1,0:T(8,128)(2,1)S(1)}, bf16[112,1024]{1,0:T(8,128)(2,1)S(1)}, u32[]{:S(2)}, u32[]{:S(2)}) collective-permute-start(bf16[112,1024]{1,0:T(8,128)(2,1)S(1)} %collective-permute-done.57), channel_id=1, source_target_pairs={{0,1},{1,0},{2,3},{3,2},{4,5},{5,4},{6,7},{7,6},{8,9},{9,8},{10,11... | collective-permute-start | bytes 688136 | tf_op jit(solution)/shard_map/ppermute | solution.py:155
  72.9 17.2 %collective-permute-start.59 = (bf16[112,1024]{1,0:T(8,128)(2,1)S(1)}, bf16[112,1024]{1,0:T(8,128)(2,1)S(1)}, u32[]{:S(2)}, u32[]{:S(2)}) collective-permute-start(bf16[112,1024]{1,0:T(8,128)(2,1)S(1)} %collective-permute-done.57), channel_id=1, source_target_pairs={{0,2},{4,0},{8,4},{12,8},{14,12},{10,14},{6,10},{2,6},{1,3},{5,1},... | collective-permute-start | bytes 688136 | tf_op jit(solution)/shard_map/ppermute | solution.py:80
  91.2 35.9 %collective-permute-start.1 = (bf16[256,1280]{1,0:T(8,128)(2,1)}, bf16[256,1280]{1,0:T(8,128)(2,1)}, u32[]{:S(2)}, u32[]{:S(2)}) collective-permute-start(bf16[256,1280]{1,0:T(8,128)(2,1)} %get-tuple-element.17), channel_id=1, source_target_pairs={{0,1},{1,0},{2,3},{3,2},{4,5},{5,4},{6,7},{7,6},{8,9},{9,8},{10,11... | collective-permute-start | bytes 1966088 | tf_op jit(solution)/shard_map/ppermute | solution.py:155
  97.6 17.5 %collective-permute-start.17 = (bf16[256,1280]{1,0:T(8,128)(2,1)}, bf16[256,1280]{1,0:T(8,128)(2,1)}, u32[]{:S(2)}, u32[]{:S(2)}) collective-permute-start(bf16[256,1280]{1,0:T(8,128)(2,1)} %get-tuple-element.18), channel_id=1, source_target_pairs={{0,2},{4,0},{8,4},{12,8},{14,12},{10,14},{6,10},{2,6},{1,3},{5,1},... | collective-permute-start | bytes 1966088 | tf_op jit(solution)/shard_map/ppermute | solution.py:80
  103.9 61.2 %collective-permute-start.16 = (bf16[256,1280]{1,0:T(8,128)(2,1)}, bf16[256,1280]{1,0:T(8,128)(2,1)}, u32[]{:S(2)}, u32[]{:S(2)}) collective-permute-start(bf16[256,1280]{1,0:T(8,128)(2,1)} %get-tuple-element.18), channel_id=1, source_target_pairs={{0,1},{1,0},{2,3},{3,2},{4,5},{5,4},{6,7},{7,6},{8,9},{9,8},{10,11... | collective-permute-start | bytes 1966088 | tf_op jit(solution)/shard_map/ppermute | solution.py:155
  104.5 20.8 %collective-permute-start.4 = (bf16[256,1280]{1,0:T(8,128)(2,1)}, bf16[256,1280]{1,0:T(8,128)(2,1)}, u32[]{:S(2)}, u32[]{:S(2)}) collective-permute-start(bf16[256,1280]{1,0:T(8,128)(2,1)} %collective-permute-done.2), channel_id=1, source_target_pairs={{0,4},{4,8},{8,12},{12,14},{14,10},{10,6},{6,2},{2,0},{1,5},{5,9},... | collective-permute-start | bytes 1966088 | tf_op jit(solution)/shard_map/ppermute | solution.py:80
  115.2 17.4 %collective-permute-start.19 = (bf16[256,1280]{1,0:T(8,128)(2,1)}, bf16[256,1280]{1,0:T(8,128)(2,1)S(1)}, u32[]{:S(2)}, u32[]{:S(2)}) collective-permute-start(bf16[256,1280]{1,0:T(8,128)(2,1)} %collective-permute-done.17), channel_id=1, source_target_pairs={{0,2},{4,0},{8,4},{12,8},{14,12},{10,14},{6,10},{2,6},{1,3},{5,1},... | collective-permute-start | bytes 1966088 | tf_op jit(solution)/shard_map/ppermute | solution.py:80
  125.3 112.6 %collective-permute-start.18 = (bf16[256,1280]{1,0:T(8,128)(2,1)}, bf16[256,1280]{1,0:T(8,128)(2,1)S(1)}, u32[]{:S(2)}, u32[]{:S(2)}) collective-permute-start(bf16[256,1280]{1,0:T(8,128)(2,1)} %collective-permute-done.17), channel_id=1, source_target_pairs={{0,1},{1,0},{2,3},{3,2},{4,5},{5,4},{6,7},{7,6},{8,9},{9,8},{10,11... | collective-permute-start | bytes 1966088 | tf_op jit(solution)/shard_map/ppermute | solution.py:155
  127.1 17.2 %collective-permute-start.6 = (bf16[256,1280]{1,0:T(8,128)(2,1)}, bf16[256,1280]{1,0:T(8,128)(2,1)S(1)}, u32[]{:S(2)}, u32[]{:S(2)}) collective-permute-start(bf16[256,1280]{1,0:T(8,128)(2,1)} %collective-permute-done.4), channel_id=1, source_target_pairs={{0,4},{4,8},{8,12},{12,14},{14,10},{10,6},{6,2},{2,0},{1,5},{5,9},... | collective-permute-start | bytes 1966088 | tf_op jit(solution)/shard_map/ppermute | solution.py:80
  144.3 94.1 %collective-permute-start.20 = (bf16[256,1280]{1,0:T(8,128)(2,1)S(1)}, bf16[256,1280]{1,0:T(8,128)(2,1)S(1)}, u32[]{:S(2)}, u32[]{:S(2)}) collective-permute-start(bf16[256,1280]{1,0:T(8,128)(2,1)S(1)} %collective-permute-done.19), channel_id=1, source_target_pairs={{0,1},{1,0},{2,3},{3,2},{4,5},{5,4},{6,7},{7,6},{8,9},{9,8},{10,11... | collective-permute-start | bytes 1966088 | tf_op jit(solution)/shard_map/ppermute | solution.py:155
  144.7 17.2 %collective-permute-start.8 = (bf16[256,1280]{1,0:T(8,128)(2,1)S(1)}, bf16[256,1280]{1,0:T(8,128)(2,1)S(1)}, u32[]{:S(2)}, u32[]{:S(2)}) collective-permute-start(bf16[256,1280]{1,0:T(8,128)(2,1)S(1)} %collective-permute-done.6), channel_id=1, source_target_pairs={{0,4},{4,8},{8,12},{12,14},{14,10},{10,6},{6,2},{2,0},{1,5},{5,9},... | collective-permute-start | bytes 1966088 | tf_op jit(solution)/shard_map/ppermute | solution.py:80
  148.9 18.3 %collective-permute-start.7 = (bf16[256,1280]{1,0:T(8,128)(2,1)S(1)}, bf16[256,1280]{1,0:T(8,128)(2,1)S(1)}, u32[]{:S(2)}, u32[]{:S(2)}) collective-permute-start(bf16[256,1280]{1,0:T(8,128)(2,1)S(1)} %collective-permute-done.6), channel_id=1, source_target_pairs={{0,1},{1,0},{2,3},{3,2},{4,5},{5,4},{6,7},{7,6},{8,9},{9,8},{10,11... | collective-permute-start | bytes 1966088 | tf_op jit(solution)/shard_map/ppermute | solution.py:155
  161.9 16.4 %collective-permute-start.23 = (bf16[256,1280]{1,0:T(8,128)(2,1)S(1)}, bf16[256,1280]{1,0:T(8,128)(2,1)S(1)}, u32[]{:S(2)}, u32[]{:S(2)}) collective-permute-start(bf16[256,1280]{1,0:T(8,128)(2,1)S(1)} %collective-permute-done.21), channel_id=1, source_target_pairs={{0,2},{4,0},{8,4},{12,8},{14,12},{10,14},{6,10},{2,6},{1,3},{5,1},... | collective-permute-start | bytes 1966088 | tf_op jit(solution)/shard_map/ppermute | solution.py:80
  165.2 19.4 %collective-permute-start.10 = (bf16[256,1280]{1,0:T(8,128)(2,1)S(1)}, bf16[256,1280]{1,0:T(8,128)(2,1)S(1)}, u32[]{:S(2)}, u32[]{:S(2)}) collective-permute-start(bf16[256,1280]{1,0:T(8,128)(2,1)S(1)} %collective-permute-done.8), channel_id=1, source_target_pairs={{0,4},{4,8},{8,12},{12,14},{14,10},{10,6},{6,2},{2,0},{1,5},{5,9},... | collective-permute-start | bytes 1966088 | tf_op jit(solution)/shard_map/ppermute | solution.py:80
  167.2 18.3 %collective-permute-start.9 = (bf16[256,1280]{1,0:T(8,128)(2,1)S(1)}, bf16[256,1280]{1,0:T(8,128)(2,1)S(1)}, u32[]{:S(2)}, u32[]{:S(2)}) collective-permute-start(bf16[256,1280]{1,0:T(8,128)(2,1)S(1)} %collective-permute-done.8), channel_id=1, source_target_pairs={{0,1},{1,0},{2,3},{3,2},{4,5},{5,4},{6,7},{7,6},{8,9},{9,8},{10,11... | collective-permute-start | bytes 1966088 | tf_op jit(solution)/shard_map/ppermute | solution.py:155
  185.5 26.8 %collective-permute-start.11 = (bf16[256,1280]{1,0:T(8,128)(2,1)S(1)}, bf16[256,1280]{1,0:T(8,128)(2,1)S(1)}, u32[]{:S(2)}, u32[]{:S(2)}) collective-permute-start(bf16[256,1280]{1,0:T(8,128)(2,1)S(1)} %collective-permute-done.10), channel_id=1, source_target_pairs={{0,1},{1,0},{2,3},{3,2},{4,5},{5,4},{6,7},{7,6},{8,9},{9,8},{10,11... | collective-permute-start | bytes 1966088 | tf_op jit(solution)/shard_map/ppermute | solution.py:155
  200.1 39.3 %collective-permute-start.22 = (bf16[256,1280]{1,0:T(8,128)(2,1)S(1)}, bf16[256,1280]{1,0:T(8,128)(2,1)S(1)}, u32[]{:S(2)}, u32[]{:S(2)}) collective-permute-start(bf16[256,1280]{1,0:T(8,128)(2,1)S(1)} %collective-permute-done.21), channel_id=1, source_target_pairs={{0,1},{1,0},{2,3},{3,2},{4,5},{5,4},{6,7},{7,6},{8,9},{9,8},{10,11... | collective-permute-start | bytes 1966088 | tf_op jit(solution)/shard_map/ppermute | solution.py:155
  (55 other events, 415.0 us)

commit v3 on v2

--- a/solution.py
+++ b/solution.py
@@ -154,23 +154,29 @@
             return [x]
         return [x, lax.ppermute(x, "core", [(0, 1), (1, 0)])]
 
+    pair_width = query_cols + pair_cols
+    recv = []
+    for h, direction in enumerate(directions):
+        adapters_padded = jnp.pad(adapter_half(h), ((0, 0), (0, pair_width - query_cols)))
+        piece = jnp.concatenate(
+            [weights[h * half_rows : (h + 1) * half_rows], adapters_padded], axis=0
+        )
+        recv.append(ring_gather(piece, n_chip, order, direction))
+
     total = None
-    adapter_pieces = []
-    for h, direction in enumerate(directions):
-        w_recv = ring_gather(weights[h * half_rows : (h + 1) * half_rows], n_chip, order, direction)
-        a_recv = ring_gather(adapter_half(h), n_chip, order, direction)
-        a_steps = []
-        for s in range(n_chip):
+    adapter_steps = [[], []]
+    for s in range(n_chip):
+        for h, direction in enumerate(directions):
             src_chip = order_table[(pos - s * direction) % n_chip]
-            w_both = swap_core(w_recv[s])
-            a_steps.append(jnp.stack(swap_core(a_recv[s])))
-            for slot, w_piece in enumerate(w_both):
+            both = swap_core(recv[h][s])
+            adapter_steps[h].append(jnp.stack([p[half_rows:, :query_cols] for p in both]))
+            for slot, p in enumerate(both):
                 src_core = me_core if slot == 0 else n_lo - 1 - me_core
                 start = (src_chip * n_lo + src_core) * weight_rows + h * half_rows
                 lhs = lax.dynamic_slice_in_dim(normed, start, half_rows, 1)
-                part = jnp.dot(lhs, w_piece, preferred_element_type=jnp.float32)
+                part = jnp.dot(lhs, p[:half_rows], preferred_element_type=jnp.float32)
                 total = part if total is None else total + part
-        adapter_pieces.append(jnp.stack(a_steps))
+    adapter_pieces = [jnp.stack(a) for a in adapter_steps]
 
     picked = prompt_adapter[0]
     prompt_count = picked.shape[0]

time: 252 us -> 224 us (0.89)
  waiting for transfers between devices: 122 us -> 92.8 us
  starting transfers between devices: 38.1 us -> 18.9 us
  local copies, waits for them, and re-layouts: 19.2 us -> 30.2 us
  matrix products: 25.1 us -> 31.6 us
    ppermute x28 -> x14, waiting for transfers between devices: 118 us -> 92.5 us  [ring_gather(): current = lax.ppermute(current, 'chip', pairs)]
    ppermute x28 -> x14, starting transfers between devices: 30.9 us -> 15.4 us  [ring_gather(): current = lax.ppermute(current, 'chip', pairs)]
    another operation x1 -> x31, local copies, waits for them, and re-layouts: 0.01 us -> 6.12 us  [the longest x30 6.11 us: shards(): jnp.stack([p[half_rows:, :query_cols] for p in both])]
    dot_general x32, matrix products: 20.1 us -> 24.1 us  [shards(): part = jnp.dot(lhs, p[:half_rows], preferred_element_type=jnp.float32)]
    ppermute x32 -> x16, starting transfers between devices: 4.97 us -> 1.28 us  [swap_core(): return [x, lax.ppermute(x, 'core', [(0, 1), (1, 0)])]]
    ppermute x1, waiting for transfers between devices: 3.39 us -> 0.2 us  [sum_blk(): return piece + lax.ppermute(piece, 'blk', [(0, 1), (1, 0)])]
  transfers between devices with their start and end apart: 62 -> 32, of which waited for: 20 -> 12; matrix products, arithmetic and copies ran while one was open for 22% -> 25% of each run, Pallas kernels for 0% -> 0%
where the time goes in v3:
time: 224 us; the launch traced here: 223 us
  waiting for transfers between devices  92.8 us (41%)
  matrix products  31.6 us (14%)
  local copies, waits for them, and re-layouts  30.2 us (13%)
  other arithmetic  26.4 us (12%)
  between operations  22.7 us (10%)
  starting transfers between devices  18.9 us (8%)
    ppermute x14, waiting for transfers between devices, ring_gather(): current = lax.ppermute(current, 'chip', pairs)  92.5 us
    dot_general x32, matrix products, shards(): part = jnp.dot(lhs, p[:half_rows], preferred_element_type=jnp.float32)  24.1 us
    ppermute x14, starting transfers between devices, ring_gather(): current = lax.ppermute(current, 'chip', pairs)  15.4 us
    unnamed x14, other arithmetic  9.09 us
    gather x2, local copies, waits for them, and re-layouts, shards(): per_half.append(adapter_pieces[h][a_step, a_slot])  6.22 us
    another operation x30, local copies, waits for them, and re-layouts, shards(): jnp.stack([p[half_rows:, :query_cols] for p in both])  6.11 us
    unnamed x43, local copies, waits for them, and re-layouts  5.04 us
  transfers between devices with their start and end apart: 32, of which 12 were waited for; matrix products, arithmetic and copies ran while one was open for 25% of the time, Pallas kernels for 0%

profile of v3, /device:TPU:0, one launch (start us, length us, event | category | flops | bytes accessed | tf_op | source)
XLA Modules:
  0.0 222.6 jit_solution(5700098759626088280)
XLA Ops:
  5.5 2.5 %collective-permute-start.5 = (bf16[368,1280]{1,0:T(8,128)(2,1)}, bf16[368,1280]{1,0:T(8,128)(2,1)}, u32[]{:S(2)}, u32[]{:S(2)}) collective-permute-start(bf16[368,1280]{1,0:T(8,128)(2,1)} %fusion.40), channel_id=1, source_target_pairs={{0,2},{4,0},{8,4},{12,8},{14,12},{10,14},{6,10},{2,6},{1,3},{5,1},... | collective-permute-start | bytes 2826248 | tf_op jit(solution)/shard_map/ppermute | solution.py:80
  8.7 1.7 collective-permute-start
  37.5 1.5 collective-permute-start.9
  44.5 16.5 %collective-permute-done.9 = bf16[368,1280]{1,0:T(8,128)(2,1)S(1)} collective-permute-done((bf16[368,1280]{1,0:T(8,128)(2,1)}, bf16[368,1280]{1,0:T(8,128)(2,1)S(1)}, u32[]{:S(2)}, u32[]{:S(2)}) %collective-permute-start.9) | collective-permute-done | bytes 942112 | tf_op jit(solution)/shard_map/ppermute | solution.py:80
  65.1 19.2 %collective-permute-done.13 = bf16[368,1280]{1,0:T(8,128)(2,1)S(1)} collective-permute-done((bf16[368,1280]{1,0:T(8,128)(2,1)S(1)}, bf16[368,1280]{1,0:T(8,128)(2,1)S(1)}, u32[]{:S(2)}, u32[]{:S(2)}) %collective-permute-start.13) | collective-permute-done | bytes 942112 | tf_op jit(solution)/shard_map/ppermute | solution.py:80
  87.5 1.8 copy-done.10
  89.4 3.3 %broadcast_select_fusion.1 = (bf16[384,4096]{1,0:T(8,128)(2,1)S(1)}, bf16[384,4096]{1,0:T(8,128)(2,1)S(1)}) fusion(bf16[384,4096]{1,0:T(8,128)(2,1)} %param.11, bf16[384,4096]{1,0:T(8,128)(2,1)} %collective-permute-done, pred[]{:T(512)S(6)} %eq.42), kind=kLoop, calls=%fused_computation.18 | loop fusion | flops 3145728 | bytes 12582913 | tf_op jit(solution)/shard_map/select_n | solution.py:107
  94.1 1.8 fusion.2
  96.8 2.0 fusion.89
  101.9 1.5 fusion.82
  113.7 17.2 %collective-permute-done.21 = bf16[368,1280]{1,0:T(8,128)(2,1)S(1)} collective-permute-done((bf16[368,1280]{1,0:T(8,128)(2,1)S(1)}, bf16[368,1280]{1,0:T(8,128)(2,1)S(1)}, u32[]{:S(2)}, u32[]{:S(2)}) %collective-permute-start.21) | collective-permute-done | bytes 942112 | tf_op jit(solution)/shard_map/ppermute | solution.py:80
  132.4 2.1 collective-permute-done.19
  138.7 15.5 %collective-permute-done.25 = bf16[368,1280]{1,0:T(8,128)(2,1)S(1)} collective-permute-done((bf16[368,1280]{1,0:T(8,128)(2,1)S(1)}, bf16[368,1280]{1,0:T(8,128)(2,1)S(1)}, u32[]{:S(2)}, u32[]{:S(2)}) %collective-permute-start.25) | collective-permute-done | bytes 942112 | tf_op jit(solution)/shard_map/ppermute | solution.py:80
  155.7 2.2 collective-permute-done.23
  162.0 15.5 %collective-permute-done.29 = bf16[368,1280]{1,0:T(8,128)(2,1)S(1)} collective-permute-done((bf16[368,1280]{1,0:T(8,128)(2,1)S(1)}, bf16[368,1280]{1,0:T(8,128)(2,1)S(1)}, u32[]{:S(2)}, u32[]{:S(2)}) %collective-permute-start.29) | collective-permute-done | bytes 942112 | tf_op jit(solution)/shard_map/ppermute | solution.py:80
  178.4 2.9 %collective-permute-done.27 = bf16[368,1280]{1,0:T(8,128)(2,1)} collective-permute-done((bf16[368,1280]{1,0:T(8,128)(2,1)S(1)}, bf16[368,1280]{1,0:T(8,128)(2,1)}, u32[]{:S(2)}, u32[]{:S(2)}) %collective-permute-start.27) | collective-permute-done | bytes 942112 | tf_op jit(solution)/shard_map/ppermute | solution.py:80
  185.5 1.7 fusion.9
  189.0 2.6 %gather_fusion.2 = bf16[4,112,1024]{2,1,0:T(8,128)(2,1)S(1)} fusion(bf16[8,2,112,1024]{3,2,1,0:T(8,128)(2,1)} %fusion.107, s32[4]{0:T(128)S(1)} %fusion.198), kind=kCustom, calls=%fused_computation.2 | custom fusion | bytes 1835040 | tf_op jit(solution)/shard_map/gather | solution.py:189
  194.5 3.6 %gather_fusion.1 = bf16[4,112,1024]{2,1,0:T(8,128)(2,1)} fusion(bf16[8,2,112,1024]{3,2,1,0:T(8,128)(2,1)} %fusion.99, s32[4]{0:T(128)S(1)} %get-tuple-element.11), kind=kCustom, calls=%fused_computation.1 | custom fusion | bytes 1835040 | tf_op jit(solution)/shard_map/gather | solution.py:189
  198.9 2.1 slice.423
  203.2 2.5 %dot_general.148 = bf16[4,3,16,4096]{3,2,1,0:T(8,128)(2,1)} reshape(bf16[4,192,1024]{2,1,0:T(8,128)(2,1)S(1)} %pad_maximum_fusion.1) | data formatting | bytes 3145728 | tf_op jit(solution)/shard_map/dot_general | solution.py:206
  205.7 3.7 %fusion.35 = f32[384,3,16]{0,2,1:T(8,128)S(1)} fusion(bf16[4,3,16,4096]{3,2,1,0:T(8,128)(2,1)} %dot_general.148, bf16[384,8192]{1,0:T(8,128)(2,1)} %copy-done.1, s32[]{:T(128)S(6)} %select_n.386, f32[384,4]{0,1:T(4,128)S(1)} %fusion.203), kind=kOutput, calls=%fused_computation.66 | convolution fusion | flops 604108800 | bytes 4798468 | tf_op jit(solution)/shard_map/dot_general | solution.py:206
  209.9 1.7 fusion.8
  219.8 1.6 fusion.27
  (227 shorter events, 73.2 us)
Async XLA Ops:
  5.0 32.5 %collective-permute-start.2 = (bf16[368,1280]{1,0:T(8,128)(2,1)}, bf16[368,1280]{1,0:T(8,128)(2,1)}, u32[]{:S(2)}, u32[]{:S(2)}) collective-permute-start(bf16[368,1280]{1,0:T(8,128)(2,1)} %fusion.40), channel_id=1, source_target_pairs={{0,1},{1,0},{2,3},{3,2},{4,5},{5,4},{6,7},{7,6},{8,9},{9,8},{10,11... | collective-permute-start | bytes 2826248 | tf_op jit(solution)/shard_map/ppermute | solution.py:155
  5.5 32.0 %collective-permute-start.5 = (bf16[368,1280]{1,0:T(8,128)(2,1)}, bf16[368,1280]{1,0:T(8,128)(2,1)}, u32[]{:S(2)}, u32[]{:S(2)}) collective-permute-start(bf16[368,1280]{1,0:T(8,128)(2,1)} %fusion.40), channel_id=1, source_target_pairs={{0,2},{4,0},{8,4},{12,8},{14,12},{10,14},{6,10},{2,6},{1,3},{5,1},... | collective-permute-start | bytes 2826248 | tf_op jit(solution)/shard_map/ppermute | solution.py:80
  8.0 32.2 %collective-permute-start.1 = (bf16[368,1280]{1,0:T(8,128)(2,1)S(1)}, bf16[368,1280]{1,0:T(8,128)(2,1)}, u32[]{:S(2)}, u32[]{:S(2)}) collective-permute-start(bf16[368,1280]{1,0:T(8,128)(2,1)S(1)} %fusion.39), channel_id=1, source_target_pairs={{0,1},{1,0},{2,3},{3,2},{4,5},{5,4},{6,7},{7,6},{8,9},{9,8},{10,11... | collective-permute-start | bytes 2826248 | tf_op jit(solution)/shard_map/ppermute | solution.py:155
  8.3 30.7 %collective-permute-start.3 = (bf16[368,1280]{1,0:T(8,128)(2,1)S(1)}, bf16[368,1280]{1,0:T(8,128)(2,1)}, u32[]{:S(2)}, u32[]{:S(2)}) collective-permute-start(bf16[368,1280]{1,0:T(8,128)(2,1)S(1)} %fusion.39), channel_id=1, source_target_pairs={{0,4},{4,8},{8,12},{12,14},{14,10},{10,6},{6,2},{2,0},{1,5},{5,9},... | collective-permute-start | bytes 2826248 | tf_op jit(solution)/shard_map/ppermute | solution.py:80
  8.7 80.7 %collective-permute-start = (bf16[384,4096]{1,0:T(8,128)(2,1)}, bf16[384,4096]{1,0:T(8,128)(2,1)}, u32[]{:S(2)}, u32[]{:S(2)}) collective-permute-start(bf16[384,4096]{1,0:T(8,128)(2,1)} %param.11), channel_id=1, source_target_pairs={{0,16},{16,0},{1,17},{17,1},{2,18},{18,2},{3,19},{19,3},{4,20},{20... | collective-permute-start | bytes 9437192 | tf_op jit(solution)/shard_map/ppermute | solution.py:106
  37.5 23.5 %collective-permute-start.6 = (bf16[368,1280]{1,0:T(8,128)(2,1)}, bf16[368,1280]{1,0:T(8,128)(2,1)S(1)}, u32[]{:S(2)}, u32[]{:S(2)}) collective-permute-start(bf16[368,1280]{1,0:T(8,128)(2,1)} %collective-permute-done.5), channel_id=1, source_target_pairs={{0,1},{1,0},{2,3},{3,2},{4,5},{5,4},{6,7},{7,6},{8,9},{9,8},{10,11... | collective-permute-start | bytes 2826248 | tf_op jit(solution)/shard_map/ppermute | solution.py:155
  37.5 23.5 %collective-permute-start.9 = (bf16[368,1280]{1,0:T(8,128)(2,1)}, bf16[368,1280]{1,0:T(8,128)(2,1)S(1)}, u32[]{:S(2)}, u32[]{:S(2)}) collective-permute-start(bf16[368,1280]{1,0:T(8,128)(2,1)} %collective-permute-done.5), channel_id=1, source_target_pairs={{0,2},{4,0},{8,4},{12,8},{14,12},{10,14},{6,10},{2,6},{1,3},{5,1},... | collective-permute-start | bytes 2826248 | tf_op jit(solution)/shard_map/ppermute | solution.py:80
  39.1 25.9 %collective-permute-start.4 = (bf16[368,1280]{1,0:T(8,128)(2,1)}, bf16[368,1280]{1,0:T(8,128)(2,1)S(1)}, u32[]{:S(2)}, u32[]{:S(2)}) collective-permute-start(bf16[368,1280]{1,0:T(8,128)(2,1)} %collective-permute-done.3), channel_id=1, source_target_pairs={{0,1},{1,0},{2,3},{3,2},{4,5},{5,4},{6,7},{7,6},{8,9},{9,8},{10,11... | collective-permute-start | bytes 2826248 | tf_op jit(solution)/shard_map/ppermute | solution.py:155
  40.2 23.4 %collective-permute-start.7 = (bf16[368,1280]{1,0:T(8,128)(2,1)}, bf16[368,1280]{1,0:T(8,128)(2,1)S(1)}, u32[]{:S(2)}, u32[]{:S(2)}) collective-permute-start(bf16[368,1280]{1,0:T(8,128)(2,1)} %collective-permute-done.3), channel_id=1, source_target_pairs={{0,4},{4,8},{8,12},{12,14},{14,10},{10,6},{6,2},{2,0},{1,5},{5,9},... | collective-permute-start | bytes 2826248 | tf_op jit(solution)/shard_map/ppermute | solution.py:80
  61.0 23.3 %collective-permute-start.10 = (bf16[368,1280]{1,0:T(8,128)(2,1)S(1)}, bf16[368,1280]{1,0:T(8,128)(2,1)S(1)}, u32[]{:S(2)}, u32[]{:S(2)}) collective-permute-start(bf16[368,1280]{1,0:T(8,128)(2,1)S(1)} %collective-permute-done.9), channel_id=1, source_target_pairs={{0,1},{1,0},{2,3},{3,2},{4,5},{5,4},{6,7},{7,6},{8,9},{9,8},{10,11... | collective-permute-start | bytes 2826248 | tf_op jit(solution)/shard_map/ppermute | solution.py:155
  61.0 23.3 %collective-permute-start.13 = (bf16[368,1280]{1,0:T(8,128)(2,1)S(1)}, bf16[368,1280]{1,0:T(8,128)(2,1)S(1)}, u32[]{:S(2)}, u32[]{:S(2)}) collective-permute-start(bf16[368,1280]{1,0:T(8,128)(2,1)S(1)} %collective-permute-done.9), channel_id=1, source_target_pairs={{0,2},{4,0},{8,4},{12,8},{14,12},{10,14},{6,10},{2,6},{1,3},{5,1},... | collective-permute-start | bytes 2826248 | tf_op jit(solution)/shard_map/ppermute | solution.py:80
  84.3 24.8 %collective-permute-start.14 = (bf16[368,1280]{1,0:T(8,128)(2,1)S(1)}, bf16[368,1280]{1,0:T(8,128)(2,1)S(1)}, u32[]{:S(2)}, u32[]{:S(2)}) collective-permute-start(bf16[368,1280]{1,0:T(8,128)(2,1)S(1)} %collective-permute-done.13), channel_id=1, source_target_pairs={{0,1},{1,0},{2,3},{3,2},{4,5},{5,4},{6,7},{7,6},{8,9},{9,8},{10,11... | collective-permute-start | bytes 2826248 | tf_op jit(solution)/shard_map/ppermute | solution.py:155
  84.3 23.3 %collective-permute-start.17 = (bf16[368,1280]{1,0:T(8,128)(2,1)S(1)}, bf16[368,1280]{1,0:T(8,128)(2,1)S(1)}, u32[]{:S(2)}, u32[]{:S(2)}) collective-permute-start(bf16[368,1280]{1,0:T(8,128)(2,1)S(1)} %collective-permute-done.13), channel_id=1, source_target_pairs={{0,2},{4,0},{8,4},{12,8},{14,12},{10,14},{6,10},{2,6},{1,3},{5,1},... | collective-permute-start | bytes 2826248 | tf_op jit(solution)/shard_map/ppermute | solution.py:80
  86.0 24.0 %collective-permute-start.12 = (bf16[368,1280]{1,0:T(8,128)(2,1)S(1)}, bf16[368,1280]{1,0:T(8,128)(2,1)S(1)}, u32[]{:S(2)}, u32[]{:S(2)}) collective-permute-start(bf16[368,1280]{1,0:T(8,128)(2,1)S(1)} %collective-permute-done.11), channel_id=1, source_target_pairs={{0,1},{1,0},{2,3},{3,2},{4,5},{5,4},{6,7},{7,6},{8,9},{9,8},{10,11... | collective-permute-start | bytes 2826248 | tf_op jit(solution)/shard_map/ppermute | solution.py:155
  86.9 24.0 %collective-permute-start.15 = (bf16[368,1280]{1,0:T(8,128)(2,1)S(1)}, bf16[368,1280]{1,0:T(8,128)(2,1)S(1)}, u32[]{:S(2)}, u32[]{:S(2)}) collective-permute-start(bf16[368,1280]{1,0:T(8,128)(2,1)S(1)} %collective-permute-done.11), channel_id=1, source_target_pairs={{0,4},{4,8},{8,12},{12,14},{14,10},{10,6},{6,2},{2,0},{1,5},{5,9},... | collective-permute-start | bytes 2826248 | tf_op jit(solution)/shard_map/ppermute | solution.py:80
  107.6 26.9 %collective-permute-start.18 = (bf16[368,1280]{1,0:T(8,128)(2,1)S(1)}, bf16[368,1280]{1,0:T(8,128)(2,1)S(1)}, u32[]{:S(2)}, u32[]{:S(2)}) collective-permute-start(bf16[368,1280]{1,0:T(8,128)(2,1)S(1)} %collective-permute-done.17), channel_id=1, source_target_pairs={{0,1},{1,0},{2,3},{3,2},{4,5},{5,4},{6,7},{7,6},{8,9},{9,8},{10,11... | collective-permute-start | bytes 2826248 | tf_op jit(solution)/shard_map/ppermute | solution.py:155
  110.9 26.0 %collective-permute-start.16 = (bf16[368,1280]{1,0:T(8,128)(2,1)S(1)}, bf16[368,1280]{1,0:T(8,128)(2,1)S(1)}, u32[]{:S(2)}, u32[]{:S(2)}) collective-permute-start(bf16[368,1280]{1,0:T(8,128)(2,1)S(1)} %collective-permute-done.15), channel_id=1, source_target_pairs={{0,1},{1,0},{2,3},{3,2},{4,5},{5,4},{6,7},{7,6},{8,9},{9,8},{10,11... | collective-permute-start | bytes 2826248 | tf_op jit(solution)/shard_map/ppermute | solution.py:155
  111.1 23.3 %collective-permute-start.19 = (bf16[368,1280]{1,0:T(8,128)(2,1)S(1)}, bf16[368,1280]{1,0:T(8,128)(2,1)S(1)}, u32[]{:S(2)}, u32[]{:S(2)}) collective-permute-start(bf16[368,1280]{1,0:T(8,128)(2,1)S(1)} %collective-permute-done.15), channel_id=1, source_target_pairs={{0,4},{4,8},{8,12},{12,14},{14,10},{10,6},{6,2},{2,0},{1,5},{5,9},... | collective-permute-start | bytes 2826248 | tf_op jit(solution)/shard_map/ppermute | solution.py:80
  130.9 27.0 %collective-permute-start.22 = (bf16[368,1280]{1,0:T(8,128)(2,1)S(1)}, bf16[368,1280]{1,0:T(8,128)(2,1)S(1)}, u32[]{:S(2)}, u32[]{:S(2)}) collective-permute-start(bf16[368,1280]{1,0:T(8,128)(2,1)S(1)} %collective-permute-done.21), channel_id=1, source_target_pairs={{0,1},{1,0},{2,3},{3,2},{4,5},{5,4},{6,7},{7,6},{8,9},{9,8},{10,11... | collective-permute-start | bytes 2826248 | tf_op jit(solution)/shard_map/ppermute | solution.py:155
  130.9 23.3 %collective-permute-start.25 = (bf16[368,1280]{1,0:T(8,128)(2,1)S(1)}, bf16[368,1280]{1,0:T(8,128)(2,1)S(1)}, u32[]{:S(2)}, u32[]{:S(2)}) collective-permute-start(bf16[368,1280]{1,0:T(8,128)(2,1)S(1)} %collective-permute-done.21), channel_id=1, source_target_pairs={{0,2},{4,0},{8,4},{12,8},{14,12},{10,14},{6,10},{2,6},{1,3},{5,1},... | collective-permute-start | bytes 2826248 | tf_op jit(solution)/shard_map/ppermute | solution.py:80
  134.5 25.7 %collective-permute-start.20 = (bf16[368,1280]{1,0:T(8,128)(2,1)S(1)}, bf16[368,1280]{1,0:T(8,128)(2,1)S(1)}, u32[]{:S(2)}, u32[]{:S(2)}) collective-permute-start(bf16[368,1280]{1,0:T(8,128)(2,1)S(1)} %collective-permute-done.19), channel_id=1, source_target_pairs={{0,1},{1,0},{2,3},{3,2},{4,5},{5,4},{6,7},{7,6},{8,9},{9,8},{10,11... | collective-permute-start | bytes 2826248 | tf_op jit(solution)/shard_map/ppermute | solution.py:155
  134.5 23.3 %collective-permute-start.23 = (bf16[368,1280]{1,0:T(8,128)(2,1)S(1)}, bf16[368,1280]{1,0:T(8,128)(2,1)S(1)}, u32[]{:S(2)}, u32[]{:S(2)}) collective-permute-start(bf16[368,1280]{1,0:T(8,128)(2,1)S(1)} %collective-permute-done.19), channel_id=1, source_target_pairs={{0,4},{4,8},{8,12},{12,14},{14,10},{10,6},{6,2},{2,0},{1,5},{5,9},... | collective-permute-start | bytes 2826248 | tf_op jit(solution)/shard_map/ppermute | solution.py:80
  154.2 23.3 %collective-permute-start.26 = (bf16[368,1280]{1,0:T(8,128)(2,1)S(1)}, bf16[368,1280]{1,0:T(8,128)(2,1)S(1)}, u32[]{:S(2)}, u32[]{:S(2)}) collective-permute-start(bf16[368,1280]{1,0:T(8,128)(2,1)S(1)} %collective-permute-done.25), channel_id=1, source_target_pairs={{0,1},{1,0},{2,3},{3,2},{4,5},{5,4},{6,7},{7,6},{8,9},{9,8},{10,11... | collective-permute-start | bytes 2826248 | tf_op jit(solution)/shard_map/ppermute | solution.py:155
  157.9 23.4 %collective-permute-start.27 = (bf16[368,1280]{1,0:T(8,128)(2,1)S(1)}, bf16[368,1280]{1,0:T(8,128)(2,1)}, u32[]{:S(2)}, u32[]{:S(2)}) collective-permute-start(bf16[368,1280]{1,0:T(8,128)(2,1)S(1)} %collective-permute-done.23), channel_id=1, source_target_pairs={{0,4},{4,8},{8,12},{12,14},{14,10},{10,6},{6,2},{2,0},{1,5},{5,9},... | collective-permute-start | bytes 2826248 | tf_op jit(solution)/shard_map/ppermute | solution.py:80
  (29 other events, 302.1 us)

commit v4 on v3

--- a/solution.py
+++ b/solution.py
@@ -154,29 +154,27 @@
             return [x]
         return [x, lax.ppermute(x, "core", [(0, 1), (1, 0)])]
 
-    pair_width = query_cols + pair_cols
-    recv = []
+    w_recv, a_recv = [], []
     for h, direction in enumerate(directions):
-        adapters_padded = jnp.pad(adapter_half(h), ((0, 0), (0, pair_width - query_cols)))
-        piece = jnp.concatenate(
-            [weights[h * half_rows : (h + 1) * half_rows], adapters_padded], axis=0
+        a_recv.append(ring_gather(adapter_half(h), n_chip, order, direction))
+        w_recv.append(
+            ring_gather(weights[h * half_rows : (h + 1) * half_rows], n_chip, order, direction)
         )
-        recv.append(ring_gather(piece, n_chip, order, direction))
+    adapter_pieces = [
+        jnp.stack([jnp.stack(swap_core(a_recv[h][s])) for s in range(n_chip)])
+        for h in range(len(directions))
+    ]
 
     total = None
-    adapter_steps = [[], []]
     for s in range(n_chip):
         for h, direction in enumerate(directions):
             src_chip = order_table[(pos - s * direction) % n_chip]
-            both = swap_core(recv[h][s])
-            adapter_steps[h].append(jnp.stack([p[half_rows:, :query_cols] for p in both]))
-            for slot, p in enumerate(both):
+            for slot, p in enumerate(swap_core(w_recv[h][s])):
                 src_core = me_core if slot == 0 else n_lo - 1 - me_core
                 start = (src_chip * n_lo + src_core) * weight_rows + h * half_rows
                 lhs = lax.dynamic_slice_in_dim(normed, start, half_rows, 1)
-                part = jnp.dot(lhs, p[:half_rows], preferred_element_type=jnp.float32)
+                part = jnp.dot(lhs, p, preferred_element_type=jnp.float32)
                 total = part if total is None else total + part
-    adapter_pieces = [jnp.stack(a) for a in adapter_steps]
 
     picked = prompt_adapter[0]
     prompt_count = picked.shape[0]

time: 224 us -> 239 us (1.067)
  starting transfers between devices: 18.9 us -> 37.5 us
  waiting for transfers between devices: 92.8 us -> 108 us
  local copies, waits for them, and re-layouts: 30.2 us -> 20.2 us
  matrix products: 31.6 us -> 24.9 us
  other arithmetic: 26.4 us -> 23.9 us
    ppermute x14 -> x28, starting transfers between devices: 15.4 us -> 31.4 us  [ring_gather(): current = lax.ppermute(current, 'chip', pairs)]
    ppermute x14 -> x28, waiting for transfers between devices: 92.5 us -> 105 us  [ring_gather(): current = lax.ppermute(current, 'chip', pairs)]
    another operation x31 -> x1, local copies, waits for them, and re-layouts: 6.12 us -> 0.01 us  [the longest x30 6.11 us: shards(): jnp.stack([p[half_rows:, :query_cols] for p in both])]
    dot_general x32, matrix products: 24.1 us -> 19.9 us  [shards(): part = jnp.dot(lhs, p, preferred_element_type=jnp.float32)]
    ppermute x1, waiting for transfers between devices: 0.2 us -> 2.86 us  [sum_blk(): return piece + lax.ppermute(piece, 'blk', [(0, 1), (1, 0)])]
    ppermute x16 -> x32, starting transfers between devices: 1.28 us -> 3.81 us  [swap_core(): return [x, lax.ppermute(x, 'core', [(0, 1), (1, 0)])]]
    dot_general x1, matrix products: 3.68 us -> 1.18 us  [shards(): lax.dot_general(normed_part, down_selected.reshape(prompt_count * 3 * ran...]
    unnamed x43 -> x35, local copies, waits for them, and re-layouts: 5.04 us -> 4.38 us
  transfers between devices with their start and end apart: 32 -> 62, of which waited for: 12 -> 21; matrix products, arithmetic and copies ran while one was open for 25% -> 23% of each run, Pallas kernels for 0% -> 0%
where the time goes in v4:
time: 239 us; the launch traced here: 238 us
  waiting for transfers between devices  108 us (45%)
  starting transfers between devices  37.5 us (16%)
  matrix products  24.9 us (10%)
  other arithmetic  23.9 us (10%)
  between operations  22.6 us (9%)
  local copies, waits for them, and re-layouts  20.2 us (8%)
    ppermute x28, waiting for transfers between devices, ring_gather(): current = lax.ppermute(current, 'chip', pairs)  105 us
    ppermute x28, starting transfers between devices, ring_gather(): current = lax.ppermute(current, 'chip', pairs)  31.4 us
    dot_general x32, matrix products, shards(): part = jnp.dot(lhs, p, preferred_element_type=jnp.float32)  19.9 us
    unnamed x14, other arithmetic  9.67 us
    gather x2, local copies, waits for them, and re-layouts, shards(): per_half.append(adapter_pieces[h][a_step, a_slot])  5.29 us
  transfers between devices with their start and end apart: 62, of which 21 were waited for; matrix products, arithmetic and copies ran while one was open for 23% of the time, Pallas kernels for 0%

profile of v4, /device:TPU:0, one launch (start us, length us, event | category | flops | bytes accessed | tf_op | source)
XLA Modules:
  0.0 237.5 jit_solution(7607090667609975037)
XLA Ops:
  4.3 2.6 %collective-permute-start.47 = (bf16[112,1024]{1,0:T(8,128)(2,1)S(1)}, bf16[112,1024]{1,0:T(8,128)(2,1)}, u32[]{:S(2)}, u32[]{:S(2)}) collective-permute-start(bf16[112,1024]{1,0:T(8,128)(2,1)S(1)} %get-tuple-element.42), channel_id=1, source_target_pairs={{0,2},{4,0},{8,4},{12,8},{14,12},{10,14},{6,10},{2,6},{1,3},{5,1},... | collective-permute-start | bytes 688136 | tf_op jit(solution)/shard_map/ppermute | solution.py:80
  43.7 2.6 %collective-permute-done.34 = bf16[112,1024]{1,0:T(8,128)(2,1)S(1)} collective-permute-done((bf16[112,1024]{1,0:T(8,128)(2,1)}, bf16[112,1024]{1,0:T(8,128)(2,1)S(1)}, u32[]{:S(2)}, u32[]{:S(2)}) %collective-permute-start.34) | collective-permute-done | bytes 229408 | tf_op jit(solution)/shard_map/ppermute | solution.py:80
  54.6 2.2 collective-permute-done.53
  60.7 4.1 %collective-permute-done.55 = bf16[112,1024]{1,0:T(8,128)(2,1)S(1)} collective-permute-done((bf16[112,1024]{1,0:T(8,128)(2,1)S(1)}, bf16[112,1024]{1,0:T(8,128)(2,1)S(1)}, u32[]{:S(2)}, u32[]{:S(2)}) %collective-permute-start.55) | collective-permute-done | bytes 229408 | tf_op jit(solution)/shard_map/ppermute | solution.py:80
  69.6 3.3 %collective-permute-done.57 = bf16[112,1024]{1,0:T(8,128)(2,1)S(1)} collective-permute-done((bf16[112,1024]{1,0:T(8,128)(2,1)S(1)}, bf16[112,1024]{1,0:T(8,128)(2,1)S(1)}, u32[]{:S(2)}, u32[]{:S(2)}) %collective-permute-start.57) | collective-permute-done | bytes 229408 | tf_op jit(solution)/shard_map/ppermute | solution.py:80
  75.3 14.3 %collective-permute-done.42 = bf16[112,1024]{1,0:T(8,128)(2,1)S(1)} collective-permute-done((bf16[112,1024]{1,0:T(8,128)(2,1)S(1)}, bf16[112,1024]{1,0:T(8,128)(2,1)S(1)}, u32[]{:S(2)}, u32[]{:S(2)}) %collective-permute-start.42) | collective-permute-done | bytes 229408 | tf_op jit(solution)/shard_map/ppermute | solution.py:80
  91.5 6.0 %collective-permute-done.44 = bf16[112,1024]{1,0:T(8,128)(2,1)S(1)} collective-permute-done((bf16[112,1024]{1,0:T(8,128)(2,1)S(1)}, bf16[112,1024]{1,0:T(8,128)(2,1)S(1)}, u32[]{:S(2)}, u32[]{:S(2)}) %collective-permute-start.44) | collective-permute-done | bytes 229408 | tf_op jit(solution)/shard_map/ppermute | solution.py:80
  100.2 2.6 %gather_fusion.2 = bf16[4,112,1024]{2,1,0:T(8,128)(2,1)S(1)} fusion(bf16[8,2,112,1024]{3,2,1,0:T(8,128)(2,1)} %fusion.54, s32[4]{0:T(128)S(1)} %fusion.161), kind=kCustom, calls=%fused_computation.2 | custom fusion | bytes 1835040 | tf_op jit(solution)/shard_map/gather | solution.py:187
  105.4 2.6 %gather_fusion.1 = bf16[4,112,1024]{2,1,0:T(8,128)(2,1)S(1)} fusion(bf16[8,2,112,1024]{3,2,1,0:T(8,128)(2,1)} %fusion.46, s32[4]{0:T(128)S(1)} %get-tuple-element.11), kind=kCustom, calls=%fused_computation.1 | custom fusion | bytes 1835040 | tf_op jit(solution)/shard_map/gather | solution.py:187
  109.7 2.3 dot_general.148
  112.1 3.0 %collective-permute-done.5 = bf16[256,1280]{1,0:T(8,128)(2,1)} collective-permute-done((bf16[256,1280]{1,0:T(8,128)(2,1)}, bf16[256,1280]{1,0:T(8,128)(2,1)}, u32[]{:S(2)}, u32[]{:S(2)}) %collective-permute-start.5) | collective-permute-done | bytes 655392 | tf_op jit(solution)/shard_map/ppermute | solution.py:80
  117.2 3.3 %broadcast_select_fusion.1 = (bf16[384,4096]{1,0:T(8,128)(2,1)S(1)}, bf16[384,4096]{1,0:T(8,128)(2,1)S(1)}) fusion(bf16[384,4096]{1,0:T(8,128)(2,1)} %param.11, bf16[384,4096]{1,0:T(8,128)(2,1)} %collective-permute-done, pred[]{:T(512)S(6)} %eq.42), kind=kLoop, calls=%fused_computation.18 | loop fusion | flops 3145728 | bytes 12582913 | tf_op jit(solution)/shard_map/select_n | solution.py:107
  121.9 1.8 fusion.2
  127.7 4.0 %collective-permute-done.7 = bf16[256,1280]{1,0:T(8,128)(2,1)S(1)} collective-permute-done((bf16[256,1280]{1,0:T(8,128)(2,1)}, bf16[256,1280]{1,0:T(8,128)(2,1)S(1)}, u32[]{:S(2)}, u32[]{:S(2)}) %collective-permute-start.7) | collective-permute-done | bytes 655392 | tf_op jit(solution)/shard_map/ppermute | solution.py:80
  138.4 11.0 %collective-permute-done.11 = bf16[256,1280]{1,0:T(8,128)(2,1)S(1)} collective-permute-done((bf16[256,1280]{1,0:T(8,128)(2,1)S(1)}, bf16[256,1280]{1,0:T(8,128)(2,1)S(1)}, u32[]{:S(2)}, u32[]{:S(2)}) %collective-permute-start.11) | collective-permute-done | bytes 655392 | tf_op jit(solution)/shard_map/ppermute | solution.py:80
  149.4 1.9 fusion.20
  154.6 13.9 %collective-permute-done.15 = bf16[256,1280]{1,0:T(8,128)(2,1)S(1)} collective-permute-done((bf16[256,1280]{1,0:T(8,128)(2,1)S(1)}, bf16[256,1280]{1,0:T(8,128)(2,1)S(1)}, u32[]{:S(2)}, u32[]{:S(2)}) %collective-permute-start.15) | collective-permute-done | bytes 655392 | tf_op jit(solution)/shard_map/ppermute | solution.py:80
  176.9 2.9 %collective-permute-done.61 = f32[384,48]{0,1:T(8,128)S(1)} collective-permute-done((f32[384,48]{0,1:T(8,128)S(1)}, f32[384,48]{0,1:T(8,128)S(1)}, u32[]{:S(2)}, u32[]{:S(2)}) %collective-permute-start.61) | collective-permute-done | bytes 73760 | tf_op jit(solution)/shard_map/ppermute | solution.py:65
  180.0 6.2 %collective-permute-done.19 = bf16[256,1280]{1,0:T(8,128)(2,1)S(1)} collective-permute-done((bf16[256,1280]{1,0:T(8,128)(2,1)S(1)}, bf16[256,1280]{1,0:T(8,128)(2,1)S(1)}, u32[]{:S(2)}, u32[]{:S(2)}) %collective-permute-start.19) | collective-permute-done | bytes 655392 | tf_op jit(solution)/shard_map/ppermute | solution.py:80
  186.7 3.6 %collective-permute-done.21 = bf16[256,1280]{1,0:T(8,128)(2,1)S(1)} collective-permute-done((bf16[256,1280]{1,0:T(8,128)(2,1)S(1)}, bf16[256,1280]{1,0:T(8,128)(2,1)S(1)}, u32[]{:S(2)}, u32[]{:S(2)}) %collective-permute-start.21) | collective-permute-done | bytes 655392 | tf_op jit(solution)/shard_map/ppermute | solution.py:80
  193.6 9.7 %collective-permute-done.23 = bf16[256,1280]{1,0:T(8,128)(2,1)S(1)} collective-permute-done((bf16[256,1280]{1,0:T(8,128)(2,1)S(1)}, bf16[256,1280]{1,0:T(8,128)(2,1)S(1)}, u32[]{:S(2)}, u32[]{:S(2)}) %collective-permute-start.23) | collective-permute-done | bytes 655392 | tf_op jit(solution)/shard_map/ppermute | solution.py:80
  203.9 4.1 %collective-permute-done.25 = bf16[256,1280]{1,0:T(8,128)(2,1)S(1)} collective-permute-done((bf16[256,1280]{1,0:T(8,128)(2,1)S(1)}, bf16[256,1280]{1,0:T(8,128)(2,1)S(1)}, u32[]{:S(2)}, u32[]{:S(2)}) %collective-permute-start.25) | collective-permute-done | bytes 655392 | tf_op jit(solution)/shard_map/ppermute | solution.py:80
  211.5 9.0 %collective-permute-done.27 = bf16[256,1280]{1,0:T(8,128)(2,1)S(1)} collective-permute-done((bf16[256,1280]{1,0:T(8,128)(2,1)S(1)}, bf16[256,1280]{1,0:T(8,128)(2,1)S(1)}, u32[]{:S(2)}, u32[]{:S(2)}) %collective-permute-start.27) | collective-permute-done | bytes 655392 | tf_op jit(solution)/shard_map/ppermute | solution.py:80
  220.5 5.3 %collective-permute-done.29 = bf16[256,1280]{1,0:T(8,128)(2,1)S(1)} collective-permute-done((bf16[256,1280]{1,0:T(8,128)(2,1)S(1)}, bf16[256,1280]{1,0:T(8,128)(2,1)S(1)}, u32[]{:S(2)}, u32[]{:S(2)}) %collective-permute-start.29) | collective-permute-done | bytes 655392 | tf_op jit(solution)/shard_map/ppermute | solution.py:80
  (248 shorter events, 92.7 us)
Async XLA Ops:
  6.9 33.8 %collective-permute-start.31 = (bf16[112,1024]{1,0:T(8,128)(2,1)S(1)}, bf16[112,1024]{1,0:T(8,128)(2,1)}, u32[]{:S(2)}, u32[]{:S(2)}) collective-permute-start(bf16[112,1024]{1,0:T(8,128)(2,1)S(1)} %get-tuple-element.41), channel_id=1, source_target_pairs={{0,1},{1,0},{2,3},{3,2},{4,5},{5,4},{6,7},{7,6},{8,9},{9,8},{10,11... | collective-permute-start | bytes 688136 | tf_op jit(solution)/shard_map/ppermute | solution.py:155
  7.0 31.3 %collective-permute-start.32 = (bf16[112,1024]{1,0:T(8,128)(2,1)S(1)}, bf16[112,1024]{1,0:T(8,128)(2,1)}, u32[]{:S(2)}, u32[]{:S(2)}) collective-permute-start(bf16[112,1024]{1,0:T(8,128)(2,1)S(1)} %get-tuple-element.41), channel_id=1, source_target_pairs={{0,4},{4,8},{8,12},{12,14},{14,10},{10,6},{6,2},{2,0},{1,5},{5,9},... | collective-permute-start | bytes 688136 | tf_op jit(solution)/shard_map/ppermute | solution.py:80
  7.4 108.3 %collective-permute-start = (bf16[384,4096]{1,0:T(8,128)(2,1)}, bf16[384,4096]{1,0:T(8,128)(2,1)}, u32[]{:S(2)}, u32[]{:S(2)}) collective-permute-start(bf16[384,4096]{1,0:T(8,128)(2,1)} %param.11), channel_id=1, source_target_pairs={{0,16},{16,0},{1,17},{17,1},{2,18},{18,2},{3,19},{19,3},{4,20},{20... | collective-permute-start | bytes 9437192 | tf_op jit(solution)/shard_map/ppermute | solution.py:106
  14.3 26.9 %collective-permute-start.48 = (bf16[112,1024]{1,0:T(8,128)(2,1)}, bf16[112,1024]{1,0:T(8,128)(2,1)S(1)}, u32[]{:S(2)}, u32[]{:S(2)}) collective-permute-start(bf16[112,1024]{1,0:T(8,128)(2,1)} %collective-permute-done.47), channel_id=1, source_target_pairs={{0,1},{1,0},{2,3},{3,2},{4,5},{5,4},{6,7},{7,6},{8,9},{9,8},{10,11... | collective-permute-start | bytes 688136 | tf_op jit(solution)/shard_map/ppermute | solution.py:155
  14.4 26.3 %collective-permute-start.49 = (bf16[112,1024]{1,0:T(8,128)(2,1)}, bf16[112,1024]{1,0:T(8,128)(2,1)S(1)}, u32[]{:S(2)}, u32[]{:S(2)}) collective-permute-start(bf16[112,1024]{1,0:T(8,128)(2,1)} %collective-permute-done.47), channel_id=1, source_target_pairs={{0,2},{4,0},{8,4},{12,8},{14,12},{10,14},{6,10},{2,6},{1,3},{5,1},... | collective-permute-start | bytes 688136 | tf_op jit(solution)/shard_map/ppermute | solution.py:80
  67.5 36.4 %collective-permute-start.3 = (bf16[256,1280]{1,0:T(8,128)(2,1)}, bf16[256,1280]{1,0:T(8,128)(2,1)}, u32[]{:S(2)}, u32[]{:S(2)}) collective-permute-start(bf16[256,1280]{1,0:T(8,128)(2,1)} %get-tuple-element.17), channel_id=1, source_target_pairs={{0,4},{4,8},{8,12},{12,14},{14,10},{10,6},{6,2},{2,0},{1,5},{5,9},... | collective-permute-start | bytes 1966088 | tf_op jit(solution)/shard_map/ppermute | solution.py:80
  68.0 21.5 %collective-permute-start.42 = (bf16[112,1024]{1,0:T(8,128)(2,1)S(1)}, bf16[112,1024]{1,0:T(8,128)(2,1)S(1)}, u32[]{:S(2)}, u32[]{:S(2)}) collective-permute-start(bf16[112,1024]{1,0:T(8,128)(2,1)S(1)} %collective-permute-done.40), channel_id=1, source_target_pairs={{0,4},{4,8},{8,12},{12,14},{14,10},{10,6},{6,2},{2,0},{1,5},{5,9},... | collective-permute-start | bytes 688136 | tf_op jit(solution)/shard_map/ppermute | solution.py:80
  91.2 40.9 %collective-permute-start.1 = (bf16[256,1280]{1,0:T(8,128)(2,1)}, bf16[256,1280]{1,0:T(8,128)(2,1)}, u32[]{:S(2)}, u32[]{:S(2)}) collective-permute-start(bf16[256,1280]{1,0:T(8,128)(2,1)} %get-tuple-element.17), channel_id=1, source_target_pairs={{0,1},{1,0},{2,3},{3,2},{4,5},{5,4},{6,7},{7,6},{8,9},{9,8},{10,11... | collective-permute-start | bytes 1966088 | tf_op jit(solution)/shard_map/ppermute | solution.py:155
  97.6 17.5 %collective-permute-start.5 = (bf16[256,1280]{1,0:T(8,128)(2,1)}, bf16[256,1280]{1,0:T(8,128)(2,1)}, u32[]{:S(2)}, u32[]{:S(2)}) collective-permute-start(bf16[256,1280]{1,0:T(8,128)(2,1)} %get-tuple-element.18), channel_id=1, source_target_pairs={{0,2},{4,0},{8,4},{12,8},{14,12},{10,14},{6,10},{2,6},{1,3},{5,1},... | collective-permute-start | bytes 1966088 | tf_op jit(solution)/shard_map/ppermute | solution.py:80
  103.9 31.1 %collective-permute-start.2 = (bf16[256,1280]{1,0:T(8,128)(2,1)}, bf16[256,1280]{1,0:T(8,128)(2,1)}, u32[]{:S(2)}, u32[]{:S(2)}) collective-permute-start(bf16[256,1280]{1,0:T(8,128)(2,1)} %get-tuple-element.18), channel_id=1, source_target_pairs={{0,1},{1,0},{2,3},{3,2},{4,5},{5,4},{6,7},{7,6},{8,9},{9,8},{10,11... | collective-permute-start | bytes 1966088 | tf_op jit(solution)/shard_map/ppermute | solution.py:155
  104.5 33.8 %collective-permute-start.4 = (bf16[256,1280]{1,0:T(8,128)(2,1)}, bf16[256,1280]{1,0:T(8,128)(2,1)}, u32[]{:S(2)}, u32[]{:S(2)}) collective-permute-start(bf16[256,1280]{1,0:T(8,128)(2,1)} %collective-permute-done.3), channel_id=1, source_target_pairs={{0,1},{1,0},{2,3},{3,2},{4,5},{5,4},{6,7},{7,6},{8,9},{9,8},{10,11... | collective-permute-start | bytes 1966088 | tf_op jit(solution)/shard_map/ppermute | solution.py:155
  115.7 18.6 %collective-permute-start.9 = (bf16[256,1280]{1,0:T(8,128)(2,1)}, bf16[256,1280]{1,0:T(8,128)(2,1)S(1)}, u32[]{:S(2)}, u32[]{:S(2)}) collective-permute-start(bf16[256,1280]{1,0:T(8,128)(2,1)} %collective-permute-done.5), channel_id=1, source_target_pairs={{0,2},{4,0},{8,4},{12,8},{14,12},{10,14},{6,10},{2,6},{1,3},{5,1},... | collective-permute-start | bytes 1966088 | tf_op jit(solution)/shard_map/ppermute | solution.py:80
  131.7 19.5 %collective-permute-start.6 = (bf16[256,1280]{1,0:T(8,128)(2,1)}, bf16[256,1280]{1,0:T(8,128)(2,1)S(1)}, u32[]{:S(2)}, u32[]{:S(2)}) collective-permute-start(bf16[256,1280]{1,0:T(8,128)(2,1)} %collective-permute-done.5), channel_id=1, source_target_pairs={{0,1},{1,0},{2,3},{3,2},{4,5},{5,4},{6,7},{7,6},{8,9},{9,8},{10,11... | collective-permute-start | bytes 1966088 | tf_op jit(solution)/shard_map/ppermute | solution.py:155
  134.3 20.2 %collective-permute-start.8 = (bf16[256,1280]{1,0:T(8,128)(2,1)S(1)}, bf16[256,1280]{1,0:T(8,128)(2,1)S(1)}, u32[]{:S(2)}, u32[]{:S(2)}) collective-permute-start(bf16[256,1280]{1,0:T(8,128)(2,1)S(1)} %collective-permute-done.7), channel_id=1, source_target_pairs={{0,1},{1,0},{2,3},{3,2},{4,5},{5,4},{6,7},{7,6},{8,9},{9,8},{10,11... | collective-permute-start | bytes 1966088 | tf_op jit(solution)/shard_map/ppermute | solution.py:155
  138.3 30.7 %collective-permute-start.10 = (bf16[256,1280]{1,0:T(8,128)(2,1)S(1)}, bf16[256,1280]{1,0:T(8,128)(2,1)S(1)}, u32[]{:S(2)}, u32[]{:S(2)}) collective-permute-start(bf16[256,1280]{1,0:T(8,128)(2,1)S(1)} %collective-permute-done.9), channel_id=1, source_target_pairs={{0,1},{1,0},{2,3},{3,2},{4,5},{5,4},{6,7},{7,6},{8,9},{9,8},{10,11... | collective-permute-start | bytes 1966088 | tf_op jit(solution)/shard_map/ppermute | solution.py:155
  149.4 23.9 %collective-permute-start.12 = (bf16[256,1280]{1,0:T(8,128)(2,1)S(1)}, bf16[256,1280]{1,0:T(8,128)(2,1)S(1)}, u32[]{:S(2)}, u32[]{:S(2)}) collective-permute-start(bf16[256,1280]{1,0:T(8,128)(2,1)S(1)} %collective-permute-done.11), channel_id=1, source_target_pairs={{0,1},{1,0},{2,3},{3,2},{4,5},{5,4},{6,7},{7,6},{8,9},{9,8},{10,11... | collective-permute-start | bytes 1966088 | tf_op jit(solution)/shard_map/ppermute | solution.py:155
  154.5 20.8 %collective-permute-start.14 = (bf16[256,1280]{1,0:T(8,128)(2,1)S(1)}, bf16[256,1280]{1,0:T(8,128)(2,1)S(1)}, u32[]{:S(2)}, u32[]{:S(2)}) collective-permute-start(bf16[256,1280]{1,0:T(8,128)(2,1)S(1)} %collective-permute-done.13), channel_id=1, source_target_pairs={{0,1},{1,0},{2,3},{3,2},{4,5},{5,4},{6,7},{7,6},{8,9},{9,8},{10,11... | collective-permute-start | bytes 1966088 | tf_op jit(solution)/shard_map/ppermute | solution.py:155
  168.5 22.3 %collective-permute-start.16 = (bf16[256,1280]{1,0:T(8,128)(2,1)S(1)}, bf16[256,1280]{1,0:T(8,128)(2,1)S(1)}, u32[]{:S(2)}, u32[]{:S(2)}) collective-permute-start(bf16[256,1280]{1,0:T(8,128)(2,1)S(1)} %collective-permute-done.15), channel_id=1, source_target_pairs={{0,1},{1,0},{2,3},{3,2},{4,5},{5,4},{6,7},{7,6},{8,9},{9,8},{10,11... | collective-permute-start | bytes 1966088 | tf_op jit(solution)/shard_map/ppermute | solution.py:155
  169.6 23.6 %collective-permute-start.18 = (bf16[256,1280]{1,0:T(8,128)(2,1)S(1)}, bf16[256,1280]{1,0:T(8,128)(2,1)S(1)}, u32[]{:S(2)}, u32[]{:S(2)}) collective-permute-start(bf16[256,1280]{1,0:T(8,128)(2,1)S(1)} %collective-permute-done.17), channel_id=1, source_target_pairs={{0,1},{1,0},{2,3},{3,2},{4,5},{5,4},{6,7},{7,6},{8,9},{9,8},{10,11... | collective-permute-start | bytes 1966088 | tf_op jit(solution)/shard_map/ppermute | solution.py:155
  186.2 22.2 %collective-permute-start.20 = (bf16[256,1280]{1,0:T(8,128)(2,1)S(1)}, bf16[256,1280]{1,0:T(8,128)(2,1)S(1)}, u32[]{:S(2)}, u32[]{:S(2)}) collective-permute-start(bf16[256,1280]{1,0:T(8,128)(2,1)S(1)} %collective-permute-done.19), channel_id=1, source_target_pairs={{0,1},{1,0},{2,3},{3,2},{4,5},{5,4},{6,7},{7,6},{8,9},{9,8},{10,11... | collective-permute-start | bytes 1966088 | tf_op jit(solution)/shard_map/ppermute | solution.py:155
  190.3 20.7 %collective-permute-start.22 = (bf16[256,1280]{1,0:T(8,128)(2,1)S(1)}, bf16[256,1280]{1,0:T(8,128)(2,1)S(1)}, u32[]{:S(2)}, u32[]{:S(2)}) collective-permute-start(bf16[256,1280]{1,0:T(8,128)(2,1)S(1)} %collective-permute-done.21), channel_id=1, source_target_pairs={{0,1},{1,0},{2,3},{3,2},{4,5},{5,4},{6,7},{7,6},{8,9},{9,8},{10,11... | collective-permute-start | bytes 1966088 | tf_op jit(solution)/shard_map/ppermute | solution.py:155
  203.3 22.9 %collective-permute-start.24 = (bf16[256,1280]{1,0:T(8,128)(2,1)S(1)}, bf16[256,1280]{1,0:T(8,128)(2,1)S(1)}, u32[]{:S(2)}, u32[]{:S(2)}) collective-permute-start(bf16[256,1280]{1,0:T(8,128)(2,1)S(1)} %collective-permute-done.23), channel_id=1, source_target_pairs={{0,1},{1,0},{2,3},{3,2},{4,5},{5,4},{6,7},{7,6},{8,9},{9,8},{10,11... | collective-permute-start | bytes 1966088 | tf_op jit(solution)/shard_map/ppermute | solution.py:155
  208.0 18.8 %collective-permute-start.26 = (bf16[256,1280]{1,0:T(8,128)(2,1)S(1)}, bf16[256,1280]{1,0:T(8,128)(2,1)S(1)}, u32[]{:S(2)}, u32[]{:S(2)}) collective-permute-start(bf16[256,1280]{1,0:T(8,128)(2,1)S(1)} %collective-permute-done.25), channel_id=1, source_target_pairs={{0,1},{1,0},{2,3},{3,2},{4,5},{5,4},{6,7},{7,6},{8,9},{9,8},{10,11... | collective-permute-start | bytes 1966088 | tf_op jit(solution)/shard_map/ppermute | solution.py:155
  208.4 17.4 %collective-permute-start.29 = (bf16[256,1280]{1,0:T(8,128)(2,1)S(1)}, bf16[256,1280]{1,0:T(8,128)(2,1)S(1)}, u32[]{:S(2)}, u32[]{:S(2)}) collective-permute-start(bf16[256,1280]{1,0:T(8,128)(2,1)S(1)} %collective-permute-done.25), channel_id=1, source_target_pairs={{0,2},{4,0},{8,4},{12,8},{14,12},{10,14},{6,10},{2,6},{1,3},{5,1},... | collective-permute-start | bytes 1966088 | tf_op jit(solution)/shard_map/ppermute | solution.py:80
  (55 other events, 463.3 us)

commit v5 on v4

--- a/solution.py
+++ b/solution.py
@@ -120,25 +120,18 @@
     half_rows = weight_rows // 2
 
     weights = jnp.concatenate([query_weight, keyvalue_weight], axis=1)
-    down_rows = adapter_down.size // query_cols
-    upq_rows = adapter_up_query.size // query_cols
-    upkv_rows = adapter_up_keyvalue.size // query_cols
-    down_flat = adapter_down.reshape(down_rows, query_cols)
-    upq_flat = adapter_up_query.reshape(upq_rows, query_cols)
-    upkv_flat = adapter_up_keyvalue.reshape(upkv_rows, query_cols)
-    dh, uh, vh = down_rows // 2, upq_rows // 2, upkv_rows // 2
-    piece_rows = dh + uh + vh
-    pad_rows = (-piece_rows) % 8
-
-    def adapter_half(h):
-        return jnp.concatenate(
-            [
-                down_flat[h * dh : (h + 1) * dh],
-                upq_flat[h * uh : (h + 1) * uh],
-                upkv_flat[h * vh : (h + 1) * vh],
-                jnp.zeros((pad_rows, query_cols), jnp.bfloat16),
-            ]
-        )
+    width = query_cols + pair_cols
+    down_size = adapter_down.size
+    upq_size = adapter_up_query.size
+    upkv_size = adapter_up_keyvalue.size
+    adapter_size = down_size + upq_size + upkv_size
+    adapter_rows = -(-adapter_size // (width * 8)) * 8
+    adapter_own = jnp.pad(
+        jnp.concatenate(
+            [adapter_down.reshape(-1), adapter_up_query.reshape(-1), adapter_up_keyvalue.reshape(-1)]
+        ),
+        (0, adapter_rows * width - adapter_size),
+    ).reshape(adapter_rows, width)
 
     order = ring_order(n_chip)
     inverse = [0] * n_chip
@@ -148,22 +141,28 @@
     inverse_table = jnp.asarray(inverse, jnp.int32)
     pos = inverse_table[me_chip]
     directions = (1, -1)
+    adapter_reach = (n_chip // 2, n_chip - 1 - n_chip // 2)
 
     def swap_core(x):
         if n_lo == 1:
             return [x]
         return [x, lax.ppermute(x, "core", [(0, 1), (1, 0)])]
 
-    w_recv, a_recv = [], []
+    w_recv = [[weights[h * half_rows : (h + 1) * half_rows]] for h in range(2)]
+    a_recv = [[], []]
     for h, direction in enumerate(directions):
-        a_recv.append(ring_gather(adapter_half(h), n_chip, order, direction))
-        w_recv.append(
-            ring_gather(weights[h * half_rows : (h + 1) * half_rows], n_chip, order, direction)
-        )
-    adapter_pieces = [
-        jnp.stack([jnp.stack(swap_core(a_recv[h][s])) for s in range(n_chip)])
-        for h in range(len(directions))
-    ]
+        pairs = [(order[i], order[(i + direction) % n_chip]) for i in range(n_chip)]
+        w_cur, a_cur = w_recv[h][0], adapter_own
+        for s in range(1, n_chip):
+            if s <= adapter_reach[h]:
+                got = lax.ppermute(jnp.concatenate([w_cur, a_cur]), "chip", pairs)
+                w_cur, a_cur = got[:half_rows], got[half_rows:]
+                a_recv[h].append(a_cur)
+            else:
+                w_cur = lax.ppermute(w_cur, "chip", pairs)
+            w_recv[h].append(w_cur)
+    adapter_list = [adapter_own] + a_recv[0] + a_recv[1]
+    adapter_pieces = jnp.stack([jnp.stack(swap_core(p)) for p in adapter_list])
 
     total = None
     for s in range(n_chip):
@@ -181,19 +180,18 @@
     a_chip = picked // n_lo
     a_core = picked % n_lo
     a_slot = (a_core != me_core).astype(jnp.int32)
-    per_half = []
-    for h, direction in enumerate(directions):
-        a_step = ((pos - inverse_table[a_chip]) * direction) % n_chip
-        per_half.append(adapter_pieces[h][a_step, a_slot])
-    down_selected = jnp.concatenate(
-        [per_half[0][:, :dh], per_half[1][:, :dh]], axis=1
-    ).reshape((prompt_count,) + adapter_down.shape[1:])
-    up_query_selected = jnp.concatenate(
-        [per_half[0][:, dh : dh + uh], per_half[1][:, dh : dh + uh]], axis=1
-    ).reshape((prompt_count,) + adapter_up_query.shape[1:])
-    up_pair_selected = jnp.concatenate(
-        [per_half[0][:, dh + uh : piece_rows], per_half[1][:, dh + uh : piece_rows]], axis=1
-    ).reshape((prompt_count,) + adapter_up_keyvalue.shape[1:])
+    distance = (pos - inverse_table[a_chip]) % n_chip
+    a_index = jnp.where(
+        distance <= adapter_reach[0], distance, adapter_reach[0] + (n_chip - distance)
+    )
+    chosen = adapter_pieces[a_index, a_slot].reshape(prompt_count, adapter_rows * width)
+    down_selected = chosen[:, :down_size].reshape((prompt_count,) + adapter_down.shape[1:])
+    up_query_selected = chosen[:, down_size : down_size + upq_size].reshape(
+        (prompt_count,) + adapter_up_query.shape[1:]
+    )
+    up_pair_selected = chosen[:, down_size + upq_size : adapter_size].reshape(
+        (prompt_count,) + adapter_up_keyvalue.shape[1:]
+    )
 
     query_plain = total[:, :query_cols]
     base_pair = total[:, query_cols:]

time: 239 us -> 237 us (level)
  matrix products: 24.9 us -> 42.6 us
  starting transfers between devices: 37.5 us -> 22.4 us
  waiting for transfers between devices: 108 us -> 93.5 us
  local copies, waits for them, and re-layouts: 20.2 us -> 27.5 us
  other arithmetic: 23.9 us -> 26.7 us
    ppermute x28 -> x14, waiting for transfers between devices: 105 us -> 84.2 us  [the longest x7 55.8 us: shards(): got = lax.ppermute(jnp.concatenate([w_cur, a_cur]), 'chip', pairs)]
    dot_general x32, matrix products: 19.9 us -> 37.5 us  [shards(): part = jnp.dot(lhs, p, preferred_element_type=jnp.float32)]
    ppermute x28 -> x14, starting transfers between devices: 31.4 us -> 15.3 us  [the longest x7 9 us: shards(): got = lax.ppermute(jnp.concatenate([w_cur, a_cur]), 'chip', pairs)]
    ppermute x1, waiting for transfers between devices: 0.01 us -> 5.68 us  [shards(): other = lax.ppermute(hidden, 'blk', [(0, 1), (1, 0)])]
    another operation x1 -> x9, local copies, waits for them, and re-layouts: 0.01 us -> 4.68 us  [the longest x8 4.61 us: shards(): adapter_pieces = jnp.stack([jnp.stack(swap_core(p)) for p in adapter_list])]
    unnamed x35 -> x58, local copies, waits for them, and re-layouts: 4.38 us -> 8.97 us
    concatenate x5 -> x3, other arithmetic: 1.63 us -> 4.22 us  [the longest x1 2.87 us: shards(): got = lax.ppermute(jnp.concatenate([w_cur, a_cur]), 'chip', pairs)]
    unnamed x14 -> x8, other arithmetic: 9.67 us -> 9.15 us
  transfers between devices with their start and end apart: 62 -> 40, of which waited for: 21 -> 13; matrix products, arithmetic and copies ran while one was open for 23% -> 35% of each run, Pallas kernels for 0% -> 0%
where the time goes in v5:
time: 237 us; the launch traced here: 235 us
  waiting for transfers between devices  93.5 us (39%)
  matrix products  42.6 us (18%)
  local copies, waits for them, and re-layouts  27.5 us (12%)
  other arithmetic  26.7 us (11%)
  between operations  22.6 us (10%)
  starting transfers between devices  22.4 us (9%)
    ppermute x7, waiting for transfers between devices, shards(): got = lax.ppermute(jnp.concatenate([w_cur, a_cur]), 'chip', pairs)  55.8 us
    dot_general x32, matrix products, shards(): part = jnp.dot(lhs, p, preferred_element_type=jnp.float32)  37.5 us
    ppermute x7, waiting for transfers between devices, shards(): w_cur = lax.ppermute(w_cur, 'chip', pairs)  28.4 us
    unnamed x8, other arithmetic  9.15 us
    ppermute x7, starting transfers between devices, shards(): got = lax.ppermute(jnp.concatenate([w_cur, a_cur]), 'chip', pairs)  9 us
    unnamed x58, local copies, waits for them, and re-layouts  8.97 us
    ppermute x7, starting transfers between devices, shards(): w_cur = lax.ppermute(w_cur, 'chip', pairs)  6.31 us
    ppermute x1, waiting for transfers between devices, shards(): other = lax.ppermute(hidden, 'blk', [(0, 1), (1, 0)])  5.68 us
  transfers between devices with their start and end apart: 40, of which 13 were waited for; matrix products, arithmetic and copies ran while one was open for 35% of the time, Pallas kernels for 0%

profile of v5, /device:TPU:0, one launch (start us, length us, event | category | flops | bytes accessed | tf_op | source)
XLA Modules:
  0.0 235.4 jit_solution(15830004303069148319)
XLA Ops:
  6.2 2.9 %pad_maximum_fusion.2 = (bf16[432,1280]{1,0:T(8,128)(2,1)}, bf16[432,1280]{1,0:T(8,128)(2,1)}) fusion(bf16[176,1280]{1,0:T(8,128)(2,1)} %reshape.505, bf16[256,1280]{1,0:T(8,128)(2,1)S(1)} %get-tuple-element.18, bf16[256,1280]{1,0:T(8,128)(2,1)} %get-tuple-element.19), kind=kLoop, calls=%fused_computation.53 | loop fusion | flops 3870720 | bytes 3973120 | tf_op jit(solution)/shard_map/concatenate | solution.py:158
  9.1 3.0 %collective-permute-start.3 = (bf16[432,1280]{1,0:T(8,128)(2,1)}, bf16[432,1280]{1,0:T(8,128)(2,1)S(1)}, u32[]{:S(2)}, u32[]{:S(2)}) collective-permute-start(bf16[432,1280]{1,0:T(8,128)(2,1)} %get-tuple-element.34), channel_id=1, source_target_pairs={{0,4},{4,8},{8,12},{12,14},{14,10},{10,6},{6,2},{2,0},{1,5},{5,9},... | collective-permute-start | bytes 3317768 | tf_op jit(solution)/shard_map/ppermute | solution.py:158
  12.1 2.0 collective-permute-start
  42.5 2.2 fusion.36
  48.2 2.0 slice_bitcast_fusion.6
  51.4 18.8 %collective-permute-done.7 = bf16[432,1280]{1,0:T(8,128)(2,1)S(1)} collective-permute-done((bf16[432,1280]{1,0:T(8,128)(2,1)S(1)}, bf16[432,1280]{1,0:T(8,128)(2,1)S(1)}, u32[]{:S(2)}, u32[]{:S(2)}) %collective-permute-start.7) | collective-permute-done | bytes 1105952 | tf_op jit(solution)/shard_map/ppermute | solution.py:158
  70.3 3.3 %collective-permute-done.9 = bf16[432,1280]{1,0:T(8,128)(2,1)S(1)} collective-permute-done((bf16[432,1280]{1,0:T(8,128)(2,1)}, bf16[432,1280]{1,0:T(8,128)(2,1)S(1)}, u32[]{:S(2)}, u32[]{:S(2)}) %collective-permute-start.9) | collective-permute-done | bytes 1105952 | tf_op jit(solution)/shard_map/ppermute | solution.py:158
  76.5 5.7 %collective-permute-done = bf16[384,4096]{1,0:T(8,128)(2,1)} collective-permute-done((bf16[384,4096]{1,0:T(8,128)(2,1)}, bf16[384,4096]{1,0:T(8,128)(2,1)}, u32[]{:S(2)}, u32[]{:S(2)}) %collective-permute-start) | collective-permute-done | bytes 3145760 | tf_op jit(solution)/shard_map/ppermute | solution.py:106
  82.1 3.3 %broadcast_select_fusion.1 = (bf16[384,4096]{1,0:T(8,128)(2,1)S(1)}, bf16[384,4096]{1,0:T(8,128)(2,1)S(1)}) fusion(bf16[384,4096]{1,0:T(8,128)(2,1)} %param.11, bf16[384,4096]{1,0:T(8,128)(2,1)} %collective-permute-done, pred[]{:T(512)S(6)} %eq.41), kind=kLoop, calls=%fused_computation.17 | loop fusion | flops 3145728 | bytes 12582913 | tf_op jit(solution)/shard_map/select_n | solution.py:107
  86.9 1.8 fusion.2
  90.0 2.0 fusion.92
  94.7 1.8 collective-permute-start.11
  100.3 23.4 %collective-permute-done.13 = bf16[432,1280]{1,0:T(8,128)(2,1)S(1)} collective-permute-done((bf16[432,1280]{1,0:T(8,128)(2,1)S(1)}, bf16[432,1280]{1,0:T(8,128)(2,1)S(1)}, u32[]{:S(2)}, u32[]{:S(2)}) %collective-permute-start.13) | collective-permute-done | bytes 1105952 | tf_op jit(solution)/shard_map/ppermute | solution.py:158
  129.9 11.2 %collective-permute-done.17 = bf16[256,1280]{1,0:T(8,128)(2,1)} collective-permute-done((bf16[256,1280]{1,0:T(8,128)(2,1)S(1)}, bf16[256,1280]{1,0:T(8,128)(2,1)}, u32[]{:S(2)}, u32[]{:S(2)}) %collective-permute-start.17) | collective-permute-done | bytes 655392 | tf_op jit(solution)/shard_map/ppermute | solution.py:162
  142.3 1.7 fusion.16
  144.0 10.4 %collective-permute-done.15 = bf16[432,1280]{1,0:T(8,128)(2,1)S(1)} collective-permute-done((bf16[432,1280]{1,0:T(8,128)(2,1)S(1)}, bf16[432,1280]{1,0:T(8,128)(2,1)S(1)}, u32[]{:S(2)}, u32[]{:S(2)}) %collective-permute-start.15) | collective-permute-done | bytes 1105952 | tf_op jit(solution)/shard_map/ppermute | solution.py:158
  154.5 2.8 %fusion.73 = f32[384,1280]{1,0:T(8,128)} fusion(bf16[256,1280]{1,0:T(8,128)(2,1)} %collective-permute-done.17, bf16[384,8192]{1,0:T(8,128)(2,1)S(1)} %fusion.2, s32[]{:T(128)S(6)} %select_n.347), kind=kOutput, calls=%fused_computation.116 | convolution fusion | flops 251658240 | bytes 2818052 | tf_op jit(solution)/shard_map/dot_general | solution.py:175
  158.7 2.8 %fusion.67 = f32[384,1280]{1,0:T(8,128)} fusion(bf16[256,1280]{1,0:T(8,128)(2,1)} %collective-permute-done.21, bf16[384,8192]{1,0:T(8,128)(2,1)S(1)} %fusion.2, s32[]{:T(128)S(6)} %select_n.355), kind=kOutput, calls=%fused_computation.110 | convolution fusion | flops 251658240 | bytes 2818052 | tf_op jit(solution)/shard_map/dot_general | solution.py:175
  164.2 2.0 fusion.41
  168.3 5.1 %gather_fusion.1 = bf16[4,176,1280]{2,1,0:T(8,128)(2,1)} fusion(bf16[8,2,176,1280]{3,2,1,0:T(8,128)(2,1)} %fusion.43, s32[4]{0:T(128)S(1)} %fusion.150), kind=kCustom, calls=%fused_computation.1 | custom fusion | bytes 3604512 | tf_op jit(solution)/shard_map/gather | solution.py:187
  173.4 2.6 %copy.49 = bf16[1,4,176,1280]{3,1,2,0:T(4,128)(2,1)S(1)} copy(bf16[1,4,176,1280]{3,2,1,0:T(8,128)(2,1)} %bitcast.246) | data formatting | bytes 3604480
  191.3 1.7 fusion.13
  193.0 6.7 %collective-permute-done.25 = bf16[256,1280]{1,0:T(8,128)(2,1)S(1)} collective-permute-done((bf16[256,1280]{1,0:T(8,128)(2,1)}, bf16[256,1280]{1,0:T(8,128)(2,1)S(1)}, u32[]{:S(2)}, u32[]{:S(2)}) %collective-permute-start.25) | collective-permute-done | bytes 655392 | tf_op jit(solution)/shard_map/ppermute | solution.py:162
  208.2 8.6 %collective-permute-done.29 = bf16[256,1280]{1,0:T(8,128)(2,1)S(1)} collective-permute-done((bf16[256,1280]{1,0:T(8,128)(2,1)S(1)}, bf16[256,1280]{1,0:T(8,128)(2,1)S(1)}, u32[]{:S(2)}, u32[]{:S(2)}) %collective-permute-start.29) | collective-permute-done | bytes 655392 | tf_op jit(solution)/shard_map/ppermute | solution.py:162
  (220 shorter events, 85.1 us)
Async XLA Ops:
  4.6 37.9 %collective-permute-start.31 = (bf16[176,1280]{1,0:T(8,128)(2,1)}, bf16[176,1280]{1,0:T(8,128)(2,1)}, u32[]{:S(2)}, u32[]{:S(2)}) collective-permute-start(bf16[176,1280]{1,0:T(8,128)(2,1)} %reshape.505), channel_id=1, source_target_pairs={{0,1},{1,0},{2,3},{3,2},{4,5},{5,4},{6,7},{7,6},{8,9},{9,8},{10,11... | collective-permute-start | bytes 1351688 | tf_op jit(solution)/shard_map/ppermute | solution.py:149
  6.1 87.0 %collective-permute-start.2 = (bf16[256,1280]{1,0:T(8,128)(2,1)}, bf16[256,1280]{1,0:T(8,128)(2,1)}, u32[]{:S(2)}, u32[]{:S(2)}) collective-permute-start(bf16[256,1280]{1,0:T(8,128)(2,1)} %get-tuple-element.19), channel_id=1, source_target_pairs={{0,1},{1,0},{2,3},{3,2},{4,5},{5,4},{6,7},{7,6},{8,9},{9,8},{10,11... | collective-permute-start | bytes 1966088 | tf_op jit(solution)/shard_map/ppermute | solution.py:149
  9.1 35.6 %collective-permute-start.3 = (bf16[432,1280]{1,0:T(8,128)(2,1)}, bf16[432,1280]{1,0:T(8,128)(2,1)S(1)}, u32[]{:S(2)}, u32[]{:S(2)}) collective-permute-start(bf16[432,1280]{1,0:T(8,128)(2,1)} %get-tuple-element.34), channel_id=1, source_target_pairs={{0,4},{4,8},{8,12},{12,14},{14,10},{10,6},{6,2},{2,0},{1,5},{5,9},... | collective-permute-start | bytes 3317768 | tf_op jit(solution)/shard_map/ppermute | solution.py:158
  12.1 34.4 %collective-permute-start.5 = (bf16[432,1280]{1,0:T(8,128)(2,1)}, bf16[432,1280]{1,0:T(8,128)(2,1)}, u32[]{:S(2)}, u32[]{:S(2)}) collective-permute-start(bf16[432,1280]{1,0:T(8,128)(2,1)} %get-tuple-element.35), channel_id=1, source_target_pairs={{0,2},{4,0},{8,4},{12,8},{14,12},{10,14},{6,10},{2,6},{1,3},{5,1},... | collective-permute-start | bytes 3317768 | tf_op jit(solution)/shard_map/ppermute | solution.py:158
  12.1 70.0 %collective-permute-start = (bf16[384,4096]{1,0:T(8,128)(2,1)}, bf16[384,4096]{1,0:T(8,128)(2,1)}, u32[]{:S(2)}, u32[]{:S(2)}) collective-permute-start(bf16[384,4096]{1,0:T(8,128)(2,1)} %param.11), channel_id=1, source_target_pairs={{0,16},{16,0},{1,17},{17,1},{2,18},{18,2},{3,19},{19,3},{4,20},{20... | collective-permute-start | bytes 9437192 | tf_op jit(solution)/shard_map/ppermute | solution.py:106
  44.7 25.5 %collective-permute-start.7 = (bf16[432,1280]{1,0:T(8,128)(2,1)S(1)}, bf16[432,1280]{1,0:T(8,128)(2,1)S(1)}, u32[]{:S(2)}, u32[]{:S(2)}) collective-permute-start(bf16[432,1280]{1,0:T(8,128)(2,1)S(1)} %collective-permute-done.3), channel_id=1, source_target_pairs={{0,4},{4,8},{8,12},{12,14},{14,10},{10,6},{6,2},{2,0},{1,5},{5,9},... | collective-permute-start | bytes 3317768 | tf_op jit(solution)/shard_map/ppermute | solution.py:158
  46.5 27.0 %collective-permute-start.9 = (bf16[432,1280]{1,0:T(8,128)(2,1)}, bf16[432,1280]{1,0:T(8,128)(2,1)S(1)}, u32[]{:S(2)}, u32[]{:S(2)}) collective-permute-start(bf16[432,1280]{1,0:T(8,128)(2,1)} %collective-permute-done.5), channel_id=1, source_target_pairs={{0,2},{4,0},{8,4},{12,8},{14,12},{10,14},{6,10},{2,6},{1,3},{5,1},... | collective-permute-start | bytes 3317768 | tf_op jit(solution)/shard_map/ppermute | solution.py:158
  50.2 44.6 %collective-permute-start.1 = (bf16[256,1280]{1,0:T(8,128)(2,1)S(1)}, bf16[256,1280]{1,0:T(8,128)(2,1)S(1)}, u32[]{:S(2)}, u32[]{:S(2)}) collective-permute-start(bf16[256,1280]{1,0:T(8,128)(2,1)S(1)} %get-tuple-element.18), channel_id=1, source_target_pairs={{0,1},{1,0},{2,3},{3,2},{4,5},{5,4},{6,7},{7,6},{8,9},{9,8},{10,11... | collective-permute-start | bytes 1966088 | tf_op jit(solution)/shard_map/ppermute | solution.py:149
  70.2 92.4 %collective-permute-start.36 = (bf16[176,1280]{1,0:T(8,128)(2,1)}, bf16[176,1280]{1,0:T(8,128)(2,1)}, u32[]{:S(2)}, u32[]{:S(2)}) collective-permute-start(bf16[176,1280]{1,0:T(8,128)(2,1)} %get-tuple-element.25), channel_id=1, source_target_pairs={{0,1},{1,0},{2,3},{3,2},{4,5},{5,4},{6,7},{7,6},{8,9},{9,8},{10,11... | collective-permute-start | bytes 1351688 | tf_op jit(solution)/shard_map/ppermute | solution.py:149
  94.7 29.5 %collective-permute-start.11 = (bf16[432,1280]{1,0:T(8,128)(2,1)S(1)}, bf16[432,1280]{1,0:T(8,128)(2,1)S(1)}, u32[]{:S(2)}, u32[]{:S(2)}) collective-permute-start(bf16[432,1280]{1,0:T(8,128)(2,1)S(1)} %collective-permute-done.7), channel_id=1, source_target_pairs={{0,4},{4,8},{8,12},{12,14},{14,10},{10,6},{6,2},{2,0},{1,5},{5,9},... | collective-permute-start | bytes 3317768 | tf_op jit(solution)/shard_map/ppermute | solution.py:158
  97.0 26.7 %collective-permute-start.13 = (bf16[432,1280]{1,0:T(8,128)(2,1)S(1)}, bf16[432,1280]{1,0:T(8,128)(2,1)S(1)}, u32[]{:S(2)}, u32[]{:S(2)}) collective-permute-start(bf16[432,1280]{1,0:T(8,128)(2,1)S(1)} %collective-permute-done.9), channel_id=1, source_target_pairs={{0,2},{4,0},{8,4},{12,8},{14,12},{10,14},{6,10},{2,6},{1,3},{5,1},... | collective-permute-start | bytes 3317768 | tf_op jit(solution)/shard_map/ppermute | solution.py:158
  123.9 17.2 %collective-permute-start.17 = (bf16[256,1280]{1,0:T(8,128)(2,1)S(1)}, bf16[256,1280]{1,0:T(8,128)(2,1)}, u32[]{:S(2)}, u32[]{:S(2)}) collective-permute-start(bf16[256,1280]{1,0:T(8,128)(2,1)S(1)} %slice.144), channel_id=1, source_target_pairs={{0,2},{4,0},{8,4},{12,8},{14,12},{10,14},{6,10},{2,6},{1,3},{5,1},... | collective-permute-start | bytes 1966088 | tf_op jit(solution)/shard_map/ppermute | solution.py:162
  126.6 39.6 %collective-permute-start.37 = (bf16[176,1280]{1,0:T(8,128)(2,1)S(1)}, bf16[176,1280]{1,0:T(8,128)(2,1)S(1)}, u32[]{:S(2)}, u32[]{:S(2)}) collective-permute-start(bf16[176,1280]{1,0:T(8,128)(2,1)S(1)} %copy-done.12), channel_id=1, source_target_pairs={{0,1},{1,0},{2,3},{3,2},{4,5},{5,4},{6,7},{7,6},{8,9},{9,8},{10,11... | collective-permute-start | bytes 1351688 | tf_op jit(solution)/shard_map/ppermute | solution.py:149
  127.7 26.7 %collective-permute-start.15 = (bf16[432,1280]{1,0:T(8,128)(2,1)S(1)}, bf16[432,1280]{1,0:T(8,128)(2,1)S(1)}, u32[]{:S(2)}, u32[]{:S(2)}) collective-permute-start(bf16[432,1280]{1,0:T(8,128)(2,1)S(1)} %collective-permute-done.11), channel_id=1, source_target_pairs={{0,4},{4,8},{8,12},{12,14},{14,10},{10,6},{6,2},{2,0},{1,5},{5,9},... | collective-permute-start | bytes 3317768 | tf_op jit(solution)/shard_map/ppermute | solution.py:158
  129.7 37.6 %collective-permute-start.38 = (bf16[176,1280]{1,0:T(8,128)(2,1)S(1)}, bf16[176,1280]{1,0:T(8,128)(2,1)S(1)}, u32[]{:S(2)}, u32[]{:S(2)}) collective-permute-start(bf16[176,1280]{1,0:T(8,128)(2,1)S(1)} %get-tuple-element.21), channel_id=1, source_target_pairs={{0,1},{1,0},{2,3},{3,2},{4,5},{5,4},{6,7},{7,6},{8,9},{9,8},{10,11... | collective-permute-start | bytes 1351688 | tf_op jit(solution)/shard_map/ppermute | solution.py:149
  158.2 33.1 %collective-permute-start.18 = (bf16[256,1280]{1,0:T(8,128)(2,1)}, bf16[256,1280]{1,0:T(8,128)(2,1)}, u32[]{:S(2)}, u32[]{:S(2)}) collective-permute-start(bf16[256,1280]{1,0:T(8,128)(2,1)} %collective-permute-done.17), channel_id=1, source_target_pairs={{0,1},{1,0},{2,3},{3,2},{4,5},{5,4},{6,7},{7,6},{8,9},{9,8},{10,11... | collective-permute-start | bytes 1966088 | tf_op jit(solution)/shard_map/ppermute | solution.py:149
  161.5 23.4 %collective-permute-start.16 = (bf16[256,1280]{1,0:T(8,128)(2,1)}, bf16[256,1280]{1,0:T(8,128)(2,1)}, u32[]{:S(2)}, u32[]{:S(2)}) collective-permute-start(bf16[256,1280]{1,0:T(8,128)(2,1)} %slice.145), channel_id=1, source_target_pairs={{0,1},{1,0},{2,3},{3,2},{4,5},{5,4},{6,7},{7,6},{8,9},{9,8},{10,11... | collective-permute-start | bytes 1966088 | tf_op jit(solution)/shard_map/ppermute | solution.py:149
  162.6 22.2 %collective-permute-start.19 = (bf16[256,1280]{1,0:T(8,128)(2,1)}, bf16[256,1280]{1,0:T(8,128)(2,1)}, u32[]{:S(2)}, u32[]{:S(2)}) collective-permute-start(bf16[256,1280]{1,0:T(8,128)(2,1)} %slice.145), channel_id=1, source_target_pairs={{0,4},{4,8},{8,12},{12,14},{14,10},{10,6},{6,2},{2,0},{1,5},{5,9},... | collective-permute-start | bytes 1966088 | tf_op jit(solution)/shard_map/ppermute | solution.py:162
  166.2 40.4 %collective-permute-start.22 = (bf16[256,1280]{1,0:T(8,128)(2,1)}, bf16[256,1280]{1,0:T(8,128)(2,1)}, u32[]{:S(2)}, u32[]{:S(2)}) collective-permute-start(bf16[256,1280]{1,0:T(8,128)(2,1)} %collective-permute-done.21), channel_id=1, source_target_pairs={{0,1},{1,0},{2,3},{3,2},{4,5},{5,4},{6,7},{7,6},{8,9},{9,8},{10,11... | collective-permute-start | bytes 1966088 | tf_op jit(solution)/shard_map/ppermute | solution.py:149
  184.8 17.4 %collective-permute-start.20 = (bf16[256,1280]{1,0:T(8,128)(2,1)}, bf16[256,1280]{1,0:T(8,128)(2,1)S(1)}, u32[]{:S(2)}, u32[]{:S(2)}) collective-permute-start(bf16[256,1280]{1,0:T(8,128)(2,1)} %collective-permute-done.19), channel_id=1, source_target_pairs={{0,1},{1,0},{2,3},{3,2},{4,5},{5,4},{6,7},{7,6},{8,9},{9,8},{10,11... | collective-permute-start | bytes 1966088 | tf_op jit(solution)/shard_map/ppermute | solution.py:149
  184.9 17.3 %collective-permute-start.23 = (bf16[256,1280]{1,0:T(8,128)(2,1)}, bf16[256,1280]{1,0:T(8,128)(2,1)S(1)}, u32[]{:S(2)}, u32[]{:S(2)}) collective-permute-start(bf16[256,1280]{1,0:T(8,128)(2,1)} %collective-permute-done.19), channel_id=1, source_target_pairs={{0,4},{4,8},{8,12},{12,14},{14,10},{10,6},{6,2},{2,0},{1,5},{5,9},... | collective-permute-start | bytes 1966088 | tf_op jit(solution)/shard_map/ppermute | solution.py:162
  199.8 22.4 %collective-permute-start.26 = (bf16[256,1280]{1,0:T(8,128)(2,1)S(1)}, bf16[256,1280]{1,0:T(8,128)(2,1)S(1)}, u32[]{:S(2)}, u32[]{:S(2)}) collective-permute-start(bf16[256,1280]{1,0:T(8,128)(2,1)S(1)} %collective-permute-done.25), channel_id=1, source_target_pairs={{0,1},{1,0},{2,3},{3,2},{4,5},{5,4},{6,7},{7,6},{8,9},{9,8},{10,11... | collective-permute-start | bytes 1966088 | tf_op jit(solution)/shard_map/ppermute | solution.py:149
  199.8 17.1 %collective-permute-start.29 = (bf16[256,1280]{1,0:T(8,128)(2,1)S(1)}, bf16[256,1280]{1,0:T(8,128)(2,1)S(1)}, u32[]{:S(2)}, u32[]{:S(2)}) collective-permute-start(bf16[256,1280]{1,0:T(8,128)(2,1)S(1)} %collective-permute-done.25), channel_id=1, source_target_pairs={{0,2},{4,0},{8,4},{12,8},{14,12},{10,14},{6,10},{2,6},{1,3},{5,1},... | collective-permute-start | bytes 1966088 | tf_op jit(solution)/shard_map/ppermute | solution.py:162
  202.2 17.2 %collective-permute-start.24 = (bf16[256,1280]{1,0:T(8,128)(2,1)S(1)}, bf16[256,1280]{1,0:T(8,128)(2,1)S(1)}, u32[]{:S(2)}, u32[]{:S(2)}) collective-permute-start(bf16[256,1280]{1,0:T(8,128)(2,1)S(1)} %collective-permute-done.23), channel_id=1, source_target_pairs={{0,1},{1,0},{2,3},{3,2},{4,5},{5,4},{6,7},{7,6},{8,9},{9,8},{10,11... | collective-permute-start | bytes 1966088 | tf_op jit(solution)/shard_map/ppermute | solution.py:149
  (40 other events, 479.5 us)

commit v6 on v5

--- a/solution.py
+++ b/solution.py
@@ -120,18 +120,19 @@
     half_rows = weight_rows // 2
 
     weights = jnp.concatenate([query_weight, keyvalue_weight], axis=1)
-    width = query_cols + pair_cols
-    down_size = adapter_down.size
-    upq_size = adapter_up_query.size
-    upkv_size = adapter_up_keyvalue.size
-    adapter_size = down_size + upq_size + upkv_size
-    adapter_rows = -(-adapter_size // (width * 8)) * 8
-    adapter_own = jnp.pad(
-        jnp.concatenate(
-            [adapter_down.reshape(-1), adapter_up_query.reshape(-1), adapter_up_keyvalue.reshape(-1)]
-        ),
-        (0, adapter_rows * width - adapter_size),
-    ).reshape(adapter_rows, width)
+    down_rows = adapter_down.size // query_cols
+    upq_rows = adapter_up_query.size // query_cols
+    upkv_rows = adapter_up_keyvalue.size // query_cols
+    adapter_rows = down_rows + upq_rows + upkv_rows
+    pad_rows = (-adapter_rows) % 8
+    adapter_own = jnp.concatenate(
+        [
+            adapter_down.reshape(down_rows, query_cols),
+            adapter_up_query.reshape(upq_rows, query_cols),
+            adapter_up_keyvalue.reshape(upkv_rows, query_cols),
+            jnp.zeros((pad_rows, query_cols), jnp.bfloat16),
+        ]
+    )
 
     order = ring_order(n_chip)
     inverse = [0] * n_chip
@@ -141,34 +142,25 @@
     inverse_table = jnp.asarray(inverse, jnp.int32)
     pos = inverse_table[me_chip]
     directions = (1, -1)
-    adapter_reach = (n_chip // 2, n_chip - 1 - n_chip // 2)
 
     def swap_core(x):
         if n_lo == 1:
             return [x]
         return [x, lax.ppermute(x, "core", [(0, 1), (1, 0)])]
 
-    w_recv = [[weights[h * half_rows : (h + 1) * half_rows]] for h in range(2)]
-    a_recv = [[], []]
-    for h, direction in enumerate(directions):
-        pairs = [(order[i], order[(i + direction) % n_chip]) for i in range(n_chip)]
-        w_cur, a_cur = w_recv[h][0], adapter_own
-        for s in range(1, n_chip):
-            if s <= adapter_reach[h]:
-                got = lax.ppermute(jnp.concatenate([w_cur, a_cur]), "chip", pairs)
-                w_cur, a_cur = got[:half_rows], got[half_rows:]
-                a_recv[h].append(a_cur)
-            else:
-                w_cur = lax.ppermute(w_cur, "chip", pairs)
-            w_recv[h].append(w_cur)
-    adapter_list = [adapter_own] + a_recv[0] + a_recv[1]
-    adapter_pieces = jnp.stack([jnp.stack(swap_core(p)) for p in adapter_list])
+    adapters_chip = lax.all_gather(adapter_own, "chip", axis=0, tiled=False)
+    adapter_pieces = jnp.stack(swap_core(adapters_chip))
+
+    recv = [
+        ring_gather(weights[h * half_rows : (h + 1) * half_rows], n_chip, order, direction)
+        for h, direction in enumerate(directions)
+    ]
 
     total = None
     for s in range(n_chip):
         for h, direction in enumerate(directions):
             src_chip = order_table[(pos - s * direction) % n_chip]
-            for slot, p in enumerate(swap_core(w_recv[h][s])):
+            for slot, p in enumerate(swap_core(recv[h][s])):
                 src_core = me_core if slot == 0 else n_lo - 1 - me_core
                 start = (src_chip * n_lo + src_core) * weight_rows + h * half_rows
                 lhs = lax.dynamic_slice_in_dim(normed, start, half_rows, 1)
@@ -177,19 +169,13 @@
 
     picked = prompt_adapter[0]
     prompt_count = picked.shape[0]
-    a_chip = picked // n_lo
-    a_core = picked % n_lo
-    a_slot = (a_core != me_core).astype(jnp.int32)
-    distance = (pos - inverse_table[a_chip]) % n_chip
-    a_index = jnp.where(
-        distance <= adapter_reach[0], distance, adapter_reach[0] + (n_chip - distance)
-    )
-    chosen = adapter_pieces[a_index, a_slot].reshape(prompt_count, adapter_rows * width)
-    down_selected = chosen[:, :down_size].reshape((prompt_count,) + adapter_down.shape[1:])
-    up_query_selected = chosen[:, down_size : down_size + upq_size].reshape(
+    a_slot = (picked % n_lo != me_core).astype(jnp.int32)
+    chosen = adapter_pieces[a_slot, picked // n_lo]
+    down_selected = chosen[:, :down_rows].reshape((prompt_count,) + adapter_down.shape[1:])
+    up_query_selected = chosen[:, down_rows : down_rows + upq_rows].reshape(
         (prompt_count,) + adapter_up_query.shape[1:]
     )
-    up_pair_selected = chosen[:, down_size + upq_size : adapter_size].reshape(
+    up_pair_selected = chosen[:, down_rows + upq_rows : adapter_rows].reshape(
         (prompt_count,) + adapter_up_keyvalue.shape[1:]
     )
 

time: 237 us -> 242 us (1.021)
  between operations: 22.6 us -> 36 us
  local copies, waits for them, and re-layouts: 27.5 us -> 18.5 us
  other arithmetic: 26.7 us -> 18.5 us
  waiting for transfers between devices: 93.5 us -> 101 us
  starting transfers between devices: 22.4 us -> 25.2 us
    unnamed x8 -> x0, other arithmetic: 9.15 us -> none
    unnamed x58 -> x37, local copies, waits for them, and re-layouts: 8.97 us -> 2.98 us
    another operation x2, other arithmetic: 1.16 us -> 6.76 us  [the longest x1 6.58 us: shards(): adapter_pieces = jnp.stack(swap_core(adapters_chip))]
    another operation x9 -> x0, local copies, waits for them, and re-layouts: 4.68 us -> none  [the longest x8 4.61 us: shards(): adapter_pieces = jnp.stack([jnp.stack(swap_core(p)) for p in adapter_list])]
    ppermute x1, waiting for transfers between devices: 5.68 us -> 10.1 us  [shards(): other = lax.ppermute(hidden, 'blk', [(0, 1), (1, 0)])]
    dot_general x32, matrix products: 37.5 us -> 33.2 us  [shards(): part = jnp.dot(lhs, p, preferred_element_type=jnp.float32)]
    ppermute x14, starting transfers between devices: 15.3 us -> 19.7 us  [ring_gather(): current = lax.ppermute(current, 'chip', pairs)]
    dot_general x0 -> x1, local copies, waits for them, and re-layouts: none -> 3.96 us  [shards(): lax.dot_general(normed_part, down_selected.reshape(prompt_count * 3 * ran...]
  transfers between devices with their start and end apart: 40 -> 34, of which waited for: 13 -> 14; matrix products, arithmetic and copies ran while one was open for 35% -> 20% of each run, Pallas kernels for 0% -> 0%
where the time goes in v6:
time: 242 us; the launch traced here: 240 us
  waiting for transfers between devices  101 us (42%)
  matrix products  41.5 us (17%)
  between operations  36 us (15%)
  starting transfers between devices  25.2 us (10%)
  local copies, waits for them, and re-layouts  18.5 us (8%)
  other arithmetic  18.5 us (8%)
    ppermute x14, waiting for transfers between devices, ring_gather(): current = lax.ppermute(current, 'chip', pairs)  86.8 us
    dot_general x32, matrix products, shards(): part = jnp.dot(lhs, p, preferred_element_type=jnp.float32)  33.2 us
    ppermute x14, starting transfers between devices, ring_gather(): current = lax.ppermute(current, 'chip', pairs)  19.7 us
    ppermute x1, waiting for transfers between devices, shards(): other = lax.ppermute(hidden, 'blk', [(0, 1), (1, 0)])  10.1 us
    another operation x1, other arithmetic, shards(): adapter_pieces = jnp.stack(swap_core(adapters_chip))  6.58 us
    gather x1, local copies, waits for them, and re-layouts, shards(): chosen = adapter_pieces[a_slot, picked // n_lo]  4.87 us
  transfers between devices with their start and end apart: 34, of which 14 were waited for; matrix products, arithmetic and copies ran while one was open for 20% of the time, Pallas kernels for 0%

profile of v6, /device:TPU:0, one launch (start us, length us, event | category | flops | bytes accessed | tf_op | source)
XLA Modules:
  0.0 240.4 jit_solution(7921100329566390023)
XLA Ops:
  7.2 3.0 %collective-permute-start = (bf16[384,4096]{1,0:T(8,128)(2,1)}, bf16[384,4096]{1,0:T(8,128)(2,1)}, u32[]{:S(2)}, u32[]{:S(2)}) collective-permute-start(bf16[384,4096]{1,0:T(8,128)(2,1)} %param.11), channel_id=1, source_target_pairs={{0,16},{16,0},{1,17},{17,1},{2,18},{18,2},{3,19},{19,3},{4,20},{20... | collective-permute-start | bytes 9437192 | tf_op jit(solution)/shard_map/ppermute | solution.py:106
  41.6 21.0 %collective-permute-done.7 = bf16[256,1280]{1,0:T(8,128)(2,1)S(1)} collective-permute-done((bf16[256,1280]{1,0:T(8,128)(2,1)}, bf16[256,1280]{1,0:T(8,128)(2,1)S(1)}, u32[]{:S(2)}, u32[]{:S(2)}) %collective-permute-start.7) | collective-permute-done | bytes 655392 | tf_op jit(solution)/shard_map/ppermute | solution.py:80
  62.6 6.0 %collective-permute-start.9 = (bf16[256,1280]{1,0:T(8,128)(2,1)}, bf16[256,1280]{1,0:T(8,128)(2,1)S(1)}, u32[]{:S(2)}, u32[]{:S(2)}) collective-permute-start(bf16[256,1280]{1,0:T(8,128)(2,1)} %collective-permute-done.5), channel_id=1, source_target_pairs={{0,2},{4,0},{8,4},{12,8},{14,12},{10,14},{6,10},{2,6},{1,3},{5,1},... | collective-permute-start | bytes 1966088 | tf_op jit(solution)/shard_map/ppermute | solution.py:80
  68.6 10.1 %collective-permute-done = bf16[384,4096]{1,0:T(8,128)(2,1)} collective-permute-done((bf16[384,4096]{1,0:T(8,128)(2,1)}, bf16[384,4096]{1,0:T(8,128)(2,1)}, u32[]{:S(2)}, u32[]{:S(2)}) %collective-permute-start) | collective-permute-done | bytes 3145760 | tf_op jit(solution)/shard_map/ppermute | solution.py:106
  78.7 1.8 collective-permute-start.11
  80.5 3.3 %broadcast_select_fusion.1 = (bf16[384,4096]{1,0:T(8,128)(2,1)S(1)}, bf16[384,4096]{1,0:T(8,128)(2,1)S(1)}) fusion(bf16[384,4096]{1,0:T(8,128)(2,1)} %param.11, bf16[384,4096]{1,0:T(8,128)(2,1)} %collective-permute-done, pred[]{:T(512)S(6)} %eq.40), kind=kLoop, calls=%fused_computation.17 | loop fusion | flops 3145728 | bytes 12582913 | tf_op jit(solution)/shard_map/select_n | solution.py:107
  85.2 1.8 fusion.2
  87.9 2.0 fusion.82
  96.7 2.4 %collective-permute-done.11 = bf16[256,1280]{1,0:T(8,128)(2,1)S(1)} collective-permute-done((bf16[256,1280]{1,0:T(8,128)(2,1)S(1)}, bf16[256,1280]{1,0:T(8,128)(2,1)S(1)}, u32[]{:S(2)}, u32[]{:S(2)}) %collective-permute-start.11) | collective-permute-done | bytes 655392 | tf_op jit(solution)/shard_map/ppermute | solution.py:80
  101.2 12.8 %collective-permute-done.13 = bf16[256,1280]{1,0:T(8,128)(2,1)S(1)} collective-permute-done((bf16[256,1280]{1,0:T(8,128)(2,1)S(1)}, bf16[256,1280]{1,0:T(8,128)(2,1)S(1)}, u32[]{:S(2)}, u32[]{:S(2)}) %collective-permute-start.13) | collective-permute-done | bytes 655392 | tf_op jit(solution)/shard_map/ppermute | solution.py:80
  114.0 1.7 collective-permute-start.15
  117.2 13.5 %collective-permute-done.15 = bf16[256,1280]{1,0:T(8,128)(2,1)S(1)} collective-permute-done((bf16[256,1280]{1,0:T(8,128)(2,1)S(1)}, bf16[256,1280]{1,0:T(8,128)(2,1)S(1)}, u32[]{:S(2)}, u32[]{:S(2)}) %collective-permute-start.15) | collective-permute-done | bytes 655392 | tf_op jit(solution)/shard_map/ppermute | solution.py:80
  136.4 12.5 %collective-permute-done.19 = bf16[256,1280]{1,0:T(8,128)(2,1)} collective-permute-done((bf16[256,1280]{1,0:T(8,128)(2,1)S(1)}, bf16[256,1280]{1,0:T(8,128)(2,1)}, u32[]{:S(2)}, u32[]{:S(2)}) %collective-permute-start.19) | collective-permute-done | bytes 655392 | tf_op jit(solution)/shard_map/ppermute | solution.py:80
  155.8 1.7 fusion.13
  157.6 8.7 %collective-permute-done.23 = bf16[256,1280]{1,0:T(8,128)(2,1)} collective-permute-done((bf16[256,1280]{1,0:T(8,128)(2,1)}, bf16[256,1280]{1,0:T(8,128)(2,1)}, u32[]{:S(2)}, u32[]{:S(2)}) %collective-permute-start.23) | collective-permute-done | bytes 655392 | tf_op jit(solution)/shard_map/ppermute | solution.py:80
  171.2 1.7 fusion.12
  175.7 9.8 %collective-permute-done.27 = bf16[256,1280]{1,0:T(8,128)(2,1)S(1)} collective-permute-done((bf16[256,1280]{1,0:T(8,128)(2,1)}, bf16[256,1280]{1,0:T(8,128)(2,1)S(1)}, u32[]{:S(2)}, u32[]{:S(2)}) %collective-permute-start.27) | collective-permute-done | bytes 655392 | tf_op jit(solution)/shard_map/ppermute | solution.py:80
  185.6 1.7 collective-permute-done.29
  197.1 6.6 %pad_maximum_fusion = bf16[2,8,216,1024]{3,2,1,0:T(8,128)(2,1)} fusion(bf16[1,8,216,1024]{3,2,1,0:T(8,128)(2,1)} %bitcast.26, bf16[1,8,216,1024]{3,2,1,0:T(8,128)(2,1)} %bitcast.188), kind=kLoop, calls=%fused_computation.6 | loop fusion | flops 3538944 | bytes 14155776 | tf_op jit(solution)/shard_map/stack | solution.py:152
  203.7 4.9 %gather_fusion = bf16[4,216,1024]{2,1,0:T(8,128)(2,1)} fusion(bf16[2,8,216,1024]{3,2,1,0:T(8,128)(2,1)} %pad_maximum_fusion, s32[4]{0:T(128)S(1)} %fusion.137), kind=kCustom, calls=%fused_computation | custom fusion | bytes 3538976 | tf_op jit(solution)/shard_map/gather | solution.py:173
  208.6 2.7 %slice.78 = bf16[4,192,1024]{2,1,0:T(8,128)(2,1)} slice(bf16[4,216,1024]{2,1,0:T(8,128)(2,1)} %gather_fusion), slice={[0:4], [0:192], [0:1024]} | slice | bytes 3145728 | tf_op jit(solution)/shard_map/slice | solution.py:174
  212.1 4.0 %dot_general.148 = bf16[4,3,16,4096]{3,2,1,0:T(8,128)(2,1)} reshape(bf16[4,192,1024]{2,1,0:T(8,128)(2,1)} %slice.78) | data formatting | bytes 3145728 | tf_op jit(solution)/shard_map/dot_general | solution.py:188
  216.1 3.5 %fusion.31 = f32[384,3,16]{0,2,1:T(8,128)S(1)} fusion(bf16[4,3,16,4096]{3,2,1,0:T(8,128)(2,1)} %dot_general.148, bf16[384,8192]{1,0:T(8,128)(2,1)} %copy-done, s32[]{:T(128)S(6)} %select_n.342, f32[384,4]{0,1:T(4,128)S(1)} %fusion.140), kind=kOutput, calls=%fused_computation.59 | convolution fusion | flops 604108800 | bytes 4798468 | tf_op jit(solution)/shard_map/dot_general | solution.py:188
  220.7 3.7 %collective-permute-done.32 = f32[384,48]{0,1:T(8,128)S(1)} collective-permute-done((f32[384,48]{0,1:T(8,128)S(1)}, f32[384,48]{0,1:T(8,128)S(1)}, u32[]{:S(2)}, u32[]{:S(2)}) %collective-permute-start.32) | collective-permute-done | bytes 73760 | tf_op jit(solution)/shard_map/ppermute | solution.py:65
  (163 shorter events, 63.5 us)
Async XLA Ops:
  7.2 159.2 %all-gather.3.cloned.1.call-start = ((), (), s32[]{:S(2)}) async-start(), calls=%async_computation | async-start | bytes 3981312 | tf_op jit(solution)/shard_map/all_gather | solution.py:151
  7.2 71.5 %collective-permute-start = (bf16[384,4096]{1,0:T(8,128)(2,1)}, bf16[384,4096]{1,0:T(8,128)(2,1)}, u32[]{:S(2)}, u32[]{:S(2)}) collective-permute-start(bf16[384,4096]{1,0:T(8,128)(2,1)} %param.11), channel_id=1, source_target_pairs={{0,16},{16,0},{1,17},{17,1},{2,18},{18,2},{3,19},{19,3},{4,20},{20... | collective-permute-start | bytes 9437192 | tf_op jit(solution)/shard_map/ppermute | solution.py:106
  11.8 79.7 %collective-permute-start.1 = (bf16[256,1280]{1,0:T(8,128)(2,1)S(1)}, bf16[256,1280]{1,0:T(8,128)(2,1)}, u32[]{:S(2)}, u32[]{:S(2)}) collective-permute-start(bf16[256,1280]{1,0:T(8,128)(2,1)S(1)} %get-tuple-element.15), channel_id=1, source_target_pairs={{0,1},{1,0},{2,3},{3,2},{4,5},{5,4},{6,7},{7,6},{8,9},{9,8},{10,11... | collective-permute-start | bytes 1966088 | tf_op jit(solution)/shard_map/ppermute | solution.py:149
  11.8 26.5 %collective-permute-start.3 = (bf16[256,1280]{1,0:T(8,128)(2,1)S(1)}, bf16[256,1280]{1,0:T(8,128)(2,1)}, u32[]{:S(2)}, u32[]{:S(2)}) collective-permute-start(bf16[256,1280]{1,0:T(8,128)(2,1)S(1)} %get-tuple-element.15), channel_id=1, source_target_pairs={{0,4},{4,8},{8,12},{12,14},{14,10},{10,6},{6,2},{2,0},{1,5},{5,9},... | collective-permute-start | bytes 1966088 | tf_op jit(solution)/shard_map/ppermute | solution.py:80
  13.5 79.6 %collective-permute-start.2 = (bf16[256,1280]{1,0:T(8,128)(2,1)S(1)}, bf16[256,1280]{1,0:T(8,128)(2,1)}, u32[]{:S(2)}, u32[]{:S(2)}) collective-permute-start(bf16[256,1280]{1,0:T(8,128)(2,1)S(1)} %get-tuple-element.16), channel_id=1, source_target_pairs={{0,1},{1,0},{2,3},{3,2},{4,5},{5,4},{6,7},{7,6},{8,9},{9,8},{10,11... | collective-permute-start | bytes 1966088 | tf_op jit(solution)/shard_map/ppermute | solution.py:149
  13.6 27.9 %collective-permute-start.5 = (bf16[256,1280]{1,0:T(8,128)(2,1)S(1)}, bf16[256,1280]{1,0:T(8,128)(2,1)}, u32[]{:S(2)}, u32[]{:S(2)}) collective-permute-start(bf16[256,1280]{1,0:T(8,128)(2,1)S(1)} %get-tuple-element.16), channel_id=1, source_target_pairs={{0,2},{4,0},{8,4},{12,8},{14,12},{10,14},{6,10},{2,6},{1,3},{5,1},... | collective-permute-start | bytes 1966088 | tf_op jit(solution)/shard_map/ppermute | solution.py:80
  38.3 24.3 %collective-permute-start.7 = (bf16[256,1280]{1,0:T(8,128)(2,1)}, bf16[256,1280]{1,0:T(8,128)(2,1)S(1)}, u32[]{:S(2)}, u32[]{:S(2)}) collective-permute-start(bf16[256,1280]{1,0:T(8,128)(2,1)} %collective-permute-done.3), channel_id=1, source_target_pairs={{0,4},{4,8},{8,12},{12,14},{14,10},{10,6},{6,2},{2,0},{1,5},{5,9},... | collective-permute-start | bytes 1966088 | tf_op jit(solution)/shard_map/ppermute | solution.py:80
  41.6 54.9 %collective-permute-start.4 = (bf16[256,1280]{1,0:T(8,128)(2,1)}, bf16[256,1280]{1,0:T(8,128)(2,1)S(1)}, u32[]{:S(2)}, u32[]{:S(2)}) collective-permute-start(bf16[256,1280]{1,0:T(8,128)(2,1)} %collective-permute-done.3), channel_id=1, source_target_pairs={{0,1},{1,0},{2,3},{3,2},{4,5},{5,4},{6,7},{7,6},{8,9},{9,8},{10,11... | collective-permute-start | bytes 1966088 | tf_op jit(solution)/shard_map/ppermute | solution.py:149
  62.6 32.4 %collective-permute-start.9 = (bf16[256,1280]{1,0:T(8,128)(2,1)}, bf16[256,1280]{1,0:T(8,128)(2,1)S(1)}, u32[]{:S(2)}, u32[]{:S(2)}) collective-permute-start(bf16[256,1280]{1,0:T(8,128)(2,1)} %collective-permute-done.5), channel_id=1, source_target_pairs={{0,2},{4,0},{8,4},{12,8},{14,12},{10,14},{6,10},{2,6},{1,3},{5,1},... | collective-permute-start | bytes 1966088 | tf_op jit(solution)/shard_map/ppermute | solution.py:80
  78.7 20.5 %collective-permute-start.11 = (bf16[256,1280]{1,0:T(8,128)(2,1)S(1)}, bf16[256,1280]{1,0:T(8,128)(2,1)S(1)}, u32[]{:S(2)}, u32[]{:S(2)}) collective-permute-start(bf16[256,1280]{1,0:T(8,128)(2,1)S(1)} %collective-permute-done.7), channel_id=1, source_target_pairs={{0,4},{4,8},{8,12},{12,14},{14,10},{10,6},{6,2},{2,0},{1,5},{5,9},... | collective-permute-start | bytes 1966088 | tf_op jit(solution)/shard_map/ppermute | solution.py:80
  91.5 24.7 %collective-permute-start.6 = (bf16[256,1280]{1,0:T(8,128)(2,1)}, bf16[256,1280]{1,0:T(8,128)(2,1)S(1)}, u32[]{:S(2)}, u32[]{:S(2)}) collective-permute-start(bf16[256,1280]{1,0:T(8,128)(2,1)} %collective-permute-done.5), channel_id=1, source_target_pairs={{0,1},{1,0},{2,3},{3,2},{4,5},{5,4},{6,7},{7,6},{8,9},{9,8},{10,11... | collective-permute-start | bytes 1966088 | tf_op jit(solution)/shard_map/ppermute | solution.py:149
  93.1 23.7 %collective-permute-start.8 = (bf16[256,1280]{1,0:T(8,128)(2,1)S(1)}, bf16[256,1280]{1,0:T(8,128)(2,1)S(1)}, u32[]{:S(2)}, u32[]{:S(2)}) collective-permute-start(bf16[256,1280]{1,0:T(8,128)(2,1)S(1)} %collective-permute-done.7), channel_id=1, source_target_pairs={{0,1},{1,0},{2,3},{3,2},{4,5},{5,4},{6,7},{7,6},{8,9},{9,8},{10,11... | collective-permute-start | bytes 1966088 | tf_op jit(solution)/shard_map/ppermute | solution.py:149
  95.0 36.6 %collective-permute-start.10 = (bf16[256,1280]{1,0:T(8,128)(2,1)S(1)}, bf16[256,1280]{1,0:T(8,128)(2,1)S(1)}, u32[]{:S(2)}, u32[]{:S(2)}) collective-permute-start(bf16[256,1280]{1,0:T(8,128)(2,1)S(1)} %collective-permute-done.9), channel_id=1, source_target_pairs={{0,1},{1,0},{2,3},{3,2},{4,5},{5,4},{6,7},{7,6},{8,9},{9,8},{10,11... | collective-permute-start | bytes 1966088 | tf_op jit(solution)/shard_map/ppermute | solution.py:149
  96.5 17.5 %collective-permute-start.13 = (bf16[256,1280]{1,0:T(8,128)(2,1)S(1)}, bf16[256,1280]{1,0:T(8,128)(2,1)S(1)}, u32[]{:S(2)}, u32[]{:S(2)}) collective-permute-start(bf16[256,1280]{1,0:T(8,128)(2,1)S(1)} %collective-permute-done.9), channel_id=1, source_target_pairs={{0,2},{4,0},{8,4},{12,8},{14,12},{10,14},{6,10},{2,6},{1,3},{5,1},... | collective-permute-start | bytes 1966088 | tf_op jit(solution)/shard_map/ppermute | solution.py:80
  99.1 35.3 %collective-permute-start.12 = (bf16[256,1280]{1,0:T(8,128)(2,1)S(1)}, bf16[256,1280]{1,0:T(8,128)(2,1)S(1)}, u32[]{:S(2)}, u32[]{:S(2)}) collective-permute-start(bf16[256,1280]{1,0:T(8,128)(2,1)S(1)} %collective-permute-done.11), channel_id=1, source_target_pairs={{0,1},{1,0},{2,3},{3,2},{4,5},{5,4},{6,7},{7,6},{8,9},{9,8},{10,11... | collective-permute-start | bytes 1966088 | tf_op jit(solution)/shard_map/ppermute | solution.py:149
  116.2 19.7 %collective-permute-start.14 = (bf16[256,1280]{1,0:T(8,128)(2,1)S(1)}, bf16[256,1280]{1,0:T(8,128)(2,1)S(1)}, u32[]{:S(2)}, u32[]{:S(2)}) collective-permute-start(bf16[256,1280]{1,0:T(8,128)(2,1)S(1)} %collective-permute-done.13), channel_id=1, source_target_pairs={{0,1},{1,0},{2,3},{3,2},{4,5},{5,4},{6,7},{7,6},{8,9},{9,8},{10,11... | collective-permute-start | bytes 1966088 | tf_op jit(solution)/shard_map/ppermute | solution.py:149
  130.6 22.9 %collective-permute-start.16 = (bf16[256,1280]{1,0:T(8,128)(2,1)S(1)}, bf16[256,1280]{1,0:T(8,128)(2,1)S(1)}, u32[]{:S(2)}, u32[]{:S(2)}) collective-permute-start(bf16[256,1280]{1,0:T(8,128)(2,1)S(1)} %collective-permute-done.15), channel_id=1, source_target_pairs={{0,1},{1,0},{2,3},{3,2},{4,5},{5,4},{6,7},{7,6},{8,9},{9,8},{10,11... | collective-permute-start | bytes 1966088 | tf_op jit(solution)/shard_map/ppermute | solution.py:149
  134.0 21.8 %collective-permute-start.18 = (bf16[256,1280]{1,0:T(8,128)(2,1)S(1)}, bf16[256,1280]{1,0:T(8,128)(2,1)S(1)}, u32[]{:S(2)}, u32[]{:S(2)}) collective-permute-start(bf16[256,1280]{1,0:T(8,128)(2,1)S(1)} %collective-permute-done.17), channel_id=1, source_target_pairs={{0,1},{1,0},{2,3},{3,2},{4,5},{5,4},{6,7},{7,6},{8,9},{9,8},{10,11... | collective-permute-start | bytes 1966088 | tf_op jit(solution)/shard_map/ppermute | solution.py:149
  134.5 17.5 %collective-permute-start.21 = (bf16[256,1280]{1,0:T(8,128)(2,1)S(1)}, bf16[256,1280]{1,0:T(8,128)(2,1)}, u32[]{:S(2)}, u32[]{:S(2)}) collective-permute-start(bf16[256,1280]{1,0:T(8,128)(2,1)S(1)} %collective-permute-done.17), channel_id=1, source_target_pairs={{0,2},{4,0},{8,4},{12,8},{14,12},{10,14},{6,10},{2,6},{1,3},{5,1},... | collective-permute-start | bytes 1966088 | tf_op jit(solution)/shard_map/ppermute | solution.py:80
  148.9 19.7 %collective-permute-start.20 = (bf16[256,1280]{1,0:T(8,128)(2,1)}, bf16[256,1280]{1,0:T(8,128)(2,1)}, u32[]{:S(2)}, u32[]{:S(2)}) collective-permute-start(bf16[256,1280]{1,0:T(8,128)(2,1)} %collective-permute-done.19), channel_id=1, source_target_pairs={{0,1},{1,0},{2,3},{3,2},{4,5},{5,4},{6,7},{7,6},{8,9},{9,8},{10,11... | collective-permute-start | bytes 1966088 | tf_op jit(solution)/shard_map/ppermute | solution.py:149
  148.9 17.5 %collective-permute-start.23 = (bf16[256,1280]{1,0:T(8,128)(2,1)}, bf16[256,1280]{1,0:T(8,128)(2,1)}, u32[]{:S(2)}, u32[]{:S(2)}) collective-permute-start(bf16[256,1280]{1,0:T(8,128)(2,1)} %collective-permute-done.19), channel_id=1, source_target_pairs={{0,4},{4,8},{8,12},{12,14},{14,10},{10,6},{6,2},{2,0},{1,5},{5,9},... | collective-permute-start | bytes 1966088 | tf_op jit(solution)/shard_map/ppermute | solution.py:80
  151.9 22.3 %collective-permute-start.22 = (bf16[256,1280]{1,0:T(8,128)(2,1)}, bf16[256,1280]{1,0:T(8,128)(2,1)S(1)}, u32[]{:S(2)}, u32[]{:S(2)}) collective-permute-start(bf16[256,1280]{1,0:T(8,128)(2,1)} %collective-permute-done.21), channel_id=1, source_target_pairs={{0,1},{1,0},{2,3},{3,2},{4,5},{5,4},{6,7},{7,6},{8,9},{9,8},{10,11... | collective-permute-start | bytes 1966088 | tf_op jit(solution)/shard_map/ppermute | solution.py:149
  166.3 22.3 %collective-permute-start.24 = (bf16[256,1280]{1,0:T(8,128)(2,1)}, bf16[256,1280]{1,0:T(8,128)(2,1)}, u32[]{:S(2)}, u32[]{:S(2)}) collective-permute-start(bf16[256,1280]{1,0:T(8,128)(2,1)} %collective-permute-done.23), channel_id=1, source_target_pairs={{0,1},{1,0},{2,3},{3,2},{4,5},{5,4},{6,7},{7,6},{8,9},{9,8},{10,11... | collective-permute-start | bytes 1966088 | tf_op jit(solution)/shard_map/ppermute | solution.py:149
  166.3 30.8 %collective-permute-start.31 = (bf16[8,216,1024]{2,1,0:T(8,128)(2,1)}, bf16[8,216,1024]{2,1,0:T(8,128)(2,1)}, u32[]{:S(2)}, u32[]{:S(2)}) collective-permute-start(bf16[8,216,1024]{2,1,0:T(8,128)(2,1)} %bitcast.187), channel_id=1, source_target_pairs={{0,1},{1,0},{2,3},{3,2},{4,5},{5,4},{6,7},{7,6},{8,9},{9,8},{10,11... | collective-permute-start | bytes 10616840 | tf_op jit(solution)/shard_map/ppermute | solution.py:149
  (26 other events, 303.9 us)
Sparse Core Ops, SparseCore 0:
  15.5 74.6 all-gather.2

commit v7 on v6

--- a/solution.py
+++ b/solution.py
@@ -151,10 +151,79 @@
     adapters_chip = lax.all_gather(adapter_own, "chip", axis=0, tiled=False)
     adapter_pieces = jnp.stack(swap_core(adapters_chip))
 
-    recv = [
-        ring_gather(weights[h * half_rows : (h + 1) * half_rows], n_chip, order, direction)
-        for h, direction in enumerate(directions)
-    ]
+    picked = prompt_adapter[0]
+    prompt_count = picked.shape[0]
+    a_slot = (picked % n_lo != me_core).astype(jnp.int32)
+    chosen = adapter_pieces[a_slot, picked // n_lo]
+    down_selected = chosen[:, :down_rows].reshape((prompt_count,) + adapter_down.shape[1:])
+    up_query_selected = chosen[:, down_rows : down_rows + upq_rows].reshape(
+        (prompt_count,) + adapter_up_query.shape[1:]
+    )
+    up_pair_selected = chosen[:, down_rows + upq_rows : adapter_rows].reshape(
+        (prompt_count,) + adapter_up_keyvalue.shape[1:]
+    )
+
+    lengths = packed_lengths[0]
+    member, position, owner, slot_index = layout(lengths, row_number)
+    rank_size = down_selected.shape[2]
+    partial_value = lax.dot_general(
+        normed_part,
+        down_selected.reshape(prompt_count * 3 * rank_size, feature_cols),
+        (((1,), (1,)), ((), ())),
+        preferred_element_type=jnp.float32,
+    )
+    partial_value = partial_value.reshape(row_number, prompt_count, 3, rank_size)
+    masked = jnp.sum(partial_value * member[:, :, None, None], axis=1).reshape(
+        row_number, 3 * rank_size
+    )
+    low_rank = sum_blk(masked, n_blk).reshape(row_number, 3, rank_size).astype(jnp.bfloat16)
+    low_float = low_rank.astype(jnp.float32)
+
+    def spread(column):
+        return (
+            (member[:, :, None] * low_float[:, None, column, :])
+            .astype(jnp.bfloat16)
+            .reshape(row_number, prompt_count * rank_size)
+        )
+
+    up_keyvalue_selected = up_pair_selected.reshape(
+        prompt_count, rank_size, KEYVALUE_LOCAL, 2, HEAD_WIDTH
+    )
+    query_update = jnp.dot(
+        spread(0),
+        up_query_selected.reshape(prompt_count * rank_size, query_cols),
+        preferred_element_type=jnp.float32,
+    )
+    key_update = jnp.dot(
+        spread(1),
+        up_keyvalue_selected[:, :, :, 0].reshape(
+            prompt_count * rank_size, KEYVALUE_LOCAL * HEAD_WIDTH
+        ),
+        preferred_element_type=jnp.float32,
+    )
+    value_update = jnp.dot(
+        spread(2),
+        up_keyvalue_selected[:, :, :, 1].reshape(
+            prompt_count * rank_size, KEYVALUE_LOCAL * HEAD_WIDTH
+        ),
+        preferred_element_type=jnp.float32,
+    )
+    cosine_table, sine_table = rope_tables(position, HEAD_WIDTH)
+
+    early = (query_update, key_update, value_update, cosine_table, sine_table)
+    tie_step = min(n_chip - 1, n_chip // 2 + 1)
+    recv = []
+    for h, direction in enumerate(directions):
+        pairs = [(order[i], order[(i + direction) % n_chip]) for i in range(n_chip)]
+        current = weights[h * half_rows : (h + 1) * half_rows]
+        got = [current]
+        for s in range(1, n_chip):
+            if s == tie_step:
+                current, early = lax.optimization_barrier((current, early))
+            current = lax.ppermute(current, "chip", pairs)
+            got.append(current)
+        recv.append(got)
+    query_update, key_update, value_update, cosine_table, sine_table = early
 
     total = None
     for s in range(n_chip):
@@ -167,67 +236,10 @@
                 part = jnp.dot(lhs, p, preferred_element_type=jnp.float32)
                 total = part if total is None else total + part
 
-    picked = prompt_adapter[0]
-    prompt_count = picked.shape[0]
-    a_slot = (picked % n_lo != me_core).astype(jnp.int32)
-    chosen = adapter_pieces[a_slot, picked // n_lo]
-    down_selected = chosen[:, :down_rows].reshape((prompt_count,) + adapter_down.shape[1:])
-    up_query_selected = chosen[:, down_rows : down_rows + upq_rows].reshape(
-        (prompt_count,) + adapter_up_query.shape[1:]
-    )
-    up_pair_selected = chosen[:, down_rows + upq_rows : adapter_rows].reshape(
-        (prompt_count,) + adapter_up_keyvalue.shape[1:]
-    )
 
     query_plain = total[:, :query_cols]
     base_pair = total[:, query_cols:]
 
-    lengths = packed_lengths[0]
-    member, position, owner, slot_index = layout(lengths, row_number)
-    rank_size = down_selected.shape[2]
-    partial_value = lax.dot_general(
-        normed_part,
-        down_selected.reshape(prompt_count * 3 * rank_size, feature_cols),
-        (((1,), (1,)), ((), ())),
-        preferred_element_type=jnp.float32,
-    )
-    partial_value = partial_value.reshape(row_number, prompt_count, 3, rank_size)
-    masked = jnp.sum(partial_value * member[:, :, None, None], axis=1).reshape(
-        row_number, 3 * rank_size
-    )
-    low_rank = sum_blk(masked, n_blk).reshape(row_number, 3, rank_size).astype(jnp.bfloat16)
-    low_float = low_rank.astype(jnp.float32)
-
-    def spread(column):
-        return (
-            (member[:, :, None] * low_float[:, None, column, :])
-            .astype(jnp.bfloat16)
-            .reshape(row_number, prompt_count * rank_size)
-        )
-
-    up_keyvalue_selected = up_pair_selected.reshape(
-        prompt_count, rank_size, KEYVALUE_LOCAL, 2, HEAD_WIDTH
-    )
-    query_update = jnp.dot(
-        spread(0),
-        up_query_selected.reshape(prompt_count * rank_size, query_cols),
-        preferred_element_type=jnp.float32,
-    )
-    key_update = jnp.dot(
-        spread(1),
-        up_keyvalue_selected[:, :, :, 0].reshape(
-            prompt_count * rank_size, KEYVALUE_LOCAL * HEAD_WIDTH
-        ),
-        preferred_element_type=jnp.float32,
-    )
-    value_update = jnp.dot(
-        spread(2),
-        up_keyvalue_selected[:, :, :, 1].reshape(
-            prompt_count * rank_size, KEYVALUE_LOCAL * HEAD_WIDTH
-        ),
-        preferred_element_type=jnp.float32,
-    )
-    cosine_table, sine_table = rope_tables(position, HEAD_WIDTH)
     query_complete = (query_plain + adapter_scale * query_update).reshape(
         row_number, QUERY_LOCAL * KEYVALUE_LOCAL, HEAD_WIDTH
     )

time: 242 us -> 261 us (1.079)
  matrix products: 41.5 us -> 65.4 us
  starting transfers between devices: 25.2 us -> 21.9 us
  waiting for transfers between devices: 101 us -> 98 us
    ppermute x14, waiting for transfers between devices: 86.8 us -> 59.5 us  [shards(): current = lax.ppermute(current, 'chip', pairs)]
    ppermute x1, waiting for transfers between devices: 10.1 us -> 35.4 us  [shards(): other = lax.ppermute(hidden, 'blk', [(0, 1), (1, 0)])]
    dot_general x32, matrix products: 33.2 us -> 55.8 us  [shards(): part = jnp.dot(lhs, p, preferred_element_type=jnp.float32)]
    ppermute x14, starting transfers between devices: 19.7 us -> 15.8 us  [shards(): current = lax.ppermute(current, 'chip', pairs)]
    another operation x1, other arithmetic: 6.58 us -> 3.45 us  [shards(): adapter_pieces = jnp.stack(swap_core(adapters_chip))]
  transfers between devices with their start and end apart: 34 -> 34, of which waited for: 14 -> 11; matrix products, arithmetic and copies ran while one was open for 20% -> 35% of each run, Pallas kernels for 0% -> 0%
where the time goes in v7:
time: 261 us; the launch traced here: 259 us
  waiting for transfers between devices  98 us (38%)
  matrix products  65.4 us (25%)
  between operations  35.9 us (14%)
  starting transfers between devices  21.9 us (8%)
  local copies, waits for them, and re-layouts  20.3 us (8%)
  other arithmetic  17.8 us (7%)
    ppermute x14, waiting for transfers between devices, shards(): current = lax.ppermute(current, 'chip', pairs)  59.5 us
    dot_general x32, matrix products, shards(): part = jnp.dot(lhs, p, preferred_element_type=jnp.float32)  55.8 us
    ppermute x1, waiting for transfers between devices, shards(): other = lax.ppermute(hidden, 'blk', [(0, 1), (1, 0)])  35.4 us
    ppermute x14, starting transfers between devices, shards(): current = lax.ppermute(current, 'chip', pairs)  15.8 us
  transfers between devices with their start and end apart: 34, of which 11 were waited for; matrix products, arithmetic and copies ran while one was open for 35% of the time, Pallas kernels for 0%

profile of v7, /device:TPU:0, one launch (start us, length us, event | category | flops | bytes accessed | tf_op | source)
XLA Modules:
  0.0 259.3 jit_solution(4700283323378292503)
XLA Ops:
  7.2 3.0 %collective-permute-start = (bf16[384,4096]{1,0:T(8,128)(2,1)}, bf16[384,4096]{1,0:T(8,128)(2,1)}, u32[]{:S(2)}, u32[]{:S(2)}) collective-permute-start(bf16[384,4096]{1,0:T(8,128)(2,1)} %param.11), channel_id=1, source_target_pairs={{0,16},{16,0},{1,17},{17,1},{2,18},{18,2},{3,19},{19,3},{4,20},{20... | collective-permute-start | bytes 9437192 | tf_op jit(solution)/shard_map/ppermute | solution.py:106
  43.3 35.4 %collective-permute-done = bf16[384,4096]{1,0:T(8,128)(2,1)} collective-permute-done((bf16[384,4096]{1,0:T(8,128)(2,1)}, bf16[384,4096]{1,0:T(8,128)(2,1)}, u32[]{:S(2)}, u32[]{:S(2)}) %collective-permute-start) | collective-permute-done | bytes 3145760 | tf_op jit(solution)/shard_map/ppermute | solution.py:106
  78.7 3.4 %broadcast_select_fusion.1 = (bf16[384,4096]{1,0:T(8,128)(2,1)S(1)}, bf16[384,4096]{1,0:T(8,128)(2,1)S(1)}) fusion(bf16[384,4096]{1,0:T(8,128)(2,1)} %param.11, bf16[384,4096]{1,0:T(8,128)(2,1)} %collective-permute-done, pred[]{:T(512)S(6)} %eq.40), kind=kLoop, calls=%fused_computation.17 | loop fusion | flops 3145728 | bytes 12582913 | tf_op jit(solution)/shard_map/select_n | solution.py:107
  88.0 2.8 %fusion.82 = f32[384,1280]{1,0:T(8,128)} fusion(bf16[256,1280]{1,0:T(8,128)(2,1)} %collective-permute-done.3, bf16[384,8192]{1,0:T(8,128)(2,1)S(1)} %fusion.2, s32[]{:T(128)S(6)} %select_n.288), kind=kOutput, calls=%fused_computation.116 | convolution fusion | flops 251658240 | bytes 2818052 | tf_op jit(solution)/shard_map/dot_general | solution.py:236
  90.9 2.8 %fusion.79 = f32[384,1280]{1,0:T(8,128)} fusion(bf16[256,1280]{1,0:T(8,128)(2,1)} %collective-permute-done.5, bf16[384,8192]{1,0:T(8,128)(2,1)S(1)} %fusion.2, s32[]{:T(128)S(6)} %select_n.292), kind=kOutput, calls=%fused_computation.113 | convolution fusion | flops 251658240 | bytes 2818052 | tf_op jit(solution)/shard_map/dot_general | solution.py:236
  95.3 2.8 %fusion.76 = f32[384,1280]{1,0:T(8,128)} fusion(bf16[256,1280]{1,0:T(8,128)(2,1)} %collective-permute-done.7, bf16[384,8192]{1,0:T(8,128)(2,1)S(1)} %fusion.2, s32[]{:T(128)S(6)} %select_n.296), kind=kOutput, calls=%fused_computation.110 | convolution fusion | flops 251658240 | bytes 2818052 | tf_op jit(solution)/shard_map/dot_general | solution.py:236
  98.5 2.9 %fusion.88 = f32[384,1280]{1,0:T(8,128)} fusion(bf16[256,1280]{1,0:T(8,128)(2,1)} %collective-permute-done.1, bf16[384,8192]{1,0:T(8,128)(2,1)S(1)} %fusion.2, s32[]{:T(128)S(6)} %select_n.283), kind=kOutput, calls=%fused_computation.122 | convolution fusion | flops 251658240 | bytes 2818052 | tf_op jit(solution)/shard_map/dot_general | solution.py:236
  101.4 2.8 %fusion.84 = f32[384,1280]{1,0:T(8,128)} fusion(bf16[256,1280]{1,0:T(8,128)(2,1)} %collective-permute-done.2, bf16[384,8192]{1,0:T(8,128)(2,1)S(1)} %fusion.2, s32[]{:T(128)S(6)} %select_n.285), kind=kOutput, calls=%fused_computation.118 | convolution fusion | flops 251658240 | bytes 2818052 | tf_op jit(solution)/shard_map/dot_general | solution.py:236
  104.3 6.8 %collective-permute-done.9 = bf16[256,1280]{1,0:T(8,128)(2,1)} collective-permute-done((bf16[256,1280]{1,0:T(8,128)(2,1)}, bf16[256,1280]{1,0:T(8,128)(2,1)}, u32[]{:S(2)}, u32[]{:S(2)}) %collective-permute-start.9) | collective-permute-done | bytes 655392 | tf_op jit(solution)/shard_map/ppermute | solution.py:223
  112.8 2.3 collective-permute-done.11
  118.2 4.1 %fusion.20 = f32[384,1280]{1,0:T(8,128)S(1)} fusion(f32[384,1280]{1,0:T(8,128)} %fusion.79, bf16[256,1280]{1,0:T(8,128)(2,1)} %collective-permute-done.4, f32[384,1280]{1,0:T(8,128)S(1)} %copy-done.2, f32[384,1280]{1,0:T(8,128)} %fusion.84, f32[384,1280]{1,0:T(8,128)S(1)} %copy-done.1, f32[384,1280]{1,0:T(8,128)S(1)} %fusion.90, f32[384,1280]{1,0:T(8,128)} %fusion.88, ...), kind=kOutput, calls=%fused_computation.44 | convolution fusion | flops 254607360 | bytes 14614532 | tf_op jit(solution)/shard_map/dot_general | solution.py:236
  122.8 8.6 %collective-permute-done.13 = bf16[256,1280]{1,0:T(8,128)(2,1)S(1)} collective-permute-done((bf16[256,1280]{1,0:T(8,128)(2,1)}, bf16[256,1280]{1,0:T(8,128)(2,1)S(1)}, u32[]{:S(2)}, u32[]{:S(2)}) %collective-permute-start.13) | collective-permute-done | bytes 655392 | tf_op jit(solution)/shard_map/ppermute | solution.py:223
  139.5 7.1 %collective-permute-done.17 = bf16[256,1280]{1,0:T(8,128)(2,1)S(1)} collective-permute-done((bf16[256,1280]{1,0:T(8,128)(2,1)S(1)}, bf16[256,1280]{1,0:T(8,128)(2,1)S(1)}, u32[]{:S(2)}, u32[]{:S(2)}) %collective-permute-start.17) | collective-permute-done | bytes 655392 | tf_op jit(solution)/shard_map/ppermute | solution.py:223
  153.1 3.5 %pad_maximum_fusion = bf16[2,8,216,1024]{3,2,1,0:T(8,128)(2,1)} fusion(bf16[1,8,216,1024]{3,2,1,0:T(8,128)(2,1)S(1)} %bitcast.190, bf16[1,8,216,1024]{3,2,1,0:T(8,128)(2,1)S(1)} %bitcast.189), kind=kLoop, calls=%fused_computation.6 | loop fusion | flops 3538944 | bytes 14155776 | tf_op jit(solution)/shard_map/stack | solution.py:152
  156.6 4.9 %gather_fusion = bf16[4,216,1024]{2,1,0:T(8,128)(2,1)} fusion(bf16[2,8,216,1024]{3,2,1,0:T(8,128)(2,1)} %pad_maximum_fusion, s32[4]{0:T(128)S(1)} %fusion.137), kind=kCustom, calls=%fused_computation | custom fusion | bytes 3538976 | tf_op jit(solution)/shard_map/gather | solution.py:157
  161.4 2.7 %slice.76 = bf16[4,192,1024]{2,1,0:T(8,128)(2,1)} slice(bf16[4,216,1024]{2,1,0:T(8,128)(2,1)} %gather_fusion), slice={[0:4], [0:192], [0:1024]} | slice | bytes 3145728 | tf_op jit(solution)/shard_map/slice | solution.py:158
  165.0 3.7 %dot_general.136 = bf16[4,3,16,4096]{3,2,1,0:T(8,128)(2,1)} reshape(bf16[4,192,1024]{2,1,0:T(8,128)(2,1)} %slice.76) | data formatting | bytes 3145728 | tf_op jit(solution)/shard_map/dot_general | solution.py:169
  168.7 3.5 %fusion.31 = f32[384,3,16]{0,2,1:T(8,128)S(1)} fusion(bf16[4,3,16,4096]{3,2,1,0:T(8,128)(2,1)} %dot_general.136, bf16[384,8192]{1,0:T(8,128)(2,1)} %copy-done, s32[]{:T(128)S(6)} %select_n.321, f32[384,4]{0,1:T(4,128)S(1)} %fusion.140), kind=kOutput, calls=%fused_computation.57 | convolution fusion | flops 604108800 | bytes 4798468 | tf_op jit(solution)/shard_map/dot_general | solution.py:169
  174.0 3.0 %collective-permute-done.20 = f32[384,48]{0,1:T(8,128)S(1)} collective-permute-done((f32[384,48]{0,1:T(8,128)S(1)}, f32[384,48]{0,1:T(8,128)S(1)}, u32[]{:S(2)}, u32[]{:S(2)}) %collective-permute-start.20) | collective-permute-done | bytes 73760 | tf_op jit(solution)/shard_map/ppermute | solution.py:65
  177.3 2.5 convolution_bitcast_fusion
  185.1 11.5 %collective-permute-done.21 = bf16[256,1280]{1,0:T(8,128)(2,1)S(1)} collective-permute-done((bf16[256,1280]{1,0:T(8,128)(2,1)}, bf16[256,1280]{1,0:T(8,128)(2,1)S(1)}, u32[]{:S(2)}, u32[]{:S(2)}) %collective-permute-start.21) | collective-permute-done | bytes 655392 | tf_op jit(solution)/shard_map/ppermute | solution.py:223
  203.3 10.5 %collective-permute-done.25 = bf16[256,1280]{1,0:T(8,128)(2,1)S(1)} collective-permute-done((bf16[256,1280]{1,0:T(8,128)(2,1)S(1)}, bf16[256,1280]{1,0:T(8,128)(2,1)S(1)}, u32[]{:S(2)}, u32[]{:S(2)}) %collective-permute-start.25) | collective-permute-done | bytes 655392 | tf_op jit(solution)/shard_map/ppermute | solution.py:223
  221.8 9.1 %collective-permute-done.29 = bf16[256,1280]{1,0:T(8,128)(2,1)S(1)} collective-permute-done((bf16[256,1280]{1,0:T(8,128)(2,1)S(1)}, bf16[256,1280]{1,0:T(8,128)(2,1)S(1)}, u32[]{:S(2)}, u32[]{:S(2)}) %collective-permute-start.29) | collective-permute-done | bytes 655392 | tf_op jit(solution)/shard_map/ppermute | solution.py:223
  230.9 2.6 collective-permute-done.31
  (172 shorter events, 81.2 us)
Async XLA Ops:
  7.2 103.9 %all-gather.3.cloned.1.call-start = ((), (), s32[]{:S(2)}) async-start(), calls=%async_computation | async-start | bytes 3981312 | tf_op jit(solution)/shard_map/all_gather | solution.py:151
  7.2 71.5 %collective-permute-start = (bf16[384,4096]{1,0:T(8,128)(2,1)}, bf16[384,4096]{1,0:T(8,128)(2,1)}, u32[]{:S(2)}, u32[]{:S(2)}) collective-permute-start(bf16[384,4096]{1,0:T(8,128)(2,1)} %param.11), channel_id=1, source_target_pairs={{0,16},{16,0},{1,17},{17,1},{2,18},{18,2},{3,19},{19,3},{4,20},{20... | collective-permute-start | bytes 9437192 | tf_op jit(solution)/shard_map/ppermute | solution.py:106
  12.8 85.3 %collective-permute-start.1 = (bf16[256,1280]{1,0:T(8,128)(2,1)}, bf16[256,1280]{1,0:T(8,128)(2,1)}, u32[]{:S(2)}, u32[]{:S(2)}) collective-permute-start(bf16[256,1280]{1,0:T(8,128)(2,1)} %get-tuple-element.39), channel_id=1, source_target_pairs={{0,1},{1,0},{2,3},{3,2},{4,5},{5,4},{6,7},{7,6},{8,9},{9,8},{10,11... | collective-permute-start | bytes 1966088 | tf_op jit(solution)/shard_map/ppermute | solution.py:149
  12.8 28.8 %collective-permute-start.3 = (bf16[256,1280]{1,0:T(8,128)(2,1)}, bf16[256,1280]{1,0:T(8,128)(2,1)}, u32[]{:S(2)}, u32[]{:S(2)}) collective-permute-start(bf16[256,1280]{1,0:T(8,128)(2,1)} %get-tuple-element.39), channel_id=1, source_target_pairs={{0,4},{4,8},{8,12},{12,14},{14,10},{10,6},{6,2},{2,0},{1,5},{5,9},... | collective-permute-start | bytes 1966088 | tf_op jit(solution)/shard_map/ppermute | solution.py:223
  14.4 87.0 %collective-permute-start.2 = (bf16[256,1280]{1,0:T(8,128)(2,1)}, bf16[256,1280]{1,0:T(8,128)(2,1)}, u32[]{:S(2)}, u32[]{:S(2)}) collective-permute-start(bf16[256,1280]{1,0:T(8,128)(2,1)} %get-tuple-element.40), channel_id=1, source_target_pairs={{0,1},{1,0},{2,3},{3,2},{4,5},{5,4},{6,7},{7,6},{8,9},{9,8},{10,11... | collective-permute-start | bytes 1966088 | tf_op jit(solution)/shard_map/ppermute | solution.py:149
  14.6 27.0 %collective-permute-start.5 = (bf16[256,1280]{1,0:T(8,128)(2,1)}, bf16[256,1280]{1,0:T(8,128)(2,1)}, u32[]{:S(2)}, u32[]{:S(2)}) collective-permute-start(bf16[256,1280]{1,0:T(8,128)(2,1)} %get-tuple-element.40), channel_id=1, source_target_pairs={{0,2},{4,0},{8,4},{12,8},{14,12},{10,14},{6,10},{2,6},{1,3},{5,1},... | collective-permute-start | bytes 1966088 | tf_op jit(solution)/shard_map/ppermute | solution.py:223
  41.7 76.4 %collective-permute-start.4 = (bf16[256,1280]{1,0:T(8,128)(2,1)}, bf16[256,1280]{1,0:T(8,128)(2,1)}, u32[]{:S(2)}, u32[]{:S(2)}) collective-permute-start(bf16[256,1280]{1,0:T(8,128)(2,1)} %collective-permute-done.3), channel_id=1, source_target_pairs={{0,1},{1,0},{2,3},{3,2},{4,5},{5,4},{6,7},{7,6},{8,9},{9,8},{10,11... | collective-permute-start | bytes 1966088 | tf_op jit(solution)/shard_map/ppermute | solution.py:149
  41.7 52.0 %collective-permute-start.7 = (bf16[256,1280]{1,0:T(8,128)(2,1)}, bf16[256,1280]{1,0:T(8,128)(2,1)}, u32[]{:S(2)}, u32[]{:S(2)}) collective-permute-start(bf16[256,1280]{1,0:T(8,128)(2,1)} %collective-permute-done.3), channel_id=1, source_target_pairs={{0,4},{4,8},{8,12},{12,14},{14,10},{10,6},{6,2},{2,0},{1,5},{5,9},... | collective-permute-start | bytes 1966088 | tf_op jit(solution)/shard_map/ppermute | solution.py:223
  78.7 43.6 %collective-permute-start.6 = (bf16[256,1280]{1,0:T(8,128)(2,1)}, bf16[256,1280]{1,0:T(8,128)(2,1)}, u32[]{:S(2)}, u32[]{:S(2)}) collective-permute-start(bf16[256,1280]{1,0:T(8,128)(2,1)} %collective-permute-done.5), channel_id=1, source_target_pairs={{0,1},{1,0},{2,3},{3,2},{4,5},{5,4},{6,7},{7,6},{8,9},{9,8},{10,11... | collective-permute-start | bytes 1966088 | tf_op jit(solution)/shard_map/ppermute | solution.py:149
  93.7 17.4 %collective-permute-start.9 = (bf16[256,1280]{1,0:T(8,128)(2,1)}, bf16[256,1280]{1,0:T(8,128)(2,1)}, u32[]{:S(2)}, u32[]{:S(2)}) collective-permute-start(bf16[256,1280]{1,0:T(8,128)(2,1)} %collective-permute-done.5), channel_id=1, source_target_pairs={{0,2},{4,0},{8,4},{12,8},{14,12},{10,14},{6,10},{2,6},{1,3},{5,1},... | collective-permute-start | bytes 1966088 | tf_op jit(solution)/shard_map/ppermute | solution.py:223
  98.1 17.0 %collective-permute-start.11 = (bf16[256,1280]{1,0:T(8,128)(2,1)}, bf16[256,1280]{1,0:T(8,128)(2,1)S(1)}, u32[]{:S(2)}, u32[]{:S(2)}) collective-permute-start(bf16[256,1280]{1,0:T(8,128)(2,1)} %collective-permute-done.7), channel_id=1, source_target_pairs={{0,4},{4,8},{8,12},{12,14},{14,10},{10,6},{6,2},{2,0},{1,5},{5,9},... | collective-permute-start | bytes 1966088 | tf_op jit(solution)/shard_map/ppermute | solution.py:223
  101.4 34.6 %collective-permute-start.8 = (bf16[256,1280]{1,0:T(8,128)(2,1)}, bf16[256,1280]{1,0:T(8,128)(2,1)}, u32[]{:S(2)}, u32[]{:S(2)}) collective-permute-start(bf16[256,1280]{1,0:T(8,128)(2,1)} %collective-permute-done.7), channel_id=1, source_target_pairs={{0,1},{1,0},{2,3},{3,2},{4,5},{5,4},{6,7},{7,6},{8,9},{9,8},{10,11... | collective-permute-start | bytes 1966088 | tf_op jit(solution)/shard_map/ppermute | solution.py:149
  111.1 41.5 %collective-permute-start.19 = (bf16[8,216,1024]{2,1,0:T(8,128)(2,1)}, bf16[8,216,1024]{2,1,0:T(8,128)(2,1)S(1)}, u32[]{:S(2)}, u32[]{:S(2)}) collective-permute-start(bf16[8,216,1024]{2,1,0:T(8,128)(2,1)} %bitcast.188), channel_id=1, source_target_pairs={{0,1},{1,0},{2,3},{3,2},{4,5},{5,4},{6,7},{7,6},{8,9},{9,8},{10,11... | collective-permute-start | bytes 10616840 | tf_op jit(solution)/shard_map/ppermute | solution.py:149
  118.1 19.7 %collective-permute-start.10 = (bf16[256,1280]{1,0:T(8,128)(2,1)}, bf16[256,1280]{1,0:T(8,128)(2,1)S(1)}, u32[]{:S(2)}, u32[]{:S(2)}) collective-permute-start(bf16[256,1280]{1,0:T(8,128)(2,1)} %collective-permute-done.9), channel_id=1, source_target_pairs={{0,1},{1,0},{2,3},{3,2},{4,5},{5,4},{6,7},{7,6},{8,9},{9,8},{10,11... | collective-permute-start | bytes 1966088 | tf_op jit(solution)/shard_map/ppermute | solution.py:149
  122.3 17.2 %collective-permute-start.15 = (bf16[256,1280]{1,0:T(8,128)(2,1)S(1)}, bf16[256,1280]{1,0:T(8,128)(2,1)}, u32[]{:S(2)}, u32[]{:S(2)}) collective-permute-start(bf16[256,1280]{1,0:T(8,128)(2,1)S(1)} %collective-permute-done.11), channel_id=1, source_target_pairs={{0,4},{4,8},{8,12},{12,14},{14,10},{10,6},{6,2},{2,0},{1,5},{5,9},... | collective-permute-start | bytes 1966088 | tf_op jit(solution)/shard_map/ppermute | solution.py:223
  139.5 44.0 %collective-permute-start.16 = (bf16[256,1280]{1,0:T(8,128)(2,1)}, bf16[256,1280]{1,0:T(8,128)(2,1)}, u32[]{:S(2)}, u32[]{:S(2)}) collective-permute-start(bf16[256,1280]{1,0:T(8,128)(2,1)} %collective-permute-done.15), channel_id=1, source_target_pairs={{0,1},{1,0},{2,3},{3,2},{4,5},{5,4},{6,7},{7,6},{8,9},{9,8},{10,11... | collective-permute-start | bytes 1966088 | tf_op jit(solution)/shard_map/ppermute | solution.py:149
  146.6 55.1 %collective-permute-start.18 = (bf16[256,1280]{1,0:T(8,128)(2,1)S(1)}, bf16[256,1280]{1,0:T(8,128)(2,1)}, u32[]{:S(2)}, u32[]{:S(2)}) collective-permute-start(bf16[256,1280]{1,0:T(8,128)(2,1)S(1)} %collective-permute-done.17), channel_id=1, source_target_pairs={{0,1},{1,0},{2,3},{3,2},{4,5},{5,4},{6,7},{7,6},{8,9},{9,8},{10,11... | collective-permute-start | bytes 1966088 | tf_op jit(solution)/shard_map/ppermute | solution.py:149
  196.6 19.6 %collective-permute-start.22 = (bf16[256,1280]{1,0:T(8,128)(2,1)S(1)}, bf16[256,1280]{1,0:T(8,128)(2,1)S(1)}, u32[]{:S(2)}, u32[]{:S(2)}) collective-permute-start(bf16[256,1280]{1,0:T(8,128)(2,1)S(1)} %collective-permute-done.21), channel_id=1, source_target_pairs={{0,1},{1,0},{2,3},{3,2},{4,5},{5,4},{6,7},{7,6},{8,9},{9,8},{10,11... | collective-permute-start | bytes 1966088 | tf_op jit(solution)/shard_map/ppermute | solution.py:149
  196.6 17.1 %collective-permute-start.25 = (bf16[256,1280]{1,0:T(8,128)(2,1)S(1)}, bf16[256,1280]{1,0:T(8,128)(2,1)S(1)}, u32[]{:S(2)}, u32[]{:S(2)}) collective-permute-start(bf16[256,1280]{1,0:T(8,128)(2,1)S(1)} %collective-permute-done.21), channel_id=1, source_target_pairs={{0,4},{4,8},{8,12},{12,14},{14,10},{10,6},{6,2},{2,0},{1,5},{5,9},... | collective-permute-start | bytes 1966088 | tf_op jit(solution)/shard_map/ppermute | solution.py:223
  197.5 22.9 %collective-permute-start.24 = (bf16[256,1280]{1,0:T(8,128)(2,1)S(1)}, bf16[256,1280]{1,0:T(8,128)(2,1)S(1)}, u32[]{:S(2)}, u32[]{:S(2)}) collective-permute-start(bf16[256,1280]{1,0:T(8,128)(2,1)S(1)} %collective-permute-done.23), channel_id=1, source_target_pairs={{0,1},{1,0},{2,3},{3,2},{4,5},{5,4},{6,7},{7,6},{8,9},{9,8},{10,11... | collective-permute-start | bytes 1966088 | tf_op jit(solution)/shard_map/ppermute | solution.py:149
  213.8 21.1 %collective-permute-start.26 = (bf16[256,1280]{1,0:T(8,128)(2,1)S(1)}, bf16[256,1280]{1,0:T(8,128)(2,1)S(1)}, u32[]{:S(2)}, u32[]{:S(2)}) collective-permute-start(bf16[256,1280]{1,0:T(8,128)(2,1)S(1)} %collective-permute-done.25), channel_id=1, source_target_pairs={{0,1},{1,0},{2,3},{3,2},{4,5},{5,4},{6,7},{7,6},{8,9},{9,8},{10,11... | collective-permute-start | bytes 1966088 | tf_op jit(solution)/shard_map/ppermute | solution.py:149
  213.8 17.1 %collective-permute-start.29 = (bf16[256,1280]{1,0:T(8,128)(2,1)S(1)}, bf16[256,1280]{1,0:T(8,128)(2,1)S(1)}, u32[]{:S(2)}, u32[]{:S(2)}) collective-permute-start(bf16[256,1280]{1,0:T(8,128)(2,1)S(1)} %collective-permute-done.25), channel_id=1, source_target_pairs={{0,4},{4,8},{8,12},{12,14},{14,10},{10,6},{6,2},{2,0},{1,5},{5,9},... | collective-permute-start | bytes 1966088 | tf_op jit(solution)/shard_map/ppermute | solution.py:223
  214.7 21.6 %collective-permute-start.28 = (bf16[256,1280]{1,0:T(8,128)(2,1)S(1)}, bf16[256,1280]{1,0:T(8,128)(2,1)S(1)}, u32[]{:S(2)}, u32[]{:S(2)}) collective-permute-start(bf16[256,1280]{1,0:T(8,128)(2,1)S(1)} %collective-permute-done.27), channel_id=1, source_target_pairs={{0,1},{1,0},{2,3},{3,2},{4,5},{5,4},{6,7},{7,6},{8,9},{9,8},{10,11... | collective-permute-start | bytes 1966088 | tf_op jit(solution)/shard_map/ppermute | solution.py:149
  216.3 17.2 %collective-permute-start.31 = (bf16[256,1280]{1,0:T(8,128)(2,1)S(1)}, bf16[256,1280]{1,0:T(8,128)(2,1)S(1)}, u32[]{:S(2)}, u32[]{:S(2)}) collective-permute-start(bf16[256,1280]{1,0:T(8,128)(2,1)S(1)} %collective-permute-done.27), channel_id=1, source_target_pairs={{0,2},{4,0},{8,4},{12,8},{14,12},{10,14},{6,10},{2,6},{1,3},{5,1},... | collective-permute-start | bytes 1966088 | tf_op jit(solution)/shard_map/ppermute | solution.py:223
  (29 other events, 234.9 us)
Sparse Core Ops, SparseCore 0:
  16.5 71.9 all-gather.2

commit v8 on v3

--- a/solution.py
+++ b/solution.py
@@ -119,7 +119,6 @@
     pair_cols = keyvalue_weight.shape[1]
     half_rows = weight_rows // 2
 
-    weights = jnp.concatenate([query_weight, keyvalue_weight], axis=1)
     down_rows = adapter_down.size // query_cols
     upq_rows = adapter_up_query.size // query_cols
     upkv_rows = adapter_up_keyvalue.size // query_cols
@@ -154,12 +153,17 @@
             return [x]
         return [x, lax.ppermute(x, "core", [(0, 1), (1, 0)])]
 
-    pair_width = query_cols + pair_cols
+    pair_rows = half_rows * pair_cols // query_cols
     recv = []
     for h, direction in enumerate(directions):
-        adapters_padded = jnp.pad(adapter_half(h), ((0, 0), (0, pair_width - query_cols)))
+        rows = slice(h * half_rows, (h + 1) * half_rows)
         piece = jnp.concatenate(
-            [weights[h * half_rows : (h + 1) * half_rows], adapters_padded], axis=0
+            [
+                query_weight[rows],
+                keyvalue_weight[rows].reshape(pair_rows, query_cols),
+                adapter_half(h),
+            ],
+            axis=0,
         )
         recv.append(ring_gather(piece, n_chip, order, direction))
 
@@ -169,12 +173,16 @@
         for h, direction in enumerate(directions):
             src_chip = order_table[(pos - s * direction) % n_chip]
             both = swap_core(recv[h][s])
-            adapter_steps[h].append(jnp.stack([p[half_rows:, :query_cols] for p in both]))
+            adapter_steps[h].append(jnp.stack([p[half_rows + pair_rows :] for p in both]))
             for slot, p in enumerate(both):
                 src_core = me_core if slot == 0 else n_lo - 1 - me_core
                 start = (src_chip * n_lo + src_core) * weight_rows + h * half_rows
                 lhs = lax.dynamic_slice_in_dim(normed, start, half_rows, 1)
-                part = jnp.dot(lhs, p[:half_rows], preferred_element_type=jnp.float32)
+                rhs = jnp.concatenate(
+                    [p[:half_rows], p[half_rows : half_rows + pair_rows].reshape(half_rows, pair_cols)],
+                    axis=1,
+                )
+                part = jnp.dot(lhs, rhs, preferred_element_type=jnp.float32)
                 total = part if total is None else total + part
     adapter_pieces = [jnp.stack(a) for a in adapter_steps]
 

time: 224 us -> 303 us (1.35)
  local copies, waits for them, and re-layouts: 30.2 us -> 146 us
  waiting for transfers between devices: 92.8 us -> 27.2 us
  matrix products: 31.6 us -> 52.9 us
    ppermute x14, waiting for transfers between devices: 92.5 us -> 27.2 us  [ring_gather(): current = lax.ppermute(current, 'chip', pairs)]
    slice x1 -> x70, local copies, waits for them, and re-layouts: 0.09 us -> 58.8 us  [the longest x36 30.1 us: shards(): p[:half_rows]]
    reshape x0 -> x32, local copies, waits for them, and re-layouts: none -> 25.3 us  [the longest x30 25.1 us: shards(): p[half_rows:half_rows + pair_rows].reshape(half_rows, pair_cols)]
    another operation x31, local copies, waits for them, and re-layouts: 6.12 us -> 29.7 us  [the longest x30 29.7 us: shards(): jnp.stack([p[half_rows + pair_rows:] for p in both])]
    dot_general x32, matrix products: 24.1 us -> 45.4 us  [shards(): part = jnp.dot(lhs, rhs, preferred_element_type=jnp.float32)]
    concatenate x2, local copies, waits for them, and re-layouts: 0.1 us -> 8.1 us  [shards(): jnp.concatenate([query_weight[rows], keyvalue_weight[rows].reshape(pair_r...]
    unnamed x14, other arithmetic: 9.09 us -> 13.4 us
    unnamed x43 -> x136, local copies, waits for them, and re-layouts: 5.04 us -> 7.66 us
  transfers between devices with their start and end apart: 32 -> 32, of which waited for: 12 -> 6; matrix products, arithmetic and copies ran while one was open for 25% -> 58% of each run, Pallas kernels for 0% -> 0%
where the time goes in v8:
time: 303 us; the launch traced here: 300 us
  local copies, waits for them, and re-layouts  146 us (48%)
  matrix products  52.9 us (17%)
  other arithmetic  29.3 us (10%)
  waiting for transfers between devices  27.2 us (9%)
  between operations  22.9 us (8%)
  starting transfers between devices  21.4 us (7%)
    dot_general x32, matrix products, shards(): part = jnp.dot(lhs, rhs, preferred_element_type=jnp.float32)  45.4 us
    slice x36, local copies, waits for them, and re-layouts, shards(): p[:half_rows]  30.1 us
    another operation x30, local copies, waits for them, and re-layouts, shards(): jnp.stack([p[half_rows + pair_rows:] for p in both])  29.7 us
    slice x32, local copies, waits for them, and re-layouts, shards(): p[half_rows:half_rows + pair_rows].reshape(half_rows, pair_cols)  27.3 us
    ppermute x14, waiting for transfers between devices, ring_gather(): current = lax.ppermute(current, 'chip', pairs)  27.2 us
    reshape x30, local copies, waits for them, and re-layouts, shards(): p[half_rows:half_rows + pair_rows].reshape(half_rows, pair_cols)  25.1 us
    ppermute x14, starting transfers between devices, ring_gather(): current = lax.ppermute(current, 'chip', pairs)  16.7 us
    unnamed x14, other arithmetic  13.4 us
  transfers between devices with their start and end apart: 32, of which 6 were waited for; matrix products, arithmetic and copies ran while one was open for 58% of the time, Pallas kernels for 0%

profile of v8, /device:TPU:0, one launch (start us, length us, event | category | flops | bytes accessed | tf_op | source)
XLA Modules:
  0.0 299.6 jit_solution(11006476623596564432)
XLA Ops:
  2.5 4.0 %concatenate.152 = bf16[432,1024]{1,0:T(8,128)(2,1)} concatenate(bf16[256,1024]{1,0:T(8,128)(2,1)S(1)} %get-tuple-element.18, bf16[64,1024]{1,0:T(8,128)(2,1)S(1)} %reshape.624, bf16[96,1024]{1,0:T(8,128)(2,1)S(1)} %get-tuple-element.22, bf16[8,1024]{1,0:T(8,128)(2,1)S(1)} %get-tuple-element.36, bf16[2,1024]{1,0:T(2,128)(2,1)S(1)} %slice.384, bf16[6,1024]{1,0:T(8,128)(2,1)S(1)} %broadcast.391), dimensions={0} | concatenate | bytes 1769472 | tf_op jit(solution)/shard_map/concatenate | solution.py:160
  7.0 2.5 collective-permute-start.5
  9.7 4.0 %concatenate.149 = bf16[432,1024]{1,0:T(8,128)(2,1)} concatenate(bf16[256,1024]{1,0:T(8,128)(2,1)S(1)} %get-tuple-element.17, bf16[64,1024]{1,0:T(8,128)(2,1)S(1)} %reshape.621, bf16[96,1024]{1,0:T(8,128)(2,1)S(1)} %get-tuple-element.21, bf16[8,1024]{1,0:T(8,128)(2,1)S(1)} %get-tuple-element.35, bf16[2,1024]{1,0:T(2,128)(2,1)S(1)} %slice.375, bf16[6,1024]{1,0:T(8,128)(2,1)S(1)} %broadcast.391), dimensions={0} | concatenate | bytes 1769472 | tf_op jit(solution)/shard_map/concatenate | solution.py:160
  60.7 5.3 %collective-permute-done.9 = bf16[432,1024]{1,0:T(8,128)(2,1)} collective-permute-done((bf16[432,1024]{1,0:T(8,128)(2,1)}, bf16[432,1024]{1,0:T(8,128)(2,1)}, u32[]{:S(2)}, u32[]{:S(2)}) %collective-permute-start.9) | collective-permute-done | bytes 884768 | tf_op jit(solution)/shard_map/ppermute | solution.py:80
  77.2 1.9 slice.512
  79.1 1.9 slice.510
  87.2 4.9 %collective-permute-done.11 = bf16[432,1024]{1,0:T(8,128)(2,1)} collective-permute-done((bf16[432,1024]{1,0:T(8,128)(2,1)}, bf16[432,1024]{1,0:T(8,128)(2,1)}, u32[]{:S(2)}, u32[]{:S(2)}) %collective-permute-start.11) | collective-permute-done | bytes 884768 | tf_op jit(solution)/shard_map/ppermute | solution.py:80
  110.7 2.3 broadcast_select_fusion.1
  134.2 2.7 fusion.99
  158.7 2.2 fusion.16
  160.9 2.6 fusion.15
  182.2 2.6 fusion.120
  185.8 2.7 fusion.13
  189.3 13.4 %collective-permute-done.23 = bf16[432,1024]{1,0:T(8,128)(2,1)} collective-permute-done((bf16[432,1024]{1,0:T(8,128)(2,1)}, bf16[432,1024]{1,0:T(8,128)(2,1)}, u32[]{:S(2)}, u32[]{:S(2)}) %collective-permute-start.23) | collective-permute-done | bytes 884768 | tf_op jit(solution)/shard_map/ppermute | solution.py:80
  204.8 2.6 fusion.127
  228.9 2.2 fusion.12
  231.2 2.6 fusion.11
  259.2 2.6 fusion.9
  263.6 2.6 gather_fusion.2
  269.0 3.6 %gather_fusion.1 = bf16[4,112,1024]{2,1,0:T(8,128)(2,1)} fusion(bf16[8,2,112,1024]{3,2,1,0:T(8,128)(2,1)} %fusion.163, s32[4]{0:T(128)S(1)} %get-tuple-element.11), kind=kCustom, calls=%fused_computation.1 | custom fusion | bytes 1835040 | tf_op jit(solution)/shard_map/gather | solution.py:197
  273.5 2.1 slice.577
  277.8 2.6 dot_general.148
  280.3 3.6 %fusion.33 = f32[384,3,16]{0,2,1:T(8,128)S(1)} fusion(bf16[4,3,16,4096]{3,2,1,0:T(8,128)(2,1)} %dot_general.148, bf16[384,8192]{1,0:T(8,128)(2,1)} %copy-done.1, s32[]{:T(128)S(6)} %select_n.386, f32[384,4]{0,1:T(4,128)S(1)} %fusion.299), kind=kOutput, calls=%fused_computation.63 | convolution fusion | flops 604108800 | bytes 4798468 | tf_op jit(solution)/shard_map/dot_general | solution.py:214
  286.7 2.2 fusion.8
  (419 shorter events, 196.8 us)
Async XLA Ops:
  6.6 37.1 %collective-permute-start.2 = (bf16[432,1024]{1,0:T(8,128)(2,1)}, bf16[432,1024]{1,0:T(8,128)(2,1)S(1)}, u32[]{:S(2)}, u32[]{:S(2)}) collective-permute-start(bf16[432,1024]{1,0:T(8,128)(2,1)} %concatenate.152), channel_id=1, source_target_pairs={{0,1},{1,0},{2,3},{3,2},{4,5},{5,4},{6,7},{7,6},{8,9},{9,8},{10,11... | collective-permute-start | bytes 2654216 | tf_op jit(solution)/shard_map/ppermute | solution.py:154
  7.0 36.6 %collective-permute-start.5 = (bf16[432,1024]{1,0:T(8,128)(2,1)}, bf16[432,1024]{1,0:T(8,128)(2,1)}, u32[]{:S(2)}, u32[]{:S(2)}) collective-permute-start(bf16[432,1024]{1,0:T(8,128)(2,1)} %concatenate.152), channel_id=1, source_target_pairs={{0,2},{4,0},{8,4},{12,8},{14,12},{10,14},{6,10},{2,6},{1,3},{5,1},... | collective-permute-start | bytes 2654216 | tf_op jit(solution)/shard_map/ppermute | solution.py:80
  13.8 32.6 %collective-permute-start.1 = (bf16[432,1024]{1,0:T(8,128)(2,1)}, bf16[432,1024]{1,0:T(8,128)(2,1)S(1)}, u32[]{:S(2)}, u32[]{:S(2)}) collective-permute-start(bf16[432,1024]{1,0:T(8,128)(2,1)} %concatenate.149), channel_id=1, source_target_pairs={{0,1},{1,0},{2,3},{3,2},{4,5},{5,4},{6,7},{7,6},{8,9},{9,8},{10,11... | collective-permute-start | bytes 2654216 | tf_op jit(solution)/shard_map/ppermute | solution.py:154
  13.9 31.3 %collective-permute-start.3 = (bf16[432,1024]{1,0:T(8,128)(2,1)}, bf16[432,1024]{1,0:T(8,128)(2,1)}, u32[]{:S(2)}, u32[]{:S(2)}) collective-permute-start(bf16[432,1024]{1,0:T(8,128)(2,1)} %concatenate.149), channel_id=1, source_target_pairs={{0,4},{4,8},{8,12},{12,14},{14,10},{10,6},{6,2},{2,0},{1,5},{5,9},... | collective-permute-start | bytes 2654216 | tf_op jit(solution)/shard_map/ppermute | solution.py:80
  14.3 96.4 %collective-permute-start = (bf16[384,4096]{1,0:T(8,128)(2,1)}, bf16[384,4096]{1,0:T(8,128)(2,1)}, u32[]{:S(2)}, u32[]{:S(2)}) collective-permute-start(bf16[384,4096]{1,0:T(8,128)(2,1)} %param.11), channel_id=1, source_target_pairs={{0,16},{16,0},{1,17},{17,1},{2,18},{18,2},{3,19},{19,3},{4,20},{20... | collective-permute-start | bytes 9437192 | tf_op jit(solution)/shard_map/ppermute | solution.py:106
  43.6 22.4 %collective-permute-start.6 = (bf16[432,1024]{1,0:T(8,128)(2,1)}, bf16[432,1024]{1,0:T(8,128)(2,1)}, u32[]{:S(2)}, u32[]{:S(2)}) collective-permute-start(bf16[432,1024]{1,0:T(8,128)(2,1)} %collective-permute-done.5), channel_id=1, source_target_pairs={{0,1},{1,0},{2,3},{3,2},{4,5},{5,4},{6,7},{7,6},{8,9},{9,8},{10,11... | collective-permute-start | bytes 2654216 | tf_op jit(solution)/shard_map/ppermute | solution.py:154
  43.7 22.4 %collective-permute-start.9 = (bf16[432,1024]{1,0:T(8,128)(2,1)}, bf16[432,1024]{1,0:T(8,128)(2,1)}, u32[]{:S(2)}, u32[]{:S(2)}) collective-permute-start(bf16[432,1024]{1,0:T(8,128)(2,1)} %collective-permute-done.5), channel_id=1, source_target_pairs={{0,2},{4,0},{8,4},{12,8},{14,12},{10,14},{6,10},{2,6},{1,3},{5,1},... | collective-permute-start | bytes 2654216 | tf_op jit(solution)/shard_map/ppermute | solution.py:80
  45.2 24.4 %collective-permute-start.4 = (bf16[432,1024]{1,0:T(8,128)(2,1)}, bf16[432,1024]{1,0:T(8,128)(2,1)S(1)}, u32[]{:S(2)}, u32[]{:S(2)}) collective-permute-start(bf16[432,1024]{1,0:T(8,128)(2,1)} %collective-permute-done.3), channel_id=1, source_target_pairs={{0,1},{1,0},{2,3},{3,2},{4,5},{5,4},{6,7},{7,6},{8,9},{9,8},{10,11... | collective-permute-start | bytes 2654216 | tf_op jit(solution)/shard_map/ppermute | solution.py:154
  66.0 27.7 %collective-permute-start.10 = (bf16[432,1024]{1,0:T(8,128)(2,1)}, bf16[432,1024]{1,0:T(8,128)(2,1)}, u32[]{:S(2)}, u32[]{:S(2)}) collective-permute-start(bf16[432,1024]{1,0:T(8,128)(2,1)} %collective-permute-done.9), channel_id=1, source_target_pairs={{0,1},{1,0},{2,3},{3,2},{4,5},{5,4},{6,7},{7,6},{8,9},{9,8},{10,11... | collective-permute-start | bytes 2654216 | tf_op jit(solution)/shard_map/ppermute | solution.py:154
  66.0 29.4 %collective-permute-start.13 = (bf16[432,1024]{1,0:T(8,128)(2,1)}, bf16[432,1024]{1,0:T(8,128)(2,1)}, u32[]{:S(2)}, u32[]{:S(2)}) collective-permute-start(bf16[432,1024]{1,0:T(8,128)(2,1)} %collective-permute-done.9), channel_id=1, source_target_pairs={{0,2},{4,0},{8,4},{12,8},{14,12},{10,14},{6,10},{2,6},{1,3},{5,1},... | collective-permute-start | bytes 2654216 | tf_op jit(solution)/shard_map/ppermute | solution.py:80
  69.7 22.4 %collective-permute-start.11 = (bf16[432,1024]{1,0:T(8,128)(2,1)}, bf16[432,1024]{1,0:T(8,128)(2,1)}, u32[]{:S(2)}, u32[]{:S(2)}) collective-permute-start(bf16[432,1024]{1,0:T(8,128)(2,1)} %collective-permute-done.7), channel_id=1, source_target_pairs={{0,4},{4,8},{8,12},{12,14},{14,10},{10,6},{6,2},{2,0},{1,5},{5,9},... | collective-permute-start | bytes 2654216 | tf_op jit(solution)/shard_map/ppermute | solution.py:80
  97.1 47.1 %collective-permute-start.14 = (bf16[432,1024]{1,0:T(8,128)(2,1)}, bf16[432,1024]{1,0:T(8,128)(2,1)}, u32[]{:S(2)}, u32[]{:S(2)}) collective-permute-start(bf16[432,1024]{1,0:T(8,128)(2,1)} %collective-permute-done.13), channel_id=1, source_target_pairs={{0,1},{1,0},{2,3},{3,2},{4,5},{5,4},{6,7},{7,6},{8,9},{9,8},{10,11... | collective-permute-start | bytes 2654216 | tf_op jit(solution)/shard_map/ppermute | solution.py:154
  97.1 39.8 %collective-permute-start.17 = (bf16[432,1024]{1,0:T(8,128)(2,1)}, bf16[432,1024]{1,0:T(8,128)(2,1)}, u32[]{:S(2)}, u32[]{:S(2)}) collective-permute-start(bf16[432,1024]{1,0:T(8,128)(2,1)} %collective-permute-done.13), channel_id=1, source_target_pairs={{0,2},{4,0},{8,4},{12,8},{14,12},{10,14},{6,10},{2,6},{1,3},{5,1},... | collective-permute-start | bytes 2654216 | tf_op jit(solution)/shard_map/ppermute | solution.py:80
  98.6 47.0 %collective-permute-start.12 = (bf16[432,1024]{1,0:T(8,128)(2,1)}, bf16[432,1024]{1,0:T(8,128)(2,1)}, u32[]{:S(2)}, u32[]{:S(2)}) collective-permute-start(bf16[432,1024]{1,0:T(8,128)(2,1)} %collective-permute-done.11), channel_id=1, source_target_pairs={{0,1},{1,0},{2,3},{3,2},{4,5},{5,4},{6,7},{7,6},{8,9},{9,8},{10,11... | collective-permute-start | bytes 2654216 | tf_op jit(solution)/shard_map/ppermute | solution.py:154
  98.9 33.2 %collective-permute-start.15 = (bf16[432,1024]{1,0:T(8,128)(2,1)}, bf16[432,1024]{1,0:T(8,128)(2,1)}, u32[]{:S(2)}, u32[]{:S(2)}) collective-permute-start(bf16[432,1024]{1,0:T(8,128)(2,1)} %collective-permute-done.11), channel_id=1, source_target_pairs={{0,4},{4,8},{8,12},{12,14},{14,10},{10,6},{6,2},{2,0},{1,5},{5,9},... | collective-permute-start | bytes 2654216 | tf_op jit(solution)/shard_map/ppermute | solution.py:80
  137.8 30.2 %collective-permute-start.18 = (bf16[432,1024]{1,0:T(8,128)(2,1)}, bf16[432,1024]{1,0:T(8,128)(2,1)S(1)}, u32[]{:S(2)}, u32[]{:S(2)}) collective-permute-start(bf16[432,1024]{1,0:T(8,128)(2,1)} %collective-permute-done.17), channel_id=1, source_target_pairs={{0,1},{1,0},{2,3},{3,2},{4,5},{5,4},{6,7},{7,6},{8,9},{9,8},{10,11... | collective-permute-start | bytes 2654216 | tf_op jit(solution)/shard_map/ppermute | solution.py:154
  137.9 31.1 %collective-permute-start.21 = (bf16[432,1024]{1,0:T(8,128)(2,1)}, bf16[432,1024]{1,0:T(8,128)(2,1)}, u32[]{:S(2)}, u32[]{:S(2)}) collective-permute-start(bf16[432,1024]{1,0:T(8,128)(2,1)} %collective-permute-done.17), channel_id=1, source_target_pairs={{0,2},{4,0},{8,4},{12,8},{14,12},{10,14},{6,10},{2,6},{1,3},{5,1},... | collective-permute-start | bytes 2654216 | tf_op jit(solution)/shard_map/ppermute | solution.py:80
  139.6 24.0 %collective-permute-start.16 = (bf16[432,1024]{1,0:T(8,128)(2,1)}, bf16[432,1024]{1,0:T(8,128)(2,1)}, u32[]{:S(2)}, u32[]{:S(2)}) collective-permute-start(bf16[432,1024]{1,0:T(8,128)(2,1)} %collective-permute-done.15), channel_id=1, source_target_pairs={{0,1},{1,0},{2,3},{3,2},{4,5},{5,4},{6,7},{7,6},{8,9},{9,8},{10,11... | collective-permute-start | bytes 2654216 | tf_op jit(solution)/shard_map/ppermute | solution.py:154
  176.6 38.7 %collective-permute-start.22 = (bf16[432,1024]{1,0:T(8,128)(2,1)}, bf16[432,1024]{1,0:T(8,128)(2,1)}, u32[]{:S(2)}, u32[]{:S(2)}) collective-permute-start(bf16[432,1024]{1,0:T(8,128)(2,1)} %collective-permute-done.21), channel_id=1, source_target_pairs={{0,1},{1,0},{2,3},{3,2},{4,5},{5,4},{6,7},{7,6},{8,9},{9,8},{10,11... | collective-permute-start | bytes 2654216 | tf_op jit(solution)/shard_map/ppermute | solution.py:154
  177.6 29.8 %collective-permute-start.25 = (bf16[432,1024]{1,0:T(8,128)(2,1)}, bf16[432,1024]{1,0:T(8,128)(2,1)}, u32[]{:S(2)}, u32[]{:S(2)}) collective-permute-start(bf16[432,1024]{1,0:T(8,128)(2,1)} %collective-permute-done.21), channel_id=1, source_target_pairs={{0,2},{4,0},{8,4},{12,8},{14,12},{10,14},{6,10},{2,6},{1,3},{5,1},... | collective-permute-start | bytes 2654216 | tf_op jit(solution)/shard_map/ppermute | solution.py:80
  180.2 36.6 %collective-permute-start.20 = (bf16[432,1024]{1,0:T(8,128)(2,1)}, bf16[432,1024]{1,0:T(8,128)(2,1)}, u32[]{:S(2)}, u32[]{:S(2)}) collective-permute-start(bf16[432,1024]{1,0:T(8,128)(2,1)} %collective-permute-done.19), channel_id=1, source_target_pairs={{0,1},{1,0},{2,3},{3,2},{4,5},{5,4},{6,7},{7,6},{8,9},{9,8},{10,11... | collective-permute-start | bytes 2654216 | tf_op jit(solution)/shard_map/ppermute | solution.py:154
  208.4 32.4 %collective-permute-start.26 = (bf16[432,1024]{1,0:T(8,128)(2,1)}, bf16[432,1024]{1,0:T(8,128)(2,1)S(1)}, u32[]{:S(2)}, u32[]{:S(2)}) collective-permute-start(bf16[432,1024]{1,0:T(8,128)(2,1)} %collective-permute-done.25), channel_id=1, source_target_pairs={{0,1},{1,0},{2,3},{3,2},{4,5},{5,4},{6,7},{7,6},{8,9},{9,8},{10,11... | collective-permute-start | bytes 2654216 | tf_op jit(solution)/shard_map/ppermute | solution.py:154
  208.5 34.7 %collective-permute-start.29 = (bf16[432,1024]{1,0:T(8,128)(2,1)}, bf16[432,1024]{1,0:T(8,128)(2,1)}, u32[]{:S(2)}, u32[]{:S(2)}) collective-permute-start(bf16[432,1024]{1,0:T(8,128)(2,1)} %collective-permute-done.25), channel_id=1, source_target_pairs={{0,2},{4,0},{8,4},{12,8},{14,12},{10,14},{6,10},{2,6},{1,3},{5,1},... | collective-permute-start | bytes 2654216 | tf_op jit(solution)/shard_map/ppermute | solution.py:80
  210.1 23.7 %collective-permute-start.24 = (bf16[432,1024]{1,0:T(8,128)(2,1)}, bf16[432,1024]{1,0:T(8,128)(2,1)}, u32[]{:S(2)}, u32[]{:S(2)}) collective-permute-start(bf16[432,1024]{1,0:T(8,128)(2,1)} %collective-permute-done.23), channel_id=1, source_target_pairs={{0,1},{1,0},{2,3},{3,2},{4,5},{5,4},{6,7},{7,6},{8,9},{9,8},{10,11... | collective-permute-start | bytes 2654216 | tf_op jit(solution)/shard_map/ppermute | solution.py:154
  (84 other events, 488.7 us)

commit v9 on v7

--- a/solution.py
+++ b/solution.py
@@ -102,6 +102,12 @@
     me_core = lax.axis_index("core")
     me_chip = lax.axis_index("chip")
 
+    own_values = hidden.astype(jnp.float32)
+    squares = sum_blk(jnp.sum(own_values * own_values, axis=1), n_blk)
+    factor = lax.rsqrt(squares / full_width + epsilon)
+    gain_part = lax.dynamic_slice_in_dim(input_norm_gain, me_blk * feature_cols, feature_cols, 0)
+    normed_part = (own_values * factor[:, None] * gain_part[None, :]).astype(jnp.bfloat16)
+
     if n_blk == 2:
         other = lax.ppermute(hidden, "blk", [(0, 1), (1, 0)])
         halves = [lax.select(me_blk == 0, hidden, other), lax.select(me_blk == 0, other, hidden)]
@@ -109,10 +115,7 @@
         halves = gather_blk(hidden, n_blk)
     full_hidden = jnp.concatenate(halves, axis=1)
     values = full_hidden.astype(jnp.float32)
-    squares = jnp.sum(values * values, axis=1)
-    factor = lax.rsqrt(squares / full_width + epsilon)
     normed = (values * factor[:, None] * input_norm_gain[None, :]).astype(jnp.bfloat16)
-    normed_part = lax.dynamic_slice_in_dim(normed, me_blk * feature_cols, feature_cols, 1)
 
     weight_rows = query_weight.shape[0]
     query_cols = query_weight.shape[1]

time: 261 us -> 270 us (1.034)
  local copies, waits for them, and re-layouts: 20.3 us -> 24.7 us
  other arithmetic: 17.8 us -> 20.9 us
    ppermute x1, waiting for transfers between devices: 35.4 us -> 0.01 us  [shards(): other = lax.ppermute(hidden, 'blk', [(0, 1), (1, 0)])]
    ppermute x1 -> x2, waiting for transfers between devices: 3.03 us -> 32.8 us  [sum_blk(): return piece + lax.ppermute(piece, 'blk', [(0, 1), (1, 0)])]
    ppermute x14, waiting for transfers between devices: 59.5 us -> 62.7 us  [shards(): current = lax.ppermute(current, 'chip', pairs)]
  transfers between devices with their start and end apart: 34 -> 35, of which waited for: 11 -> 12; matrix products, arithmetic and copies ran while one was open for 35% -> 37% of each run, Pallas kernels for 0% -> 0%
where the time goes in v9:
time: 270 us; the launch traced here: 268 us
  waiting for transfers between devices  95.6 us (35%)
  matrix products  67.8 us (25%)
  between operations  35.5 us (13%)
  local copies, waits for them, and re-layouts  24.7 us (9%)
  starting transfers between devices  23.2 us (9%)
  other arithmetic  20.9 us (8%)
    ppermute x14, waiting for transfers between devices, shards(): current = lax.ppermute(current, 'chip', pairs)  62.7 us
    dot_general x32, matrix products, shards(): part = jnp.dot(lhs, p, preferred_element_type=jnp.float32)  58.4 us
    ppermute x2, waiting for transfers between devices, sum_blk(): return piece + lax.ppermute(piece, 'blk', [(0, 1), (1, 0)])  32.8 us
    ppermute x14, starting transfers between devices, shards(): current = lax.ppermute(current, 'chip', pairs)  16.2 us
  transfers between devices with their start and end apart: 35, of which 12 were waited for; matrix products, arithmetic and copies ran while one was open for 37% of the time, Pallas kernels for 0%

profile of v9, /device:TPU:0, one launch (start us, length us, event | category | flops | bytes accessed | tf_op | source)
XLA Modules:
  0.0 267.6 jit_solution(14933806142323485018)
XLA Ops:
  7.2 3.0 %collective-permute-start = (bf16[384,4096]{1,0:T(8,128)(2,1)}, bf16[384,4096]{1,0:T(8,128)(2,1)}, u32[]{:S(2)}, u32[]{:S(2)}) collective-permute-start(bf16[384,4096]{1,0:T(8,128)(2,1)} %param.11), channel_id=1, source_target_pairs={{0,16},{16,0},{1,17},{17,1},{2,18},{18,2},{3,19},{19,3},{4,20},{20... | collective-permute-start | bytes 9437192 | tf_op jit(solution)/shard_map/ppermute | solution.py:112
  48.4 30.3 %collective-permute-done.1 = f32[384]{0:T(512)} collective-permute-done((f32[384]{0:T(512)S(1)}, f32[384]{0:T(512)}, u32[]{:S(2)}, u32[]{:S(2)}) %collective-permute-start.1) | collective-permute-done | bytes 1568 | tf_op jit(solution)/shard_map/ppermute | solution.py:65
  89.8 2.8 %fusion.79 = f32[384,1280]{1,0:T(8,128)} fusion(bf16[256,1280]{1,0:T(8,128)(2,1)} %collective-permute-done.6, bf16[384,8192]{1,0:T(8,128)(2,1)S(1)} %multiply_convert_fusion, s32[]{:T(128)S(6)} %select_n.292), kind=kOutput, calls=%fused_computation.112 | convolution fusion | flops 251658240 | bytes 2818052 | tf_op jit(solution)/shard_map/dot_general | solution.py:239
  92.6 2.8 %fusion.82 = f32[384,1280]{1,0:T(8,128)} fusion(bf16[256,1280]{1,0:T(8,128)(2,1)} %collective-permute-done.4, bf16[384,8192]{1,0:T(8,128)(2,1)S(1)} %multiply_convert_fusion, s32[]{:T(128)S(6)} %select_n.288), kind=kOutput, calls=%fused_computation.115 | convolution fusion | flops 251658240 | bytes 2818052 | tf_op jit(solution)/shard_map/dot_general | solution.py:239
  95.4 3.7 %collective-permute-done.8 = bf16[256,1280]{1,0:T(8,128)(2,1)} collective-permute-done((bf16[256,1280]{1,0:T(8,128)(2,1)}, bf16[256,1280]{1,0:T(8,128)(2,1)}, u32[]{:S(2)}, u32[]{:S(2)}) %collective-permute-start.8) | collective-permute-done | bytes 655392 | tf_op jit(solution)/shard_map/ppermute | solution.py:226
  101.6 2.8 %fusion.76 = f32[384,1280]{1,0:T(8,128)} fusion(bf16[256,1280]{1,0:T(8,128)(2,1)} %collective-permute-done.8, bf16[384,8192]{1,0:T(8,128)(2,1)S(1)} %multiply_convert_fusion, s32[]{:T(128)S(6)} %select_n.296), kind=kOutput, calls=%fused_computation.109 | convolution fusion | flops 251658240 | bytes 2818052 | tf_op jit(solution)/shard_map/dot_general | solution.py:239
  104.4 2.8 %fusion.84 = f32[384,1280]{1,0:T(8,128)} fusion(bf16[256,1280]{1,0:T(8,128)(2,1)} %collective-permute-done.3, bf16[384,8192]{1,0:T(8,128)(2,1)S(1)} %multiply_convert_fusion, s32[]{:T(128)S(6)} %select_n.285), kind=kOutput, calls=%fused_computation.117 | convolution fusion | flops 251658240 | bytes 2818052 | tf_op jit(solution)/shard_map/dot_general | solution.py:239
  109.1 7.5 %collective-permute-done.10 = bf16[256,1280]{1,0:T(8,128)(2,1)} collective-permute-done((bf16[256,1280]{1,0:T(8,128)(2,1)}, bf16[256,1280]{1,0:T(8,128)(2,1)}, u32[]{:S(2)}, u32[]{:S(2)}) %collective-permute-start.10) | collective-permute-done | bytes 655392 | tf_op jit(solution)/shard_map/ppermute | solution.py:226
  118.4 2.7 %collective-permute-done.12 = bf16[256,1280]{1,0:T(8,128)(2,1)} collective-permute-done((bf16[256,1280]{1,0:T(8,128)(2,1)}, bf16[256,1280]{1,0:T(8,128)(2,1)}, u32[]{:S(2)}, u32[]{:S(2)}) %collective-permute-start.12) | collective-permute-done | bytes 655392 | tf_op jit(solution)/shard_map/ppermute | solution.py:226
  124.3 4.6 %fusion.20 = f32[384,1280]{1,0:T(8,128)S(1)} fusion(f32[384,1280]{1,0:T(8,128)} %fusion.79, bf16[256,1280]{1,0:T(8,128)(2,1)} %collective-permute-done.5, f32[384,1280]{1,0:T(8,128)} %fusion.82, f32[384,1280]{1,0:T(8,128)} %fusion.84, f32[384,1280]{1,0:T(8,128)S(1)} %copy-done.4, f32[384,1280]{1,0:T(8,128)S(1)} %copy-done.5, f32[384,1280]{1,0:T(8,128)} %fusion.88, ...), kind=kOutput, calls=%fused_computation.43 | convolution fusion | flops 254607360 | bytes 14614532 | tf_op jit(solution)/shard_map/dot_general | solution.py:239
  129.5 7.2 %collective-permute-done.14 = bf16[256,1280]{1,0:T(8,128)(2,1)S(1)} collective-permute-done((bf16[256,1280]{1,0:T(8,128)(2,1)}, bf16[256,1280]{1,0:T(8,128)(2,1)S(1)}, u32[]{:S(2)}, u32[]{:S(2)}) %collective-permute-start.14) | collective-permute-done | bytes 655392 | tf_op jit(solution)/shard_map/ppermute | solution.py:226
  143.6 2.7 %collective-permute-done.16 = bf16[256,1280]{1,0:T(8,128)(2,1)} collective-permute-done((bf16[256,1280]{1,0:T(8,128)(2,1)}, bf16[256,1280]{1,0:T(8,128)(2,1)}, u32[]{:S(2)}, u32[]{:S(2)}) %collective-permute-start.16) | collective-permute-done | bytes 655392 | tf_op jit(solution)/shard_map/ppermute | solution.py:226
  146.3 5.1 %collective-permute-done.18 = bf16[256,1280]{1,0:T(8,128)(2,1)} collective-permute-done((bf16[256,1280]{1,0:T(8,128)(2,1)S(1)}, bf16[256,1280]{1,0:T(8,128)(2,1)}, u32[]{:S(2)}, u32[]{:S(2)}) %collective-permute-start.18) | collective-permute-done | bytes 655392 | tf_op jit(solution)/shard_map/ppermute | solution.py:226
  155.9 2.8 %fusion.15 = f32[384,1280]{1,0:T(8,128)} fusion(f32[384,1280]{1,0:T(8,128)S(1)} %fusion.64, f32[384,1280]{1,0:T(8,128)S(1)} %fusion.16, bf16[256,1280]{1,0:T(8,128)(2,1)S(1)} %collective-permute-done.15, bf16[384,8192]{1,0:T(8,128)(2,1)} %copy-done, s32[]{:T(128)S(6)} %select_n.309), kind=kOutput, calls=%fused_computation.33 | convolution fusion | flops 252641280 | bytes 6750212 | tf_op jit(solution)/shard_map/dot_general | solution.py:239
  158.8 3.4 %pad_maximum_fusion = bf16[2,8,216,1024]{3,2,1,0:T(8,128)(2,1)} fusion(bf16[1,8,216,1024]{3,2,1,0:T(8,128)(2,1)S(1)} %bitcast.190, bf16[1,8,216,1024]{3,2,1,0:T(8,128)(2,1)S(1)} %bitcast.189), kind=kLoop, calls=%fused_computation.4 | loop fusion | flops 3538944 | bytes 14155776 | tf_op jit(solution)/shard_map/stack | solution.py:155
  162.2 4.9 %gather_fusion = bf16[4,216,1024]{2,1,0:T(8,128)(2,1)} fusion(bf16[2,8,216,1024]{3,2,1,0:T(8,128)(2,1)} %pad_maximum_fusion, s32[4]{0:T(128)S(1)} %fusion.136), kind=kCustom, calls=%fused_computation | custom fusion | bytes 3538976 | tf_op jit(solution)/shard_map/gather | solution.py:160
  167.1 2.7 %slice.76 = bf16[4,192,1024]{2,1,0:T(8,128)(2,1)} slice(bf16[4,216,1024]{2,1,0:T(8,128)(2,1)} %gather_fusion), slice={[0:4], [0:192], [0:1024]} | slice | bytes 3145728 | tf_op jit(solution)/shard_map/slice | solution.py:161
  171.2 3.8 %dot_general.136 = bf16[4,3,16,4096]{3,2,1,0:T(8,128)(2,1)} reshape(bf16[4,192,1024]{2,1,0:T(8,128)(2,1)} %slice.76) | data formatting | bytes 3145728 | tf_op jit(solution)/shard_map/dot_general | solution.py:172
  175.0 3.3 %fusion.31 = f32[384,3,16]{0,2,1:T(8,128)} fusion(bf16[4,3,16,4096]{3,2,1,0:T(8,128)(2,1)} %dot_general.136, bf16[384,4096]{1,0:T(8,128)(2,1)S(1)} %copy-done.1, f32[4096]{0:T(1024)S(1)} %dynamic-slice-done, f32[384]{0:T(512)} %copy-done.16, f32[384,4]{0,1:T(4,128)} %fusion.139), kind=kOutput, calls=%fused_computation.56 | convolution fusion | flops 610400256 | bytes 4816384 | tf_op jit(solution)/shard_map/dot_general | solution.py:172
  180.7 2.5 collective-permute-done.21
  193.2 11.2 %collective-permute-done.22 = bf16[256,1280]{1,0:T(8,128)(2,1)S(1)} collective-permute-done((bf16[256,1280]{1,0:T(8,128)(2,1)}, bf16[256,1280]{1,0:T(8,128)(2,1)S(1)}, u32[]{:S(2)}, u32[]{:S(2)}) %collective-permute-start.22) | collective-permute-done | bytes 655392 | tf_op jit(solution)/shard_map/ppermute | solution.py:226
  211.0 10.5 %collective-permute-done.26 = bf16[256,1280]{1,0:T(8,128)(2,1)S(1)} collective-permute-done((bf16[256,1280]{1,0:T(8,128)(2,1)S(1)}, bf16[256,1280]{1,0:T(8,128)(2,1)S(1)}, u32[]{:S(2)}, u32[]{:S(2)}) %collective-permute-start.26) | collective-permute-done | bytes 655392 | tf_op jit(solution)/shard_map/ppermute | solution.py:226
  229.6 9.0 %collective-permute-done.30 = bf16[256,1280]{1,0:T(8,128)(2,1)S(1)} collective-permute-done((bf16[256,1280]{1,0:T(8,128)(2,1)S(1)}, bf16[256,1280]{1,0:T(8,128)(2,1)S(1)}, u32[]{:S(2)}, u32[]{:S(2)}) %collective-permute-start.30) | collective-permute-done | bytes 655392 | tf_op jit(solution)/shard_map/ppermute | solution.py:226
  238.7 3.0 %collective-permute-done.32 = bf16[256,1280]{1,0:T(8,128)(2,1)S(1)} collective-permute-done((bf16[256,1280]{1,0:T(8,128)(2,1)S(1)}, bf16[256,1280]{1,0:T(8,128)(2,1)S(1)}, u32[]{:S(2)}, u32[]{:S(2)}) %collective-permute-start.32) | collective-permute-done | bytes 655392 | tf_op jit(solution)/shard_map/ppermute | solution.py:226
  (172 shorter events, 96.8 us)
Async XLA Ops:
  7.2 109.4 %all-gather.3.cloned.1.call-start = ((), (), s32[]{:S(2)}) async-start(), calls=%async_computation | async-start | bytes 3981312 | tf_op jit(solution)/shard_map/all_gather | solution.py:154
  7.2 74.6 %collective-permute-start = (bf16[384,4096]{1,0:T(8,128)(2,1)}, bf16[384,4096]{1,0:T(8,128)(2,1)}, u32[]{:S(2)}, u32[]{:S(2)}) collective-permute-start(bf16[384,4096]{1,0:T(8,128)(2,1)} %param.11), channel_id=1, source_target_pairs={{0,16},{16,0},{1,17},{17,1},{2,18},{18,2},{3,19},{19,3},{4,20},{20... | collective-permute-start | bytes 9437192 | tf_op jit(solution)/shard_map/ppermute | solution.py:112
  13.9 90.5 %collective-permute-start.3 = (bf16[256,1280]{1,0:T(8,128)(2,1)}, bf16[256,1280]{1,0:T(8,128)(2,1)}, u32[]{:S(2)}, u32[]{:S(2)}) collective-permute-start(bf16[256,1280]{1,0:T(8,128)(2,1)} %get-tuple-element.40), channel_id=1, source_target_pairs={{0,1},{1,0},{2,3},{3,2},{4,5},{5,4},{6,7},{7,6},{8,9},{9,8},{10,11... | collective-permute-start | bytes 1966088 | tf_op jit(solution)/shard_map/ppermute | solution.py:152
  13.9 66.0 %collective-permute-start.6 = (bf16[256,1280]{1,0:T(8,128)(2,1)}, bf16[256,1280]{1,0:T(8,128)(2,1)}, u32[]{:S(2)}, u32[]{:S(2)}) collective-permute-start(bf16[256,1280]{1,0:T(8,128)(2,1)} %get-tuple-element.40), channel_id=1, source_target_pairs={{0,2},{4,0},{8,4},{12,8},{14,12},{10,14},{6,10},{2,6},{1,3},{5,1},... | collective-permute-start | bytes 1966088 | tf_op jit(solution)/shard_map/ppermute | solution.py:226
  16.1 62.6 %collective-permute-start.1 = (f32[384]{0:T(512)S(1)}, f32[384]{0:T(512)}, u32[]{:S(2)}, u32[]{:S(2)}) collective-permute-start(f32[384]{0:T(512)S(1)} %fusion), channel_id=1, source_target_pairs={{0,16},{16,0},{1,17},{17,1},{2,18},{18,2},{3,19},{19,3},{4,20},{20... | collective-permute-start | bytes 4616 | tf_op jit(solution)/shard_map/ppermute | solution.py:65
  16.7 62.7 %collective-permute-start.4 = (bf16[256,1280]{1,0:T(8,128)(2,1)}, bf16[256,1280]{1,0:T(8,128)(2,1)}, u32[]{:S(2)}, u32[]{:S(2)}) collective-permute-start(bf16[256,1280]{1,0:T(8,128)(2,1)} %get-tuple-element.39), channel_id=1, source_target_pairs={{0,4},{4,8},{8,12},{12,14},{14,10},{10,6},{6,2},{2,0},{1,5},{5,9},... | collective-permute-start | bytes 1966088 | tf_op jit(solution)/shard_map/ppermute | solution.py:226
  78.7 28.5 %collective-permute-start.2 = (bf16[256,1280]{1,0:T(8,128)(2,1)}, bf16[256,1280]{1,0:T(8,128)(2,1)S(1)}, u32[]{:S(2)}, u32[]{:S(2)}) collective-permute-start(bf16[256,1280]{1,0:T(8,128)(2,1)} %get-tuple-element.39), channel_id=1, source_target_pairs={{0,1},{1,0},{2,3},{3,2},{4,5},{5,4},{6,7},{7,6},{8,9},{9,8},{10,11... | collective-permute-start | bytes 1966088 | tf_op jit(solution)/shard_map/ppermute | solution.py:152
  79.4 44.8 %collective-permute-start.5 = (bf16[256,1280]{1,0:T(8,128)(2,1)}, bf16[256,1280]{1,0:T(8,128)(2,1)}, u32[]{:S(2)}, u32[]{:S(2)}) collective-permute-start(bf16[256,1280]{1,0:T(8,128)(2,1)} %collective-permute-done.4), channel_id=1, source_target_pairs={{0,1},{1,0},{2,3},{3,2},{4,5},{5,4},{6,7},{7,6},{8,9},{9,8},{10,11... | collective-permute-start | bytes 1966088 | tf_op jit(solution)/shard_map/ppermute | solution.py:152
  80.0 19.1 %collective-permute-start.8 = (bf16[256,1280]{1,0:T(8,128)(2,1)}, bf16[256,1280]{1,0:T(8,128)(2,1)}, u32[]{:S(2)}, u32[]{:S(2)}) collective-permute-start(bf16[256,1280]{1,0:T(8,128)(2,1)} %collective-permute-done.4), channel_id=1, source_target_pairs={{0,4},{4,8},{8,12},{12,14},{14,10},{10,6},{6,2},{2,0},{1,5},{5,9},... | collective-permute-start | bytes 1966088 | tf_op jit(solution)/shard_map/ppermute | solution.py:226
  81.8 47.1 %collective-permute-start.7 = (bf16[256,1280]{1,0:T(8,128)(2,1)}, bf16[256,1280]{1,0:T(8,128)(2,1)}, u32[]{:S(2)}, u32[]{:S(2)}) collective-permute-start(bf16[256,1280]{1,0:T(8,128)(2,1)} %collective-permute-done.6), channel_id=1, source_target_pairs={{0,1},{1,0},{2,3},{3,2},{4,5},{5,4},{6,7},{7,6},{8,9},{9,8},{10,11... | collective-permute-start | bytes 1966088 | tf_op jit(solution)/shard_map/ppermute | solution.py:152
  99.1 17.5 %collective-permute-start.10 = (bf16[256,1280]{1,0:T(8,128)(2,1)}, bf16[256,1280]{1,0:T(8,128)(2,1)}, u32[]{:S(2)}, u32[]{:S(2)}) collective-permute-start(bf16[256,1280]{1,0:T(8,128)(2,1)} %collective-permute-done.6), channel_id=1, source_target_pairs={{0,2},{4,0},{8,4},{12,8},{14,12},{10,14},{6,10},{2,6},{1,3},{5,1},... | collective-permute-start | bytes 1966088 | tf_op jit(solution)/shard_map/ppermute | solution.py:226
  107.3 34.0 %collective-permute-start.9 = (bf16[256,1280]{1,0:T(8,128)(2,1)}, bf16[256,1280]{1,0:T(8,128)(2,1)}, u32[]{:S(2)}, u32[]{:S(2)}) collective-permute-start(bf16[256,1280]{1,0:T(8,128)(2,1)} %collective-permute-done.8), channel_id=1, source_target_pairs={{0,1},{1,0},{2,3},{3,2},{4,5},{5,4},{6,7},{7,6},{8,9},{9,8},{10,11... | collective-permute-start | bytes 1966088 | tf_op jit(solution)/shard_map/ppermute | solution.py:152
  116.6 42.1 %collective-permute-start.20 = (bf16[8,216,1024]{2,1,0:T(8,128)(2,1)}, bf16[8,216,1024]{2,1,0:T(8,128)(2,1)S(1)}, u32[]{:S(2)}, u32[]{:S(2)}) collective-permute-start(bf16[8,216,1024]{2,1,0:T(8,128)(2,1)} %bitcast.188), channel_id=1, source_target_pairs={{0,1},{1,0},{2,3},{3,2},{4,5},{5,4},{6,7},{7,6},{8,9},{9,8},{10,11... | collective-permute-start | bytes 10616840 | tf_op jit(solution)/shard_map/ppermute | solution.py:152
  124.2 18.8 %collective-permute-start.11 = (bf16[256,1280]{1,0:T(8,128)(2,1)}, bf16[256,1280]{1,0:T(8,128)(2,1)S(1)}, u32[]{:S(2)}, u32[]{:S(2)}) collective-permute-start(bf16[256,1280]{1,0:T(8,128)(2,1)} %collective-permute-done.10), channel_id=1, source_target_pairs={{0,1},{1,0},{2,3},{3,2},{4,5},{5,4},{6,7},{7,6},{8,9},{9,8},{10,11... | collective-permute-start | bytes 1966088 | tf_op jit(solution)/shard_map/ppermute | solution.py:152
  128.9 17.4 %collective-permute-start.16 = (bf16[256,1280]{1,0:T(8,128)(2,1)}, bf16[256,1280]{1,0:T(8,128)(2,1)}, u32[]{:S(2)}, u32[]{:S(2)}) collective-permute-start(bf16[256,1280]{1,0:T(8,128)(2,1)} %collective-permute-done.12), channel_id=1, source_target_pairs={{0,4},{4,8},{8,12},{12,14},{14,10},{10,6},{6,2},{2,0},{1,5},{5,9},... | collective-permute-start | bytes 1966088 | tf_op jit(solution)/shard_map/ppermute | solution.py:226
  146.3 45.1 %collective-permute-start.17 = (bf16[256,1280]{1,0:T(8,128)(2,1)}, bf16[256,1280]{1,0:T(8,128)(2,1)}, u32[]{:S(2)}, u32[]{:S(2)}) collective-permute-start(bf16[256,1280]{1,0:T(8,128)(2,1)} %collective-permute-done.16), channel_id=1, source_target_pairs={{0,1},{1,0},{2,3},{3,2},{4,5},{5,4},{6,7},{7,6},{8,9},{9,8},{10,11... | collective-permute-start | bytes 1966088 | tf_op jit(solution)/shard_map/ppermute | solution.py:152
  151.4 57.9 %collective-permute-start.19 = (bf16[256,1280]{1,0:T(8,128)(2,1)}, bf16[256,1280]{1,0:T(8,128)(2,1)}, u32[]{:S(2)}, u32[]{:S(2)}) collective-permute-start(bf16[256,1280]{1,0:T(8,128)(2,1)} %collective-permute-done.18), channel_id=1, source_target_pairs={{0,1},{1,0},{2,3},{3,2},{4,5},{5,4},{6,7},{7,6},{8,9},{9,8},{10,11... | collective-permute-start | bytes 1966088 | tf_op jit(solution)/shard_map/ppermute | solution.py:152
  204.4 20.1 %collective-permute-start.23 = (bf16[256,1280]{1,0:T(8,128)(2,1)S(1)}, bf16[256,1280]{1,0:T(8,128)(2,1)S(1)}, u32[]{:S(2)}, u32[]{:S(2)}) collective-permute-start(bf16[256,1280]{1,0:T(8,128)(2,1)S(1)} %collective-permute-done.22), channel_id=1, source_target_pairs={{0,1},{1,0},{2,3},{3,2},{4,5},{5,4},{6,7},{7,6},{8,9},{9,8},{10,11... | collective-permute-start | bytes 1966088 | tf_op jit(solution)/shard_map/ppermute | solution.py:152
  204.4 17.1 %collective-permute-start.26 = (bf16[256,1280]{1,0:T(8,128)(2,1)S(1)}, bf16[256,1280]{1,0:T(8,128)(2,1)S(1)}, u32[]{:S(2)}, u32[]{:S(2)}) collective-permute-start(bf16[256,1280]{1,0:T(8,128)(2,1)S(1)} %collective-permute-done.22), channel_id=1, source_target_pairs={{0,4},{4,8},{8,12},{12,14},{14,10},{10,6},{6,2},{2,0},{1,5},{5,9},... | collective-permute-start | bytes 1966088 | tf_op jit(solution)/shard_map/ppermute | solution.py:226
  205.8 22.5 %collective-permute-start.25 = (bf16[256,1280]{1,0:T(8,128)(2,1)S(1)}, bf16[256,1280]{1,0:T(8,128)(2,1)S(1)}, u32[]{:S(2)}, u32[]{:S(2)}) collective-permute-start(bf16[256,1280]{1,0:T(8,128)(2,1)S(1)} %collective-permute-done.24), channel_id=1, source_target_pairs={{0,1},{1,0},{2,3},{3,2},{4,5},{5,4},{6,7},{7,6},{8,9},{9,8},{10,11... | collective-permute-start | bytes 1966088 | tf_op jit(solution)/shard_map/ppermute | solution.py:152
  221.5 21.5 %collective-permute-start.27 = (bf16[256,1280]{1,0:T(8,128)(2,1)S(1)}, bf16[256,1280]{1,0:T(8,128)(2,1)S(1)}, u32[]{:S(2)}, u32[]{:S(2)}) collective-permute-start(bf16[256,1280]{1,0:T(8,128)(2,1)S(1)} %collective-permute-done.26), channel_id=1, source_target_pairs={{0,1},{1,0},{2,3},{3,2},{4,5},{5,4},{6,7},{7,6},{8,9},{9,8},{10,11... | collective-permute-start | bytes 1966088 | tf_op jit(solution)/shard_map/ppermute | solution.py:152
  221.5 17.1 %collective-permute-start.30 = (bf16[256,1280]{1,0:T(8,128)(2,1)S(1)}, bf16[256,1280]{1,0:T(8,128)(2,1)S(1)}, u32[]{:S(2)}, u32[]{:S(2)}) collective-permute-start(bf16[256,1280]{1,0:T(8,128)(2,1)S(1)} %collective-permute-done.26), channel_id=1, source_target_pairs={{0,4},{4,8},{8,12},{12,14},{14,10},{10,6},{6,2},{2,0},{1,5},{5,9},... | collective-permute-start | bytes 1966088 | tf_op jit(solution)/shard_map/ppermute | solution.py:226
  222.9 21.6 %collective-permute-start.29 = (bf16[256,1280]{1,0:T(8,128)(2,1)S(1)}, bf16[256,1280]{1,0:T(8,128)(2,1)S(1)}, u32[]{:S(2)}, u32[]{:S(2)}) collective-permute-start(bf16[256,1280]{1,0:T(8,128)(2,1)S(1)} %collective-permute-done.28), channel_id=1, source_target_pairs={{0,1},{1,0},{2,3},{3,2},{4,5},{5,4},{6,7},{7,6},{8,9},{9,8},{10,11... | collective-permute-start | bytes 1966088 | tf_op jit(solution)/shard_map/ppermute | solution.py:152
  224.5 17.2 %collective-permute-start.32 = (bf16[256,1280]{1,0:T(8,128)(2,1)S(1)}, bf16[256,1280]{1,0:T(8,128)(2,1)S(1)}, u32[]{:S(2)}, u32[]{:S(2)}) collective-permute-start(bf16[256,1280]{1,0:T(8,128)(2,1)S(1)} %collective-permute-done.28), channel_id=1, source_target_pairs={{0,2},{4,0},{8,4},{12,8},{14,12},{10,14},{6,10},{2,6},{1,3},{5,1},... | collective-permute-start | bytes 1966088 | tf_op jit(solution)/shard_map/ppermute | solution.py:226
  (29 other events, 253.0 us)
Sparse Core Ops, SparseCore 0:
  21.0 67.2 all-gather.2

commit v10 on v3

--- a/solution.py
+++ b/solution.py
@@ -102,12 +102,7 @@
     me_core = lax.axis_index("core")
     me_chip = lax.axis_index("chip")
 
-    if n_blk == 2:
-        other = lax.ppermute(hidden, "blk", [(0, 1), (1, 0)])
-        halves = [lax.select(me_blk == 0, hidden, other), lax.select(me_blk == 0, other, hidden)]
-    else:
-        halves = gather_blk(hidden, n_blk)
-    full_hidden = jnp.concatenate(halves, axis=1)
+    full_hidden = lax.all_gather(hidden, "blk", axis=1, tiled=True)
     values = full_hidden.astype(jnp.float32)
     squares = jnp.sum(values * values, axis=1)
     factor = lax.rsqrt(squares / full_width + epsilon)

time: 224 us -> 260 us (1.16)
  between operations: 22.7 us -> 36.2 us
  local copies, waits for them, and re-layouts: 30.2 us -> 43.6 us
  matrix products: 31.6 us -> 36.6 us
  other arithmetic: 26.4 us -> 29 us
    unnamed x43 -> x111, local copies, waits for them, and re-layouts: 5.04 us -> 14 us
    dot_general x32, matrix products: 24.1 us -> 29.1 us  [shards(): part = jnp.dot(lhs, p[:half_rows], preferred_element_type=jnp.float32)]
    another operation x30, local copies, waits for them, and re-layouts: 6.11 us -> 10.8 us  [shards(): jnp.stack([p[half_rows:, :query_cols] for p in both])]
    select_n x1 -> x0, other arithmetic: 3.25 us -> none  [shards(): lax.select(me_blk == 0, hidden, other)]
    reduce_sum x1, other arithmetic: 1.48 us -> 4.25 us  [shards(): squares = jnp.sum(values * values, axis=1)]
    unnamed x14, other arithmetic: 9.09 us -> 11.8 us
  transfers between devices with their start and end apart: 32 -> 32, of which waited for: 12 -> 8; matrix products, arithmetic and copies ran while one was open for 25% -> 26% of each run, Pallas kernels for 0% -> 0%
where the time goes in v10:
time: 260 us; the launch traced here: 258 us
  waiting for transfers between devices  93 us (36%)
  local copies, waits for them, and re-layouts  43.6 us (17%)
  matrix products  36.6 us (14%)
  between operations  36.2 us (14%)
  other arithmetic  29 us (11%)
  starting transfers between devices  19.6 us (8%)
    ppermute x14, waiting for transfers between devices, ring_gather(): current = lax.ppermute(current, 'chip', pairs)  92.9 us
    dot_general x32, matrix products, shards(): part = jnp.dot(lhs, p[:half_rows], preferred_element_type=jnp.float32)  29.1 us
    ppermute x14, starting transfers between devices, ring_gather(): current = lax.ppermute(current, 'chip', pairs)  15.7 us
    unnamed x111, local copies, waits for them, and re-layouts  14 us
    unnamed x14, other arithmetic  11.8 us
    another operation x30, local copies, waits for them, and re-layouts, shards(): jnp.stack([p[half_rows:, :query_cols] for p in both])  10.8 us
    gather x2, local copies, waits for them, and re-layouts, shards(): per_half.append(adapter_pieces[h][a_step, a_slot])  6.22 us
  transfers between devices with their start and end apart: 32, of which 8 were waited for; matrix products, arithmetic and copies ran while one was open for 26% of the time, Pallas kernels for 0%

profile of v10, /device:TPU:0, one launch (start us, length us, event | category | flops | bytes accessed | tf_op | source)
XLA Modules:
  0.0 258.0 jit_solution(900718872685228360)
XLA Ops:
  12.0 2.5 collective-permute-start.4
  49.9 15.8 %collective-permute-done.8 = bf16[368,1280]{1,0:T(8,128)(2,1)S(1)} collective-permute-done((bf16[368,1280]{1,0:T(8,128)(2,1)}, bf16[368,1280]{1,0:T(8,128)(2,1)S(1)}, u32[]{:S(2)}, u32[]{:S(2)}) %collective-permute-start.8) | collective-permute-done | bytes 942112 | tf_op jit(solution)/shard_map/ppermute | solution.py:80
  65.7 1.7 collective-permute-start.12
  69.9 19.1 %collective-permute-done.12 = bf16[368,1280]{1,0:T(8,128)(2,1)S(1)} collective-permute-done((bf16[368,1280]{1,0:T(8,128)(2,1)S(1)}, bf16[368,1280]{1,0:T(8,128)(2,1)S(1)}, u32[]{:S(2)}, u32[]{:S(2)}) %collective-permute-start.12) | collective-permute-done | bytes 942112 | tf_op jit(solution)/shard_map/ppermute | solution.py:80
  89.0 1.7 collective-permute-start.16
  93.2 19.1 %collective-permute-done.16 = bf16[368,1280]{1,0:T(8,128)(2,1)S(1)} collective-permute-done((bf16[368,1280]{1,0:T(8,128)(2,1)S(1)}, bf16[368,1280]{1,0:T(8,128)(2,1)S(1)}, u32[]{:S(2)}, u32[]{:S(2)}) %collective-permute-start.16) | collective-permute-done | bytes 942112 | tf_op jit(solution)/shard_map/ppermute | solution.py:80
  112.3 1.7 collective-permute-start.20
  116.5 19.1 %collective-permute-done.20 = bf16[368,1280]{1,0:T(8,128)(2,1)S(1)} collective-permute-done((bf16[368,1280]{1,0:T(8,128)(2,1)S(1)}, bf16[368,1280]{1,0:T(8,128)(2,1)S(1)}, u32[]{:S(2)}, u32[]{:S(2)}) %collective-permute-start.20) | collective-permute-done | bytes 942112 | tf_op jit(solution)/shard_map/ppermute | solution.py:80
  135.6 1.7 collective-permute-start.24
  139.8 19.2 %collective-permute-done.24 = bf16[368,1280]{1,0:T(8,128)(2,1)} collective-permute-done((bf16[368,1280]{1,0:T(8,128)(2,1)S(1)}, bf16[368,1280]{1,0:T(8,128)(2,1)}, u32[]{:S(2)}, u32[]{:S(2)}) %collective-permute-start.24) | collective-permute-done | bytes 942112 | tf_op jit(solution)/shard_map/ppermute | solution.py:80
  159.0 1.7 collective-permute-start.28
  165.4 4.3 %fusion = f32[384]{0:T(512)S(1)} fusion(bf16[384,8192]{1,0:T(8,128)(2,1)} %all-gather.2.cloned.1.call-done), kind=kLoop, calls=%fused_computation.5 | loop fusion | flops 9436800 | bytes 6292992 | tf_op jit(solution)/shard_map/reduce_sum | solution.py:107
  170.0 2.1 fusion.2
  172.6 2.0 convolution_add_fusion.16
  186.2 1.6 fusion.21
  197.8 1.6 fusion.56
  212.4 2.8 %fusion.9 = f32[384,1280]{1,0:T(8,128)} fusion(f32[384,1280]{1,0:T(8,128)S(1)} %fusion.50, f32[384,1280]{1,0:T(8,128)S(1)} %fusion.10, bf16[368,1280]{1,0:T(8,128)(2,1)} %collective-permute-done.25, bf16[384,8192]{1,0:T(8,128)(2,1)S(1)} %fusion.2, s32[]{:T(128)S(6)} %select_n.364), kind=kOutput, calls=%fused_computation.20 | convolution fusion | flops 252641280 | bytes 6750212 | tf_op jit(solution)/shard_map/dot_general | solution.py:172
  217.0 2.6 %gather_fusion.2 = bf16[4,112,1024]{2,1,0:T(8,128)(2,1)S(1)} fusion(bf16[8,2,112,1024]{3,2,1,0:T(8,128)(2,1)} %fusion.106, s32[4]{0:T(128)S(1)} %fusion.196), kind=kCustom, calls=%fused_computation.2 | custom fusion | bytes 1835040 | tf_op jit(solution)/shard_map/gather | solution.py:184
  222.5 3.6 %gather_fusion.1 = bf16[4,112,1024]{2,1,0:T(8,128)(2,1)} fusion(bf16[8,2,112,1024]{3,2,1,0:T(8,128)(2,1)} %fusion.98, s32[4]{0:T(128)S(1)} %get-tuple-element.11), kind=kCustom, calls=%fused_computation.1 | custom fusion | bytes 1835040 | tf_op jit(solution)/shard_map/gather | solution.py:184
  227.0 2.1 slice.423
  231.2 2.3 dot_general.148
  233.5 3.7 %fusion.36 = f32[384,3,16]{0,2,1:T(8,128)S(1)} fusion(bf16[4,3,16,4096]{3,2,1,0:T(8,128)(2,1)} %dot_general.148, bf16[384,8192]{1,0:T(8,128)(2,1)} %copy-done.1, s32[]{:T(128)S(6)} %select_n.373, f32[384,4]{0,1:T(4,128)S(1)} %fusion.201), kind=kOutput, calls=%fused_computation.67 | convolution fusion | flops 604108800 | bytes 4798468 | tf_op jit(solution)/shard_map/dot_general | solution.py:201
  237.2 1.6 collective-permute-start.30
  238.8 1.7 fusion.8
  (295 shorter events, 86.8 us)
Async XLA Ops:
  7.2 158.2 %all-gather.2.cloned.1.call-start = ((), (), s32[]{:S(2)}) async-start(), calls=%async_computation | async-start | bytes 9437184 | tf_op jit(solution)/shard_map/all_gather | solution.py:105
  11.5 32.6 %collective-permute-start.1 = (bf16[368,1280]{1,0:T(8,128)(2,1)}, bf16[368,1280]{1,0:T(8,128)(2,1)}, u32[]{:S(2)}, u32[]{:S(2)}) collective-permute-start(bf16[368,1280]{1,0:T(8,128)(2,1)} %fusion.41), channel_id=1, source_target_pairs={{0,1},{1,0},{2,3},{3,2},{4,5},{5,4},{6,7},{7,6},{8,9},{9,8},{10,11... | collective-permute-start | bytes 2826248 | tf_op jit(solution)/shard_map/ppermute | solution.py:150
  12.0 30.2 %collective-permute-start.4 = (bf16[368,1280]{1,0:T(8,128)(2,1)}, bf16[368,1280]{1,0:T(8,128)(2,1)}, u32[]{:S(2)}, u32[]{:S(2)}) collective-permute-start(bf16[368,1280]{1,0:T(8,128)(2,1)} %fusion.41), channel_id=1, source_target_pairs={{0,2},{4,0},{8,4},{12,8},{14,12},{10,14},{6,10},{2,6},{1,3},{5,1},... | collective-permute-start | bytes 2826248 | tf_op jit(solution)/shard_map/ppermute | solution.py:80
  14.6 32.6 %collective-permute-start = (bf16[368,1280]{1,0:T(8,128)(2,1)S(1)}, bf16[368,1280]{1,0:T(8,128)(2,1)}, u32[]{:S(2)}, u32[]{:S(2)}) collective-permute-start(bf16[368,1280]{1,0:T(8,128)(2,1)S(1)} %fusion.40), channel_id=1, source_target_pairs={{0,1},{1,0},{2,3},{3,2},{4,5},{5,4},{6,7},{7,6},{8,9},{9,8},{10,11... | collective-permute-start | bytes 2826248 | tf_op jit(solution)/shard_map/ppermute | solution.py:150
  14.9 29.0 %collective-permute-start.2 = (bf16[368,1280]{1,0:T(8,128)(2,1)S(1)}, bf16[368,1280]{1,0:T(8,128)(2,1)}, u32[]{:S(2)}, u32[]{:S(2)}) collective-permute-start(bf16[368,1280]{1,0:T(8,128)(2,1)S(1)} %fusion.40), channel_id=1, source_target_pairs={{0,4},{4,8},{8,12},{12,14},{14,10},{10,6},{6,2},{2,0},{1,5},{5,9},... | collective-permute-start | bytes 2826248 | tf_op jit(solution)/shard_map/ppermute | solution.py:80
  42.2 25.4 %collective-permute-start.5 = (bf16[368,1280]{1,0:T(8,128)(2,1)}, bf16[368,1280]{1,0:T(8,128)(2,1)S(1)}, u32[]{:S(2)}, u32[]{:S(2)}) collective-permute-start(bf16[368,1280]{1,0:T(8,128)(2,1)} %collective-permute-done.4), channel_id=1, source_target_pairs={{0,1},{1,0},{2,3},{3,2},{4,5},{5,4},{6,7},{7,6},{8,9},{9,8},{10,11... | collective-permute-start | bytes 2826248 | tf_op jit(solution)/shard_map/ppermute | solution.py:150
  42.3 23.4 %collective-permute-start.8 = (bf16[368,1280]{1,0:T(8,128)(2,1)}, bf16[368,1280]{1,0:T(8,128)(2,1)S(1)}, u32[]{:S(2)}, u32[]{:S(2)}) collective-permute-start(bf16[368,1280]{1,0:T(8,128)(2,1)} %collective-permute-done.4), channel_id=1, source_target_pairs={{0,2},{4,0},{8,4},{12,8},{14,12},{10,14},{6,10},{2,6},{1,3},{5,1},... | collective-permute-start | bytes 2826248 | tf_op jit(solution)/shard_map/ppermute | solution.py:80
  43.9 25.0 %collective-permute-start.3 = (bf16[368,1280]{1,0:T(8,128)(2,1)}, bf16[368,1280]{1,0:T(8,128)(2,1)S(1)}, u32[]{:S(2)}, u32[]{:S(2)}) collective-permute-start(bf16[368,1280]{1,0:T(8,128)(2,1)} %collective-permute-done.2), channel_id=1, source_target_pairs={{0,1},{1,0},{2,3},{3,2},{4,5},{5,4},{6,7},{7,6},{8,9},{9,8},{10,11... | collective-permute-start | bytes 2826248 | tf_op jit(solution)/shard_map/ppermute | solution.py:150
  44.1 23.3 %collective-permute-start.6 = (bf16[368,1280]{1,0:T(8,128)(2,1)}, bf16[368,1280]{1,0:T(8,128)(2,1)S(1)}, u32[]{:S(2)}, u32[]{:S(2)}) collective-permute-start(bf16[368,1280]{1,0:T(8,128)(2,1)} %collective-permute-done.2), channel_id=1, source_target_pairs={{0,4},{4,8},{8,12},{12,14},{14,10},{10,6},{6,2},{2,0},{1,5},{5,9},... | collective-permute-start | bytes 2826248 | tf_op jit(solution)/shard_map/ppermute | solution.py:80
  65.7 25.2 %collective-permute-start.9 = (bf16[368,1280]{1,0:T(8,128)(2,1)S(1)}, bf16[368,1280]{1,0:T(8,128)(2,1)S(1)}, u32[]{:S(2)}, u32[]{:S(2)}) collective-permute-start(bf16[368,1280]{1,0:T(8,128)(2,1)S(1)} %collective-permute-done.8), channel_id=1, source_target_pairs={{0,1},{1,0},{2,3},{3,2},{4,5},{5,4},{6,7},{7,6},{8,9},{9,8},{10,11... | collective-permute-start | bytes 2826248 | tf_op jit(solution)/shard_map/ppermute | solution.py:150
  65.7 23.3 %collective-permute-start.12 = (bf16[368,1280]{1,0:T(8,128)(2,1)S(1)}, bf16[368,1280]{1,0:T(8,128)(2,1)S(1)}, u32[]{:S(2)}, u32[]{:S(2)}) collective-permute-start(bf16[368,1280]{1,0:T(8,128)(2,1)S(1)} %collective-permute-done.8), channel_id=1, source_target_pairs={{0,2},{4,0},{8,4},{12,8},{14,12},{10,14},{6,10},{2,6},{1,3},{5,1},... | collective-permute-start | bytes 2826248 | tf_op jit(solution)/shard_map/ppermute | solution.py:80
  67.4 24.8 %collective-permute-start.7 = (bf16[368,1280]{1,0:T(8,128)(2,1)S(1)}, bf16[368,1280]{1,0:T(8,128)(2,1)S(1)}, u32[]{:S(2)}, u32[]{:S(2)}) collective-permute-start(bf16[368,1280]{1,0:T(8,128)(2,1)S(1)} %collective-permute-done.6), channel_id=1, source_target_pairs={{0,1},{1,0},{2,3},{3,2},{4,5},{5,4},{6,7},{7,6},{8,9},{9,8},{10,11... | collective-permute-start | bytes 2826248 | tf_op jit(solution)/shard_map/ppermute | solution.py:150
  89.0 25.2 %collective-permute-start.13 = (bf16[368,1280]{1,0:T(8,128)(2,1)S(1)}, bf16[368,1280]{1,0:T(8,128)(2,1)S(1)}, u32[]{:S(2)}, u32[]{:S(2)}) collective-permute-start(bf16[368,1280]{1,0:T(8,128)(2,1)S(1)} %collective-permute-done.12), channel_id=1, source_target_pairs={{0,1},{1,0},{2,3},{3,2},{4,5},{5,4},{6,7},{7,6},{8,9},{9,8},{10,11... | collective-permute-start | bytes 2826248 | tf_op jit(solution)/shard_map/ppermute | solution.py:150
  90.7 24.8 %collective-permute-start.11 = (bf16[368,1280]{1,0:T(8,128)(2,1)S(1)}, bf16[368,1280]{1,0:T(8,128)(2,1)S(1)}, u32[]{:S(2)}, u32[]{:S(2)}) collective-permute-start(bf16[368,1280]{1,0:T(8,128)(2,1)S(1)} %collective-permute-done.10), channel_id=1, source_target_pairs={{0,1},{1,0},{2,3},{3,2},{4,5},{5,4},{6,7},{7,6},{8,9},{9,8},{10,11... | collective-permute-start | bytes 2826248 | tf_op jit(solution)/shard_map/ppermute | solution.py:150
  112.3 25.2 %collective-permute-start.17 = (bf16[368,1280]{1,0:T(8,128)(2,1)S(1)}, bf16[368,1280]{1,0:T(8,128)(2,1)S(1)}, u32[]{:S(2)}, u32[]{:S(2)}) collective-permute-start(bf16[368,1280]{1,0:T(8,128)(2,1)S(1)} %collective-permute-done.16), channel_id=1, source_target_pairs={{0,1},{1,0},{2,3},{3,2},{4,5},{5,4},{6,7},{7,6},{8,9},{9,8},{10,11... | collective-permute-start | bytes 2826248 | tf_op jit(solution)/shard_map/ppermute | solution.py:150
  114.1 24.8 %collective-permute-start.15 = (bf16[368,1280]{1,0:T(8,128)(2,1)S(1)}, bf16[368,1280]{1,0:T(8,128)(2,1)S(1)}, u32[]{:S(2)}, u32[]{:S(2)}) collective-permute-start(bf16[368,1280]{1,0:T(8,128)(2,1)S(1)} %collective-permute-done.14), channel_id=1, source_target_pairs={{0,1},{1,0},{2,3},{3,2},{4,5},{5,4},{6,7},{7,6},{8,9},{9,8},{10,11... | collective-permute-start | bytes 2826248 | tf_op jit(solution)/shard_map/ppermute | solution.py:150
  135.6 25.3 %collective-permute-start.21 = (bf16[368,1280]{1,0:T(8,128)(2,1)S(1)}, bf16[368,1280]{1,0:T(8,128)(2,1)S(1)}, u32[]{:S(2)}, u32[]{:S(2)}) collective-permute-start(bf16[368,1280]{1,0:T(8,128)(2,1)S(1)} %collective-permute-done.20), channel_id=1, source_target_pairs={{0,1},{1,0},{2,3},{3,2},{4,5},{5,4},{6,7},{7,6},{8,9},{9,8},{10,11... | collective-permute-start | bytes 2826248 | tf_op jit(solution)/shard_map/ppermute | solution.py:150
  135.6 23.4 %collective-permute-start.24 = (bf16[368,1280]{1,0:T(8,128)(2,1)S(1)}, bf16[368,1280]{1,0:T(8,128)(2,1)}, u32[]{:S(2)}, u32[]{:S(2)}) collective-permute-start(bf16[368,1280]{1,0:T(8,128)(2,1)S(1)} %collective-permute-done.20), channel_id=1, source_target_pairs={{0,2},{4,0},{8,4},{12,8},{14,12},{10,14},{6,10},{2,6},{1,3},{5,1},... | collective-permute-start | bytes 2826248 | tf_op jit(solution)/shard_map/ppermute | solution.py:80
  137.5 25.0 %collective-permute-start.19 = (bf16[368,1280]{1,0:T(8,128)(2,1)S(1)}, bf16[368,1280]{1,0:T(8,128)(2,1)S(1)}, u32[]{:S(2)}, u32[]{:S(2)}) collective-permute-start(bf16[368,1280]{1,0:T(8,128)(2,1)S(1)} %collective-permute-done.18), channel_id=1, source_target_pairs={{0,1},{1,0},{2,3},{3,2},{4,5},{5,4},{6,7},{7,6},{8,9},{9,8},{10,11... | collective-permute-start | bytes 2826248 | tf_op jit(solution)/shard_map/ppermute | solution.py:150
  137.5 23.4 %collective-permute-start.22 = (bf16[368,1280]{1,0:T(8,128)(2,1)S(1)}, bf16[368,1280]{1,0:T(8,128)(2,1)}, u32[]{:S(2)}, u32[]{:S(2)}) collective-permute-start(bf16[368,1280]{1,0:T(8,128)(2,1)S(1)} %collective-permute-done.18), channel_id=1, source_target_pairs={{0,4},{4,8},{8,12},{12,14},{14,10},{10,6},{6,2},{2,0},{1,5},{5,9},... | collective-permute-start | bytes 2826248 | tf_op jit(solution)/shard_map/ppermute | solution.py:80
  159.0 42.8 %collective-permute-start.25 = (bf16[368,1280]{1,0:T(8,128)(2,1)}, bf16[368,1280]{1,0:T(8,128)(2,1)}, u32[]{:S(2)}, u32[]{:S(2)}) collective-permute-start(bf16[368,1280]{1,0:T(8,128)(2,1)} %collective-permute-done.24), channel_id=1, source_target_pairs={{0,1},{1,0},{2,3},{3,2},{4,5},{5,4},{6,7},{7,6},{8,9},{9,8},{10,11... | collective-permute-start | bytes 2826248 | tf_op jit(solution)/shard_map/ppermute | solution.py:150
  159.0 42.7 %collective-permute-start.28 = (bf16[368,1280]{1,0:T(8,128)(2,1)}, bf16[368,1280]{1,0:T(8,128)(2,1)}, u32[]{:S(2)}, u32[]{:S(2)}) collective-permute-start(bf16[368,1280]{1,0:T(8,128)(2,1)} %collective-permute-done.24), channel_id=1, source_target_pairs={{0,2},{4,0},{8,4},{12,8},{14,12},{10,14},{6,10},{2,6},{1,3},{5,1},... | collective-permute-start | bytes 2826248 | tf_op jit(solution)/shard_map/ppermute | solution.py:80
  160.9 43.6 %collective-permute-start.23 = (bf16[368,1280]{1,0:T(8,128)(2,1)}, bf16[368,1280]{1,0:T(8,128)(2,1)}, u32[]{:S(2)}, u32[]{:S(2)}) collective-permute-start(bf16[368,1280]{1,0:T(8,128)(2,1)} %collective-permute-done.22), channel_id=1, source_target_pairs={{0,1},{1,0},{2,3},{3,2},{4,5},{5,4},{6,7},{7,6},{8,9},{9,8},{10,11... | collective-permute-start | bytes 2826248 | tf_op jit(solution)/shard_map/ppermute | solution.py:150
  160.9 44.6 %collective-permute-start.26 = (bf16[368,1280]{1,0:T(8,128)(2,1)}, bf16[368,1280]{1,0:T(8,128)(2,1)}, u32[]{:S(2)}, u32[]{:S(2)}) collective-permute-start(bf16[368,1280]{1,0:T(8,128)(2,1)} %collective-permute-done.22), channel_id=1, source_target_pairs={{0,4},{4,8},{8,12},{12,14},{14,10},{10,6},{6,2},{2,0},{1,5},{5,9},... | collective-permute-start | bytes 2826248 | tf_op jit(solution)/shard_map/ppermute | solution.py:80
  (63 other events, 677.4 us)
Sparse Core Ops, SparseCore 0:
  15.4 81.7 all-gather.1

commit v11 on v9

--- a/solution.py
+++ b/solution.py
@@ -213,22 +213,12 @@
     )
     cosine_table, sine_table = rope_tables(position, HEAD_WIDTH)
 
-    early = (query_update, key_update, value_update, cosine_table, sine_table)
-    tie_step = min(n_chip - 1, n_chip // 2 + 1)
-    recv = []
-    for h, direction in enumerate(directions):
-        pairs = [(order[i], order[(i + direction) % n_chip]) for i in range(n_chip)]
-        current = weights[h * half_rows : (h + 1) * half_rows]
-        got = [current]
-        for s in range(1, n_chip):
-            if s == tie_step:
-                current, early = lax.optimization_barrier((current, early))
-            current = lax.ppermute(current, "chip", pairs)
-            got.append(current)
-        recv.append(got)
-    query_update, key_update, value_update, cosine_table, sine_table = early
-
-    total = None
+    recv = [
+        ring_gather(weights[h * half_rows : (h + 1) * half_rows], n_chip, order, direction)
+        for h, direction in enumerate(directions)
+    ]
+
+    total = adapter_scale * jnp.concatenate([query_update, key_update, value_update], axis=1)
     for s in range(n_chip):
         for h, direction in enumerate(directions):
             src_chip = order_table[(pos - s * direction) % n_chip]
@@ -237,27 +227,19 @@
                 start = (src_chip * n_lo + src_core) * weight_rows + h * half_rows
                 lhs = lax.dynamic_slice_in_dim(normed, start, half_rows, 1)
                 part = jnp.dot(lhs, p, preferred_element_type=jnp.float32)
-                total = part if total is None else total + part
+                total = total + part
 
 
     query_plain = total[:, :query_cols]
     base_pair = total[:, query_cols:]
 
-    query_complete = (query_plain + adapter_scale * query_update).reshape(
-        row_number, QUERY_LOCAL * KEYVALUE_LOCAL, HEAD_WIDTH
-    )
+    query_complete = query_plain.reshape(row_number, QUERY_LOCAL * KEYVALUE_LOCAL, HEAD_WIDTH)
     query_states = apply_rotation(query_complete, cosine_table, sine_table).astype(jnp.bfloat16)
     keyvalue_plain = base_pair.reshape(row_number, KEYVALUE_LOCAL, 2, HEAD_WIDTH)
-    key_vectors = apply_rotation(
-        keyvalue_plain[:, :, 0]
-        + adapter_scale * key_update.reshape(row_number, KEYVALUE_LOCAL, HEAD_WIDTH),
-        cosine_table,
-        sine_table,
-    ).astype(jnp.bfloat16)
-    value_vectors = (
-        keyvalue_plain[:, :, 1]
-        + adapter_scale * value_update.reshape(row_number, KEYVALUE_LOCAL, HEAD_WIDTH)
-    ).astype(jnp.bfloat16)
+    key_vectors = apply_rotation(keyvalue_plain[:, :, 0], cosine_table, sine_table).astype(
+        jnp.bfloat16
+    )
+    value_vectors = keyvalue_plain[:, :, 1].astype(jnp.bfloat16)
     grouped = query_states.reshape(row_number, KEYVALUE_LOCAL, QUERY_LOCAL, HEAD_WIDTH)
     scores = jnp.einsum(
         "tkgc,skc->kgts", grouped, key_vectors, preferred_element_type=jnp.float32

time: 270 us -> 273 us (1.011)
  waiting for transfers between devices: 95.6 us -> 72.5 us
  matrix products: 67.8 us -> 83.2 us
  starting transfers between devices: 23.2 us -> 34.4 us
    ppermute x2, waiting for transfers between devices: 32.8 us -> 2.83 us  [sum_blk(): return piece + lax.ppermute(piece, 'blk', [(0, 1), (1, 0)])]
    dot_general x32, matrix products: 58.4 us -> 74.7 us  [shards(): part = jnp.dot(lhs, p, preferred_element_type=jnp.float32)]
    ppermute x14, starting transfers between devices: 16.2 us -> 25.5 us  [ring_gather(): current = lax.ppermute(current, 'chip', pairs)]
    ppermute x14, waiting for transfers between devices: 62.7 us -> 69.6 us  [ring_gather(): current = lax.ppermute(current, 'chip', pairs)]
    unnamed x39 -> x96, local copies, waits for them, and re-layouts: 5.18 us -> 7.42 us
  transfers between devices with their start and end apart: 35 -> 35, of which waited for: 12 -> 10; matrix products, arithmetic and copies ran while one was open for 37% -> 41% of each run, Pallas kernels for 0% -> 0%
where the time goes in v11:
time: 273 us; the launch traced here: 272 us
  matrix products  83.2 us (30%)
  waiting for transfers between devices  72.5 us (27%)
  between operations  35.4 us (13%)
  starting transfers between devices  34.4 us (13%)
  local copies, waits for them, and re-layouts  24.2 us (9%)
  other arithmetic  22.2 us (8%)
    dot_general x32, matrix products, shards(): part = jnp.dot(lhs, p, preferred_element_type=jnp.float32)  74.7 us
    ppermute x14, waiting for transfers between devices, ring_gather(): current = lax.ppermute(current, 'chip', pairs)  69.6 us
    ppermute x14, starting transfers between devices, ring_gather(): current = lax.ppermute(current, 'chip', pairs)  25.5 us
    unnamed x96, local copies, waits for them, and re-layouts  7.42 us
  transfers between devices with their start and end apart: 35, of which 10 were waited for; matrix products, arithmetic and copies ran while one was open for 41% of the time, Pallas kernels for 0%

profile of v11, /device:TPU:0, one launch (start us, length us, event | category | flops | bytes accessed | tf_op | source)
XLA Modules:
  0.0 271.8 jit_solution(7771171717343746992)
XLA Ops:
  7.2 3.0 %collective-permute-start.3 = (bf16[384,4096]{1,0:T(8,128)(2,1)}, bf16[384,4096]{1,0:T(8,128)(2,1)}, u32[]{:S(2)}, u32[]{:S(2)}) collective-permute-start(bf16[384,4096]{1,0:T(8,128)(2,1)} %param.11), channel_id=1, source_target_pairs={{0,16},{16,0},{1,17},{17,1},{2,18},{18,2},{3,19},{19,3},{4,20},{20... | collective-permute-start | bytes 9437192 | tf_op jit(solution)/shard_map/ppermute | solution.py:112
  19.0 12.4 %collective-permute-done.6 = bf16[256,1280]{1,0:T(8,128)(2,1)} collective-permute-done((bf16[256,1280]{1,0:T(8,128)(2,1)}, bf16[256,1280]{1,0:T(8,128)(2,1)}, u32[]{:S(2)}, u32[]{:S(2)}) %collective-permute-start.6) | collective-permute-done | bytes 655392 | tf_op jit(solution)/shard_map/ppermute | solution.py:80
  62.8 22.7 %collective-permute-done.14 = bf16[256,1280]{1,0:T(8,128)(2,1)} collective-permute-done((bf16[256,1280]{1,0:T(8,128)(2,1)}, bf16[256,1280]{1,0:T(8,128)(2,1)}, u32[]{:S(2)}, u32[]{:S(2)}) %collective-permute-start.14) | collective-permute-done | bytes 655392 | tf_op jit(solution)/shard_map/ppermute | solution.py:80
  85.5 12.1 %collective-permute-start.18 = (bf16[256,1280]{1,0:T(8,128)(2,1)}, bf16[256,1280]{1,0:T(8,128)(2,1)}, u32[]{:S(2)}, u32[]{:S(2)}) collective-permute-start(bf16[256,1280]{1,0:T(8,128)(2,1)} %collective-permute-done.14), channel_id=1, source_target_pairs={{0,4},{4,8},{8,12},{12,14},{14,10},{10,6},{6,2},{2,0},{1,5},{5,9},... | collective-permute-start | bytes 1966088 | tf_op jit(solution)/shard_map/ppermute | solution.py:80
  97.6 6.5 %collective-permute-done.16 = bf16[256,1280]{1,0:T(8,128)(2,1)} collective-permute-done((bf16[256,1280]{1,0:T(8,128)(2,1)}, bf16[256,1280]{1,0:T(8,128)(2,1)}, u32[]{:S(2)}, u32[]{:S(2)}) %collective-permute-start.16) | collective-permute-done | bytes 655392 | tf_op jit(solution)/shard_map/ppermute | solution.py:80
  105.6 12.1 %collective-permute-done.18 = bf16[256,1280]{1,0:T(8,128)(2,1)} collective-permute-done((bf16[256,1280]{1,0:T(8,128)(2,1)}, bf16[256,1280]{1,0:T(8,128)(2,1)}, u32[]{:S(2)}, u32[]{:S(2)}) %collective-permute-start.18) | collective-permute-done | bytes 655392 | tf_op jit(solution)/shard_map/ppermute | solution.py:80
  126.4 3.3 %fusion.87 = f32[384,1280]{1,0:T(8,128)} fusion(bf16[256,1280]{1,0:T(8,128)(2,1)} %collective-permute-done.6, bf16[384,8192]{1,0:T(8,128)(2,1)S(1)} %multiply_convert_fusion, s32[]{:T(128)S(6)} %select_n.293), kind=kOutput, calls=%fused_computation.123 | convolution fusion | flops 251658240 | bytes 2818052 | tf_op jit(solution)/shard_map/dot_general | solution.py:229
  135.3 2.9 %fusion.78 = f32[384,1280]{1,0:T(8,128)} fusion(bf16[256,1280]{1,0:T(8,128)(2,1)} %collective-permute-done.12, bf16[384,8192]{1,0:T(8,128)(2,1)} %copy-done, s32[]{:T(128)S(6)} %select_n.305), kind=kOutput, calls=%fused_computation.114 | convolution fusion | flops 251658240 | bytes 2818052 | tf_op jit(solution)/shard_map/dot_general | solution.py:229
  138.2 2.9 %fusion.75 = f32[384,1280]{1,0:T(8,128)} fusion(bf16[256,1280]{1,0:T(8,128)(2,1)} %collective-permute-done.14, bf16[384,8192]{1,0:T(8,128)(2,1)} %copy-done, s32[]{:T(128)S(6)} %select_n.309), kind=kOutput, calls=%fused_computation.111 | convolution fusion | flops 251658240 | bytes 2818052 | tf_op jit(solution)/shard_map/dot_general | solution.py:229
  141.1 3.0 %fusion.72 = f32[384,1280]{1,0:T(8,128)} fusion(bf16[256,1280]{1,0:T(8,128)(2,1)} %collective-permute-done.16, bf16[384,8192]{1,0:T(8,128)(2,1)} %copy-done, s32[]{:T(128)S(6)} %select_n.313), kind=kOutput, calls=%fused_computation.108 | convolution fusion | flops 251658240 | bytes 2818052 | tf_op jit(solution)/shard_map/dot_general | solution.py:229
  144.1 2.9 %fusion.69 = f32[384,1280]{1,0:T(8,128)} fusion(bf16[256,1280]{1,0:T(8,128)(2,1)} %collective-permute-done.18, bf16[384,8192]{1,0:T(8,128)(2,1)} %copy-done, s32[]{:T(128)S(6)} %select_n.317), kind=kOutput, calls=%fused_computation.105 | convolution fusion | flops 251658240 | bytes 2818052 | tf_op jit(solution)/shard_map/dot_general | solution.py:229
  147.0 2.9 %fusion.66 = f32[384,1280]{1,0:T(8,128)} fusion(bf16[256,1280]{1,0:T(8,128)(2,1)} %collective-permute-done.20, bf16[384,8192]{1,0:T(8,128)(2,1)} %copy-done, s32[]{:T(128)S(6)} %select_n.321), kind=kOutput, calls=%fused_computation.102 | convolution fusion | flops 251658240 | bytes 2818052 | tf_op jit(solution)/shard_map/dot_general | solution.py:229
  152.5 2.9 %fusion.93 = f32[384,1280]{1,0:T(8,128)} fusion(bf16[256,1280]{1,0:T(8,128)(2,1)} %collective-permute-done.4, bf16[384,8192]{1,0:T(8,128)(2,1)} %copy-done, s32[]{:T(128)S(6)} %select_n.288), kind=kOutput, calls=%fused_computation.129 | convolution fusion | flops 251658240 | bytes 2818052 | tf_op jit(solution)/shard_map/dot_general | solution.py:229
  155.4 2.9 %fusion.89 = f32[384,1280]{1,0:T(8,128)} fusion(bf16[256,1280]{1,0:T(8,128)(2,1)} %collective-permute-done.5, bf16[384,8192]{1,0:T(8,128)(2,1)} %copy-done, s32[]{:T(128)S(6)} %select_n.290), kind=kOutput, calls=%fused_computation.125 | convolution fusion | flops 251658240 | bytes 2818052 | tf_op jit(solution)/shard_map/dot_general | solution.py:229
  158.4 3.0 %fusion.63 = f32[384,1280]{1,0:T(8,128)} fusion(bf16[256,1280]{1,0:T(8,128)(2,1)} %collective-permute-done.22, bf16[384,8192]{1,0:T(8,128)(2,1)} %copy-done, s32[]{:T(128)S(6)} %select_n.325), kind=kOutput, calls=%fused_computation.99 | convolution fusion | flops 251658240 | bytes 2818052 | tf_op jit(solution)/shard_map/dot_general | solution.py:229
  161.4 6.0 %collective-permute-done.26 = bf16[256,1280]{1,0:T(8,128)(2,1)S(1)} collective-permute-done((bf16[256,1280]{1,0:T(8,128)(2,1)}, bf16[256,1280]{1,0:T(8,128)(2,1)S(1)}, u32[]{:S(2)}, u32[]{:S(2)}) %collective-permute-start.26) | collective-permute-done | bytes 655392 | tf_op jit(solution)/shard_map/ppermute | solution.py:80
  169.4 2.9 %fusion.60 = f32[384,1280]{1,0:T(8,128)} fusion(bf16[256,1280]{1,0:T(8,128)(2,1)} %collective-permute-done.24, bf16[384,8192]{1,0:T(8,128)(2,1)} %copy-done, s32[]{:T(128)S(6)} %select_n.329), kind=kOutput, calls=%fused_computation.96 | convolution fusion | flops 251658240 | bytes 2818052 | tf_op jit(solution)/shard_map/dot_general | solution.py:229
  178.3 4.9 %collective-permute-done.30 = bf16[256,1280]{1,0:T(8,128)(2,1)S(1)} collective-permute-done((bf16[256,1280]{1,0:T(8,128)(2,1)S(1)}, bf16[256,1280]{1,0:T(8,128)(2,1)S(1)}, u32[]{:S(2)}, u32[]{:S(2)}) %collective-permute-start.30) | collective-permute-done | bytes 655392 | tf_op jit(solution)/shard_map/ppermute | solution.py:80
  183.2 2.9 %fusion.51 = f32[384,1280]{1,0:T(8,128)} fusion(bf16[256,1280]{1,0:T(8,128)(2,1)S(1)} %collective-permute-done.30, bf16[384,8192]{1,0:T(8,128)(2,1)} %copy-done, s32[]{:T(128)S(6)} %select_n.341), kind=kOutput, calls=%fused_computation.87 | convolution fusion | flops 251658240 | bytes 2818052 | tf_op jit(solution)/shard_map/dot_general | solution.py:229
  191.9 3.4 %pad_maximum_fusion = bf16[2,8,216,1024]{3,2,1,0:T(8,128)(2,1)} fusion(bf16[1,8,216,1024]{3,2,1,0:T(8,128)(2,1)S(1)} %bitcast.199, bf16[1,8,216,1024]{3,2,1,0:T(8,128)(2,1)S(1)} %bitcast.198), kind=kLoop, calls=%fused_computation.4 | loop fusion | flops 3538944 | bytes 14155776 | tf_op jit(solution)/shard_map/stack | solution.py:155
  195.3 4.9 %gather_fusion = bf16[4,216,1024]{2,1,0:T(8,128)(2,1)} fusion(bf16[2,8,216,1024]{3,2,1,0:T(8,128)(2,1)} %pad_maximum_fusion, s32[4]{0:T(128)S(1)} %fusion.145), kind=kCustom, calls=%fused_computation | custom fusion | bytes 3538976 | tf_op jit(solution)/shard_map/gather | solution.py:160
  203.8 3.7 %dot_general.116 = bf16[4,3,16,4096]{3,2,1,0:T(8,128)(2,1)} reshape(bf16[4,192,1024]{2,1,0:T(8,128)(2,1)} %slice.74) | data formatting | bytes 3145728 | tf_op jit(solution)/shard_map/dot_general | solution.py:172
  207.5 3.3 %fusion.35 = f32[384,3,16]{0,2,1:T(8,128)} fusion(bf16[4,3,16,4096]{3,2,1,0:T(8,128)(2,1)} %dot_general.116, bf16[384,4096]{1,0:T(8,128)(2,1)S(1)} %copy-done.1, f32[4096]{0:T(1024)S(1)} %dynamic-slice-done, f32[384]{0:T(512)S(1)} %copy-done.40, f32[384,4]{0,1:T(4,128)S(1)} %copy-done.37), kind=kOutput, calls=%fused_computation.62 | convolution fusion | flops 610400256 | bytes 4816384 | tf_op jit(solution)/shard_map/dot_general | solution.py:172
  218.5 4.2 %fusion.24 = f32[384,1280]{1,0:T(8,128)S(1)} fusion(f32[384,1280]{1,0:T(8,128)} %fusion.87, f32[384,1280]{1,0:T(8,128)} %fusion.89, f32[384,1280]{1,0:T(8,128)} %fusion.91, f32[384,1280]{1,0:T(8,128)} %fusion.93, f32[384,128]{1,0:T(8,128)S(1)} %fusion.156, f32[384,128]{1,0:T(8,128)S(1)} %fusion.155, f32[384,1024]{1,0:T(8,128)S(1)} %convolution_bitcast_fusion, ...), kind=kOutput, calls=%fused_computation.48 | convolution fusion | flops 255590400 | bytes 12648452 | tf_op jit(solution)/shard_map/dot_general | solution.py:229
  (227 shorter events, 104.5 us)
Async XLA Ops:
  7.2 128.2 %all-gather.3.cloned.1.call-start = ((), (), s32[]{:S(2)}) async-start(), calls=%async_computation | async-start | bytes 3981312 | tf_op jit(solution)/shard_map/all_gather | solution.py:154
  7.2 113.0 %collective-permute-start.3 = (bf16[384,4096]{1,0:T(8,128)(2,1)}, bf16[384,4096]{1,0:T(8,128)(2,1)}, u32[]{:S(2)}, u32[]{:S(2)}) collective-permute-start(bf16[384,4096]{1,0:T(8,128)(2,1)} %param.11), channel_id=1, source_target_pairs={{0,16},{16,0},{1,17},{17,1},{2,18},{18,2},{3,19},{19,3},{4,20},{20... | collective-permute-start | bytes 9437192 | tf_op jit(solution)/shard_map/ppermute | solution.py:112
  13.9 17.5 %collective-permute-start.6 = (bf16[256,1280]{1,0:T(8,128)(2,1)}, bf16[256,1280]{1,0:T(8,128)(2,1)}, u32[]{:S(2)}, u32[]{:S(2)}) collective-permute-start(bf16[256,1280]{1,0:T(8,128)(2,1)} %get-tuple-element.15), channel_id=1, source_target_pairs={{0,4},{4,8},{8,12},{12,14},{14,10},{10,6},{6,2},{2,0},{1,5},{5,9},... | collective-permute-start | bytes 1966088 | tf_op jit(solution)/shard_map/ppermute | solution.py:80
  15.4 20.0 %collective-permute-start.8 = (bf16[256,1280]{1,0:T(8,128)(2,1)}, bf16[256,1280]{1,0:T(8,128)(2,1)}, u32[]{:S(2)}, u32[]{:S(2)}) collective-permute-start(bf16[256,1280]{1,0:T(8,128)(2,1)} %get-tuple-element.16), channel_id=1, source_target_pairs={{0,2},{4,0},{8,4},{12,8},{14,12},{10,14},{6,10},{2,6},{1,3},{5,1},... | collective-permute-start | bytes 1966088 | tf_op jit(solution)/shard_map/ppermute | solution.py:80
  15.9 134.1 %collective-permute-start.4 = (bf16[256,1280]{1,0:T(8,128)(2,1)}, bf16[256,1280]{1,0:T(8,128)(2,1)}, u32[]{:S(2)}, u32[]{:S(2)}) collective-permute-start(bf16[256,1280]{1,0:T(8,128)(2,1)} %get-tuple-element.15), channel_id=1, source_target_pairs={{0,1},{1,0},{2,3},{3,2},{4,5},{5,4},{6,7},{7,6},{8,9},{9,8},{10,11... | collective-permute-start | bytes 1966088 | tf_op jit(solution)/shard_map/ppermute | solution.py:152
  31.4 26.9 %collective-permute-start.10 = (bf16[256,1280]{1,0:T(8,128)(2,1)}, bf16[256,1280]{1,0:T(8,128)(2,1)}, u32[]{:S(2)}, u32[]{:S(2)}) collective-permute-start(bf16[256,1280]{1,0:T(8,128)(2,1)} %collective-permute-done.6), channel_id=1, source_target_pairs={{0,4},{4,8},{8,12},{12,14},{14,10},{10,6},{6,2},{2,0},{1,5},{5,9},... | collective-permute-start | bytes 1966088 | tf_op jit(solution)/shard_map/ppermute | solution.py:80
  35.5 25.0 %collective-permute-start.12 = (bf16[256,1280]{1,0:T(8,128)(2,1)}, bf16[256,1280]{1,0:T(8,128)(2,1)}, u32[]{:S(2)}, u32[]{:S(2)}) collective-permute-start(bf16[256,1280]{1,0:T(8,128)(2,1)} %collective-permute-done.8), channel_id=1, source_target_pairs={{0,2},{4,0},{8,4},{12,8},{14,12},{10,14},{6,10},{2,6},{1,3},{5,1},... | collective-permute-start | bytes 1966088 | tf_op jit(solution)/shard_map/ppermute | solution.py:80
  36.1 69.4 %collective-permute-start = (f32[384]{0:T(512)S(1)}, f32[384]{0:T(512)S(1)}, u32[]{:S(2)}, u32[]{:S(2)}) collective-permute-start(f32[384]{0:T(512)S(1)} %fusion), channel_id=1, source_target_pairs={{0,16},{16,0},{1,17},{17,1},{2,18},{18,2},{3,19},{19,3},{4,20},{20... | collective-permute-start | bytes 4616 | tf_op jit(solution)/shard_map/ppermute | solution.py:65
  58.3 27.2 %collective-permute-start.14 = (bf16[256,1280]{1,0:T(8,128)(2,1)}, bf16[256,1280]{1,0:T(8,128)(2,1)}, u32[]{:S(2)}, u32[]{:S(2)}) collective-permute-start(bf16[256,1280]{1,0:T(8,128)(2,1)} %collective-permute-done.10), channel_id=1, source_target_pairs={{0,4},{4,8},{8,12},{12,14},{14,10},{10,6},{6,2},{2,0},{1,5},{5,9},... | collective-permute-start | bytes 1966088 | tf_op jit(solution)/shard_map/ppermute | solution.py:80
  60.4 43.7 %collective-permute-start.16 = (bf16[256,1280]{1,0:T(8,128)(2,1)}, bf16[256,1280]{1,0:T(8,128)(2,1)}, u32[]{:S(2)}, u32[]{:S(2)}) collective-permute-start(bf16[256,1280]{1,0:T(8,128)(2,1)} %collective-permute-done.12), channel_id=1, source_target_pairs={{0,2},{4,0},{8,4},{12,8},{14,12},{10,14},{6,10},{2,6},{1,3},{5,1},... | collective-permute-start | bytes 1966088 | tf_op jit(solution)/shard_map/ppermute | solution.py:80
  85.5 32.2 %collective-permute-start.18 = (bf16[256,1280]{1,0:T(8,128)(2,1)}, bf16[256,1280]{1,0:T(8,128)(2,1)}, u32[]{:S(2)}, u32[]{:S(2)}) collective-permute-start(bf16[256,1280]{1,0:T(8,128)(2,1)} %collective-permute-done.14), channel_id=1, source_target_pairs={{0,4},{4,8},{8,12},{12,14},{14,10},{10,6},{6,2},{2,0},{1,5},{5,9},... | collective-permute-start | bytes 1966088 | tf_op jit(solution)/shard_map/ppermute | solution.py:80
  104.1 16.1 %collective-permute-start.20 = (bf16[256,1280]{1,0:T(8,128)(2,1)}, bf16[256,1280]{1,0:T(8,128)(2,1)}, u32[]{:S(2)}, u32[]{:S(2)}) collective-permute-start(bf16[256,1280]{1,0:T(8,128)(2,1)} %collective-permute-done.16), channel_id=1, source_target_pairs={{0,2},{4,0},{8,4},{12,8},{14,12},{10,14},{6,10},{2,6},{1,3},{5,1},... | collective-permute-start | bytes 1966088 | tf_op jit(solution)/shard_map/ppermute | solution.py:80
  105.5 49.8 %collective-permute-start.5 = (bf16[256,1280]{1,0:T(8,128)(2,1)}, bf16[256,1280]{1,0:T(8,128)(2,1)}, u32[]{:S(2)}, u32[]{:S(2)}) collective-permute-start(bf16[256,1280]{1,0:T(8,128)(2,1)} %get-tuple-element.16), channel_id=1, source_target_pairs={{0,1},{1,0},{2,3},{3,2},{4,5},{5,4},{6,7},{7,6},{8,9},{9,8},{10,11... | collective-permute-start | bytes 1966088 | tf_op jit(solution)/shard_map/ppermute | solution.py:152
  117.7 32.8 %collective-permute-start.22 = (bf16[256,1280]{1,0:T(8,128)(2,1)}, bf16[256,1280]{1,0:T(8,128)(2,1)}, u32[]{:S(2)}, u32[]{:S(2)}) collective-permute-start(bf16[256,1280]{1,0:T(8,128)(2,1)} %collective-permute-done.18), channel_id=1, source_target_pairs={{0,4},{4,8},{8,12},{12,14},{14,10},{10,6},{6,2},{2,0},{1,5},{5,9},... | collective-permute-start | bytes 1966088 | tf_op jit(solution)/shard_map/ppermute | solution.py:80
  120.2 35.2 %collective-permute-start.24 = (bf16[256,1280]{1,0:T(8,128)(2,1)}, bf16[256,1280]{1,0:T(8,128)(2,1)}, u32[]{:S(2)}, u32[]{:S(2)}) collective-permute-start(bf16[256,1280]{1,0:T(8,128)(2,1)} %collective-permute-done.20), channel_id=1, source_target_pairs={{0,2},{4,0},{8,4},{12,8},{14,12},{10,14},{6,10},{2,6},{1,3},{5,1},... | collective-permute-start | bytes 1966088 | tf_op jit(solution)/shard_map/ppermute | solution.py:80
  135.3 56.5 %collective-permute-start.1 = (bf16[8,216,1024]{2,1,0:T(8,128)(2,1)}, bf16[8,216,1024]{2,1,0:T(8,128)(2,1)S(1)}, u32[]{:S(2)}, u32[]{:S(2)}) collective-permute-start(bf16[8,216,1024]{2,1,0:T(8,128)(2,1)} %bitcast.197), channel_id=1, source_target_pairs={{0,1},{1,0},{2,3},{3,2},{4,5},{5,4},{6,7},{7,6},{8,9},{9,8},{10,11... | collective-permute-start | bytes 10616840 | tf_op jit(solution)/shard_map/ppermute | solution.py:152
  149.9 72.8 %collective-permute-start.7 = (bf16[256,1280]{1,0:T(8,128)(2,1)}, bf16[256,1280]{1,0:T(8,128)(2,1)}, u32[]{:S(2)}, u32[]{:S(2)}) collective-permute-start(bf16[256,1280]{1,0:T(8,128)(2,1)} %collective-permute-done.6), channel_id=1, source_target_pairs={{0,1},{1,0},{2,3},{3,2},{4,5},{5,4},{6,7},{7,6},{8,9},{9,8},{10,11... | collective-permute-start | bytes 1966088 | tf_op jit(solution)/shard_map/ppermute | solution.py:152
  150.5 16.9 %collective-permute-start.26 = (bf16[256,1280]{1,0:T(8,128)(2,1)}, bf16[256,1280]{1,0:T(8,128)(2,1)S(1)}, u32[]{:S(2)}, u32[]{:S(2)}) collective-permute-start(bf16[256,1280]{1,0:T(8,128)(2,1)} %collective-permute-done.22), channel_id=1, source_target_pairs={{0,4},{4,8},{8,12},{12,14},{14,10},{10,6},{6,2},{2,0},{1,5},{5,9},... | collective-permute-start | bytes 1966088 | tf_op jit(solution)/shard_map/ppermute | solution.py:80
  155.3 69.6 %collective-permute-start.9 = (bf16[256,1280]{1,0:T(8,128)(2,1)}, bf16[256,1280]{1,0:T(8,128)(2,1)}, u32[]{:S(2)}, u32[]{:S(2)}) collective-permute-start(bf16[256,1280]{1,0:T(8,128)(2,1)} %collective-permute-done.8), channel_id=1, source_target_pairs={{0,1},{1,0},{2,3},{3,2},{4,5},{5,4},{6,7},{7,6},{8,9},{9,8},{10,11... | collective-permute-start | bytes 1966088 | tf_op jit(solution)/shard_map/ppermute | solution.py:152
  155.4 17.4 %collective-permute-start.28 = (bf16[256,1280]{1,0:T(8,128)(2,1)}, bf16[256,1280]{1,0:T(8,128)(2,1)S(1)}, u32[]{:S(2)}, u32[]{:S(2)}) collective-permute-start(bf16[256,1280]{1,0:T(8,128)(2,1)} %collective-permute-done.24), channel_id=1, source_target_pairs={{0,2},{4,0},{8,4},{12,8},{14,12},{10,14},{6,10},{2,6},{1,3},{5,1},... | collective-permute-start | bytes 1966088 | tf_op jit(solution)/shard_map/ppermute | solution.py:80
  167.4 15.9 %collective-permute-start.30 = (bf16[256,1280]{1,0:T(8,128)(2,1)S(1)}, bf16[256,1280]{1,0:T(8,128)(2,1)S(1)}, u32[]{:S(2)}, u32[]{:S(2)}) collective-permute-start(bf16[256,1280]{1,0:T(8,128)(2,1)S(1)} %collective-permute-done.26), channel_id=1, source_target_pairs={{0,4},{4,8},{8,12},{12,14},{14,10},{10,6},{6,2},{2,0},{1,5},{5,9},... | collective-permute-start | bytes 1966088 | tf_op jit(solution)/shard_map/ppermute | solution.py:80
  172.7 16.3 %collective-permute-start.32 = (bf16[256,1280]{1,0:T(8,128)(2,1)S(1)}, bf16[256,1280]{1,0:T(8,128)(2,1)S(1)}, u32[]{:S(2)}, u32[]{:S(2)}) collective-permute-start(bf16[256,1280]{1,0:T(8,128)(2,1)S(1)} %collective-permute-done.28), channel_id=1, source_target_pairs={{0,2},{4,0},{8,4},{12,8},{14,12},{10,14},{6,10},{2,6},{1,3},{5,1},... | collective-permute-start | bytes 1966088 | tf_op jit(solution)/shard_map/ppermute | solution.py:80
  183.2 43.7 %collective-permute-start.11 = (bf16[256,1280]{1,0:T(8,128)(2,1)}, bf16[256,1280]{1,0:T(8,128)(2,1)}, u32[]{:S(2)}, u32[]{:S(2)}) collective-permute-start(bf16[256,1280]{1,0:T(8,128)(2,1)} %collective-permute-done.10), channel_id=1, source_target_pairs={{0,1},{1,0},{2,3},{3,2},{4,5},{5,4},{6,7},{7,6},{8,9},{9,8},{10,11... | collective-permute-start | bytes 1966088 | tf_op jit(solution)/shard_map/ppermute | solution.py:152
  189.0 40.2 %collective-permute-start.13 = (bf16[256,1280]{1,0:T(8,128)(2,1)}, bf16[256,1280]{1,0:T(8,128)(2,1)}, u32[]{:S(2)}, u32[]{:S(2)}) collective-permute-start(bf16[256,1280]{1,0:T(8,128)(2,1)} %collective-permute-done.12), channel_id=1, source_target_pairs={{0,1},{1,0},{2,3},{3,2},{4,5},{5,4},{6,7},{7,6},{8,9},{9,8},{10,11... | collective-permute-start | bytes 1966088 | tf_op jit(solution)/shard_map/ppermute | solution.py:152
  (56 other events, 464.2 us)
Sparse Core Ops, SparseCore 0:
  19.1 93.5 all-gather.2

commit v12 on v3

--- a/solution.py
+++ b/solution.py
@@ -184,9 +184,18 @@
     a_core = picked % n_lo
     a_slot = (a_core != me_core).astype(jnp.int32)
     per_half = []
+    piece_ids = jnp.arange(n_chip * n_lo, dtype=jnp.int32)
     for h, direction in enumerate(directions):
         a_step = ((pos - inverse_table[a_chip]) * direction) % n_chip
-        per_half.append(adapter_pieces[h][a_step, a_slot])
+        one_hot = (a_step[:, None] * n_lo + a_slot[:, None] == piece_ids[None, :]).astype(
+            jnp.bfloat16
+        )
+        stacked = adapter_pieces[h].reshape((n_chip * n_lo,) + adapter_pieces[h].shape[2:])
+        per_half.append(
+            jnp.einsum("pk,krc->prc", one_hot, stacked, preferred_element_type=jnp.float32).astype(
+                jnp.bfloat16
+            )
+        )
     down_selected = jnp.concatenate(
         [per_half[0][:, :dh], per_half[1][:, :dh]], axis=1
     ).reshape((prompt_count,) + adapter_down.shape[1:])

time: 224 us -> 215 us (0.960)
  other arithmetic: 26.4 us -> 16.3 us
  local copies, waits for them, and re-layouts: 30.2 us -> 22.4 us
  waiting for transfers between devices: 92.8 us -> 97.7 us
  matrix products: 31.6 us -> 35.9 us
    unnamed x14, other arithmetic: 9.09 us -> 0.45 us
    gather x2 -> x0, local copies, waits for them, and re-layouts: 6.22 us -> none  [shards(): per_half.append(adapter_pieces[h][a_step, a_slot])]
    ppermute x14, waiting for transfers between devices: 92.5 us -> 97.3 us  [ring_gather(): current = lax.ppermute(current, 'chip', pairs)]
    dot_general x0 -> x2, matrix products: none -> 4.49 us  [shards(): jnp.einsum('pk,krc->prc', one_hot, stacked, preferred_element_type=jnp.fl...]
    unnamed x43 -> x57, local copies, waits for them, and re-layouts: 5.04 us -> 4.34 us
  transfers between devices with their start and end apart: 32 -> 32, of which waited for: 12 -> 13; matrix products, arithmetic and copies ran while one was open for 25% -> 21% of each run, Pallas kernels for 0% -> 0%
where the time goes in v12:
time: 215 us; the launch traced here: 214 us
  waiting for transfers between devices  97.7 us (45%)
  matrix products  35.9 us (17%)
  between operations  23.1 us (11%)
  local copies, waits for them, and re-layouts  22.4 us (10%)
  starting transfers between devices  18.9 us (9%)
  other arithmetic  16.3 us (8%)
    ppermute x14, waiting for transfers between devices, ring_gather(): current = lax.ppermute(current, 'chip', pairs)  97.3 us
    dot_general x32, matrix products, shards(): part = jnp.dot(lhs, p[:half_rows], preferred_element_type=jnp.float32)  23.8 us
    ppermute x14, starting transfers between devices, ring_gather(): current = lax.ppermute(current, 'chip', pairs)  15.6 us
    another operation x30, local copies, waits for them, and re-layouts, shards(): jnp.stack([p[half_rows:, :query_cols] for p in both])  5.18 us
    dot_general x2, matrix products, shards(): jnp.einsum('pk,krc->prc', one_hot, stacked, preferred_element_type=jnp.fl...  4.49 us
    unnamed x57, local copies, waits for them, and re-layouts  4.34 us
  transfers between devices with their start and end apart: 32, of which 13 were waited for; matrix products, arithmetic and copies ran while one was open for 21% of the time, Pallas kernels for 0%

profile of v12, /device:TPU:0, one launch (start us, length us, event | category | flops | bytes accessed | tf_op | source)
XLA Modules:
  0.0 214.2 jit_solution(9570699894513682350)
XLA Ops:
  5.5 2.5 %collective-permute-start.5 = (bf16[368,1280]{1,0:T(8,128)(2,1)}, bf16[368,1280]{1,0:T(8,128)(2,1)}, u32[]{:S(2)}, u32[]{:S(2)}) collective-permute-start(bf16[368,1280]{1,0:T(8,128)(2,1)} %fusion.50), channel_id=1, source_target_pairs={{0,2},{4,0},{8,4},{12,8},{14,12},{10,14},{6,10},{2,6},{1,3},{5,1},... | collective-permute-start | bytes 2826248 | tf_op jit(solution)/shard_map/ppermute | solution.py:80
  8.7 1.7 collective-permute-start
  38.2 1.5 collective-permute-start.9
  44.5 17.3 %collective-permute-done.9 = bf16[368,1280]{1,0:T(8,128)(2,1)S(1)} collective-permute-done((bf16[368,1280]{1,0:T(8,128)(2,1)}, bf16[368,1280]{1,0:T(8,128)(2,1)S(1)}, u32[]{:S(2)}, u32[]{:S(2)}) %collective-permute-start.9) | collective-permute-done | bytes 942112 | tf_op jit(solution)/shard_map/ppermute | solution.py:80
  61.7 1.5 collective-permute-start.13
  65.1 19.9 %collective-permute-done.13 = bf16[368,1280]{1,0:T(8,128)(2,1)S(1)} collective-permute-done((bf16[368,1280]{1,0:T(8,128)(2,1)S(1)}, bf16[368,1280]{1,0:T(8,128)(2,1)S(1)}, u32[]{:S(2)}, u32[]{:S(2)}) %collective-permute-start.13) | collective-permute-done | bytes 942112 | tf_op jit(solution)/shard_map/ppermute | solution.py:80
  85.0 1.5 collective-permute-start.17
  87.8 3.3 %broadcast_select_fusion.1 = (bf16[384,4096]{1,0:T(8,128)(2,1)S(1)}, bf16[384,4096]{1,0:T(8,128)(2,1)S(1)}) fusion(bf16[384,4096]{1,0:T(8,128)(2,1)} %param.11, bf16[384,4096]{1,0:T(8,128)(2,1)} %collective-permute-done, pred[]{:T(512)S(6)} %eq.68), kind=kLoop, calls=%fused_computation.20 | loop fusion | flops 3145728 | bytes 12582913 | tf_op jit(solution)/shard_map/select_n | solution.py:107
  92.6 1.8 fusion.2
  95.3 2.0 fusion.99
  97.3 1.5 fusion.97
  98.8 1.5 fusion.95
  100.4 1.5 fusion.92
  112.4 1.5 fusion.20
  115.0 16.6 %collective-permute-done.21 = bf16[368,1280]{1,0:T(8,128)(2,1)S(1)} collective-permute-done((bf16[368,1280]{1,0:T(8,128)(2,1)S(1)}, bf16[368,1280]{1,0:T(8,128)(2,1)S(1)}, u32[]{:S(2)}, u32[]{:S(2)}) %collective-permute-start.21) | collective-permute-done | bytes 942112 | tf_op jit(solution)/shard_map/ppermute | solution.py:80
  136.4 18.6 %collective-permute-done.25 = bf16[368,1280]{1,0:T(8,128)(2,1)S(1)} collective-permute-done((bf16[368,1280]{1,0:T(8,128)(2,1)S(1)}, bf16[368,1280]{1,0:T(8,128)(2,1)S(1)}, u32[]{:S(2)}, u32[]{:S(2)}) %collective-permute-start.25) | collective-permute-done | bytes 942112 | tf_op jit(solution)/shard_map/ppermute | solution.py:80
  159.8 18.5 %collective-permute-done.29 = bf16[368,1280]{1,0:T(8,128)(2,1)S(1)} collective-permute-done((bf16[368,1280]{1,0:T(8,128)(2,1)S(1)}, bf16[368,1280]{1,0:T(8,128)(2,1)S(1)}, u32[]{:S(2)}, u32[]{:S(2)}) %collective-permute-start.29) | collective-permute-done | bytes 942112 | tf_op jit(solution)/shard_map/ppermute | solution.py:80
  178.2 2.3 %collective-permute-done.27 = bf16[368,1280]{1,0:T(8,128)(2,1)S(1)} collective-permute-done((bf16[368,1280]{1,0:T(8,128)(2,1)S(1)}, bf16[368,1280]{1,0:T(8,128)(2,1)S(1)}, u32[]{:S(2)}, u32[]{:S(2)}) %collective-permute-start.27) | collective-permute-done | bytes 942112 | tf_op jit(solution)/shard_map/ppermute | solution.py:80
  181.9 1.8 fusion.13
  183.9 2.2 %fusion.34 = bf16[4,112,1024]{2,0,1:T(4,128)(2,1)S(1)} fusion(bf16[16,112,1024]{2,1,0:T(8,128)(2,1)S(1)} %bitcast.289, s32[4]{0:T(128)S(1)} %fusion.203), kind=kOutput, calls=%fused_computation.63 | convolution fusion | flops 15138880 | bytes 4587536 | tf_op jit(solution)/shard_map/pk,krc->prc/dot_general | solution.py:195
  186.5 2.2 %fusion.31 = bf16[4,112,1024]{2,0,1:T(4,128)(2,1)S(1)} fusion(bf16[16,112,1024]{2,1,0:T(8,128)(2,1)S(1)} %bitcast.288, s32[4]{0:T(128)S(1)} %get-tuple-element.11), kind=kOutput, calls=%fused_computation.62 | convolution fusion | flops 15138880 | bytes 4587536 | tf_op jit(solution)/shard_map/pk,krc->prc/dot_general | solution.py:195
  194.8 2.5 %dot_general.156 = bf16[4,3,16,4096]{3,2,1,0:T(8,128)(2,1)} reshape(bf16[4,192,1024]{2,1,0:T(8,128)(2,1)S(1)} %copy.27) | data formatting | bytes 3145728 | tf_op jit(solution)/shard_map/dot_general | solution.py:215
  197.3 3.7 %fusion.45 = f32[384,3,16]{0,2,1:T(8,128)S(1)} fusion(bf16[4,3,16,4096]{3,2,1,0:T(8,128)(2,1)} %dot_general.156, bf16[384,8192]{1,0:T(8,128)(2,1)} %copy-done.1, s32[]{:T(128)S(6)} %select_n.349, f32[384,4]{0,1:T(4,128)} %fusion.211), kind=kOutput, calls=%fused_computation.70 | convolution fusion | flops 604108800 | bytes 4798468 | tf_op jit(solution)/shard_map/dot_general | solution.py:215
  211.4 1.6 fusion.37
  (244 shorter events, 61.9 us)
Async XLA Ops:
  5.0 33.2 %collective-permute-start.2 = (bf16[368,1280]{1,0:T(8,128)(2,1)}, bf16[368,1280]{1,0:T(8,128)(2,1)}, u32[]{:S(2)}, u32[]{:S(2)}) collective-permute-start(bf16[368,1280]{1,0:T(8,128)(2,1)} %fusion.50), channel_id=1, source_target_pairs={{0,1},{1,0},{2,3},{3,2},{4,5},{5,4},{6,7},{7,6},{8,9},{9,8},{10,11... | collective-permute-start | bytes 2826248 | tf_op jit(solution)/shard_map/ppermute | solution.py:155
  5.5 32.8 %collective-permute-start.5 = (bf16[368,1280]{1,0:T(8,128)(2,1)}, bf16[368,1280]{1,0:T(8,128)(2,1)}, u32[]{:S(2)}, u32[]{:S(2)}) collective-permute-start(bf16[368,1280]{1,0:T(8,128)(2,1)} %fusion.50), channel_id=1, source_target_pairs={{0,2},{4,0},{8,4},{12,8},{14,12},{10,14},{6,10},{2,6},{1,3},{5,1},... | collective-permute-start | bytes 2826248 | tf_op jit(solution)/shard_map/ppermute | solution.py:80
  8.0 32.9 %collective-permute-start.1 = (bf16[368,1280]{1,0:T(8,128)(2,1)S(1)}, bf16[368,1280]{1,0:T(8,128)(2,1)}, u32[]{:S(2)}, u32[]{:S(2)}) collective-permute-start(bf16[368,1280]{1,0:T(8,128)(2,1)S(1)} %fusion.49), channel_id=1, source_target_pairs={{0,1},{1,0},{2,3},{3,2},{4,5},{5,4},{6,7},{7,6},{8,9},{9,8},{10,11... | collective-permute-start | bytes 2826248 | tf_op jit(solution)/shard_map/ppermute | solution.py:155
  8.3 31.5 %collective-permute-start.3 = (bf16[368,1280]{1,0:T(8,128)(2,1)S(1)}, bf16[368,1280]{1,0:T(8,128)(2,1)}, u32[]{:S(2)}, u32[]{:S(2)}) collective-permute-start(bf16[368,1280]{1,0:T(8,128)(2,1)S(1)} %fusion.49), channel_id=1, source_target_pairs={{0,4},{4,8},{8,12},{12,14},{14,10},{10,6},{6,2},{2,0},{1,5},{5,9},... | collective-permute-start | bytes 2826248 | tf_op jit(solution)/shard_map/ppermute | solution.py:80
  8.7 79.2 %collective-permute-start = (bf16[384,4096]{1,0:T(8,128)(2,1)}, bf16[384,4096]{1,0:T(8,128)(2,1)}, u32[]{:S(2)}, u32[]{:S(2)}) collective-permute-start(bf16[384,4096]{1,0:T(8,128)(2,1)} %param.11), channel_id=1, source_target_pairs={{0,16},{16,0},{1,17},{17,1},{2,18},{18,2},{3,19},{19,3},{4,20},{20... | collective-permute-start | bytes 9437192 | tf_op jit(solution)/shard_map/ppermute | solution.py:106
  38.2 23.5 %collective-permute-start.6 = (bf16[368,1280]{1,0:T(8,128)(2,1)}, bf16[368,1280]{1,0:T(8,128)(2,1)S(1)}, u32[]{:S(2)}, u32[]{:S(2)}) collective-permute-start(bf16[368,1280]{1,0:T(8,128)(2,1)} %collective-permute-done.5), channel_id=1, source_target_pairs={{0,1},{1,0},{2,3},{3,2},{4,5},{5,4},{6,7},{7,6},{8,9},{9,8},{10,11... | collective-permute-start | bytes 2826248 | tf_op jit(solution)/shard_map/ppermute | solution.py:155
  38.2 23.5 %collective-permute-start.9 = (bf16[368,1280]{1,0:T(8,128)(2,1)}, bf16[368,1280]{1,0:T(8,128)(2,1)S(1)}, u32[]{:S(2)}, u32[]{:S(2)}) collective-permute-start(bf16[368,1280]{1,0:T(8,128)(2,1)} %collective-permute-done.5), channel_id=1, source_target_pairs={{0,2},{4,0},{8,4},{12,8},{14,12},{10,14},{6,10},{2,6},{1,3},{5,1},... | collective-permute-start | bytes 2826248 | tf_op jit(solution)/shard_map/ppermute | solution.py:80
  39.8 25.1 %collective-permute-start.4 = (bf16[368,1280]{1,0:T(8,128)(2,1)}, bf16[368,1280]{1,0:T(8,128)(2,1)S(1)}, u32[]{:S(2)}, u32[]{:S(2)}) collective-permute-start(bf16[368,1280]{1,0:T(8,128)(2,1)} %collective-permute-done.3), channel_id=1, source_target_pairs={{0,1},{1,0},{2,3},{3,2},{4,5},{5,4},{6,7},{7,6},{8,9},{9,8},{10,11... | collective-permute-start | bytes 2826248 | tf_op jit(solution)/shard_map/ppermute | solution.py:155
  40.9 23.4 %collective-permute-start.7 = (bf16[368,1280]{1,0:T(8,128)(2,1)}, bf16[368,1280]{1,0:T(8,128)(2,1)S(1)}, u32[]{:S(2)}, u32[]{:S(2)}) collective-permute-start(bf16[368,1280]{1,0:T(8,128)(2,1)} %collective-permute-done.3), channel_id=1, source_target_pairs={{0,4},{4,8},{8,12},{12,14},{14,10},{10,6},{6,2},{2,0},{1,5},{5,9},... | collective-permute-start | bytes 2826248 | tf_op jit(solution)/shard_map/ppermute | solution.py:80
  61.7 23.3 %collective-permute-start.10 = (bf16[368,1280]{1,0:T(8,128)(2,1)S(1)}, bf16[368,1280]{1,0:T(8,128)(2,1)S(1)}, u32[]{:S(2)}, u32[]{:S(2)}) collective-permute-start(bf16[368,1280]{1,0:T(8,128)(2,1)S(1)} %collective-permute-done.9), channel_id=1, source_target_pairs={{0,1},{1,0},{2,3},{3,2},{4,5},{5,4},{6,7},{7,6},{8,9},{9,8},{10,11... | collective-permute-start | bytes 2826248 | tf_op jit(solution)/shard_map/ppermute | solution.py:155
  85.0 28.9 %collective-permute-start.14 = (bf16[368,1280]{1,0:T(8,128)(2,1)S(1)}, bf16[368,1280]{1,0:T(8,128)(2,1)S(1)}, u32[]{:S(2)}, u32[]{:S(2)}) collective-permute-start(bf16[368,1280]{1,0:T(8,128)(2,1)S(1)} %collective-permute-done.13), channel_id=1, source_target_pairs={{0,1},{1,0},{2,3},{3,2},{4,5},{5,4},{6,7},{7,6},{8,9},{9,8},{10,11... | collective-permute-start | bytes 2826248 | tf_op jit(solution)/shard_map/ppermute | solution.py:155
  86.7 23.5 %collective-permute-start.12 = (bf16[368,1280]{1,0:T(8,128)(2,1)S(1)}, bf16[368,1280]{1,0:T(8,128)(2,1)}, u32[]{:S(2)}, u32[]{:S(2)}) collective-permute-start(bf16[368,1280]{1,0:T(8,128)(2,1)S(1)} %collective-permute-done.11), channel_id=1, source_target_pairs={{0,1},{1,0},{2,3},{3,2},{4,5},{5,4},{6,7},{7,6},{8,9},{9,8},{10,11... | collective-permute-start | bytes 2826248 | tf_op jit(solution)/shard_map/ppermute | solution.py:155
  86.8 23.3 %collective-permute-start.15 = (bf16[368,1280]{1,0:T(8,128)(2,1)S(1)}, bf16[368,1280]{1,0:T(8,128)(2,1)S(1)}, u32[]{:S(2)}, u32[]{:S(2)}) collective-permute-start(bf16[368,1280]{1,0:T(8,128)(2,1)S(1)} %collective-permute-done.11), channel_id=1, source_target_pairs={{0,4},{4,8},{8,12},{12,14},{14,10},{10,6},{6,2},{2,0},{1,5},{5,9},... | collective-permute-start | bytes 2826248 | tf_op jit(solution)/shard_map/ppermute | solution.py:80
  108.3 25.4 %collective-permute-start.18 = (bf16[368,1280]{1,0:T(8,128)(2,1)S(1)}, bf16[368,1280]{1,0:T(8,128)(2,1)S(1)}, u32[]{:S(2)}, u32[]{:S(2)}) collective-permute-start(bf16[368,1280]{1,0:T(8,128)(2,1)S(1)} %collective-permute-done.17), channel_id=1, source_target_pairs={{0,1},{1,0},{2,3},{3,2},{4,5},{5,4},{6,7},{7,6},{8,9},{9,8},{10,11... | collective-permute-start | bytes 2826248 | tf_op jit(solution)/shard_map/ppermute | solution.py:155
  108.3 23.3 %collective-permute-start.21 = (bf16[368,1280]{1,0:T(8,128)(2,1)S(1)}, bf16[368,1280]{1,0:T(8,128)(2,1)S(1)}, u32[]{:S(2)}, u32[]{:S(2)}) collective-permute-start(bf16[368,1280]{1,0:T(8,128)(2,1)S(1)} %collective-permute-done.17), channel_id=1, source_target_pairs={{0,2},{4,0},{8,4},{12,8},{14,12},{10,14},{6,10},{2,6},{1,3},{5,1},... | collective-permute-start | bytes 2826248 | tf_op jit(solution)/shard_map/ppermute | solution.py:80
  110.1 25.2 %collective-permute-start.16 = (bf16[368,1280]{1,0:T(8,128)(2,1)S(1)}, bf16[368,1280]{1,0:T(8,128)(2,1)S(1)}, u32[]{:S(2)}, u32[]{:S(2)}) collective-permute-start(bf16[368,1280]{1,0:T(8,128)(2,1)S(1)} %collective-permute-done.15), channel_id=1, source_target_pairs={{0,1},{1,0},{2,3},{3,2},{4,5},{5,4},{6,7},{7,6},{8,9},{9,8},{10,11... | collective-permute-start | bytes 2826248 | tf_op jit(solution)/shard_map/ppermute | solution.py:155
  110.2 23.5 %collective-permute-start.19 = (bf16[368,1280]{1,0:T(8,128)(2,1)S(1)}, bf16[368,1280]{1,0:T(8,128)(2,1)S(1)}, u32[]{:S(2)}, u32[]{:S(2)}) collective-permute-start(bf16[368,1280]{1,0:T(8,128)(2,1)S(1)} %collective-permute-done.15), channel_id=1, source_target_pairs={{0,4},{4,8},{8,12},{12,14},{14,10},{10,6},{6,2},{2,0},{1,5},{5,9},... | collective-permute-start | bytes 2826248 | tf_op jit(solution)/shard_map/ppermute | solution.py:80
  131.6 27.0 %collective-permute-start.22 = (bf16[368,1280]{1,0:T(8,128)(2,1)S(1)}, bf16[368,1280]{1,0:T(8,128)(2,1)S(1)}, u32[]{:S(2)}, u32[]{:S(2)}) collective-permute-start(bf16[368,1280]{1,0:T(8,128)(2,1)S(1)} %collective-permute-done.21), channel_id=1, source_target_pairs={{0,1},{1,0},{2,3},{3,2},{4,5},{5,4},{6,7},{7,6},{8,9},{9,8},{10,11... | collective-permute-start | bytes 2826248 | tf_op jit(solution)/shard_map/ppermute | solution.py:155
  131.6 23.3 %collective-permute-start.25 = (bf16[368,1280]{1,0:T(8,128)(2,1)S(1)}, bf16[368,1280]{1,0:T(8,128)(2,1)S(1)}, u32[]{:S(2)}, u32[]{:S(2)}) collective-permute-start(bf16[368,1280]{1,0:T(8,128)(2,1)S(1)} %collective-permute-done.21), channel_id=1, source_target_pairs={{0,2},{4,0},{8,4},{12,8},{14,12},{10,14},{6,10},{2,6},{1,3},{5,1},... | collective-permute-start | bytes 2826248 | tf_op jit(solution)/shard_map/ppermute | solution.py:80
  133.7 23.4 %collective-permute-start.20 = (bf16[368,1280]{1,0:T(8,128)(2,1)S(1)}, bf16[368,1280]{1,0:T(8,128)(2,1)S(1)}, u32[]{:S(2)}, u32[]{:S(2)}) collective-permute-start(bf16[368,1280]{1,0:T(8,128)(2,1)S(1)} %collective-permute-done.19), channel_id=1, source_target_pairs={{0,1},{1,0},{2,3},{3,2},{4,5},{5,4},{6,7},{7,6},{8,9},{9,8},{10,11... | collective-permute-start | bytes 2826248 | tf_op jit(solution)/shard_map/ppermute | solution.py:155
  133.8 23.3 %collective-permute-start.23 = (bf16[368,1280]{1,0:T(8,128)(2,1)S(1)}, bf16[368,1280]{1,0:T(8,128)(2,1)S(1)}, u32[]{:S(2)}, u32[]{:S(2)}) collective-permute-start(bf16[368,1280]{1,0:T(8,128)(2,1)S(1)} %collective-permute-done.19), channel_id=1, source_target_pairs={{0,4},{4,8},{8,12},{12,14},{14,10},{10,6},{6,2},{2,0},{1,5},{5,9},... | collective-permute-start | bytes 2826248 | tf_op jit(solution)/shard_map/ppermute | solution.py:80
  154.9 23.3 %collective-permute-start.29 = (bf16[368,1280]{1,0:T(8,128)(2,1)S(1)}, bf16[368,1280]{1,0:T(8,128)(2,1)S(1)}, u32[]{:S(2)}, u32[]{:S(2)}) collective-permute-start(bf16[368,1280]{1,0:T(8,128)(2,1)S(1)} %collective-permute-done.25), channel_id=1, source_target_pairs={{0,2},{4,0},{8,4},{12,8},{14,12},{10,14},{6,10},{2,6},{1,3},{5,1},... | collective-permute-start | bytes 2826248 | tf_op jit(solution)/shard_map/ppermute | solution.py:80
  157.1 24.3 %collective-permute-start.24 = (bf16[368,1280]{1,0:T(8,128)(2,1)S(1)}, bf16[368,1280]{1,0:T(8,128)(2,1)S(1)}, u32[]{:S(2)}, u32[]{:S(2)}) collective-permute-start(bf16[368,1280]{1,0:T(8,128)(2,1)S(1)} %collective-permute-done.23), channel_id=1, source_target_pairs={{0,1},{1,0},{2,3},{3,2},{4,5},{5,4},{6,7},{7,6},{8,9},{9,8},{10,11... | collective-permute-start | bytes 2826248 | tf_op jit(solution)/shard_map/ppermute | solution.py:155
  157.2 23.3 %collective-permute-start.27 = (bf16[368,1280]{1,0:T(8,128)(2,1)S(1)}, bf16[368,1280]{1,0:T(8,128)(2,1)S(1)}, u32[]{:S(2)}, u32[]{:S(2)}) collective-permute-start(bf16[368,1280]{1,0:T(8,128)(2,1)S(1)} %collective-permute-done.23), channel_id=1, source_target_pairs={{0,4},{4,8},{8,12},{12,14},{14,10},{10,6},{6,2},{2,0},{1,5},{5,9},... | collective-permute-start | bytes 2826248 | tf_op jit(solution)/shard_map/ppermute | solution.py:80
  (36 other events, 302.7 us)

commit v13 on v12

--- a/solution.py
+++ b/solution.py
@@ -123,7 +123,14 @@
     down_rows = adapter_down.size // query_cols
     upq_rows = adapter_up_query.size // query_cols
     upkv_rows = adapter_up_keyvalue.size // query_cols
-    down_flat = adapter_down.reshape(down_rows, query_cols)
+    quarters = feature_cols // query_cols
+    map_rows = adapter_down.size // feature_cols
+    half_maps = map_rows // 2
+    down_flat = (
+        adapter_down.reshape(2, half_maps, quarters, query_cols)
+        .transpose(0, 2, 1, 3)
+        .reshape(down_rows, query_cols)
+    )
     upq_flat = adapter_up_query.reshape(upq_rows, query_cols)
     upkv_flat = adapter_up_keyvalue.reshape(upkv_rows, query_cols)
     dh, uh, vh = down_rows // 2, upq_rows // 2, upkv_rows // 2
@@ -196,9 +203,6 @@
                 jnp.bfloat16
             )
         )
-    down_selected = jnp.concatenate(
-        [per_half[0][:, :dh], per_half[1][:, :dh]], axis=1
-    ).reshape((prompt_count,) + adapter_down.shape[1:])
     up_query_selected = jnp.concatenate(
         [per_half[0][:, dh : dh + uh], per_half[1][:, dh : dh + uh]], axis=1
     ).reshape((prompt_count,) + adapter_up_query.shape[1:])
@@ -211,13 +215,21 @@
 
     lengths = packed_lengths[0]
     member, position, owner, slot_index = layout(lengths, row_number)
-    rank_size = down_selected.shape[2]
-    partial_value = lax.dot_general(
-        normed_part,
-        down_selected.reshape(prompt_count * 3 * rank_size, feature_cols),
-        (((1,), (1,)), ((), ())),
-        preferred_element_type=jnp.float32,
-    )
+    rank_size = adapter_down.shape[2]
+    halves_value = []
+    for h in range(2):
+        value = None
+        for q in range(quarters):
+            maps = per_half[h][:, q * half_maps : (q + 1) * half_maps]
+            term = lax.dot_general(
+                normed_part[:, q * query_cols : (q + 1) * query_cols],
+                maps.reshape(prompt_count * half_maps, query_cols),
+                (((1,), (1,)), ((), ())),
+                preferred_element_type=jnp.float32,
+            ).reshape(row_number, prompt_count, half_maps)
+            value = term if value is None else value + term
+        halves_value.append(value)
+    partial_value = jnp.concatenate(halves_value, axis=2)
     partial_value = partial_value.reshape(row_number, prompt_count, 3, rank_size)
     masked = jnp.sum(partial_value * member[:, :, None, None], axis=1).reshape(
         row_number, 3 * rank_size

time: 215 us -> 218 us (1.014)
  matrix products: 35.9 us -> 47 us
  waiting for transfers between devices: 97.7 us -> 93.6 us
  local copies, waits for them, and re-layouts: 22.4 us -> 19.2 us
  other arithmetic: 16.3 us -> 14.1 us
    dot_general x1 -> x8, matrix products: 3.7 us -> 12.4 us  [shards(): lax.dot_general(normed_part[:, q * query_cols:(q + 1) * query_cols], maps...]
    ppermute x14, waiting for transfers between devices: 97.3 us -> 93.2 us  [ring_gather(): current = lax.ppermute(current, 'chip', pairs)]
    dot_general x1 -> x0, local copies, waits for them, and re-layouts: 2.5 us -> none  [shards(): lax.dot_general(normed_part, down_selected.reshape(prompt_count * 3 * ran...]
    dot_general x32, matrix products: 23.8 us -> 26.3 us  [shards(): part = jnp.dot(lhs, p[:half_rows], preferred_element_type=jnp.float32)]
  transfers between devices with their start and end apart: 32 -> 32, of which waited for: 13 -> 10; matrix products, arithmetic and copies ran while one was open for 21% -> 23% of each run, Pallas kernels for 0% -> 0%
where the time goes in v13:
time: 218 us; the launch traced here: 217 us
  waiting for transfers between devices  93.6 us (43%)
  matrix products  47 us (22%)
  between operations  23.1 us (11%)
  starting transfers between devices  19.4 us (9%)
  local copies, waits for them, and re-layouts  19.2 us (9%)
  other arithmetic  14.1 us (6%)
    ppermute x14, waiting for transfers between devices, ring_gather(): current = lax.ppermute(current, 'chip', pairs)  93.2 us
    dot_general x32, matrix products, shards(): part = jnp.dot(lhs, p[:half_rows], preferred_element_type=jnp.float32)  26.3 us
    ppermute x14, starting transfers between devices, ring_gather(): current = lax.ppermute(current, 'chip', pairs)  15.4 us
    dot_general x8, matrix products, shards(): lax.dot_general(normed_part[:, q * query_cols:(q + 1) * query_cols], maps...  12.4 us
    another operation x30, local copies, waits for them, and re-layouts, shards(): jnp.stack([p[half_rows:, :query_cols] for p in both])  7.06 us
    dot_general x2, matrix products, shards(): jnp.einsum('pk,krc->prc', one_hot, stacked, preferred_element_type=jnp.fl...  4.49 us
  transfers between devices with their start and end apart: 32, of which 10 were waited for; matrix products, arithmetic and copies ran while one was open for 23% of the time, Pallas kernels for 0%

profile of v13, /device:TPU:0, one launch (start us, length us, event | category | flops | bytes accessed | tf_op | source)
XLA Modules:
  0.0 216.5 jit_solution(3879747524247707448)
XLA Ops:
  5.8 2.5 %collective-permute-start.5 = (bf16[368,1280]{1,0:T(8,128)(2,1)}, bf16[368,1280]{1,0:T(8,128)(2,1)}, u32[]{:S(2)}, u32[]{:S(2)}) collective-permute-start(bf16[368,1280]{1,0:T(8,128)(2,1)} %fusion.41), channel_id=1, source_target_pairs={{0,2},{4,0},{8,4},{12,8},{14,12},{10,14},{6,10},{2,6},{1,3},{5,1},... | collective-permute-start | bytes 2826248 | tf_op jit(solution)/shard_map/ppermute | solution.py:80
  9.0 1.7 collective-permute-start
  37.3 1.5 collective-permute-start.9
  43.5 17.3 %collective-permute-done.9 = bf16[368,1280]{1,0:T(8,128)(2,1)S(1)} collective-permute-done((bf16[368,1280]{1,0:T(8,128)(2,1)}, bf16[368,1280]{1,0:T(8,128)(2,1)S(1)}, u32[]{:S(2)}, u32[]{:S(2)}) %collective-permute-start.9) | collective-permute-done | bytes 942112 | tf_op jit(solution)/shard_map/ppermute | solution.py:80
  60.8 1.5 collective-permute-start.13
  64.1 20.0 %collective-permute-done.13 = bf16[368,1280]{1,0:T(8,128)(2,1)} collective-permute-done((bf16[368,1280]{1,0:T(8,128)(2,1)S(1)}, bf16[368,1280]{1,0:T(8,128)(2,1)}, u32[]{:S(2)}, u32[]{:S(2)}) %collective-permute-start.13) | collective-permute-done | bytes 942112 | tf_op jit(solution)/shard_map/ppermute | solution.py:80
  84.2 1.5 collective-permute-start.17
  87.8 3.3 %broadcast_select_fusion.1 = (bf16[384,4096]{1,0:T(8,128)(2,1)S(1)}, bf16[384,4096]{1,0:T(8,128)(2,1)S(1)}) fusion(bf16[384,4096]{1,0:T(8,128)(2,1)} %param.11, bf16[384,4096]{1,0:T(8,128)(2,1)} %collective-permute-done, pred[]{:T(512)S(6)} %eq.68), kind=kLoop, calls=%fused_computation.17 | loop fusion | flops 3145728 | bytes 12582913 | tf_op jit(solution)/shard_map/select_n | solution.py:107
  92.6 1.8 fusion.2
  95.2 2.0 fusion.90
  116.5 15.0 %collective-permute-done.21 = bf16[368,1280]{1,0:T(8,128)(2,1)S(1)} collective-permute-done((bf16[368,1280]{1,0:T(8,128)(2,1)S(1)}, bf16[368,1280]{1,0:T(8,128)(2,1)S(1)}, u32[]{:S(2)}, u32[]{:S(2)}) %collective-permute-start.21) | collective-permute-done | bytes 942112 | tf_op jit(solution)/shard_map/ppermute | solution.py:80
  135.8 18.9 %collective-permute-done.25 = bf16[368,1280]{1,0:T(8,128)(2,1)S(1)} collective-permute-done((bf16[368,1280]{1,0:T(8,128)(2,1)S(1)}, bf16[368,1280]{1,0:T(8,128)(2,1)S(1)}, u32[]{:S(2)}, u32[]{:S(2)}) %collective-permute-start.25) | collective-permute-done | bytes 942112 | tf_op jit(solution)/shard_map/ppermute | solution.py:80
  159.0 19.0 %collective-permute-done.29 = bf16[368,1280]{1,0:T(8,128)(2,1)S(1)} collective-permute-done((bf16[368,1280]{1,0:T(8,128)(2,1)S(1)}, bf16[368,1280]{1,0:T(8,128)(2,1)S(1)}, u32[]{:S(2)}, u32[]{:S(2)}) %collective-permute-start.29) | collective-permute-done | bytes 942112 | tf_op jit(solution)/shard_map/ppermute | solution.py:80
  178.0 1.7 collective-permute-done.27
  181.2 1.8 fusion.10
  183.1 2.2 %fusion.28 = bf16[4,112,1024]{2,0,1:T(4,128)(2,1)S(1)} fusion(bf16[16,112,1024]{2,1,0:T(8,128)(2,1)S(1)} %bitcast.295, s32[4]{0:T(128)S(1)} %get-tuple-element.11), kind=kOutput, calls=%fused_computation.58 | convolution fusion | flops 15138880 | bytes 4587536 | tf_op jit(solution)/shard_map/pk,krc->prc/dot_general | solution.py:202
  187.5 2.2 %fusion.31 = bf16[4,112,1024]{2,0,1:T(4,128)(2,1)S(1)} fusion(bf16[16,112,1024]{2,1,0:T(8,128)(2,1)S(1)} %bitcast.296, s32[4]{0:T(128)S(1)} %fusion.212), kind=kOutput, calls=%fused_computation.59 | convolution fusion | flops 15138880 | bytes 4587536 | tf_op jit(solution)/shard_map/pk,krc->prc/dot_general | solution.py:202
  191.1 1.6 fusion.93
  192.6 1.5 fusion.92
  194.2 1.5 convolution_add_fusion.19
  195.8 1.5 convolution_add_fusion.16
  197.3 1.7 convolution_add_fusion.18
  205.6 1.6 convolution_add_fusion
  213.7 1.6 fusion.34
  (255 shorter events, 68.3 us)
Async XLA Ops:
  5.3 32.0 %collective-permute-start.2 = (bf16[368,1280]{1,0:T(8,128)(2,1)}, bf16[368,1280]{1,0:T(8,128)(2,1)}, u32[]{:S(2)}, u32[]{:S(2)}) collective-permute-start(bf16[368,1280]{1,0:T(8,128)(2,1)} %fusion.41), channel_id=1, source_target_pairs={{0,1},{1,0},{2,3},{3,2},{4,5},{5,4},{6,7},{7,6},{8,9},{9,8},{10,11... | collective-permute-start | bytes 2826248 | tf_op jit(solution)/shard_map/ppermute | solution.py:162
  5.8 31.5 %collective-permute-start.5 = (bf16[368,1280]{1,0:T(8,128)(2,1)}, bf16[368,1280]{1,0:T(8,128)(2,1)}, u32[]{:S(2)}, u32[]{:S(2)}) collective-permute-start(bf16[368,1280]{1,0:T(8,128)(2,1)} %fusion.41), channel_id=1, source_target_pairs={{0,2},{4,0},{8,4},{12,8},{14,12},{10,14},{6,10},{2,6},{1,3},{5,1},... | collective-permute-start | bytes 2826248 | tf_op jit(solution)/shard_map/ppermute | solution.py:80
  8.3 31.6 %collective-permute-start.1 = (bf16[368,1280]{1,0:T(8,128)(2,1)S(1)}, bf16[368,1280]{1,0:T(8,128)(2,1)}, u32[]{:S(2)}, u32[]{:S(2)}) collective-permute-start(bf16[368,1280]{1,0:T(8,128)(2,1)S(1)} %fusion.40), channel_id=1, source_target_pairs={{0,1},{1,0},{2,3},{3,2},{4,5},{5,4},{6,7},{7,6},{8,9},{9,8},{10,11... | collective-permute-start | bytes 2826248 | tf_op jit(solution)/shard_map/ppermute | solution.py:162
  8.6 30.2 %collective-permute-start.3 = (bf16[368,1280]{1,0:T(8,128)(2,1)S(1)}, bf16[368,1280]{1,0:T(8,128)(2,1)}, u32[]{:S(2)}, u32[]{:S(2)}) collective-permute-start(bf16[368,1280]{1,0:T(8,128)(2,1)S(1)} %fusion.40), channel_id=1, source_target_pairs={{0,4},{4,8},{8,12},{12,14},{14,10},{10,6},{6,2},{2,0},{1,5},{5,9},... | collective-permute-start | bytes 2826248 | tf_op jit(solution)/shard_map/ppermute | solution.py:80
  9.0 78.8 %collective-permute-start = (bf16[384,4096]{1,0:T(8,128)(2,1)}, bf16[384,4096]{1,0:T(8,128)(2,1)}, u32[]{:S(2)}, u32[]{:S(2)}) collective-permute-start(bf16[384,4096]{1,0:T(8,128)(2,1)} %param.11), channel_id=1, source_target_pairs={{0,16},{16,0},{1,17},{17,1},{2,18},{18,2},{3,19},{19,3},{4,20},{20... | collective-permute-start | bytes 9437192 | tf_op jit(solution)/shard_map/ppermute | solution.py:106
  37.3 23.5 %collective-permute-start.6 = (bf16[368,1280]{1,0:T(8,128)(2,1)}, bf16[368,1280]{1,0:T(8,128)(2,1)S(1)}, u32[]{:S(2)}, u32[]{:S(2)}) collective-permute-start(bf16[368,1280]{1,0:T(8,128)(2,1)} %collective-permute-done.5), channel_id=1, source_target_pairs={{0,1},{1,0},{2,3},{3,2},{4,5},{5,4},{6,7},{7,6},{8,9},{9,8},{10,11... | collective-permute-start | bytes 2826248 | tf_op jit(solution)/shard_map/ppermute | solution.py:162
  37.3 23.5 %collective-permute-start.9 = (bf16[368,1280]{1,0:T(8,128)(2,1)}, bf16[368,1280]{1,0:T(8,128)(2,1)S(1)}, u32[]{:S(2)}, u32[]{:S(2)}) collective-permute-start(bf16[368,1280]{1,0:T(8,128)(2,1)} %collective-permute-done.5), channel_id=1, source_target_pairs={{0,2},{4,0},{8,4},{12,8},{14,12},{10,14},{6,10},{2,6},{1,3},{5,1},... | collective-permute-start | bytes 2826248 | tf_op jit(solution)/shard_map/ppermute | solution.py:80
  38.8 25.1 %collective-permute-start.4 = (bf16[368,1280]{1,0:T(8,128)(2,1)}, bf16[368,1280]{1,0:T(8,128)(2,1)S(1)}, u32[]{:S(2)}, u32[]{:S(2)}) collective-permute-start(bf16[368,1280]{1,0:T(8,128)(2,1)} %collective-permute-done.3), channel_id=1, source_target_pairs={{0,1},{1,0},{2,3},{3,2},{4,5},{5,4},{6,7},{7,6},{8,9},{9,8},{10,11... | collective-permute-start | bytes 2826248 | tf_op jit(solution)/shard_map/ppermute | solution.py:162
  40.0 23.4 %collective-permute-start.7 = (bf16[368,1280]{1,0:T(8,128)(2,1)}, bf16[368,1280]{1,0:T(8,128)(2,1)S(1)}, u32[]{:S(2)}, u32[]{:S(2)}) collective-permute-start(bf16[368,1280]{1,0:T(8,128)(2,1)} %collective-permute-done.3), channel_id=1, source_target_pairs={{0,4},{4,8},{8,12},{12,14},{14,10},{10,6},{6,2},{2,0},{1,5},{5,9},... | collective-permute-start | bytes 2826248 | tf_op jit(solution)/shard_map/ppermute | solution.py:80
  60.8 23.4 %collective-permute-start.10 = (bf16[368,1280]{1,0:T(8,128)(2,1)S(1)}, bf16[368,1280]{1,0:T(8,128)(2,1)S(1)}, u32[]{:S(2)}, u32[]{:S(2)}) collective-permute-start(bf16[368,1280]{1,0:T(8,128)(2,1)S(1)} %collective-permute-done.9), channel_id=1, source_target_pairs={{0,1},{1,0},{2,3},{3,2},{4,5},{5,4},{6,7},{7,6},{8,9},{9,8},{10,11... | collective-permute-start | bytes 2826248 | tf_op jit(solution)/shard_map/ppermute | solution.py:162
  60.8 23.4 %collective-permute-start.13 = (bf16[368,1280]{1,0:T(8,128)(2,1)S(1)}, bf16[368,1280]{1,0:T(8,128)(2,1)}, u32[]{:S(2)}, u32[]{:S(2)}) collective-permute-start(bf16[368,1280]{1,0:T(8,128)(2,1)S(1)} %collective-permute-done.9), channel_id=1, source_target_pairs={{0,2},{4,0},{8,4},{12,8},{14,12},{10,14},{6,10},{2,6},{1,3},{5,1},... | collective-permute-start | bytes 2826248 | tf_op jit(solution)/shard_map/ppermute | solution.py:80
  84.2 25.6 %collective-permute-start.14 = (bf16[368,1280]{1,0:T(8,128)(2,1)}, bf16[368,1280]{1,0:T(8,128)(2,1)}, u32[]{:S(2)}, u32[]{:S(2)}) collective-permute-start(bf16[368,1280]{1,0:T(8,128)(2,1)} %collective-permute-done.13), channel_id=1, source_target_pairs={{0,1},{1,0},{2,3},{3,2},{4,5},{5,4},{6,7},{7,6},{8,9},{9,8},{10,11... | collective-permute-start | bytes 2826248 | tf_op jit(solution)/shard_map/ppermute | solution.py:162
  84.2 23.9 %collective-permute-start.17 = (bf16[368,1280]{1,0:T(8,128)(2,1)}, bf16[368,1280]{1,0:T(8,128)(2,1)S(1)}, u32[]{:S(2)}, u32[]{:S(2)}) collective-permute-start(bf16[368,1280]{1,0:T(8,128)(2,1)} %collective-permute-done.13), channel_id=1, source_target_pairs={{0,2},{4,0},{8,4},{12,8},{14,12},{10,14},{6,10},{2,6},{1,3},{5,1},... | collective-permute-start | bytes 2826248 | tf_op jit(solution)/shard_map/ppermute | solution.py:80
  85.8 25.7 %collective-permute-start.12 = (bf16[368,1280]{1,0:T(8,128)(2,1)S(1)}, bf16[368,1280]{1,0:T(8,128)(2,1)}, u32[]{:S(2)}, u32[]{:S(2)}) collective-permute-start(bf16[368,1280]{1,0:T(8,128)(2,1)S(1)} %collective-permute-done.11), channel_id=1, source_target_pairs={{0,1},{1,0},{2,3},{3,2},{4,5},{5,4},{6,7},{7,6},{8,9},{9,8},{10,11... | collective-permute-start | bytes 2826248 | tf_op jit(solution)/shard_map/ppermute | solution.py:162
  86.0 23.7 %collective-permute-start.15 = (bf16[368,1280]{1,0:T(8,128)(2,1)S(1)}, bf16[368,1280]{1,0:T(8,128)(2,1)S(1)}, u32[]{:S(2)}, u32[]{:S(2)}) collective-permute-start(bf16[368,1280]{1,0:T(8,128)(2,1)S(1)} %collective-permute-done.11), channel_id=1, source_target_pairs={{0,4},{4,8},{8,12},{12,14},{14,10},{10,6},{6,2},{2,0},{1,5},{5,9},... | collective-permute-start | bytes 2826248 | tf_op jit(solution)/shard_map/ppermute | solution.py:80
  108.1 24.8 %collective-permute-start.18 = (bf16[368,1280]{1,0:T(8,128)(2,1)S(1)}, bf16[368,1280]{1,0:T(8,128)(2,1)S(1)}, u32[]{:S(2)}, u32[]{:S(2)}) collective-permute-start(bf16[368,1280]{1,0:T(8,128)(2,1)S(1)} %collective-permute-done.17), channel_id=1, source_target_pairs={{0,1},{1,0},{2,3},{3,2},{4,5},{5,4},{6,7},{7,6},{8,9},{9,8},{10,11... | collective-permute-start | bytes 2826248 | tf_op jit(solution)/shard_map/ppermute | solution.py:162
  109.8 23.3 %collective-permute-start.19 = (bf16[368,1280]{1,0:T(8,128)(2,1)S(1)}, bf16[368,1280]{1,0:T(8,128)(2,1)S(1)}, u32[]{:S(2)}, u32[]{:S(2)}) collective-permute-start(bf16[368,1280]{1,0:T(8,128)(2,1)S(1)} %collective-permute-done.15), channel_id=1, source_target_pairs={{0,4},{4,8},{8,12},{12,14},{14,10},{10,6},{6,2},{2,0},{1,5},{5,9},... | collective-permute-start | bytes 2826248 | tf_op jit(solution)/shard_map/ppermute | solution.py:80
  131.4 25.0 %collective-permute-start.22 = (bf16[368,1280]{1,0:T(8,128)(2,1)S(1)}, bf16[368,1280]{1,0:T(8,128)(2,1)S(1)}, u32[]{:S(2)}, u32[]{:S(2)}) collective-permute-start(bf16[368,1280]{1,0:T(8,128)(2,1)S(1)} %collective-permute-done.21), channel_id=1, source_target_pairs={{0,1},{1,0},{2,3},{3,2},{4,5},{5,4},{6,7},{7,6},{8,9},{9,8},{10,11... | collective-permute-start | bytes 2826248 | tf_op jit(solution)/shard_map/ppermute | solution.py:162
  131.4 23.3 %collective-permute-start.25 = (bf16[368,1280]{1,0:T(8,128)(2,1)S(1)}, bf16[368,1280]{1,0:T(8,128)(2,1)S(1)}, u32[]{:S(2)}, u32[]{:S(2)}) collective-permute-start(bf16[368,1280]{1,0:T(8,128)(2,1)S(1)} %collective-permute-done.21), channel_id=1, source_target_pairs={{0,2},{4,0},{8,4},{12,8},{14,12},{10,14},{6,10},{2,6},{1,3},{5,1},... | collective-permute-start | bytes 2826248 | tf_op jit(solution)/shard_map/ppermute | solution.py:80
  133.1 24.0 %collective-permute-start.20 = (bf16[368,1280]{1,0:T(8,128)(2,1)S(1)}, bf16[368,1280]{1,0:T(8,128)(2,1)S(1)}, u32[]{:S(2)}, u32[]{:S(2)}) collective-permute-start(bf16[368,1280]{1,0:T(8,128)(2,1)S(1)} %collective-permute-done.19), channel_id=1, source_target_pairs={{0,1},{1,0},{2,3},{3,2},{4,5},{5,4},{6,7},{7,6},{8,9},{9,8},{10,11... | collective-permute-start | bytes 2826248 | tf_op jit(solution)/shard_map/ppermute | solution.py:162
  154.7 25.0 %collective-permute-start.26 = (bf16[368,1280]{1,0:T(8,128)(2,1)S(1)}, bf16[368,1280]{1,0:T(8,128)(2,1)S(1)}, u32[]{:S(2)}, u32[]{:S(2)}) collective-permute-start(bf16[368,1280]{1,0:T(8,128)(2,1)S(1)} %collective-permute-done.25), channel_id=1, source_target_pairs={{0,1},{1,0},{2,3},{3,2},{4,5},{5,4},{6,7},{7,6},{8,9},{9,8},{10,11... | collective-permute-start | bytes 2826248 | tf_op jit(solution)/shard_map/ppermute | solution.py:162
  154.7 23.3 %collective-permute-start.29 = (bf16[368,1280]{1,0:T(8,128)(2,1)S(1)}, bf16[368,1280]{1,0:T(8,128)(2,1)S(1)}, u32[]{:S(2)}, u32[]{:S(2)}) collective-permute-start(bf16[368,1280]{1,0:T(8,128)(2,1)S(1)} %collective-permute-done.25), channel_id=1, source_target_pairs={{0,2},{4,0},{8,4},{12,8},{14,12},{10,14},{6,10},{2,6},{1,3},{5,1},... | collective-permute-start | bytes 2826248 | tf_op jit(solution)/shard_map/ppermute | solution.py:80
  156.4 23.4 %collective-permute-start.24 = (bf16[368,1280]{1,0:T(8,128)(2,1)S(1)}, bf16[368,1280]{1,0:T(8,128)(2,1)S(1)}, u32[]{:S(2)}, u32[]{:S(2)}) collective-permute-start(bf16[368,1280]{1,0:T(8,128)(2,1)S(1)} %collective-permute-done.23), channel_id=1, source_target_pairs={{0,1},{1,0},{2,3},{3,2},{4,5},{5,4},{6,7},{7,6},{8,9},{9,8},{10,11... | collective-permute-start | bytes 2826248 | tf_op jit(solution)/shard_map/ppermute | solution.py:162
  156.4 23.3 %collective-permute-start.27 = (bf16[368,1280]{1,0:T(8,128)(2,1)S(1)}, bf16[368,1280]{1,0:T(8,128)(2,1)S(1)}, u32[]{:S(2)}, u32[]{:S(2)}) collective-permute-start(bf16[368,1280]{1,0:T(8,128)(2,1)S(1)} %collective-permute-done.23), channel_id=1, source_target_pairs={{0,4},{4,8},{8,12},{12,14},{14,10},{10,6},{6,2},{2,0},{1,5},{5,9},... | collective-permute-start | bytes 2826248 | tf_op jit(solution)/shard_map/ppermute | solution.py:80
  (38 other events, 353.4 us)

commit v14 on v3

--- a/solution.py
+++ b/solution.py
@@ -169,14 +169,13 @@
         for h, direction in enumerate(directions):
             src_chip = order_table[(pos - s * direction) % n_chip]
             both = swap_core(recv[h][s])
-            adapter_steps[h].append(jnp.stack([p[half_rows:, :query_cols] for p in both]))
+            adapter_steps[h].append([p[half_rows:, :query_cols] for p in both])
             for slot, p in enumerate(both):
                 src_core = me_core if slot == 0 else n_lo - 1 - me_core
                 start = (src_chip * n_lo + src_core) * weight_rows + h * half_rows
                 lhs = lax.dynamic_slice_in_dim(normed, start, half_rows, 1)
                 part = jnp.dot(lhs, p[:half_rows], preferred_element_type=jnp.float32)
                 total = part if total is None else total + part
-    adapter_pieces = [jnp.stack(a) for a in adapter_steps]
 
     picked = prompt_adapter[0]
     prompt_count = picked.shape[0]
@@ -186,7 +185,14 @@
     per_half = []
     for h, direction in enumerate(directions):
         a_step = ((pos - inverse_table[a_chip]) * direction) % n_chip
-        per_half.append(adapter_pieces[h][a_step, a_slot])
+        picked_piece = a_step * n_lo + a_slot
+        chosen = None
+        for s in range(n_chip):
+            for slot in range(n_lo):
+                weight = (picked_piece == s * n_lo + slot).astype(jnp.float32)[:, None, None]
+                term = weight * adapter_steps[h][s][slot].astype(jnp.float32)[None]
+                chosen = term if chosen is None else chosen + term
+        per_half.append(chosen.astype(jnp.bfloat16))
     down_selected = jnp.concatenate(
         [per_half[0][:, :dh], per_half[1][:, :dh]], axis=1
     ).reshape((prompt_count,) + adapter_down.shape[1:])

time: 224 us -> 212 us (0.946)
  local copies, waits for them, and re-layouts: 30.2 us -> 17.9 us
  waiting for transfers between devices: 92.8 us -> 89.7 us
    convert_element_type x0 -> x37, other arithmetic: none -> 12.9 us  [the longest x31 6.85 us: shards(): term = weight * adapter_steps[h][s][slot].astype(jnp.float32)[None]]
    unnamed x14 -> x0, other arithmetic: 9.09 us -> none
    gather x2 -> x0, local copies, waits for them, and re-layouts: 6.22 us -> none  [shards(): per_half.append(adapter_pieces[h][a_step, a_slot])]
    another operation x31 -> x1, local copies, waits for them, and re-layouts: 6.12 us -> 0.01 us  [the longest x30 6.11 us: shards(): jnp.stack([p[half_rows:, :query_cols] for p in both])]
    ppermute x14, waiting for transfers between devices: 92.5 us -> 89.1 us  [ring_gather(): current = lax.ppermute(current, 'chip', pairs)]
    unnamed x43 -> x55, local copies, waits for them, and re-layouts: 5.04 us -> 7.12 us
  transfers between devices with their start and end apart: 32 -> 32, of which waited for: 12 -> 10; matrix products, arithmetic and copies ran while one was open for 25% -> 23% of each run, Pallas kernels for 0% -> 0%
where the time goes in v14:
time: 212 us; the launch traced here: 211 us
  waiting for transfers between devices  89.7 us (42%)
  matrix products  32.4 us (15%)
  other arithmetic  28.1 us (13%)
  between operations  22.7 us (11%)
  starting transfers between devices  19.9 us (9%)
  local copies, waits for them, and re-layouts  17.9 us (8%)
    ppermute x14, waiting for transfers between devices, ring_gather(): current = lax.ppermute(current, 'chip', pairs)  89.1 us
    dot_general x32, matrix products, shards(): part = jnp.dot(lhs, p[:half_rows], preferred_element_type=jnp.float32)  24.8 us
    ppermute x14, starting transfers between devices, ring_gather(): current = lax.ppermute(current, 'chip', pairs)  15.3 us
    unnamed x55, local copies, waits for them, and re-layouts  7.12 us
    convert_element_type x31, other arithmetic, shards(): term = weight * adapter_steps[h][s][slot].astype(jnp.float32)[None]  6.85 us
    convert_element_type x2, other arithmetic, shards(): per_half.append(chosen.astype(jnp.bfloat16))  4.71 us
  transfers between devices with their start and end apart: 32, of which 10 were waited for; matrix products, arithmetic and copies ran while one was open for 23% of the time, Pallas kernels for 0%

profile of v14, /device:TPU:0, one launch (start us, length us, event | category | flops | bytes accessed | tf_op | source)
XLA Modules:
  0.0 210.7 jit_solution(5894577756110294299)
XLA Ops:
  5.1 3.0 %collective-permute-start.3 = (bf16[368,1280]{1,0:T(8,128)(2,1)}, bf16[368,1280]{1,0:T(8,128)(2,1)}, u32[]{:S(2)}, u32[]{:S(2)}) collective-permute-start(bf16[368,1280]{1,0:T(8,128)(2,1)} %fusion.39), channel_id=1, source_target_pairs={{0,4},{4,8},{8,12},{12,14},{14,10},{10,6},{6,2},{2,0},{1,5},{5,9},... | collective-permute-start | bytes 2826248 | tf_op jit(solution)/shard_map/ppermute | solution.py:80
  9.6 1.7 collective-permute-start
  38.3 1.6 collective-permute-start.7
  44.9 16.4 %collective-permute-done.7 = bf16[368,1280]{1,0:T(8,128)(2,1)S(1)} collective-permute-done((bf16[368,1280]{1,0:T(8,128)(2,1)}, bf16[368,1280]{1,0:T(8,128)(2,1)S(1)}, u32[]{:S(2)}, u32[]{:S(2)}) %collective-permute-start.7) | collective-permute-done | bytes 942112 | tf_op jit(solution)/shard_map/ppermute | solution.py:80
  61.3 1.6 collective-permute-start.11
  64.2 19.2 %collective-permute-done.11 = bf16[368,1280]{1,0:T(8,128)(2,1)S(1)} collective-permute-done((bf16[368,1280]{1,0:T(8,128)(2,1)S(1)}, bf16[368,1280]{1,0:T(8,128)(2,1)S(1)}, u32[]{:S(2)}, u32[]{:S(2)}) %collective-permute-start.11) | collective-permute-done | bytes 942112 | tf_op jit(solution)/shard_map/ppermute | solution.py:80
  83.3 1.6 collective-permute-start.15
  86.6 3.3 %broadcast_select_fusion.1 = (bf16[384,4096]{1,0:T(8,128)(2,1)S(1)}, bf16[384,4096]{1,0:T(8,128)(2,1)S(1)}) fusion(bf16[384,4096]{1,0:T(8,128)(2,1)} %param.11, bf16[384,4096]{1,0:T(8,128)(2,1)} %collective-permute-done, pred[]{:T(512)S(6)} %eq.266), kind=kLoop, calls=%fused_computation.16 | loop fusion | flops 3145728 | bytes 12582913 | tf_op jit(solution)/shard_map/select_n | solution.py:107
  91.4 1.8 fusion.2
  94.1 2.0 fusion.89
  106.1 1.6 collective-permute-start.19
  113.5 1.6 fusion.15
  115.1 14.1 %collective-permute-done.19 = bf16[368,1280]{1,0:T(8,128)(2,1)S(1)} collective-permute-done((bf16[368,1280]{1,0:T(8,128)(2,1)S(1)}, bf16[368,1280]{1,0:T(8,128)(2,1)S(1)}, u32[]{:S(2)}, u32[]{:S(2)}) %collective-permute-start.19) | collective-permute-done | bytes 942112 | tf_op jit(solution)/shard_map/ppermute | solution.py:80
  129.2 1.6 collective-permute-start.23
  133.6 17.8 %collective-permute-done.23 = bf16[368,1280]{1,0:T(8,128)(2,1)S(1)} collective-permute-done((bf16[368,1280]{1,0:T(8,128)(2,1)S(1)}, bf16[368,1280]{1,0:T(8,128)(2,1)S(1)}, u32[]{:S(2)}, u32[]{:S(2)}) %collective-permute-start.23) | collective-permute-done | bytes 942112 | tf_op jit(solution)/shard_map/ppermute | solution.py:80
  151.4 1.6 collective-permute-start.27
  156.6 16.1 %collective-permute-done.27 = bf16[368,1280]{1,0:T(8,128)(2,1)S(1)} collective-permute-done((bf16[368,1280]{1,0:T(8,128)(2,1)S(1)}, bf16[368,1280]{1,0:T(8,128)(2,1)S(1)}, u32[]{:S(2)}, u32[]{:S(2)}) %collective-permute-start.27) | collective-permute-done | bytes 942112 | tf_op jit(solution)/shard_map/ppermute | solution.py:80
  172.8 3.5 %collective-permute-done.29 = bf16[368,1280]{1,0:T(8,128)(2,1)S(1)} collective-permute-done((bf16[368,1280]{1,0:T(8,128)(2,1)S(1)}, bf16[368,1280]{1,0:T(8,128)(2,1)S(1)}, u32[]{:S(2)}, u32[]{:S(2)}) %collective-permute-start.29) | collective-permute-done | bytes 942112 | tf_op jit(solution)/shard_map/ppermute | solution.py:80
  177.7 1.7 fusion.9
  180.4 2.4 %add_convert_fusion.1 = bf16[4,112,1024]{2,1,0:T(8,128)(2,1)S(1)} fusion(f32[112,1024]{1,0:T(8,128)S(1)} %slice_convert_fusion.15, f32[4]{0:T(128)S(1)} %get-tuple-element.64, f32[112,1024]{1,0:T(8,128)S(1)} %slice_convert_fusion.16, f32[4]{0:T(128)S(1)} %get-tuple-element.51, f32[112,1024]{1,0:T(8,128)S(1)} %slice_convert_fusion.17, ...), kind=kLoop, calls=%fused_computation.51 | loop fusion | flops 14680064 | bytes 8257792 | tf_op jit(solution)/shard_map/convert_element_type | solution.py:195
  184.8 2.4 %add_convert_fusion = bf16[4,112,1024]{2,1,0:T(8,128)(2,1)S(1)} fusion(f32[112,1024]{1,0:T(8,128)S(1)} %slice_convert_fusion, f32[4]{0:T(128)S(1)} %get-tuple-element.79, f32[112,1024]{1,0:T(8,128)S(1)} %slice_convert_fusion.1, f32[4]{0:T(128)S(1)} %get-tuple-element.66, f32[112,1024]{1,0:T(8,128)S(1)} %slice_convert_fusion.2, f32[4]{0:T(128)S(1)} %get-tuple-element.67, ...), kind=kLoop, calls=%fused_computation.50 | loop fusion | flops 14680064 | bytes 8257792 | tf_op jit(solution)/shard_map/convert_element_type | solution.py:195
  191.2 2.5 %dot_general.148 = bf16[4,3,16,4096]{3,2,1,0:T(8,128)(2,1)} reshape(bf16[4,192,1024]{2,1,0:T(8,128)(2,1)S(1)} %pad_maximum_fusion.1) | data formatting | bytes 3145728 | tf_op jit(solution)/shard_map/dot_general | solution.py:212
  193.7 3.7 %fusion.35 = f32[384,3,16]{0,2,1:T(8,128)S(1)} fusion(bf16[4,3,16,4096]{3,2,1,0:T(8,128)(2,1)} %dot_general.148, bf16[384,8192]{1,0:T(8,128)(2,1)} %copy-done.1, s32[]{:T(128)S(6)} %select_n.529, f32[384,4]{0,1:T(4,128)S(1)} %fusion.182), kind=kOutput, calls=%fused_computation.66 | convolution fusion | flops 604108800 | bytes 4798468 | tf_op jit(solution)/shard_map/dot_general | solution.py:212
  207.9 1.6 fusion.27
  (225 shorter events, 63.8 us)
Async XLA Ops:
  5.1 33.2 %collective-permute-start.3 = (bf16[368,1280]{1,0:T(8,128)(2,1)}, bf16[368,1280]{1,0:T(8,128)(2,1)}, u32[]{:S(2)}, u32[]{:S(2)}) collective-permute-start(bf16[368,1280]{1,0:T(8,128)(2,1)} %fusion.39), channel_id=1, source_target_pairs={{0,4},{4,8},{8,12},{12,14},{14,10},{10,6},{6,2},{2,0},{1,5},{5,9},... | collective-permute-start | bytes 2826248 | tf_op jit(solution)/shard_map/ppermute | solution.py:80
  8.1 34.2 %collective-permute-start.1 = (bf16[368,1280]{1,0:T(8,128)(2,1)}, bf16[368,1280]{1,0:T(8,128)(2,1)}, u32[]{:S(2)}, u32[]{:S(2)}) collective-permute-start(bf16[368,1280]{1,0:T(8,128)(2,1)} %fusion.39), channel_id=1, source_target_pairs={{0,1},{1,0},{2,3},{3,2},{4,5},{5,4},{6,7},{7,6},{8,9},{9,8},{10,11... | collective-permute-start | bytes 2826248 | tf_op jit(solution)/shard_map/ppermute | solution.py:155
  9.1 30.8 %collective-permute-start.5 = (bf16[368,1280]{1,0:T(8,128)(2,1)}, bf16[368,1280]{1,0:T(8,128)(2,1)}, u32[]{:S(2)}, u32[]{:S(2)}) collective-permute-start(bf16[368,1280]{1,0:T(8,128)(2,1)} %fusion.40), channel_id=1, source_target_pairs={{0,2},{4,0},{8,4},{12,8},{14,12},{10,14},{6,10},{2,6},{1,3},{5,1},... | collective-permute-start | bytes 2826248 | tf_op jit(solution)/shard_map/ppermute | solution.py:80
  9.1 34.2 %collective-permute-start.2 = (bf16[368,1280]{1,0:T(8,128)(2,1)}, bf16[368,1280]{1,0:T(8,128)(2,1)}, u32[]{:S(2)}, u32[]{:S(2)}) collective-permute-start(bf16[368,1280]{1,0:T(8,128)(2,1)} %fusion.40), channel_id=1, source_target_pairs={{0,1},{1,0},{2,3},{3,2},{4,5},{5,4},{6,7},{7,6},{8,9},{9,8},{10,11... | collective-permute-start | bytes 2826248 | tf_op jit(solution)/shard_map/ppermute | solution.py:155
  9.6 77.0 %collective-permute-start = (bf16[384,4096]{1,0:T(8,128)(2,1)}, bf16[384,4096]{1,0:T(8,128)(2,1)}, u32[]{:S(2)}, u32[]{:S(2)}) collective-permute-start(bf16[384,4096]{1,0:T(8,128)(2,1)} %param.11), channel_id=1, source_target_pairs={{0,16},{16,0},{1,17},{17,1},{2,18},{18,2},{3,19},{19,3},{4,20},{20... | collective-permute-start | bytes 9437192 | tf_op jit(solution)/shard_map/ppermute | solution.py:106
  38.3 23.0 %collective-permute-start.7 = (bf16[368,1280]{1,0:T(8,128)(2,1)}, bf16[368,1280]{1,0:T(8,128)(2,1)S(1)}, u32[]{:S(2)}, u32[]{:S(2)}) collective-permute-start(bf16[368,1280]{1,0:T(8,128)(2,1)} %collective-permute-done.3), channel_id=1, source_target_pairs={{0,4},{4,8},{8,12},{12,14},{14,10},{10,6},{6,2},{2,0},{1,5},{5,9},... | collective-permute-start | bytes 2826248 | tf_op jit(solution)/shard_map/ppermute | solution.py:80
  39.9 23.0 %collective-permute-start.9 = (bf16[368,1280]{1,0:T(8,128)(2,1)}, bf16[368,1280]{1,0:T(8,128)(2,1)S(1)}, u32[]{:S(2)}, u32[]{:S(2)}) collective-permute-start(bf16[368,1280]{1,0:T(8,128)(2,1)} %collective-permute-done.5), channel_id=1, source_target_pairs={{0,2},{4,0},{8,4},{12,8},{14,12},{10,14},{6,10},{2,6},{1,3},{5,1},... | collective-permute-start | bytes 2826248 | tf_op jit(solution)/shard_map/ppermute | solution.py:80
  61.3 22.0 %collective-permute-start.11 = (bf16[368,1280]{1,0:T(8,128)(2,1)S(1)}, bf16[368,1280]{1,0:T(8,128)(2,1)S(1)}, u32[]{:S(2)}, u32[]{:S(2)}) collective-permute-start(bf16[368,1280]{1,0:T(8,128)(2,1)S(1)} %collective-permute-done.7), channel_id=1, source_target_pairs={{0,4},{4,8},{8,12},{12,14},{14,10},{10,6},{6,2},{2,0},{1,5},{5,9},... | collective-permute-start | bytes 2826248 | tf_op jit(solution)/shard_map/ppermute | solution.py:80
  62.9 22.1 %collective-permute-start.13 = (bf16[368,1280]{1,0:T(8,128)(2,1)S(1)}, bf16[368,1280]{1,0:T(8,128)(2,1)S(1)}, u32[]{:S(2)}, u32[]{:S(2)}) collective-permute-start(bf16[368,1280]{1,0:T(8,128)(2,1)S(1)} %collective-permute-done.9), channel_id=1, source_target_pairs={{0,2},{4,0},{8,4},{12,8},{14,12},{10,14},{6,10},{2,6},{1,3},{5,1},... | collective-permute-start | bytes 2826248 | tf_op jit(solution)/shard_map/ppermute | solution.py:80
  63.6 22.1 %collective-permute-start.10 = (bf16[368,1280]{1,0:T(8,128)(2,1)S(1)}, bf16[368,1280]{1,0:T(8,128)(2,1)S(1)}, u32[]{:S(2)}, u32[]{:S(2)}) collective-permute-start(bf16[368,1280]{1,0:T(8,128)(2,1)S(1)} %collective-permute-done.9), channel_id=1, source_target_pairs={{0,1},{1,0},{2,3},{3,2},{4,5},{5,4},{6,7},{7,6},{8,9},{9,8},{10,11... | collective-permute-start | bytes 2826248 | tf_op jit(solution)/shard_map/ppermute | solution.py:155
  83.3 22.8 %collective-permute-start.15 = (bf16[368,1280]{1,0:T(8,128)(2,1)S(1)}, bf16[368,1280]{1,0:T(8,128)(2,1)S(1)}, u32[]{:S(2)}, u32[]{:S(2)}) collective-permute-start(bf16[368,1280]{1,0:T(8,128)(2,1)S(1)} %collective-permute-done.11), channel_id=1, source_target_pairs={{0,4},{4,8},{8,12},{12,14},{14,10},{10,6},{6,2},{2,0},{1,5},{5,9},... | collective-permute-start | bytes 2826248 | tf_op jit(solution)/shard_map/ppermute | solution.py:80
  85.0 24.4 %collective-permute-start.12 = (bf16[368,1280]{1,0:T(8,128)(2,1)S(1)}, bf16[368,1280]{1,0:T(8,128)(2,1)}, u32[]{:S(2)}, u32[]{:S(2)}) collective-permute-start(bf16[368,1280]{1,0:T(8,128)(2,1)S(1)} %collective-permute-done.11), channel_id=1, source_target_pairs={{0,1},{1,0},{2,3},{3,2},{4,5},{5,4},{6,7},{7,6},{8,9},{9,8},{10,11... | collective-permute-start | bytes 2826248 | tf_op jit(solution)/shard_map/ppermute | solution.py:155
  85.1 23.3 %collective-permute-start.17 = (bf16[368,1280]{1,0:T(8,128)(2,1)S(1)}, bf16[368,1280]{1,0:T(8,128)(2,1)S(1)}, u32[]{:S(2)}, u32[]{:S(2)}) collective-permute-start(bf16[368,1280]{1,0:T(8,128)(2,1)S(1)} %collective-permute-done.13), channel_id=1, source_target_pairs={{0,2},{4,0},{8,4},{12,8},{14,12},{10,14},{6,10},{2,6},{1,3},{5,1},... | collective-permute-start | bytes 2826248 | tf_op jit(solution)/shard_map/ppermute | solution.py:80
  85.7 26.8 %collective-permute-start.14 = (bf16[368,1280]{1,0:T(8,128)(2,1)S(1)}, bf16[368,1280]{1,0:T(8,128)(2,1)}, u32[]{:S(2)}, u32[]{:S(2)}) collective-permute-start(bf16[368,1280]{1,0:T(8,128)(2,1)S(1)} %collective-permute-done.13), channel_id=1, source_target_pairs={{0,1},{1,0},{2,3},{3,2},{4,5},{5,4},{6,7},{7,6},{8,9},{9,8},{10,11... | collective-permute-start | bytes 2826248 | tf_op jit(solution)/shard_map/ppermute | solution.py:155
  106.1 23.1 %collective-permute-start.19 = (bf16[368,1280]{1,0:T(8,128)(2,1)S(1)}, bf16[368,1280]{1,0:T(8,128)(2,1)S(1)}, u32[]{:S(2)}, u32[]{:S(2)}) collective-permute-start(bf16[368,1280]{1,0:T(8,128)(2,1)S(1)} %collective-permute-done.15), channel_id=1, source_target_pairs={{0,4},{4,8},{8,12},{12,14},{14,10},{10,6},{6,2},{2,0},{1,5},{5,9},... | collective-permute-start | bytes 2826248 | tf_op jit(solution)/shard_map/ppermute | solution.py:80
  107.7 24.2 %collective-permute-start.16 = (bf16[368,1280]{1,0:T(8,128)(2,1)S(1)}, bf16[368,1280]{1,0:T(8,128)(2,1)S(1)}, u32[]{:S(2)}, u32[]{:S(2)}) collective-permute-start(bf16[368,1280]{1,0:T(8,128)(2,1)S(1)} %collective-permute-done.15), channel_id=1, source_target_pairs={{0,1},{1,0},{2,3},{3,2},{4,5},{5,4},{6,7},{7,6},{8,9},{9,8},{10,11... | collective-permute-start | bytes 2826248 | tf_op jit(solution)/shard_map/ppermute | solution.py:155
  108.4 22.6 %collective-permute-start.21 = (bf16[368,1280]{1,0:T(8,128)(2,1)S(1)}, bf16[368,1280]{1,0:T(8,128)(2,1)S(1)}, u32[]{:S(2)}, u32[]{:S(2)}) collective-permute-start(bf16[368,1280]{1,0:T(8,128)(2,1)S(1)} %collective-permute-done.17), channel_id=1, source_target_pairs={{0,2},{4,0},{8,4},{12,8},{14,12},{10,14},{6,10},{2,6},{1,3},{5,1},... | collective-permute-start | bytes 2826248 | tf_op jit(solution)/shard_map/ppermute | solution.py:80
  109.4 23.6 %collective-permute-start.18 = (bf16[368,1280]{1,0:T(8,128)(2,1)S(1)}, bf16[368,1280]{1,0:T(8,128)(2,1)S(1)}, u32[]{:S(2)}, u32[]{:S(2)}) collective-permute-start(bf16[368,1280]{1,0:T(8,128)(2,1)S(1)} %collective-permute-done.17), channel_id=1, source_target_pairs={{0,1},{1,0},{2,3},{3,2},{4,5},{5,4},{6,7},{7,6},{8,9},{9,8},{10,11... | collective-permute-start | bytes 2826248 | tf_op jit(solution)/shard_map/ppermute | solution.py:155
  129.2 22.2 %collective-permute-start.23 = (bf16[368,1280]{1,0:T(8,128)(2,1)S(1)}, bf16[368,1280]{1,0:T(8,128)(2,1)S(1)}, u32[]{:S(2)}, u32[]{:S(2)}) collective-permute-start(bf16[368,1280]{1,0:T(8,128)(2,1)S(1)} %collective-permute-done.19), channel_id=1, source_target_pairs={{0,4},{4,8},{8,12},{12,14},{14,10},{10,6},{6,2},{2,0},{1,5},{5,9},... | collective-permute-start | bytes 2826248 | tf_op jit(solution)/shard_map/ppermute | solution.py:80
  130.8 24.7 %collective-permute-start.20 = (bf16[368,1280]{1,0:T(8,128)(2,1)S(1)}, bf16[368,1280]{1,0:T(8,128)(2,1)S(1)}, u32[]{:S(2)}, u32[]{:S(2)}) collective-permute-start(bf16[368,1280]{1,0:T(8,128)(2,1)S(1)} %collective-permute-done.19), channel_id=1, source_target_pairs={{0,1},{1,0},{2,3},{3,2},{4,5},{5,4},{6,7},{7,6},{8,9},{9,8},{10,11... | collective-permute-start | bytes 2826248 | tf_op jit(solution)/shard_map/ppermute | solution.py:155
  131.0 23.0 %collective-permute-start.25 = (bf16[368,1280]{1,0:T(8,128)(2,1)S(1)}, bf16[368,1280]{1,0:T(8,128)(2,1)S(1)}, u32[]{:S(2)}, u32[]{:S(2)}) collective-permute-start(bf16[368,1280]{1,0:T(8,128)(2,1)S(1)} %collective-permute-done.21), channel_id=1, source_target_pairs={{0,2},{4,0},{8,4},{12,8},{14,12},{10,14},{6,10},{2,6},{1,3},{5,1},... | collective-permute-start | bytes 2826248 | tf_op jit(solution)/shard_map/ppermute | solution.py:80
  132.0 24.1 %collective-permute-start.22 = (bf16[368,1280]{1,0:T(8,128)(2,1)S(1)}, bf16[368,1280]{1,0:T(8,128)(2,1)S(1)}, u32[]{:S(2)}, u32[]{:S(2)}) collective-permute-start(bf16[368,1280]{1,0:T(8,128)(2,1)S(1)} %collective-permute-done.21), channel_id=1, source_target_pairs={{0,1},{1,0},{2,3},{3,2},{4,5},{5,4},{6,7},{7,6},{8,9},{9,8},{10,11... | collective-permute-start | bytes 2826248 | tf_op jit(solution)/shard_map/ppermute | solution.py:155
  154.1 22.2 %collective-permute-start.29 = (bf16[368,1280]{1,0:T(8,128)(2,1)S(1)}, bf16[368,1280]{1,0:T(8,128)(2,1)S(1)}, u32[]{:S(2)}, u32[]{:S(2)}) collective-permute-start(bf16[368,1280]{1,0:T(8,128)(2,1)S(1)} %collective-permute-done.25), channel_id=1, source_target_pairs={{0,2},{4,0},{8,4},{12,8},{14,12},{10,14},{6,10},{2,6},{1,3},{5,1},... | collective-permute-start | bytes 2826248 | tf_op jit(solution)/shard_map/ppermute | solution.py:80
  155.5 22.2 %collective-permute-start.26 = (bf16[368,1280]{1,0:T(8,128)(2,1)S(1)}, bf16[368,1280]{1,0:T(8,128)(2,1)S(1)}, u32[]{:S(2)}, u32[]{:S(2)}) collective-permute-start(bf16[368,1280]{1,0:T(8,128)(2,1)S(1)} %collective-permute-done.25), channel_id=1, source_target_pairs={{0,1},{1,0},{2,3},{3,2},{4,5},{5,4},{6,7},{7,6},{8,9},{9,8},{10,11... | collective-permute-start | bytes 2826248 | tf_op jit(solution)/shard_map/ppermute | solution.py:155
  (35 other events, 295.0 us)

commit v15 on v14

--- a/solution.py
+++ b/solution.py
@@ -193,9 +193,6 @@
                 term = weight * adapter_steps[h][s][slot].astype(jnp.float32)[None]
                 chosen = term if chosen is None else chosen + term
         per_half.append(chosen.astype(jnp.bfloat16))
-    down_selected = jnp.concatenate(
-        [per_half[0][:, :dh], per_half[1][:, :dh]], axis=1
-    ).reshape((prompt_count,) + adapter_down.shape[1:])
     up_query_selected = jnp.concatenate(
         [per_half[0][:, dh : dh + uh], per_half[1][:, dh : dh + uh]], axis=1
     ).reshape((prompt_count,) + adapter_up_query.shape[1:])
@@ -208,12 +205,19 @@
 
     lengths = packed_lengths[0]
     member, position, owner, slot_index = layout(lengths, row_number)
-    rank_size = down_selected.shape[2]
-    partial_value = lax.dot_general(
-        normed_part,
-        down_selected.reshape(prompt_count * 3 * rank_size, feature_cols),
-        (((1,), (1,)), ((), ())),
-        preferred_element_type=jnp.float32,
+    rank_size = adapter_down.shape[2]
+    half_maps = adapter_down.size // feature_cols // 2
+    partial_value = jnp.concatenate(
+        [
+            lax.dot_general(
+                normed_part,
+                per_half[h][:, :dh].reshape(prompt_count * half_maps, feature_cols),
+                (((1,), (1,)), ((), ())),
+                preferred_element_type=jnp.float32,
+            ).reshape(row_number, prompt_count, half_maps)
+            for h in range(2)
+        ],
+        axis=2,
     )
     partial_value = partial_value.reshape(row_number, prompt_count, 3, rank_size)
     masked = jnp.sum(partial_value * member[:, :, None, None], axis=1).reshape(

time: 212 us -> 215 us (1.014)
  local copies, waits for them, and re-layouts: 17.9 us -> 23.2 us
  other arithmetic: 28.1 us -> 24.7 us
  waiting for transfers between devices: 89.7 us -> 92.6 us
  matrix products: 32.4 us -> 30.2 us
    ppermute x14, waiting for transfers between devices: 89.1 us -> 92.6 us  [ring_gather(): current = lax.ppermute(current, 'chip', pairs)]
    dot_general x32, matrix products: 24.8 us -> 22 us  [shards(): part = jnp.dot(lhs, p[:half_rows], preferred_element_type=jnp.float32)]
    dot_general x1 -> x2, local copies, waits for them, and re-layouts: 2.47 us -> 4.75 us  [shards(): lax.dot_general(normed_part, per_half[h][:, :dh].reshape(prompt_count * h...]
    dot_general x1 -> x2, matrix products: 3.69 us -> 4.36 us  [shards(): lax.dot_general(normed_part, per_half[h][:, :dh].reshape(prompt_count * h...]
    unnamed x55 -> x59, local copies, waits for them, and re-layouts: 7.12 us -> 7 us
  transfers between devices with their start and end apart: 32 -> 32, of which waited for: 10 -> 9; matrix products, arithmetic and copies ran while one was open for 23% -> 22% of each run, Pallas kernels for 0% -> 0%
where the time goes in v15:
time: 215 us; the launch traced here: 214 us
  waiting for transfers between devices  92.6 us (43%)
  matrix products  30.2 us (14%)
  other arithmetic  24.7 us (11%)
  local copies, waits for them, and re-layouts  23.2 us (11%)
  between operations  22.9 us (11%)
  starting transfers between devices  20.2 us (9%)
    ppermute x14, waiting for transfers between devices, ring_gather(): current = lax.ppermute(current, 'chip', pairs)  92.6 us
    dot_general x32, matrix products, shards(): part = jnp.dot(lhs, p[:half_rows], preferred_element_type=jnp.float32)  22 us
    ppermute x14, starting transfers between devices, ring_gather(): current = lax.ppermute(current, 'chip', pairs)  15.4 us
    unnamed x59, local copies, waits for them, and re-layouts  7 us
    convert_element_type x31, other arithmetic, shards(): term = weight * adapter_steps[h][s][slot].astype(jnp.float32)[None]  4.98 us
    dot_general x2, local copies, waits for them, and re-layouts, shards(): lax.dot_general(normed_part, per_half[h][:, :dh].reshape(prompt_count * h...  4.75 us
    convert_element_type x2, other arithmetic, shards(): per_half.append(chosen.astype(jnp.bfloat16))  4.73 us
    dot_general x2, matrix products, shards(): lax.dot_general(normed_part, per_half[h][:, :dh].reshape(prompt_count * h...  4.36 us
  transfers between devices with their start and end apart: 32, of which 9 were waited for; matrix products, arithmetic and copies ran while one was open for 22% of the time, Pallas kernels for 0%

profile of v15, /device:TPU:0, one launch (start us, length us, event | category | flops | bytes accessed | tf_op | source)
XLA Modules:
  0.0 213.8 jit_solution(13848804900815986648)
XLA Ops:
  4.1 3.1 %collective-permute-start.3 = (bf16[368,1280]{1,0:T(8,128)(2,1)S(1)}, bf16[368,1280]{1,0:T(8,128)(2,1)}, u32[]{:S(2)}, u32[]{:S(2)}) collective-permute-start(bf16[368,1280]{1,0:T(8,128)(2,1)S(1)} %fusion.36), channel_id=1, source_target_pairs={{0,4},{4,8},{8,12},{12,14},{14,10},{10,6},{6,2},{2,0},{1,5},{5,9},... | collective-permute-start | bytes 2826248 | tf_op jit(solution)/shard_map/ppermute | solution.py:80
  8.7 1.7 collective-permute-start
  37.5 1.6 collective-permute-start.7
  44.1 16.4 %collective-permute-done.7 = bf16[368,1280]{1,0:T(8,128)(2,1)S(1)} collective-permute-done((bf16[368,1280]{1,0:T(8,128)(2,1)}, bf16[368,1280]{1,0:T(8,128)(2,1)S(1)}, u32[]{:S(2)}, u32[]{:S(2)}) %collective-permute-start.7) | collective-permute-done | bytes 942112 | tf_op jit(solution)/shard_map/ppermute | solution.py:80
  63.4 19.2 %collective-permute-done.11 = bf16[368,1280]{1,0:T(8,128)(2,1)S(1)} collective-permute-done((bf16[368,1280]{1,0:T(8,128)(2,1)S(1)}, bf16[368,1280]{1,0:T(8,128)(2,1)S(1)}, u32[]{:S(2)}, u32[]{:S(2)}) %collective-permute-start.11) | collective-permute-done | bytes 942112 | tf_op jit(solution)/shard_map/ppermute | solution.py:80
  85.8 3.3 %broadcast_select_fusion.1 = (bf16[384,4096]{1,0:T(8,128)(2,1)S(1)}, bf16[384,4096]{1,0:T(8,128)(2,1)S(1)}) fusion(bf16[384,4096]{1,0:T(8,128)(2,1)} %param.11, bf16[384,4096]{1,0:T(8,128)(2,1)} %collective-permute-done, pred[]{:T(512)S(6)} %eq.266), kind=kLoop, calls=%fused_computation.17 | loop fusion | flops 3145728 | bytes 12582913 | tf_op jit(solution)/shard_map/select_n | solution.py:107
  90.5 1.8 fusion.2
  93.2 2.0 fusion.86
  104.6 1.6 collective-permute-start.19
  110.1 17.2 %collective-permute-done.19 = bf16[368,1280]{1,0:T(8,128)(2,1)S(1)} collective-permute-done((bf16[368,1280]{1,0:T(8,128)(2,1)S(1)}, bf16[368,1280]{1,0:T(8,128)(2,1)S(1)}, u32[]{:S(2)}, u32[]{:S(2)}) %collective-permute-start.19) | collective-permute-done | bytes 942112 | tf_op jit(solution)/shard_map/ppermute | solution.py:80
  127.4 1.6 collective-permute-start.23
  132.7 16.6 %collective-permute-done.23 = bf16[368,1280]{1,0:T(8,128)(2,1)S(1)} collective-permute-done((bf16[368,1280]{1,0:T(8,128)(2,1)S(1)}, bf16[368,1280]{1,0:T(8,128)(2,1)S(1)}, u32[]{:S(2)}, u32[]{:S(2)}) %collective-permute-start.23) | collective-permute-done | bytes 942112 | tf_op jit(solution)/shard_map/ppermute | solution.py:80
  149.2 1.6 collective-permute-start.27
  154.8 15.4 %collective-permute-done.27 = bf16[368,1280]{1,0:T(8,128)(2,1)S(1)} collective-permute-done((bf16[368,1280]{1,0:T(8,128)(2,1)S(1)}, bf16[368,1280]{1,0:T(8,128)(2,1)S(1)}, u32[]{:S(2)}, u32[]{:S(2)}) %collective-permute-start.27) | collective-permute-done | bytes 942112 | tf_op jit(solution)/shard_map/ppermute | solution.py:80
  170.4 3.8 %collective-permute-done.29 = bf16[368,1280]{1,0:T(8,128)(2,1)S(1)} collective-permute-done((bf16[368,1280]{1,0:T(8,128)(2,1)S(1)}, bf16[368,1280]{1,0:T(8,128)(2,1)S(1)}, u32[]{:S(2)}, u32[]{:S(2)}) %collective-permute-start.29) | collective-permute-done | bytes 942112 | tf_op jit(solution)/shard_map/ppermute | solution.py:80
  175.1 1.8 fusion.43
  176.9 1.7 fusion.10
  179.5 2.4 %add_convert_fusion.1 = bf16[4,112,1024]{2,1,0:T(8,128)(2,1)S(1)} fusion(f32[112,1024]{1,0:T(8,128)S(1)} %slice_convert_fusion.15, f32[4]{0:T(128)S(1)} %get-tuple-element.64, f32[112,1024]{1,0:T(8,128)S(1)} %slice_convert_fusion.16, f32[4]{0:T(128)S(1)} %get-tuple-element.51, f32[112,1024]{1,0:T(8,128)S(1)} %slice_convert_fusion.17, ...), kind=kLoop, calls=%fused_computation.54 | loop fusion | flops 14680064 | bytes 8257792 | tf_op jit(solution)/shard_map/convert_element_type | solution.py:195
  182.9 2.4 %add_convert_fusion = bf16[4,112,1024]{2,1,0:T(8,128)(2,1)S(1)} fusion(f32[112,1024]{1,0:T(8,128)S(1)} %slice_convert_fusion, f32[4]{0:T(128)S(1)} %get-tuple-element.79, f32[112,1024]{1,0:T(8,128)S(1)} %slice_convert_fusion.1, f32[4]{0:T(128)S(1)} %get-tuple-element.66, f32[112,1024]{1,0:T(8,128)S(1)} %slice_convert_fusion.2, f32[4]{0:T(128)S(1)} %get-tuple-element.67, ...), kind=kLoop, calls=%fused_computation.53 | loop fusion | flops 14680064 | bytes 8257792 | tf_op jit(solution)/shard_map/convert_element_type | solution.py:195
  187.3 2.5 %dot_general.153 = bf16[4,24,4096]{2,1,0:T(8,128)(2,1)} reshape(bf16[4,96,1024]{2,1,0:T(8,128)(2,1)} %slice.419) | data formatting | bytes 1572864 | tf_op jit(solution)/shard_map/dot_general | solution.py:212
  189.7 2.3 %dot_general.155 = bf16[4,24,4096]{2,1,0:T(8,128)(2,1)} reshape(bf16[4,96,1024]{2,1,0:T(8,128)(2,1)} %slice.435) | data formatting | bytes 1572864 | tf_op jit(solution)/shard_map/dot_general | solution.py:212
  192.0 3.3 %fusion.7 = f32[384,4,24]{0,2,1:T(8,128)S(1)} fusion(bf16[4,24,4096]{2,1,0:T(8,128)(2,1)} %dot_general.153, bf16[384,8192]{1,0:T(8,128)(2,1)} %copy-done.1, s32[]{:T(128)S(6)} %select_n.529), kind=kOutput, calls=%fused_computation.14 | convolution fusion | flops 301989888 | bytes 4079620 | tf_op jit(solution)/shard_map/dot_general | solution.py:212
  201.0 2.1 reshape.865
  211.0 1.6 fusion.30
  (231 shorter events, 64.1 us)
Async XLA Ops:
  4.1 33.4 %collective-permute-start.3 = (bf16[368,1280]{1,0:T(8,128)(2,1)S(1)}, bf16[368,1280]{1,0:T(8,128)(2,1)}, u32[]{:S(2)}, u32[]{:S(2)}) collective-permute-start(bf16[368,1280]{1,0:T(8,128)(2,1)S(1)} %fusion.36), channel_id=1, source_target_pairs={{0,4},{4,8},{8,12},{12,14},{14,10},{10,6},{6,2},{2,0},{1,5},{5,9},... | collective-permute-start | bytes 2826248 | tf_op jit(solution)/shard_map/ppermute | solution.py:80
  7.2 34.3 %collective-permute-start.1 = (bf16[368,1280]{1,0:T(8,128)(2,1)S(1)}, bf16[368,1280]{1,0:T(8,128)(2,1)}, u32[]{:S(2)}, u32[]{:S(2)}) collective-permute-start(bf16[368,1280]{1,0:T(8,128)(2,1)S(1)} %fusion.36), channel_id=1, source_target_pairs={{0,1},{1,0},{2,3},{3,2},{4,5},{5,4},{6,7},{7,6},{8,9},{9,8},{10,11... | collective-permute-start | bytes 2826248 | tf_op jit(solution)/shard_map/ppermute | solution.py:155
  8.2 30.9 %collective-permute-start.5 = (bf16[368,1280]{1,0:T(8,128)(2,1)}, bf16[368,1280]{1,0:T(8,128)(2,1)}, u32[]{:S(2)}, u32[]{:S(2)}) collective-permute-start(bf16[368,1280]{1,0:T(8,128)(2,1)} %fusion.37), channel_id=1, source_target_pairs={{0,2},{4,0},{8,4},{12,8},{14,12},{10,14},{6,10},{2,6},{1,3},{5,1},... | collective-permute-start | bytes 2826248 | tf_op jit(solution)/shard_map/ppermute | solution.py:80
  8.2 34.4 %collective-permute-start.2 = (bf16[368,1280]{1,0:T(8,128)(2,1)}, bf16[368,1280]{1,0:T(8,128)(2,1)}, u32[]{:S(2)}, u32[]{:S(2)}) collective-permute-start(bf16[368,1280]{1,0:T(8,128)(2,1)} %fusion.37), channel_id=1, source_target_pairs={{0,1},{1,0},{2,3},{3,2},{4,5},{5,4},{6,7},{7,6},{8,9},{9,8},{10,11... | collective-permute-start | bytes 2826248 | tf_op jit(solution)/shard_map/ppermute | solution.py:155
  8.7 77.1 %collective-permute-start = (bf16[384,4096]{1,0:T(8,128)(2,1)}, bf16[384,4096]{1,0:T(8,128)(2,1)}, u32[]{:S(2)}, u32[]{:S(2)}) collective-permute-start(bf16[384,4096]{1,0:T(8,128)(2,1)} %param.11), channel_id=1, source_target_pairs={{0,16},{16,0},{1,17},{17,1},{2,18},{18,2},{3,19},{19,3},{4,20},{20... | collective-permute-start | bytes 9437192 | tf_op jit(solution)/shard_map/ppermute | solution.py:106
  37.5 23.0 %collective-permute-start.7 = (bf16[368,1280]{1,0:T(8,128)(2,1)}, bf16[368,1280]{1,0:T(8,128)(2,1)S(1)}, u32[]{:S(2)}, u32[]{:S(2)}) collective-permute-start(bf16[368,1280]{1,0:T(8,128)(2,1)} %collective-permute-done.3), channel_id=1, source_target_pairs={{0,4},{4,8},{8,12},{12,14},{14,10},{10,6},{6,2},{2,0},{1,5},{5,9},... | collective-permute-start | bytes 2826248 | tf_op jit(solution)/shard_map/ppermute | solution.py:80
  39.1 23.0 %collective-permute-start.9 = (bf16[368,1280]{1,0:T(8,128)(2,1)}, bf16[368,1280]{1,0:T(8,128)(2,1)S(1)}, u32[]{:S(2)}, u32[]{:S(2)}) collective-permute-start(bf16[368,1280]{1,0:T(8,128)(2,1)} %collective-permute-done.5), channel_id=1, source_target_pairs={{0,2},{4,0},{8,4},{12,8},{14,12},{10,14},{6,10},{2,6},{1,3},{5,1},... | collective-permute-start | bytes 2826248 | tf_op jit(solution)/shard_map/ppermute | solution.py:80
  60.5 22.0 %collective-permute-start.11 = (bf16[368,1280]{1,0:T(8,128)(2,1)S(1)}, bf16[368,1280]{1,0:T(8,128)(2,1)S(1)}, u32[]{:S(2)}, u32[]{:S(2)}) collective-permute-start(bf16[368,1280]{1,0:T(8,128)(2,1)S(1)} %collective-permute-done.7), channel_id=1, source_target_pairs={{0,4},{4,8},{8,12},{12,14},{14,10},{10,6},{6,2},{2,0},{1,5},{5,9},... | collective-permute-start | bytes 2826248 | tf_op jit(solution)/shard_map/ppermute | solution.py:80
  62.1 22.1 %collective-permute-start.13 = (bf16[368,1280]{1,0:T(8,128)(2,1)S(1)}, bf16[368,1280]{1,0:T(8,128)(2,1)S(1)}, u32[]{:S(2)}, u32[]{:S(2)}) collective-permute-start(bf16[368,1280]{1,0:T(8,128)(2,1)S(1)} %collective-permute-done.9), channel_id=1, source_target_pairs={{0,2},{4,0},{8,4},{12,8},{14,12},{10,14},{6,10},{2,6},{1,3},{5,1},... | collective-permute-start | bytes 2826248 | tf_op jit(solution)/shard_map/ppermute | solution.py:80
  62.7 22.5 %collective-permute-start.10 = (bf16[368,1280]{1,0:T(8,128)(2,1)S(1)}, bf16[368,1280]{1,0:T(8,128)(2,1)S(1)}, u32[]{:S(2)}, u32[]{:S(2)}) collective-permute-start(bf16[368,1280]{1,0:T(8,128)(2,1)S(1)} %collective-permute-done.9), channel_id=1, source_target_pairs={{0,1},{1,0},{2,3},{3,2},{4,5},{5,4},{6,7},{7,6},{8,9},{9,8},{10,11... | collective-permute-start | bytes 2826248 | tf_op jit(solution)/shard_map/ppermute | solution.py:155
  82.5 22.1 %collective-permute-start.15 = (bf16[368,1280]{1,0:T(8,128)(2,1)S(1)}, bf16[368,1280]{1,0:T(8,128)(2,1)S(1)}, u32[]{:S(2)}, u32[]{:S(2)}) collective-permute-start(bf16[368,1280]{1,0:T(8,128)(2,1)S(1)} %collective-permute-done.11), channel_id=1, source_target_pairs={{0,4},{4,8},{8,12},{12,14},{14,10},{10,6},{6,2},{2,0},{1,5},{5,9},... | collective-permute-start | bytes 2826248 | tf_op jit(solution)/shard_map/ppermute | solution.py:80
  84.2 24.4 %collective-permute-start.12 = (bf16[368,1280]{1,0:T(8,128)(2,1)S(1)}, bf16[368,1280]{1,0:T(8,128)(2,1)S(1)}, u32[]{:S(2)}, u32[]{:S(2)}) collective-permute-start(bf16[368,1280]{1,0:T(8,128)(2,1)S(1)} %collective-permute-done.11), channel_id=1, source_target_pairs={{0,1},{1,0},{2,3},{3,2},{4,5},{5,4},{6,7},{7,6},{8,9},{9,8},{10,11... | collective-permute-start | bytes 2826248 | tf_op jit(solution)/shard_map/ppermute | solution.py:155
  84.3 23.3 %collective-permute-start.17 = (bf16[368,1280]{1,0:T(8,128)(2,1)S(1)}, bf16[368,1280]{1,0:T(8,128)(2,1)S(1)}, u32[]{:S(2)}, u32[]{:S(2)}) collective-permute-start(bf16[368,1280]{1,0:T(8,128)(2,1)S(1)} %collective-permute-done.13), channel_id=1, source_target_pairs={{0,2},{4,0},{8,4},{12,8},{14,12},{10,14},{6,10},{2,6},{1,3},{5,1},... | collective-permute-start | bytes 2826248 | tf_op jit(solution)/shard_map/ppermute | solution.py:80
  85.2 24.4 %collective-permute-start.14 = (bf16[368,1280]{1,0:T(8,128)(2,1)S(1)}, bf16[368,1280]{1,0:T(8,128)(2,1)S(1)}, u32[]{:S(2)}, u32[]{:S(2)}) collective-permute-start(bf16[368,1280]{1,0:T(8,128)(2,1)S(1)} %collective-permute-done.13), channel_id=1, source_target_pairs={{0,1},{1,0},{2,3},{3,2},{4,5},{5,4},{6,7},{7,6},{8,9},{9,8},{10,11... | collective-permute-start | bytes 2826248 | tf_op jit(solution)/shard_map/ppermute | solution.py:155
  104.6 22.8 %collective-permute-start.19 = (bf16[368,1280]{1,0:T(8,128)(2,1)S(1)}, bf16[368,1280]{1,0:T(8,128)(2,1)S(1)}, u32[]{:S(2)}, u32[]{:S(2)}) collective-permute-start(bf16[368,1280]{1,0:T(8,128)(2,1)S(1)} %collective-permute-done.15), channel_id=1, source_target_pairs={{0,4},{4,8},{8,12},{12,14},{14,10},{10,6},{6,2},{2,0},{1,5},{5,9},... | collective-permute-start | bytes 2826248 | tf_op jit(solution)/shard_map/ppermute | solution.py:80
  106.2 24.8 %collective-permute-start.16 = (bf16[368,1280]{1,0:T(8,128)(2,1)S(1)}, bf16[368,1280]{1,0:T(8,128)(2,1)S(1)}, u32[]{:S(2)}, u32[]{:S(2)}) collective-permute-start(bf16[368,1280]{1,0:T(8,128)(2,1)S(1)} %collective-permute-done.15), channel_id=1, source_target_pairs={{0,1},{1,0},{2,3},{3,2},{4,5},{5,4},{6,7},{7,6},{8,9},{9,8},{10,11... | collective-permute-start | bytes 2826248 | tf_op jit(solution)/shard_map/ppermute | solution.py:155
  107.6 22.5 %collective-permute-start.21 = (bf16[368,1280]{1,0:T(8,128)(2,1)S(1)}, bf16[368,1280]{1,0:T(8,128)(2,1)S(1)}, u32[]{:S(2)}, u32[]{:S(2)}) collective-permute-start(bf16[368,1280]{1,0:T(8,128)(2,1)S(1)} %collective-permute-done.17), channel_id=1, source_target_pairs={{0,2},{4,0},{8,4},{12,8},{14,12},{10,14},{6,10},{2,6},{1,3},{5,1},... | collective-permute-start | bytes 2826248 | tf_op jit(solution)/shard_map/ppermute | solution.py:80
  108.6 23.5 %collective-permute-start.18 = (bf16[368,1280]{1,0:T(8,128)(2,1)S(1)}, bf16[368,1280]{1,0:T(8,128)(2,1)S(1)}, u32[]{:S(2)}, u32[]{:S(2)}) collective-permute-start(bf16[368,1280]{1,0:T(8,128)(2,1)S(1)} %collective-permute-done.17), channel_id=1, source_target_pairs={{0,1},{1,0},{2,3},{3,2},{4,5},{5,4},{6,7},{7,6},{8,9},{9,8},{10,11... | collective-permute-start | bytes 2826248 | tf_op jit(solution)/shard_map/ppermute | solution.py:155
  127.4 21.9 %collective-permute-start.23 = (bf16[368,1280]{1,0:T(8,128)(2,1)S(1)}, bf16[368,1280]{1,0:T(8,128)(2,1)S(1)}, u32[]{:S(2)}, u32[]{:S(2)}) collective-permute-start(bf16[368,1280]{1,0:T(8,128)(2,1)S(1)} %collective-permute-done.19), channel_id=1, source_target_pairs={{0,4},{4,8},{8,12},{12,14},{14,10},{10,6},{6,2},{2,0},{1,5},{5,9},... | collective-permute-start | bytes 2826248 | tf_op jit(solution)/shard_map/ppermute | solution.py:80
  129.0 24.7 %collective-permute-start.20 = (bf16[368,1280]{1,0:T(8,128)(2,1)S(1)}, bf16[368,1280]{1,0:T(8,128)(2,1)S(1)}, u32[]{:S(2)}, u32[]{:S(2)}) collective-permute-start(bf16[368,1280]{1,0:T(8,128)(2,1)S(1)} %collective-permute-done.19), channel_id=1, source_target_pairs={{0,1},{1,0},{2,3},{3,2},{4,5},{5,4},{6,7},{7,6},{8,9},{9,8},{10,11... | collective-permute-start | bytes 2826248 | tf_op jit(solution)/shard_map/ppermute | solution.py:155
  130.1 22.1 %collective-permute-start.25 = (bf16[368,1280]{1,0:T(8,128)(2,1)S(1)}, bf16[368,1280]{1,0:T(8,128)(2,1)S(1)}, u32[]{:S(2)}, u32[]{:S(2)}) collective-permute-start(bf16[368,1280]{1,0:T(8,128)(2,1)S(1)} %collective-permute-done.21), channel_id=1, source_target_pairs={{0,2},{4,0},{8,4},{12,8},{14,12},{10,14},{6,10},{2,6},{1,3},{5,1},... | collective-permute-start | bytes 2826248 | tf_op jit(solution)/shard_map/ppermute | solution.py:80
  131.1 23.2 %collective-permute-start.22 = (bf16[368,1280]{1,0:T(8,128)(2,1)S(1)}, bf16[368,1280]{1,0:T(8,128)(2,1)S(1)}, u32[]{:S(2)}, u32[]{:S(2)}) collective-permute-start(bf16[368,1280]{1,0:T(8,128)(2,1)S(1)} %collective-permute-done.21), channel_id=1, source_target_pairs={{0,1},{1,0},{2,3},{3,2},{4,5},{5,4},{6,7},{7,6},{8,9},{9,8},{10,11... | collective-permute-start | bytes 2826248 | tf_op jit(solution)/shard_map/ppermute | solution.py:155
  152.3 21.9 %collective-permute-start.29 = (bf16[368,1280]{1,0:T(8,128)(2,1)S(1)}, bf16[368,1280]{1,0:T(8,128)(2,1)S(1)}, u32[]{:S(2)}, u32[]{:S(2)}) collective-permute-start(bf16[368,1280]{1,0:T(8,128)(2,1)S(1)} %collective-permute-done.25), channel_id=1, source_target_pairs={{0,2},{4,0},{8,4},{12,8},{14,12},{10,14},{6,10},{2,6},{1,3},{5,1},... | collective-permute-start | bytes 2826248 | tf_op jit(solution)/shard_map/ppermute | solution.py:80
  153.6 23.2 %collective-permute-start.26 = (bf16[368,1280]{1,0:T(8,128)(2,1)S(1)}, bf16[368,1280]{1,0:T(8,128)(2,1)S(1)}, u32[]{:S(2)}, u32[]{:S(2)}) collective-permute-start(bf16[368,1280]{1,0:T(8,128)(2,1)S(1)} %collective-permute-done.25), channel_id=1, source_target_pairs={{0,1},{1,0},{2,3},{3,2},{4,5},{5,4},{6,7},{7,6},{8,9},{9,8},{10,11... | collective-permute-start | bytes 2826248 | tf_op jit(solution)/shard_map/ppermute | solution.py:155
  (36 other events, 311.3 us)

commit v16 on v14

--- a/solution.py
+++ b/solution.py
@@ -189,10 +189,12 @@
         chosen = None
         for s in range(n_chip):
             for slot in range(n_lo):
-                weight = (picked_piece == s * n_lo + slot).astype(jnp.float32)[:, None, None]
-                term = weight * adapter_steps[h][s][slot].astype(jnp.float32)[None]
-                chosen = term if chosen is None else chosen + term
-        per_half.append(chosen.astype(jnp.bfloat16))
+                piece = jnp.broadcast_to(
+                    adapter_steps[h][s][slot][None], (prompt_count,) + adapter_steps[h][s][slot].shape
+                )
+                hit = (picked_piece == s * n_lo + slot)[:, None, None]
+                chosen = piece if chosen is None else jnp.where(hit, piece, chosen)
+        per_half.append(chosen)
     down_selected = jnp.concatenate(
         [per_half[0][:, :dh], per_half[1][:, :dh]], axis=1
     ).reshape((prompt_count,) + adapter_down.shape[1:])

time: 212 us -> 222 us (1.047)
  other arithmetic: 28.1 us -> 17.9 us
  local copies, waits for them, and re-layouts: 17.9 us -> 25.8 us
  waiting for transfers between devices: 89.7 us -> 97.3 us
  matrix products: 32.4 us -> 38 us
    convert_element_type x37 -> x0, other arithmetic: 12.9 us -> none  [the longest x31 6.85 us: shards(): term = weight * adapter_steps[h][s][slot].astype(jnp.float32)[None]]
    slice x0 -> x30, local copies, waits for them, and re-layouts: none -> 10.8 us  [shards(): adapter_steps[h].append([p[half_rows:, :query_cols] for p in both])]
    ppermute x14, waiting for transfers between devices: 89.1 us -> 96.7 us  [ring_gather(): current = lax.ppermute(current, 'chip', pairs)]
    dot_general x32, matrix products: 24.8 us -> 30.4 us  [shards(): part = jnp.dot(lhs, p[:half_rows], preferred_element_type=jnp.float32)]
    unnamed x55 -> x47, local copies, waits for them, and re-layouts: 7.12 us -> 4.17 us
  transfers between devices with their start and end apart: 32 -> 32, of which waited for: 10 -> 11; matrix products, arithmetic and copies ran while one was open for 23% -> 26% of each run, Pallas kernels for 0% -> 0%
where the time goes in v16:
time: 222 us; the launch traced here: 221 us
  waiting for transfers between devices  97.3 us (44%)
  matrix products  38 us (17%)
  local copies, waits for them, and re-layouts  25.8 us (12%)
  between operations  22.7 us (10%)
  starting transfers between devices  19.2 us (9%)
  other arithmetic  17.9 us (8%)
    ppermute x14, waiting for transfers between devices, ring_gather(): current = lax.ppermute(current, 'chip', pairs)  96.7 us
    dot_general x32, matrix products, shards(): part = jnp.dot(lhs, p[:half_rows], preferred_element_type=jnp.float32)  30.4 us
    ppermute x14, starting transfers between devices, ring_gather(): current = lax.ppermute(current, 'chip', pairs)  16.2 us
    slice x30, local copies, waits for them, and re-layouts, shards(): adapter_steps[h].append([p[half_rows:, :query_cols] for p in both])  10.8 us
  transfers between devices with their start and end apart: 32, of which 11 were waited for; matrix products, arithmetic and copies ran while one was open for 26% of the time, Pallas kernels for 0%

profile of v16, /device:TPU:0, one launch (start us, length us, event | category | flops | bytes accessed | tf_op | source)
XLA Modules:
  0.0 220.8 jit_solution(15916005838355568631)
XLA Ops:
  4.1 3.1 %collective-permute-start.3 = (bf16[368,1280]{1,0:T(8,128)(2,1)S(1)}, bf16[368,1280]{1,0:T(8,128)(2,1)}, u32[]{:S(2)}, u32[]{:S(2)}) collective-permute-start(bf16[368,1280]{1,0:T(8,128)(2,1)S(1)} %fusion.39), channel_id=1, source_target_pairs={{0,4},{4,8},{8,12},{12,14},{14,10},{10,6},{6,2},{2,0},{1,5},{5,9},... | collective-permute-start | bytes 2826248 | tf_op jit(solution)/shard_map/ppermute | solution.py:80
  11.6 16.5 %collective-permute-done.3 = bf16[368,1280]{1,0:T(8,128)(2,1)} collective-permute-done((bf16[368,1280]{1,0:T(8,128)(2,1)S(1)}, bf16[368,1280]{1,0:T(8,128)(2,1)}, u32[]{:S(2)}, u32[]{:S(2)}) %collective-permute-start.3) | collective-permute-done | bytes 942112 | tf_op jit(solution)/shard_map/ppermute | solution.py:80
  28.0 1.8 collective-permute-start.7
  29.9 3.1 %collective-permute-done.5 = bf16[368,1280]{1,0:T(8,128)(2,1)} collective-permute-done((bf16[368,1280]{1,0:T(8,128)(2,1)}, bf16[368,1280]{1,0:T(8,128)(2,1)}, u32[]{:S(2)}, u32[]{:S(2)}) %collective-permute-start.5) | collective-permute-done | bytes 942112 | tf_op jit(solution)/shard_map/ppermute | solution.py:80
  35.0 15.5 %collective-permute-done.7 = bf16[368,1280]{1,0:T(8,128)(2,1)} collective-permute-done((bf16[368,1280]{1,0:T(8,128)(2,1)}, bf16[368,1280]{1,0:T(8,128)(2,1)}, u32[]{:S(2)}, u32[]{:S(2)}) %collective-permute-start.7) | collective-permute-done | bytes 942112 | tf_op jit(solution)/shard_map/ppermute | solution.py:80
  51.9 3.6 %collective-permute-done.9 = bf16[368,1280]{1,0:T(8,128)(2,1)} collective-permute-done((bf16[368,1280]{1,0:T(8,128)(2,1)}, bf16[368,1280]{1,0:T(8,128)(2,1)}, u32[]{:S(2)}, u32[]{:S(2)}) %collective-permute-start.9) | collective-permute-done | bytes 942112 | tf_op jit(solution)/shard_map/ppermute | solution.py:80
  86.9 1.6 collective-permute-start.15
  93.3 3.3 %broadcast_select_fusion.1 = (bf16[384,4096]{1,0:T(8,128)(2,1)S(1)}, bf16[384,4096]{1,0:T(8,128)(2,1)S(1)}) fusion(bf16[384,4096]{1,0:T(8,128)(2,1)} %param.11, bf16[384,4096]{1,0:T(8,128)(2,1)} %collective-permute-done, pred[]{:T(512)S(6)} %eq.252), kind=kLoop, calls=%fused_computation.16 | loop fusion | flops 3145728 | bytes 12582913 | tf_op jit(solution)/shard_map/select_n | solution.py:107
  98.1 1.8 fusion.2
  100.8 2.0 fusion.89
  105.9 1.5 fusion.82
  115.9 1.6 fusion.18
  117.5 1.6 fusion.17
  119.1 1.6 collective-permute-start.19
  123.7 18.8 %collective-permute-done.19 = bf16[368,1280]{1,0:T(8,128)(2,1)S(1)} collective-permute-done((bf16[368,1280]{1,0:T(8,128)(2,1)S(1)}, bf16[368,1280]{1,0:T(8,128)(2,1)S(1)}, u32[]{:S(2)}, u32[]{:S(2)}) %collective-permute-start.19) | collective-permute-done | bytes 942112 | tf_op jit(solution)/shard_map/ppermute | solution.py:80
  142.5 1.6 collective-permute-start.23
  146.8 18.2 %collective-permute-done.23 = bf16[368,1280]{1,0:T(8,128)(2,1)S(1)} collective-permute-done((bf16[368,1280]{1,0:T(8,128)(2,1)S(1)}, bf16[368,1280]{1,0:T(8,128)(2,1)S(1)}, u32[]{:S(2)}, u32[]{:S(2)}) %collective-permute-start.23) | collective-permute-done | bytes 942112 | tf_op jit(solution)/shard_map/ppermute | solution.py:80
  164.9 1.6 collective-permute-start.27
  169.9 16.7 %collective-permute-done.27 = bf16[368,1280]{1,0:T(8,128)(2,1)S(1)} collective-permute-done((bf16[368,1280]{1,0:T(8,128)(2,1)S(1)}, bf16[368,1280]{1,0:T(8,128)(2,1)S(1)}, u32[]{:S(2)}, u32[]{:S(2)}) %collective-permute-start.27) | collective-permute-done | bytes 942112 | tf_op jit(solution)/shard_map/ppermute | solution.py:80
  186.6 3.3 %collective-permute-done.29 = bf16[368,1280]{1,0:T(8,128)(2,1)S(1)} collective-permute-done((bf16[368,1280]{1,0:T(8,128)(2,1)S(1)}, bf16[368,1280]{1,0:T(8,128)(2,1)S(1)}, u32[]{:S(2)}, u32[]{:S(2)}) %collective-permute-start.29) | collective-permute-done | bytes 942112 | tf_op jit(solution)/shard_map/ppermute | solution.py:80
  191.3 1.8 fusion.9
  201.4 2.5 %dot_general.148 = bf16[4,3,16,4096]{3,2,1,0:T(8,128)(2,1)} reshape(bf16[4,192,1024]{2,1,0:T(8,128)(2,1)S(1)} %pad_maximum_fusion.1) | data formatting | bytes 3145728 | tf_op jit(solution)/shard_map/dot_general | solution.py:214
  203.9 3.7 %fusion.35 = f32[384,3,16]{0,2,1:T(8,128)S(1)} fusion(bf16[4,3,16,4096]{3,2,1,0:T(8,128)(2,1)} %dot_general.148, bf16[384,8192]{1,0:T(8,128)(2,1)} %copy-done.1, s32[]{:T(128)S(6)} %select_n.608, f32[384,4]{0,1:T(4,128)S(1)} %fusion.182), kind=kOutput, calls=%fused_computation.64 | convolution fusion | flops 604108800 | bytes 4798468 | tf_op jit(solution)/shard_map/dot_general | solution.py:214
  218.1 1.6 fusion.27
  (217 shorter events, 69.8 us)
Async XLA Ops:
  4.1 24.0 %collective-permute-start.3 = (bf16[368,1280]{1,0:T(8,128)(2,1)S(1)}, bf16[368,1280]{1,0:T(8,128)(2,1)}, u32[]{:S(2)}, u32[]{:S(2)}) collective-permute-start(bf16[368,1280]{1,0:T(8,128)(2,1)S(1)} %fusion.39), channel_id=1, source_target_pairs={{0,4},{4,8},{8,12},{12,14},{14,10},{10,6},{6,2},{2,0},{1,5},{5,9},... | collective-permute-start | bytes 2826248 | tf_op jit(solution)/shard_map/ppermute | solution.py:80
  7.1 22.7 %collective-permute-start.1 = (bf16[368,1280]{1,0:T(8,128)(2,1)S(1)}, bf16[368,1280]{1,0:T(8,128)(2,1)}, u32[]{:S(2)}, u32[]{:S(2)}) collective-permute-start(bf16[368,1280]{1,0:T(8,128)(2,1)S(1)} %fusion.39), channel_id=1, source_target_pairs={{0,1},{1,0},{2,3},{3,2},{4,5},{5,4},{6,7},{7,6},{8,9},{9,8},{10,11... | collective-permute-start | bytes 2826248 | tf_op jit(solution)/shard_map/ppermute | solution.py:155
  7.1 86.2 %collective-permute-start = (bf16[384,4096]{1,0:T(8,128)(2,1)}, bf16[384,4096]{1,0:T(8,128)(2,1)}, u32[]{:S(2)}, u32[]{:S(2)}) collective-permute-start(bf16[384,4096]{1,0:T(8,128)(2,1)} %param.11), channel_id=1, source_target_pairs={{0,16},{16,0},{1,17},{17,1},{2,18},{18,2},{3,19},{19,3},{4,20},{20... | collective-permute-start | bytes 9437192 | tf_op jit(solution)/shard_map/ppermute | solution.py:106
  9.7 23.3 %collective-permute-start.5 = (bf16[368,1280]{1,0:T(8,128)(2,1)}, bf16[368,1280]{1,0:T(8,128)(2,1)}, u32[]{:S(2)}, u32[]{:S(2)}) collective-permute-start(bf16[368,1280]{1,0:T(8,128)(2,1)} %fusion.40), channel_id=1, source_target_pairs={{0,2},{4,0},{8,4},{12,8},{14,12},{10,14},{6,10},{2,6},{1,3},{5,1},... | collective-permute-start | bytes 2826248 | tf_op jit(solution)/shard_map/ppermute | solution.py:80
  10.1 23.3 %collective-permute-start.2 = (bf16[368,1280]{1,0:T(8,128)(2,1)}, bf16[368,1280]{1,0:T(8,128)(2,1)}, u32[]{:S(2)}, u32[]{:S(2)}) collective-permute-start(bf16[368,1280]{1,0:T(8,128)(2,1)} %fusion.40), channel_id=1, source_target_pairs={{0,1},{1,0},{2,3},{3,2},{4,5},{5,4},{6,7},{7,6},{8,9},{9,8},{10,11... | collective-permute-start | bytes 2826248 | tf_op jit(solution)/shard_map/ppermute | solution.py:155
  33.0 22.5 %collective-permute-start.9 = (bf16[368,1280]{1,0:T(8,128)(2,1)}, bf16[368,1280]{1,0:T(8,128)(2,1)}, u32[]{:S(2)}, u32[]{:S(2)}) collective-permute-start(bf16[368,1280]{1,0:T(8,128)(2,1)} %collective-permute-done.5), channel_id=1, source_target_pairs={{0,2},{4,0},{8,4},{12,8},{14,12},{10,14},{6,10},{2,6},{1,3},{5,1},... | collective-permute-start | bytes 2826248 | tf_op jit(solution)/shard_map/ppermute | solution.py:80
  33.5 22.5 %collective-permute-start.6 = (bf16[368,1280]{1,0:T(8,128)(2,1)}, bf16[368,1280]{1,0:T(8,128)(2,1)}, u32[]{:S(2)}, u32[]{:S(2)}) collective-permute-start(bf16[368,1280]{1,0:T(8,128)(2,1)} %collective-permute-done.5), channel_id=1, source_target_pairs={{0,1},{1,0},{2,3},{3,2},{4,5},{5,4},{6,7},{7,6},{8,9},{9,8},{10,11... | collective-permute-start | bytes 2826248 | tf_op jit(solution)/shard_map/ppermute | solution.py:155
  50.4 36.5 %collective-permute-start.11 = (bf16[368,1280]{1,0:T(8,128)(2,1)}, bf16[368,1280]{1,0:T(8,128)(2,1)}, u32[]{:S(2)}, u32[]{:S(2)}) collective-permute-start(bf16[368,1280]{1,0:T(8,128)(2,1)} %collective-permute-done.7), channel_id=1, source_target_pairs={{0,4},{4,8},{8,12},{12,14},{14,10},{10,6},{6,2},{2,0},{1,5},{5,9},... | collective-permute-start | bytes 2826248 | tf_op jit(solution)/shard_map/ppermute | solution.py:80
  51.9 38.9 %collective-permute-start.8 = (bf16[368,1280]{1,0:T(8,128)(2,1)}, bf16[368,1280]{1,0:T(8,128)(2,1)}, u32[]{:S(2)}, u32[]{:S(2)}) collective-permute-start(bf16[368,1280]{1,0:T(8,128)(2,1)} %collective-permute-done.7), channel_id=1, source_target_pairs={{0,1},{1,0},{2,3},{3,2},{4,5},{5,4},{6,7},{7,6},{8,9},{9,8},{10,11... | collective-permute-start | bytes 2826248 | tf_op jit(solution)/shard_map/ppermute | solution.py:155
  55.5 34.1 %collective-permute-start.13 = (bf16[368,1280]{1,0:T(8,128)(2,1)}, bf16[368,1280]{1,0:T(8,128)(2,1)}, u32[]{:S(2)}, u32[]{:S(2)}) collective-permute-start(bf16[368,1280]{1,0:T(8,128)(2,1)} %collective-permute-done.9), channel_id=1, source_target_pairs={{0,2},{4,0},{8,4},{12,8},{14,12},{10,14},{6,10},{2,6},{1,3},{5,1},... | collective-permute-start | bytes 2826248 | tf_op jit(solution)/shard_map/ppermute | solution.py:80
  56.0 36.3 %collective-permute-start.10 = (bf16[368,1280]{1,0:T(8,128)(2,1)}, bf16[368,1280]{1,0:T(8,128)(2,1)}, u32[]{:S(2)}, u32[]{:S(2)}) collective-permute-start(bf16[368,1280]{1,0:T(8,128)(2,1)} %collective-permute-done.9), channel_id=1, source_target_pairs={{0,1},{1,0},{2,3},{3,2},{4,5},{5,4},{6,7},{7,6},{8,9},{9,8},{10,11... | collective-permute-start | bytes 2826248 | tf_op jit(solution)/shard_map/ppermute | solution.py:155
  86.9 32.2 %collective-permute-start.15 = (bf16[368,1280]{1,0:T(8,128)(2,1)}, bf16[368,1280]{1,0:T(8,128)(2,1)S(1)}, u32[]{:S(2)}, u32[]{:S(2)}) collective-permute-start(bf16[368,1280]{1,0:T(8,128)(2,1)} %collective-permute-done.11), channel_id=1, source_target_pairs={{0,4},{4,8},{8,12},{12,14},{14,10},{10,6},{6,2},{2,0},{1,5},{5,9},... | collective-permute-start | bytes 2826248 | tf_op jit(solution)/shard_map/ppermute | solution.py:80
  89.6 32.1 %collective-permute-start.12 = (bf16[368,1280]{1,0:T(8,128)(2,1)}, bf16[368,1280]{1,0:T(8,128)(2,1)S(1)}, u32[]{:S(2)}, u32[]{:S(2)}) collective-permute-start(bf16[368,1280]{1,0:T(8,128)(2,1)} %collective-permute-done.11), channel_id=1, source_target_pairs={{0,1},{1,0},{2,3},{3,2},{4,5},{5,4},{6,7},{7,6},{8,9},{9,8},{10,11... | collective-permute-start | bytes 2826248 | tf_op jit(solution)/shard_map/ppermute | solution.py:155
  90.8 30.2 %collective-permute-start.17 = (bf16[368,1280]{1,0:T(8,128)(2,1)}, bf16[368,1280]{1,0:T(8,128)(2,1)S(1)}, u32[]{:S(2)}, u32[]{:S(2)}) collective-permute-start(bf16[368,1280]{1,0:T(8,128)(2,1)} %collective-permute-done.13), channel_id=1, source_target_pairs={{0,2},{4,0},{8,4},{12,8},{14,12},{10,14},{6,10},{2,6},{1,3},{5,1},... | collective-permute-start | bytes 2826248 | tf_op jit(solution)/shard_map/ppermute | solution.py:80
  92.3 29.5 %collective-permute-start.14 = (bf16[368,1280]{1,0:T(8,128)(2,1)}, bf16[368,1280]{1,0:T(8,128)(2,1)S(1)}, u32[]{:S(2)}, u32[]{:S(2)}) collective-permute-start(bf16[368,1280]{1,0:T(8,128)(2,1)} %collective-permute-done.13), channel_id=1, source_target_pairs={{0,1},{1,0},{2,3},{3,2},{4,5},{5,4},{6,7},{7,6},{8,9},{9,8},{10,11... | collective-permute-start | bytes 2826248 | tf_op jit(solution)/shard_map/ppermute | solution.py:155
  119.1 23.3 %collective-permute-start.19 = (bf16[368,1280]{1,0:T(8,128)(2,1)S(1)}, bf16[368,1280]{1,0:T(8,128)(2,1)S(1)}, u32[]{:S(2)}, u32[]{:S(2)}) collective-permute-start(bf16[368,1280]{1,0:T(8,128)(2,1)S(1)} %collective-permute-done.15), channel_id=1, source_target_pairs={{0,4},{4,8},{8,12},{12,14},{14,10},{10,6},{6,2},{2,0},{1,5},{5,9},... | collective-permute-start | bytes 2826248 | tf_op jit(solution)/shard_map/ppermute | solution.py:80
  120.8 24.0 %collective-permute-start.16 = (bf16[368,1280]{1,0:T(8,128)(2,1)S(1)}, bf16[368,1280]{1,0:T(8,128)(2,1)S(1)}, u32[]{:S(2)}, u32[]{:S(2)}) collective-permute-start(bf16[368,1280]{1,0:T(8,128)(2,1)S(1)} %collective-permute-done.15), channel_id=1, source_target_pairs={{0,1},{1,0},{2,3},{3,2},{4,5},{5,4},{6,7},{7,6},{8,9},{9,8},{10,11... | collective-permute-start | bytes 2826248 | tf_op jit(solution)/shard_map/ppermute | solution.py:155
  121.0 23.3 %collective-permute-start.21 = (bf16[368,1280]{1,0:T(8,128)(2,1)S(1)}, bf16[368,1280]{1,0:T(8,128)(2,1)S(1)}, u32[]{:S(2)}, u32[]{:S(2)}) collective-permute-start(bf16[368,1280]{1,0:T(8,128)(2,1)S(1)} %collective-permute-done.17), channel_id=1, source_target_pairs={{0,2},{4,0},{8,4},{12,8},{14,12},{10,14},{6,10},{2,6},{1,3},{5,1},... | collective-permute-start | bytes 2826248 | tf_op jit(solution)/shard_map/ppermute | solution.py:80
  121.7 23.2 %collective-permute-start.18 = (bf16[368,1280]{1,0:T(8,128)(2,1)S(1)}, bf16[368,1280]{1,0:T(8,128)(2,1)S(1)}, u32[]{:S(2)}, u32[]{:S(2)}) collective-permute-start(bf16[368,1280]{1,0:T(8,128)(2,1)S(1)} %collective-permute-done.17), channel_id=1, source_target_pairs={{0,1},{1,0},{2,3},{3,2},{4,5},{5,4},{6,7},{7,6},{8,9},{9,8},{10,11... | collective-permute-start | bytes 2826248 | tf_op jit(solution)/shard_map/ppermute | solution.py:155
  144.0 23.8 %collective-permute-start.20 = (bf16[368,1280]{1,0:T(8,128)(2,1)S(1)}, bf16[368,1280]{1,0:T(8,128)(2,1)S(1)}, u32[]{:S(2)}, u32[]{:S(2)}) collective-permute-start(bf16[368,1280]{1,0:T(8,128)(2,1)S(1)} %collective-permute-done.19), channel_id=1, source_target_pairs={{0,1},{1,0},{2,3},{3,2},{4,5},{5,4},{6,7},{7,6},{8,9},{9,8},{10,11... | collective-permute-start | bytes 2826248 | tf_op jit(solution)/shard_map/ppermute | solution.py:155
  144.3 23.1 %collective-permute-start.25 = (bf16[368,1280]{1,0:T(8,128)(2,1)S(1)}, bf16[368,1280]{1,0:T(8,128)(2,1)S(1)}, u32[]{:S(2)}, u32[]{:S(2)}) collective-permute-start(bf16[368,1280]{1,0:T(8,128)(2,1)S(1)} %collective-permute-done.21), channel_id=1, source_target_pairs={{0,2},{4,0},{8,4},{12,8},{14,12},{10,14},{6,10},{2,6},{1,3},{5,1},... | collective-permute-start | bytes 2826248 | tf_op jit(solution)/shard_map/ppermute | solution.py:80
  144.8 23.2 %collective-permute-start.22 = (bf16[368,1280]{1,0:T(8,128)(2,1)S(1)}, bf16[368,1280]{1,0:T(8,128)(2,1)S(1)}, u32[]{:S(2)}, u32[]{:S(2)}) collective-permute-start(bf16[368,1280]{1,0:T(8,128)(2,1)S(1)} %collective-permute-done.21), channel_id=1, source_target_pairs={{0,1},{1,0},{2,3},{3,2},{4,5},{5,4},{6,7},{7,6},{8,9},{9,8},{10,11... | collective-permute-start | bytes 2826248 | tf_op jit(solution)/shard_map/ppermute | solution.py:155
  166.5 23.4 %collective-permute-start.24 = (bf16[368,1280]{1,0:T(8,128)(2,1)S(1)}, bf16[368,1280]{1,0:T(8,128)(2,1)S(1)}, u32[]{:S(2)}, u32[]{:S(2)}) collective-permute-start(bf16[368,1280]{1,0:T(8,128)(2,1)S(1)} %collective-permute-done.23), channel_id=1, source_target_pairs={{0,1},{1,0},{2,3},{3,2},{4,5},{5,4},{6,7},{7,6},{8,9},{9,8},{10,11... | collective-permute-start | bytes 2826248 | tf_op jit(solution)/shard_map/ppermute | solution.py:155
  167.4 22.5 %collective-permute-start.29 = (bf16[368,1280]{1,0:T(8,128)(2,1)S(1)}, bf16[368,1280]{1,0:T(8,128)(2,1)S(1)}, u32[]{:S(2)}, u32[]{:S(2)}) collective-permute-start(bf16[368,1280]{1,0:T(8,128)(2,1)S(1)} %collective-permute-done.25), channel_id=1, source_target_pairs={{0,2},{4,0},{8,4},{12,8},{14,12},{10,14},{6,10},{2,6},{1,3},{5,1},... | collective-permute-start | bytes 2826248 | tf_op jit(solution)/shard_map/ppermute | solution.py:80
  (31 other events, 334.1 us)
